TPU v7x, 512 devices: a whole 4x4x16 slice. The times are simulated.
512 devices in a mesh: dp: 32 (over z_lo, x), fly: 16 (over z_hi, y, core).
Axes of the slice: x: 4, y: 4, z: 16 (z_hi: 2, z_lo: 8; z = z_hi * 8 + z_lo), core: 2. Of those that a mesh axis runs over, the one named last changes fastest.
Arguments:
- tokens: bfloat16 [4096, 8192], P('dp', 'fly'), may hold values from -6 to 6
- hidden_grad: bfloat16 [4096, 16384], P('dp', 'fly'), may hold values from -6 to 6
- w_up: bfloat16 [6, 256, 16384], P(None, 'dp', 'fly'), may hold values from -0.15625 to 0.15625
- pattern: int32 [6, 64], P(None, 'fly'), may hold values 0 or 1
Outputs:
- input_grad: bfloat16 [4096, 8192], P('dp', 'fly')
- weight_grad: float32 [6, 256, 16384], P(None, 'dp', 'fly')
Inputs may be any that keep to these rules, and one draw needn't show every extreme that they name: pattern[t, f] is 1 where block f of factor t is kept and 0 where it is dropped.
All inputs are finite; a program needn't handle non-finite values.
Results may differ from a plain program's by a relative error of at most 0.0049.
Values may be sent and summed in bfloat16 or wider, within the bound.
No kernel may reach another device: no remote copies, remote signals or barrier semaphores. Data moves between devices by JAX's collectives and lax.ppermute only.
A program may use at most 64 MiB of HBM per device.

v0:
```python
import jax
import jax.numpy as jnp
from jax import lax
from jax.sharding import PartitionSpec as P

BS = 256


def partner_2(block, axis, bit):
    count = lax.axis_size(axis)
    route = []
    for low in range(count):
        high = low | 1 << bit
        if high != low and high < count:
            route += [(low, high), (high, low)]
    return lax.ppermute(block, axis, route)


def shifted(value, axis, by):
    devices = lax.axis_size(axis)
    return lax.ppermute(value, axis, [(i, (i + by) % devices) for i in range(devices)])


def flip_blocks(values, stride):
    if stride == 0:
        return values
    row_count, block_count, inner_size = values.shape
    shaped = values.reshape(row_count, block_count // (2 * stride), 2, stride, inner_size)
    return shaped[:, :, ::-1].reshape(row_count, block_count, inner_size)


def stride_of(factor):
    return 0 if factor == 0 else 2 ** (factor - 1)


def pick_rows(stacked, index, replicas):
    return lax.dynamic_index_in_dim(stacked, index % replicas, 1, keepdims=False)


def body(tokens, hidden_grad, w_up, pattern):
    row_count, local_width = tokens.shape
    factor_count = w_up.shape[0]
    hidden_width = hidden_grad.shape[1]
    local_blocks = local_width // BS
    group_width = hidden_width // local_blocks
    weights = lax.all_gather(w_up, "dp", axis=1, tiled=True)
    keep_cols = jnp.broadcast_to(pattern[:, :, None], (factor_count, pattern.shape[1], BS)).reshape(
        factor_count, hidden_width
    )
    masked = (weights * keep_cols.astype(jnp.bfloat16)[:, None, :]).reshape(
        factor_count, BS, local_blocks, group_width
    )
    keep_f = keep_cols.astype(jnp.float32)
    token_blocks = tokens.reshape(row_count, local_blocks, BS)
    gathered = []
    for factor in range(factor_count):
        stride = stride_of(factor)
        if stride < local_blocks:
            gathered.append(flip_blocks(token_blocks, stride))
        else:
            bit_number = (stride // local_blocks).bit_length() - 1
            partner = partner_2(tokens, "fly", bit_number)
            gathered.append(partner.reshape(row_count, local_blocks, BS))
    pre_act = jnp.zeros((row_count, local_blocks, group_width), jnp.float32)
    for factor in range(factor_count):
        pre_act = pre_act + jnp.einsum(
            "ngb,bgc->ngc", gathered[factor], masked[factor], preferred_element_type=jnp.float32
        )
    squash = jax.nn.sigmoid(pre_act)
    derivative = squash * (1.0 + pre_act * (1.0 - squash))
    grad_pre = (
        hidden_grad.reshape(row_count, local_blocks, group_width).astype(jnp.float32) * derivative
    ).astype(jnp.bfloat16)
    input_total = jnp.zeros((row_count, local_blocks, BS), jnp.float32)
    for factor in range(factor_count):
        stride = stride_of(factor)
        contrib = jnp.einsum(
            "ngc,bgc->ngb", grad_pre, masked[factor], preferred_element_type=jnp.float32
        )
        if stride < local_blocks:
            input_total = input_total + flip_blocks(contrib, stride)
        else:
            bit_number = (stride // local_blocks).bit_length() - 1
            returned = partner_2(contrib.reshape(row_count, local_width), "fly", bit_number)
            input_total = input_total + returned.reshape(row_count, local_blocks, BS)
    input_grad = input_total.reshape(row_count, local_width).astype(jnp.bfloat16)
    replicas = lax.axis_size("dp")
    place = lax.axis_index("dp")
    row_share = BS // replicas
    terms = []
    for factor in range(factor_count):
        product_term = jnp.einsum(
            "ngb,ngc->bgc", gathered[factor], grad_pre, preferred_element_type=jnp.float32
        )
        terms.append(product_term.reshape(BS, hidden_width) * keep_f[factor][None, :])
    term_stack = jnp.stack(terms).reshape(factor_count, replicas, row_share, hidden_width)

    def turn_one(step, carry):
        return shifted(carry, "dp", 1) + pick_rows(
            term_stack, place - step - 2 + 2 * replicas, replicas
        )

    summed = lax.fori_loop(
        0, replicas - 1, turn_one, pick_rows(term_stack, place - 1 + replicas, replicas)
    )
    weight_grad = summed * (1.0 / replicas)
    return (input_grad, weight_grad)


def solution(mesh):
    return jax.shard_map(
        body,
        mesh=mesh,
        in_specs=(P("dp", "fly"), P("dp", "fly"), P(None, "dp", "fly"), P(None, "fly")),
        out_specs=(P("dp", "fly"), P(None, "dp", "fly")),
        check_vma=False,
    )
```

profile of v0, /device:TPU:24, one launch (start us, length us, event | category | flops | bytes accessed | tf_op | source)
XLA Modules:
  0.0 878.9 jit_solution(7239345191191575717)
XLA Ops:
  9.6 15.7 %collective-permute-start.4 = (bf16[128,512]{0,1:T(8,128)(2,1)}, bf16[128,512]{0,1:T(8,128)(2,1)}, u32[]{:S(2)}, u32[]{:S(2)}) collective-permute-start(bf16[128,512]{0,1:T(8,128)(2,1)} %copy.43), channel_id=1, source_target_pairs={{0,8},{8,0},{1,9},{9,1},{2,10},{10,2},{3,11},{11,3},{4,12},{12,4},... | collective-permute-start | bytes 393224 | tf_op jit(solution)/shard_map/ppermute | solution.py:16
  25.3 3.1 collective-permute-start.3
  37.8 211.6 %all-gather.2.cloned.1.call-done = bf16[6,256,1024]{2,1,0:T(8,128)(2,1)} async-done(((bf16[6,8,1024]{2,1,0:T(8,128)(2,1)}), bf16[6,256,1024]{2,1,0:T(8,128)(2,1)}) %all-gather.2.cloned.1.call-update) | async-done | bytes 3145744 | tf_op jit(solution)/shard_map/all_gather | solution.py:46
  276.6 7.2 collective-permute-start.8
  285.8 3.0 collective-permute-start.6
  290.9 2.3 copy.67
  293.1 3.1 reshape.263
  296.2 2.3 copy.68
  298.5 3.1 reshape.264
  301.6 2.3 copy.70
  303.9 3.1 reshape.265
  307.0 2.3 copy.72
  309.2 3.1 reshape.266
  313.6 3.2 reshape.267
  318.1 3.2 reshape.268
  323.7 2.6 copy-done.9
  326.3 542.7 %while.17 = (s32[]{:T(128)}, f32[6,8,1024]{2,1,0:T(8,128)S(1)}, s32[]{:T(128)}, f32[6,32,8,1024]{3,2,1,0:T(8,128)}, s32[]{:T(128)}, /*index=5*/s32[]{:T(128)}, s32[]{:T(128)}, s32[]{:T(128)}, s32[]{:T(128)}) while((s32[]{:T(128)}, f32[6,8,1024]{2,1,0:T(8,128)S(1)}, s32[]{:T(128)}, f32[6,32,8,1024]{3,2,1,0:T(8,128)}, s32[]{:T(128)}, ...), condition=%wide.region_1.2_spmd, body=%wide.region_0.1_spmd.sunk | while | flops 49170 | bytes 1376560 | solution.py:103
  328.2 16.0 %collective-permute-done = f32[6,8,1024]{2,1,0:T(8,128)S(1)} collective-permute-done((f32[6,8,1024]{2,1,0:T(8,128)S(1)}, f32[6,8,1024]{2,1,0:T(8,128)S(1)}, u32[]{:S(2)}, u32[]{:S(2)}) %collective-permute-start) | collective-permute-done | bytes 196640 | tf_op jit(solution)/shard_map/while/body/eval_jaxpr/ppermute | solution.py:21
  347.1 15.1 %collective-permute-done = f32[6,8,1024]{2,1,0:T(8,128)S(1)} collective-permute-done((f32[6,8,1024]{2,1,0:T(8,128)S(1)}, f32[6,8,1024]{2,1,0:T(8,128)S(1)}, u32[]{:S(2)}, u32[]{:S(2)}) %collective-permute-start) | collective-permute-done | bytes 196640 | tf_op jit(solution)/shard_map/while/body/eval_jaxpr/ppermute | solution.py:21
  365.1 14.3 %collective-permute-done = f32[6,8,1024]{2,1,0:T(8,128)S(1)} collective-permute-done((f32[6,8,1024]{2,1,0:T(8,128)S(1)}, f32[6,8,1024]{2,1,0:T(8,128)S(1)}, u32[]{:S(2)}, u32[]{:S(2)}) %collective-permute-start) | collective-permute-done | bytes 196640 | tf_op jit(solution)/shard_map/while/body/eval_jaxpr/ppermute | solution.py:21
  382.4 14.3 %collective-permute-done = f32[6,8,1024]{2,1,0:T(8,128)S(1)} collective-permute-done((f32[6,8,1024]{2,1,0:T(8,128)S(1)}, f32[6,8,1024]{2,1,0:T(8,128)S(1)}, u32[]{:S(2)}, u32[]{:S(2)}) %collective-permute-start) | collective-permute-done | bytes 196640 | tf_op jit(solution)/shard_map/while/body/eval_jaxpr/ppermute | solution.py:21
  399.6 14.3 %collective-permute-done = f32[6,8,1024]{2,1,0:T(8,128)S(1)} collective-permute-done((f32[6,8,1024]{2,1,0:T(8,128)S(1)}, f32[6,8,1024]{2,1,0:T(8,128)S(1)}, u32[]{:S(2)}, u32[]{:S(2)}) %collective-permute-start) | collective-permute-done | bytes 196640 | tf_op jit(solution)/shard_map/while/body/eval_jaxpr/ppermute | solution.py:21
  416.9 14.3 %collective-permute-done = f32[6,8,1024]{2,1,0:T(8,128)S(1)} collective-permute-done((f32[6,8,1024]{2,1,0:T(8,128)S(1)}, f32[6,8,1024]{2,1,0:T(8,128)S(1)}, u32[]{:S(2)}, u32[]{:S(2)}) %collective-permute-start) | collective-permute-done | bytes 196640 | tf_op jit(solution)/shard_map/while/body/eval_jaxpr/ppermute | solution.py:21
  434.1 14.3 %collective-permute-done = f32[6,8,1024]{2,1,0:T(8,128)S(1)} collective-permute-done((f32[6,8,1024]{2,1,0:T(8,128)S(1)}, f32[6,8,1024]{2,1,0:T(8,128)S(1)}, u32[]{:S(2)}, u32[]{:S(2)}) %collective-permute-start) | collective-permute-done | bytes 196640 | tf_op jit(solution)/shard_map/while/body/eval_jaxpr/ppermute | solution.py:21
  451.3 14.3 %collective-permute-done = f32[6,8,1024]{2,1,0:T(8,128)S(1)} collective-permute-done((f32[6,8,1024]{2,1,0:T(8,128)S(1)}, f32[6,8,1024]{2,1,0:T(8,128)S(1)}, u32[]{:S(2)}, u32[]{:S(2)}) %collective-permute-start) | collective-permute-done | bytes 196640 | tf_op jit(solution)/shard_map/while/body/eval_jaxpr/ppermute | solution.py:21
  468.6 14.3 %collective-permute-done = f32[6,8,1024]{2,1,0:T(8,128)S(1)} collective-permute-done((f32[6,8,1024]{2,1,0:T(8,128)S(1)}, f32[6,8,1024]{2,1,0:T(8,128)S(1)}, u32[]{:S(2)}, u32[]{:S(2)}) %collective-permute-start) | collective-permute-done | bytes 196640 | tf_op jit(solution)/shard_map/while/body/eval_jaxpr/ppermute | solution.py:21
  485.8 14.3 %collective-permute-done = f32[6,8,1024]{2,1,0:T(8,128)S(1)} collective-permute-done((f32[6,8,1024]{2,1,0:T(8,128)S(1)}, f32[6,8,1024]{2,1,0:T(8,128)S(1)}, u32[]{:S(2)}, u32[]{:S(2)}) %collective-permute-start) | collective-permute-done | bytes 196640 | tf_op jit(solution)/shard_map/while/body/eval_jaxpr/ppermute | solution.py:21
  503.1 14.3 %collective-permute-done = f32[6,8,1024]{2,1,0:T(8,128)S(1)} collective-permute-done((f32[6,8,1024]{2,1,0:T(8,128)S(1)}, f32[6,8,1024]{2,1,0:T(8,128)S(1)}, u32[]{:S(2)}, u32[]{:S(2)}) %collective-permute-start) | collective-permute-done | bytes 196640 | tf_op jit(solution)/shard_map/while/body/eval_jaxpr/ppermute | solution.py:21
  520.3 14.3 %collective-permute-done = f32[6,8,1024]{2,1,0:T(8,128)S(1)} collective-permute-done((f32[6,8,1024]{2,1,0:T(8,128)S(1)}, f32[6,8,1024]{2,1,0:T(8,128)S(1)}, u32[]{:S(2)}, u32[]{:S(2)}) %collective-permute-start) | collective-permute-done | bytes 196640 | tf_op jit(solution)/shard_map/while/body/eval_jaxpr/ppermute | solution.py:21
  537.6 14.3 %collective-permute-done = f32[6,8,1024]{2,1,0:T(8,128)S(1)} collective-permute-done((f32[6,8,1024]{2,1,0:T(8,128)S(1)}, f32[6,8,1024]{2,1,0:T(8,128)S(1)}, u32[]{:S(2)}, u32[]{:S(2)}) %collective-permute-start) | collective-permute-done | bytes 196640 | tf_op jit(solution)/shard_map/while/body/eval_jaxpr/ppermute | solution.py:21
  554.8 15.2 %collective-permute-done = f32[6,8,1024]{2,1,0:T(8,128)S(1)} collective-permute-done((f32[6,8,1024]{2,1,0:T(8,128)S(1)}, f32[6,8,1024]{2,1,0:T(8,128)S(1)}, u32[]{:S(2)}, u32[]{:S(2)}) %collective-permute-start) | collective-permute-done | bytes 196640 | tf_op jit(solution)/shard_map/while/body/eval_jaxpr/ppermute | solution.py:21
  572.9 16.3 %collective-permute-done = f32[6,8,1024]{2,1,0:T(8,128)S(1)} collective-permute-done((f32[6,8,1024]{2,1,0:T(8,128)S(1)}, f32[6,8,1024]{2,1,0:T(8,128)S(1)}, u32[]{:S(2)}, u32[]{:S(2)}) %collective-permute-start) | collective-permute-done | bytes 196640 | tf_op jit(solution)/shard_map/while/body/eval_jaxpr/ppermute | solution.py:21
  592.1 15.6 %collective-permute-done = f32[6,8,1024]{2,1,0:T(8,128)S(1)} collective-permute-done((f32[6,8,1024]{2,1,0:T(8,128)S(1)}, f32[6,8,1024]{2,1,0:T(8,128)S(1)}, u32[]{:S(2)}, u32[]{:S(2)}) %collective-permute-start) | collective-permute-done | bytes 196640 | tf_op jit(solution)/shard_map/while/body/eval_jaxpr/ppermute | solution.py:21
  610.6 14.7 %collective-permute-done = f32[6,8,1024]{2,1,0:T(8,128)S(1)} collective-permute-done((f32[6,8,1024]{2,1,0:T(8,128)S(1)}, f32[6,8,1024]{2,1,0:T(8,128)S(1)}, u32[]{:S(2)}, u32[]{:S(2)}) %collective-permute-start) | collective-permute-done | bytes 196640 | tf_op jit(solution)/shard_map/while/body/eval_jaxpr/ppermute | solution.py:21
  628.3 14.3 %collective-permute-done = f32[6,8,1024]{2,1,0:T(8,128)S(1)} collective-permute-done((f32[6,8,1024]{2,1,0:T(8,128)S(1)}, f32[6,8,1024]{2,1,0:T(8,128)S(1)}, u32[]{:S(2)}, u32[]{:S(2)}) %collective-permute-start) | collective-permute-done | bytes 196640 | tf_op jit(solution)/shard_map/while/body/eval_jaxpr/ppermute | solution.py:21
  645.5 14.3 %collective-permute-done = f32[6,8,1024]{2,1,0:T(8,128)S(1)} collective-permute-done((f32[6,8,1024]{2,1,0:T(8,128)S(1)}, f32[6,8,1024]{2,1,0:T(8,128)S(1)}, u32[]{:S(2)}, u32[]{:S(2)}) %collective-permute-start) | collective-permute-done | bytes 196640 | tf_op jit(solution)/shard_map/while/body/eval_jaxpr/ppermute | solution.py:21
  662.8 14.3 %collective-permute-done = f32[6,8,1024]{2,1,0:T(8,128)S(1)} collective-permute-done((f32[6,8,1024]{2,1,0:T(8,128)S(1)}, f32[6,8,1024]{2,1,0:T(8,128)S(1)}, u32[]{:S(2)}, u32[]{:S(2)}) %collective-permute-start) | collective-permute-done | bytes 196640 | tf_op jit(solution)/shard_map/while/body/eval_jaxpr/ppermute | solution.py:21
  680.0 14.3 %collective-permute-done = f32[6,8,1024]{2,1,0:T(8,128)S(1)} collective-permute-done((f32[6,8,1024]{2,1,0:T(8,128)S(1)}, f32[6,8,1024]{2,1,0:T(8,128)S(1)}, u32[]{:S(2)}, u32[]{:S(2)}) %collective-permute-start) | collective-permute-done | bytes 196640 | tf_op jit(solution)/shard_map/while/body/eval_jaxpr/ppermute | solution.py:21
  697.2 14.3 %collective-permute-done = f32[6,8,1024]{2,1,0:T(8,128)S(1)} collective-permute-done((f32[6,8,1024]{2,1,0:T(8,128)S(1)}, f32[6,8,1024]{2,1,0:T(8,128)S(1)}, u32[]{:S(2)}, u32[]{:S(2)}) %collective-permute-start) | collective-permute-done | bytes 196640 | tf_op jit(solution)/shard_map/while/body/eval_jaxpr/ppermute | solution.py:21
  714.5 14.3 %collective-permute-done = f32[6,8,1024]{2,1,0:T(8,128)S(1)} collective-permute-done((f32[6,8,1024]{2,1,0:T(8,128)S(1)}, f32[6,8,1024]{2,1,0:T(8,128)S(1)}, u32[]{:S(2)}, u32[]{:S(2)}) %collective-permute-start) | collective-permute-done | bytes 196640 | tf_op jit(solution)/shard_map/while/body/eval_jaxpr/ppermute | solution.py:21
  731.7 14.3 %collective-permute-done = f32[6,8,1024]{2,1,0:T(8,128)S(1)} collective-permute-done((f32[6,8,1024]{2,1,0:T(8,128)S(1)}, f32[6,8,1024]{2,1,0:T(8,128)S(1)}, u32[]{:S(2)}, u32[]{:S(2)}) %collective-permute-start) | collective-permute-done | bytes 196640 | tf_op jit(solution)/shard_map/while/body/eval_jaxpr/ppermute | solution.py:21
  749.0 14.3 %collective-permute-done = f32[6,8,1024]{2,1,0:T(8,128)S(1)} collective-permute-done((f32[6,8,1024]{2,1,0:T(8,128)S(1)}, f32[6,8,1024]{2,1,0:T(8,128)S(1)}, u32[]{:S(2)}, u32[]{:S(2)}) %collective-permute-start) | collective-permute-done | bytes 196640 | tf_op jit(solution)/shard_map/while/body/eval_jaxpr/ppermute | solution.py:21
  766.2 14.3 %collective-permute-done = f32[6,8,1024]{2,1,0:T(8,128)S(1)} collective-permute-done((f32[6,8,1024]{2,1,0:T(8,128)S(1)}, f32[6,8,1024]{2,1,0:T(8,128)S(1)}, u32[]{:S(2)}, u32[]{:S(2)}) %collective-permute-start) | collective-permute-done | bytes 196640 | tf_op jit(solution)/shard_map/while/body/eval_jaxpr/ppermute | solution.py:21
  783.5 14.3 %collective-permute-done = f32[6,8,1024]{2,1,0:T(8,128)S(1)} collective-permute-done((f32[6,8,1024]{2,1,0:T(8,128)S(1)}, f32[6,8,1024]{2,1,0:T(8,128)S(1)}, u32[]{:S(2)}, u32[]{:S(2)}) %collective-permute-start) | collective-permute-done | bytes 196640 | tf_op jit(solution)/shard_map/while/body/eval_jaxpr/ppermute | solution.py:21
  800.7 14.4 %collective-permute-done = f32[6,8,1024]{2,1,0:T(8,128)S(1)} collective-permute-done((f32[6,8,1024]{2,1,0:T(8,128)S(1)}, f32[6,8,1024]{2,1,0:T(8,128)S(1)}, u32[]{:S(2)}, u32[]{:S(2)}) %collective-permute-start) | collective-permute-done | bytes 196640 | tf_op jit(solution)/shard_map/while/body/eval_jaxpr/ppermute | solution.py:21
  818.0 15.5 %collective-permute-done = f32[6,8,1024]{2,1,0:T(8,128)S(1)} collective-permute-done((f32[6,8,1024]{2,1,0:T(8,128)S(1)}, f32[6,8,1024]{2,1,0:T(8,128)S(1)}, u32[]{:S(2)}, u32[]{:S(2)}) %collective-permute-start) | collective-permute-done | bytes 196640 | tf_op jit(solution)/shard_map/while/body/eval_jaxpr/ppermute | solution.py:21
  836.5 14.3 %collective-permute-done = f32[6,8,1024]{2,1,0:T(8,128)S(1)} collective-permute-done((f32[6,8,1024]{2,1,0:T(8,128)S(1)}, f32[6,8,1024]{2,1,0:T(8,128)S(1)}, u32[]{:S(2)}, u32[]{:S(2)}) %collective-permute-start) | collective-permute-done | bytes 196640 | tf_op jit(solution)/shard_map/while/body/eval_jaxpr/ppermute | solution.py:21
  853.7 14.3 %collective-permute-done = f32[6,8,1024]{2,1,0:T(8,128)S(1)} collective-permute-done((f32[6,8,1024]{2,1,0:T(8,128)S(1)}, f32[6,8,1024]{2,1,0:T(8,128)S(1)}, u32[]{:S(2)}, u32[]{:S(2)}) %collective-permute-start) | collective-permute-done | bytes 196640 | tf_op jit(solution)/shard_map/while/body/eval_jaxpr/ppermute | solution.py:21
  (157 shorter events, 139.6 us)
Async XLA Ops:
  7.2 242.3 %all-gather.2.cloned.1.call-start = ((), (), s32[]{:S(2)}) async-start(), calls=%async_computation | async-start | bytes 3244032 | tf_op jit(solution)/shard_map/all_gather | solution.py:46
  9.6 247.6 %collective-permute-start.4 = (bf16[128,512]{0,1:T(8,128)(2,1)}, bf16[128,512]{0,1:T(8,128)(2,1)}, u32[]{:S(2)}, u32[]{:S(2)}) collective-permute-start(bf16[128,512]{0,1:T(8,128)(2,1)} %copy.43), channel_id=1, source_target_pairs={{0,8},{8,0},{1,9},{9,1},{2,10},{10,2},{3,11},{11,3},{4,12},{12,4},... | collective-permute-start | bytes 393224 | tf_op jit(solution)/shard_map/ppermute | solution.py:16
  25.3 233.2 %collective-permute-start.3 = (bf16[128,512]{0,1:T(8,128)(2,1)}, bf16[128,512]{0,1:T(8,128)(2,1)}, u32[]{:S(2)}, u32[]{:S(2)}) collective-permute-start(bf16[128,512]{0,1:T(8,128)(2,1)} %copy.43), channel_id=1, source_target_pairs={{0,4},{4,0},{1,5},{5,1},{2,6},{6,2},{3,7},{7,3},{8,12},{12,8},{9,1... | collective-permute-start | bytes 393224 | tf_op jit(solution)/shard_map/ppermute | solution.py:16
  28.4 231.3 %collective-permute-start.2 = (bf16[128,512]{0,1:T(8,128)(2,1)}, bf16[128,512]{0,1:T(8,128)(2,1)}, u32[]{:S(2)}, u32[]{:S(2)}) collective-permute-start(bf16[128,512]{0,1:T(8,128)(2,1)} %copy.43), channel_id=1, source_target_pairs={{0,2},{2,0},{1,3},{3,1},{4,6},{6,4},{5,7},{7,5},{8,10},{10,8},{9,1... | collective-permute-start | bytes 393224 | tf_op jit(solution)/shard_map/ppermute | solution.py:16
  30.4 230.6 %collective-permute-start.1 = (bf16[128,512]{0,1:T(8,128)(2,1)}, bf16[128,512]{0,1:T(8,128)(2,1)}, u32[]{:S(2)}, u32[]{:S(2)}) collective-permute-start(bf16[128,512]{0,1:T(8,128)(2,1)} %copy.43), channel_id=1, source_target_pairs={{0,1},{1,0},{2,3},{3,2},{4,5},{5,4},{6,7},{7,6},{8,9},{9,8},{10,11... | collective-permute-start | bytes 393224 | tf_op jit(solution)/shard_map/ppermute | solution.py:16
  36.2 217.3 %copy-start.7 = (bf16[128,1,2,1,256]{4,0,2,3,1:T(8,128)(2,1)}, bf16[128,1,2,1,256]{4,0,2,3,1:T(8,128)(2,1)S(1)}, u32[]{:S(2)}) copy-start(bf16[128,1,2,1,256]{4,0,2,3,1:T(8,128)(2,1)S(1)} %rev.4) | copy-start | bytes 393220
  249.4 3.7 copy-start.6
  257.2 9.1 %copy-start.5 = (bf16[1,256,1024]{1,2,0:T(8,128)(2,1)S(1)}, bf16[1,256,1024]{1,2,0:T(8,128)(2,1)}, u32[]{:S(2)}) copy-start(bf16[1,256,1024]{1,2,0:T(8,128)(2,1)} %copy.42) | copy-start | bytes 1572868
  258.5 10.1 %copy-start.8 = (bf16[128,1,2,1,256]{4,0,2,3,1:T(8,128)(2,1)S(1)}, bf16[128,1,2,1,256]{4,0,2,3,1:T(8,128)(2,1)}, u32[]{:S(2)}) copy-start(bf16[128,1,2,1,256]{4,0,2,3,1:T(8,128)(2,1)} %copy-done.7) | copy-start | bytes 393220
  276.6 593.4 %collective-permute-start.8 = (f32[128,512]{0,1:T(8,128)}, f32[128,512]{0,1:T(8,128)S(1)}, u32[]{:S(2)}, u32[]{:S(2)}) collective-permute-start(f32[128,512]{0,1:T(8,128)} %bitcast.26), channel_id=1, source_target_pairs={{0,8},{8,0},{1,9},{9,1},{2,10},{10,2},{3,11},{11,3},{4,12},{12,4},... | collective-permute-start | bytes 786440 | tf_op jit(solution)/shard_map/ppermute | solution.py:16
  283.9 586.2 %collective-permute-start.7 = (f32[128,512]{0,1:T(8,128)}, f32[128,512]{0,1:T(8,128)}, u32[]{:S(2)}, u32[]{:S(2)}) collective-permute-start(f32[128,512]{0,1:T(8,128)} %bitcast.23), channel_id=1, source_target_pairs={{0,4},{4,0},{1,5},{5,1},{2,6},{6,2},{3,7},{7,3},{8,12},{12,8},{9,1... | collective-permute-start | bytes 786440 | tf_op jit(solution)/shard_map/ppermute | solution.py:16
  285.8 584.3 %collective-permute-start.6 = (f32[128,512]{0,1:T(8,128)}, f32[128,512]{0,1:T(8,128)}, u32[]{:S(2)}, u32[]{:S(2)}) collective-permute-start(f32[128,512]{0,1:T(8,128)} %bitcast.20), channel_id=1, source_target_pairs={{0,2},{2,0},{1,3},{3,1},{4,6},{6,4},{5,7},{7,5},{8,10},{10,8},{9,1... | collective-permute-start | bytes 786440 | tf_op jit(solution)/shard_map/ppermute | solution.py:16
  288.8 581.3 %collective-permute-start.5 = (f32[128,512]{0,1:T(8,128)}, f32[128,512]{0,1:T(8,128)}, u32[]{:S(2)}, u32[]{:S(2)}) collective-permute-start(f32[128,512]{0,1:T(8,128)} %bitcast.17), channel_id=1, source_target_pairs={{0,1},{1,0},{2,3},{3,2},{4,5},{5,4},{6,7},{7,6},{8,9},{9,8},{10,11... | collective-permute-start | bytes 786440 | tf_op jit(solution)/shard_map/ppermute | solution.py:16
  313.6 7.7 copy-start
  316.8 6.5 copy-start.11
  318.1 4.9 copy-start.1
  318.1 5.3 copy-start.10
  326.3 17.9 %collective-permute-start = (f32[6,8,1024]{2,1,0:T(8,128)S(1)}, f32[6,8,1024]{2,1,0:T(8,128)S(1)}, u32[]{:S(2)}, u32[]{:S(2)}) collective-permute-start(f32[6,8,1024]{2,1,0:T(8,128)S(1)} %get-tuple-element.217), channel_id=1, source_target_pairs={{0,16},{16,32},{32,48},{48,64},{64,80},{80,96},{96,112},{112,128},... | collective-permute-start | bytes 589832 | tf_op jit(solution)/shard_map/while/body/eval_jaxpr/ppermute | solution.py:21
  345.2 17.1 %collective-permute-start = (f32[6,8,1024]{2,1,0:T(8,128)S(1)}, f32[6,8,1024]{2,1,0:T(8,128)S(1)}, u32[]{:S(2)}, u32[]{:S(2)}) collective-permute-start(f32[6,8,1024]{2,1,0:T(8,128)S(1)} %get-tuple-element.217), channel_id=1, source_target_pairs={{0,16},{16,32},{32,48},{48,64},{64,80},{80,96},{96,112},{112,128},... | collective-permute-start | bytes 589832 | tf_op jit(solution)/shard_map/while/body/eval_jaxpr/ppermute | solution.py:21
  363.2 16.3 %collective-permute-start = (f32[6,8,1024]{2,1,0:T(8,128)S(1)}, f32[6,8,1024]{2,1,0:T(8,128)S(1)}, u32[]{:S(2)}, u32[]{:S(2)}) collective-permute-start(f32[6,8,1024]{2,1,0:T(8,128)S(1)} %get-tuple-element.217), channel_id=1, source_target_pairs={{0,16},{16,32},{32,48},{48,64},{64,80},{80,96},{96,112},{112,128},... | collective-permute-start | bytes 589832 | tf_op jit(solution)/shard_map/while/body/eval_jaxpr/ppermute | solution.py:21
  380.4 16.3 %collective-permute-start = (f32[6,8,1024]{2,1,0:T(8,128)S(1)}, f32[6,8,1024]{2,1,0:T(8,128)S(1)}, u32[]{:S(2)}, u32[]{:S(2)}) collective-permute-start(f32[6,8,1024]{2,1,0:T(8,128)S(1)} %get-tuple-element.217), channel_id=1, source_target_pairs={{0,16},{16,32},{32,48},{48,64},{64,80},{80,96},{96,112},{112,128},... | collective-permute-start | bytes 589832 | tf_op jit(solution)/shard_map/while/body/eval_jaxpr/ppermute | solution.py:21
  397.7 16.3 %collective-permute-start = (f32[6,8,1024]{2,1,0:T(8,128)S(1)}, f32[6,8,1024]{2,1,0:T(8,128)S(1)}, u32[]{:S(2)}, u32[]{:S(2)}) collective-permute-start(f32[6,8,1024]{2,1,0:T(8,128)S(1)} %get-tuple-element.217), channel_id=1, source_target_pairs={{0,16},{16,32},{32,48},{48,64},{64,80},{80,96},{96,112},{112,128},... | collective-permute-start | bytes 589832 | tf_op jit(solution)/shard_map/while/body/eval_jaxpr/ppermute | solution.py:21
  414.9 16.3 %collective-permute-start = (f32[6,8,1024]{2,1,0:T(8,128)S(1)}, f32[6,8,1024]{2,1,0:T(8,128)S(1)}, u32[]{:S(2)}, u32[]{:S(2)}) collective-permute-start(f32[6,8,1024]{2,1,0:T(8,128)S(1)} %get-tuple-element.217), channel_id=1, source_target_pairs={{0,16},{16,32},{32,48},{48,64},{64,80},{80,96},{96,112},{112,128},... | collective-permute-start | bytes 589832 | tf_op jit(solution)/shard_map/while/body/eval_jaxpr/ppermute | solution.py:21
  432.1 16.3 %collective-permute-start = (f32[6,8,1024]{2,1,0:T(8,128)S(1)}, f32[6,8,1024]{2,1,0:T(8,128)S(1)}, u32[]{:S(2)}, u32[]{:S(2)}) collective-permute-start(f32[6,8,1024]{2,1,0:T(8,128)S(1)} %get-tuple-element.217), channel_id=1, source_target_pairs={{0,16},{16,32},{32,48},{48,64},{64,80},{80,96},{96,112},{112,128},... | collective-permute-start | bytes 589832 | tf_op jit(solution)/shard_map/while/body/eval_jaxpr/ppermute | solution.py:21
  449.4 16.3 %collective-permute-start = (f32[6,8,1024]{2,1,0:T(8,128)S(1)}, f32[6,8,1024]{2,1,0:T(8,128)S(1)}, u32[]{:S(2)}, u32[]{:S(2)}) collective-permute-start(f32[6,8,1024]{2,1,0:T(8,128)S(1)} %get-tuple-element.217), channel_id=1, source_target_pairs={{0,16},{16,32},{32,48},{48,64},{64,80},{80,96},{96,112},{112,128},... | collective-permute-start | bytes 589832 | tf_op jit(solution)/shard_map/while/body/eval_jaxpr/ppermute | solution.py:21
  466.6 16.3 %collective-permute-start = (f32[6,8,1024]{2,1,0:T(8,128)S(1)}, f32[6,8,1024]{2,1,0:T(8,128)S(1)}, u32[]{:S(2)}, u32[]{:S(2)}) collective-permute-start(f32[6,8,1024]{2,1,0:T(8,128)S(1)} %get-tuple-element.217), channel_id=1, source_target_pairs={{0,16},{16,32},{32,48},{48,64},{64,80},{80,96},{96,112},{112,128},... | collective-permute-start | bytes 589832 | tf_op jit(solution)/shard_map/while/body/eval_jaxpr/ppermute | solution.py:21
  483.9 16.3 %collective-permute-start = (f32[6,8,1024]{2,1,0:T(8,128)S(1)}, f32[6,8,1024]{2,1,0:T(8,128)S(1)}, u32[]{:S(2)}, u32[]{:S(2)}) collective-permute-start(f32[6,8,1024]{2,1,0:T(8,128)S(1)} %get-tuple-element.217), channel_id=1, source_target_pairs={{0,16},{16,32},{32,48},{48,64},{64,80},{80,96},{96,112},{112,128},... | collective-permute-start | bytes 589832 | tf_op jit(solution)/shard_map/while/body/eval_jaxpr/ppermute | solution.py:21
  501.1 16.3 %collective-permute-start = (f32[6,8,1024]{2,1,0:T(8,128)S(1)}, f32[6,8,1024]{2,1,0:T(8,128)S(1)}, u32[]{:S(2)}, u32[]{:S(2)}) collective-permute-start(f32[6,8,1024]{2,1,0:T(8,128)S(1)} %get-tuple-element.217), channel_id=1, source_target_pairs={{0,16},{16,32},{32,48},{48,64},{64,80},{80,96},{96,112},{112,128},... | collective-permute-start | bytes 589832 | tf_op jit(solution)/shard_map/while/body/eval_jaxpr/ppermute | solution.py:21
  518.4 16.3 %collective-permute-start = (f32[6,8,1024]{2,1,0:T(8,128)S(1)}, f32[6,8,1024]{2,1,0:T(8,128)S(1)}, u32[]{:S(2)}, u32[]{:S(2)}) collective-permute-start(f32[6,8,1024]{2,1,0:T(8,128)S(1)} %get-tuple-element.217), channel_id=1, source_target_pairs={{0,16},{16,32},{32,48},{48,64},{64,80},{80,96},{96,112},{112,128},... | collective-permute-start | bytes 589832 | tf_op jit(solution)/shard_map/while/body/eval_jaxpr/ppermute | solution.py:21
  535.6 16.3 %collective-permute-start = (f32[6,8,1024]{2,1,0:T(8,128)S(1)}, f32[6,8,1024]{2,1,0:T(8,128)S(1)}, u32[]{:S(2)}, u32[]{:S(2)}) collective-permute-start(f32[6,8,1024]{2,1,0:T(8,128)S(1)} %get-tuple-element.217), channel_id=1, source_target_pairs={{0,16},{16,32},{32,48},{48,64},{64,80},{80,96},{96,112},{112,128},... | collective-permute-start | bytes 589832 | tf_op jit(solution)/shard_map/while/body/eval_jaxpr/ppermute | solution.py:21
  552.9 17.1 %collective-permute-start = (f32[6,8,1024]{2,1,0:T(8,128)S(1)}, f32[6,8,1024]{2,1,0:T(8,128)S(1)}, u32[]{:S(2)}, u32[]{:S(2)}) collective-permute-start(f32[6,8,1024]{2,1,0:T(8,128)S(1)} %get-tuple-element.217), channel_id=1, source_target_pairs={{0,16},{16,32},{32,48},{48,64},{64,80},{80,96},{96,112},{112,128},... | collective-permute-start | bytes 589832 | tf_op jit(solution)/shard_map/while/body/eval_jaxpr/ppermute | solution.py:21
  570.9 18.3 %collective-permute-start = (f32[6,8,1024]{2,1,0:T(8,128)S(1)}, f32[6,8,1024]{2,1,0:T(8,128)S(1)}, u32[]{:S(2)}, u32[]{:S(2)}) collective-permute-start(f32[6,8,1024]{2,1,0:T(8,128)S(1)} %get-tuple-element.217), channel_id=1, source_target_pairs={{0,16},{16,32},{32,48},{48,64},{64,80},{80,96},{96,112},{112,128},... | collective-permute-start | bytes 589832 | tf_op jit(solution)/shard_map/while/body/eval_jaxpr/ppermute | solution.py:21
  590.2 17.5 %collective-permute-start = (f32[6,8,1024]{2,1,0:T(8,128)S(1)}, f32[6,8,1024]{2,1,0:T(8,128)S(1)}, u32[]{:S(2)}, u32[]{:S(2)}) collective-permute-start(f32[6,8,1024]{2,1,0:T(8,128)S(1)} %get-tuple-element.217), channel_id=1, source_target_pairs={{0,16},{16,32},{32,48},{48,64},{64,80},{80,96},{96,112},{112,128},... | collective-permute-start | bytes 589832 | tf_op jit(solution)/shard_map/while/body/eval_jaxpr/ppermute | solution.py:21
  608.7 16.7 %collective-permute-start = (f32[6,8,1024]{2,1,0:T(8,128)S(1)}, f32[6,8,1024]{2,1,0:T(8,128)S(1)}, u32[]{:S(2)}, u32[]{:S(2)}) collective-permute-start(f32[6,8,1024]{2,1,0:T(8,128)S(1)} %get-tuple-element.217), channel_id=1, source_target_pairs={{0,16},{16,32},{32,48},{48,64},{64,80},{80,96},{96,112},{112,128},... | collective-permute-start | bytes 589832 | tf_op jit(solution)/shard_map/while/body/eval_jaxpr/ppermute | solution.py:21
  626.3 16.3 %collective-permute-start = (f32[6,8,1024]{2,1,0:T(8,128)S(1)}, f32[6,8,1024]{2,1,0:T(8,128)S(1)}, u32[]{:S(2)}, u32[]{:S(2)}) collective-permute-start(f32[6,8,1024]{2,1,0:T(8,128)S(1)} %get-tuple-element.217), channel_id=1, source_target_pairs={{0,16},{16,32},{32,48},{48,64},{64,80},{80,96},{96,112},{112,128},... | collective-permute-start | bytes 589832 | tf_op jit(solution)/shard_map/while/body/eval_jaxpr/ppermute | solution.py:21
  643.6 16.3 %collective-permute-start = (f32[6,8,1024]{2,1,0:T(8,128)S(1)}, f32[6,8,1024]{2,1,0:T(8,128)S(1)}, u32[]{:S(2)}, u32[]{:S(2)}) collective-permute-start(f32[6,8,1024]{2,1,0:T(8,128)S(1)} %get-tuple-element.217), channel_id=1, source_target_pairs={{0,16},{16,32},{32,48},{48,64},{64,80},{80,96},{96,112},{112,128},... | collective-permute-start | bytes 589832 | tf_op jit(solution)/shard_map/while/body/eval_jaxpr/ppermute | solution.py:21
  660.8 16.3 %collective-permute-start = (f32[6,8,1024]{2,1,0:T(8,128)S(1)}, f32[6,8,1024]{2,1,0:T(8,128)S(1)}, u32[]{:S(2)}, u32[]{:S(2)}) collective-permute-start(f32[6,8,1024]{2,1,0:T(8,128)S(1)} %get-tuple-element.217), channel_id=1, source_target_pairs={{0,16},{16,32},{32,48},{48,64},{64,80},{80,96},{96,112},{112,128},... | collective-permute-start | bytes 589832 | tf_op jit(solution)/shard_map/while/body/eval_jaxpr/ppermute | solution.py:21
  678.0 16.3 %collective-permute-start = (f32[6,8,1024]{2,1,0:T(8,128)S(1)}, f32[6,8,1024]{2,1,0:T(8,128)S(1)}, u32[]{:S(2)}, u32[]{:S(2)}) collective-permute-start(f32[6,8,1024]{2,1,0:T(8,128)S(1)} %get-tuple-element.217), channel_id=1, source_target_pairs={{0,16},{16,32},{32,48},{48,64},{64,80},{80,96},{96,112},{112,128},... | collective-permute-start | bytes 589832 | tf_op jit(solution)/shard_map/while/body/eval_jaxpr/ppermute | solution.py:21
  695.3 16.3 %collective-permute-start = (f32[6,8,1024]{2,1,0:T(8,128)S(1)}, f32[6,8,1024]{2,1,0:T(8,128)S(1)}, u32[]{:S(2)}, u32[]{:S(2)}) collective-permute-start(f32[6,8,1024]{2,1,0:T(8,128)S(1)} %get-tuple-element.217), channel_id=1, source_target_pairs={{0,16},{16,32},{32,48},{48,64},{64,80},{80,96},{96,112},{112,128},... | collective-permute-start | bytes 589832 | tf_op jit(solution)/shard_map/while/body/eval_jaxpr/ppermute | solution.py:21
  712.5 16.3 %collective-permute-start = (f32[6,8,1024]{2,1,0:T(8,128)S(1)}, f32[6,8,1024]{2,1,0:T(8,128)S(1)}, u32[]{:S(2)}, u32[]{:S(2)}) collective-permute-start(f32[6,8,1024]{2,1,0:T(8,128)S(1)} %get-tuple-element.217), channel_id=1, source_target_pairs={{0,16},{16,32},{32,48},{48,64},{64,80},{80,96},{96,112},{112,128},... | collective-permute-start | bytes 589832 | tf_op jit(solution)/shard_map/while/body/eval_jaxpr/ppermute | solution.py:21
  729.8 16.3 %collective-permute-start = (f32[6,8,1024]{2,1,0:T(8,128)S(1)}, f32[6,8,1024]{2,1,0:T(8,128)S(1)}, u32[]{:S(2)}, u32[]{:S(2)}) collective-permute-start(f32[6,8,1024]{2,1,0:T(8,128)S(1)} %get-tuple-element.217), channel_id=1, source_target_pairs={{0,16},{16,32},{32,48},{48,64},{64,80},{80,96},{96,112},{112,128},... | collective-permute-start | bytes 589832 | tf_op jit(solution)/shard_map/while/body/eval_jaxpr/ppermute | solution.py:21
  747.0 16.3 %collective-permute-start = (f32[6,8,1024]{2,1,0:T(8,128)S(1)}, f32[6,8,1024]{2,1,0:T(8,128)S(1)}, u32[]{:S(2)}, u32[]{:S(2)}) collective-permute-start(f32[6,8,1024]{2,1,0:T(8,128)S(1)} %get-tuple-element.217), channel_id=1, source_target_pairs={{0,16},{16,32},{32,48},{48,64},{64,80},{80,96},{96,112},{112,128},... | collective-permute-start | bytes 589832 | tf_op jit(solution)/shard_map/while/body/eval_jaxpr/ppermute | solution.py:21
  764.3 16.3 %collective-permute-start = (f32[6,8,1024]{2,1,0:T(8,128)S(1)}, f32[6,8,1024]{2,1,0:T(8,128)S(1)}, u32[]{:S(2)}, u32[]{:S(2)}) collective-permute-start(f32[6,8,1024]{2,1,0:T(8,128)S(1)} %get-tuple-element.217), channel_id=1, source_target_pairs={{0,16},{16,32},{32,48},{48,64},{64,80},{80,96},{96,112},{112,128},... | collective-permute-start | bytes 589832 | tf_op jit(solution)/shard_map/while/body/eval_jaxpr/ppermute | solution.py:21
  781.5 16.3 %collective-permute-start = (f32[6,8,1024]{2,1,0:T(8,128)S(1)}, f32[6,8,1024]{2,1,0:T(8,128)S(1)}, u32[]{:S(2)}, u32[]{:S(2)}) collective-permute-start(f32[6,8,1024]{2,1,0:T(8,128)S(1)} %get-tuple-element.217), channel_id=1, source_target_pairs={{0,16},{16,32},{32,48},{48,64},{64,80},{80,96},{96,112},{112,128},... | collective-permute-start | bytes 589832 | tf_op jit(solution)/shard_map/while/body/eval_jaxpr/ppermute | solution.py:21
  798.8 16.3 %collective-permute-start = (f32[6,8,1024]{2,1,0:T(8,128)S(1)}, f32[6,8,1024]{2,1,0:T(8,128)S(1)}, u32[]{:S(2)}, u32[]{:S(2)}) collective-permute-start(f32[6,8,1024]{2,1,0:T(8,128)S(1)} %get-tuple-element.217), channel_id=1, source_target_pairs={{0,16},{16,32},{32,48},{48,64},{64,80},{80,96},{96,112},{112,128},... | collective-permute-start | bytes 589832 | tf_op jit(solution)/shard_map/while/body/eval_jaxpr/ppermute | solution.py:21
  816.1 17.5 %collective-permute-start = (f32[6,8,1024]{2,1,0:T(8,128)S(1)}, f32[6,8,1024]{2,1,0:T(8,128)S(1)}, u32[]{:S(2)}, u32[]{:S(2)}) collective-permute-start(f32[6,8,1024]{2,1,0:T(8,128)S(1)} %get-tuple-element.217), channel_id=1, source_target_pairs={{0,16},{16,32},{32,48},{48,64},{64,80},{80,96},{96,112},{112,128},... | collective-permute-start | bytes 589832 | tf_op jit(solution)/shard_map/while/body/eval_jaxpr/ppermute | solution.py:21
  834.5 16.3 %collective-permute-start = (f32[6,8,1024]{2,1,0:T(8,128)S(1)}, f32[6,8,1024]{2,1,0:T(8,128)S(1)}, u32[]{:S(2)}, u32[]{:S(2)}) collective-permute-start(f32[6,8,1024]{2,1,0:T(8,128)S(1)} %get-tuple-element.217), channel_id=1, source_target_pairs={{0,16},{16,32},{32,48},{48,64},{64,80},{80,96},{96,112},{112,128},... | collective-permute-start | bytes 589832 | tf_op jit(solution)/shard_map/while/body/eval_jaxpr/ppermute | solution.py:21
  851.8 16.3 %collective-permute-start = (f32[6,8,1024]{2,1,0:T(8,128)S(1)}, f32[6,8,1024]{2,1,0:T(8,128)S(1)}, u32[]{:S(2)}, u32[]{:S(2)}) collective-permute-start(f32[6,8,1024]{2,1,0:T(8,128)S(1)} %get-tuple-element.217), channel_id=1, source_target_pairs={{0,16},{16,32},{32,48},{48,64},{64,80},{80,96},{96,112},{112,128},... | collective-permute-start | bytes 589832 | tf_op jit(solution)/shard_map/while/body/eval_jaxpr/ppermute | solution.py:21
  (4 other events, 8.6 us)
Sparse Core Ops, SparseCore 0:
  10.1 239.3 all-gather.1
where the time goes:
time: 884 us; the launch traced here: 879 us
  waiting for transfers between devices  665 us (75%)
  starting transfers between devices  96.5 us (11%)
  local copies, waits for them, and re-layouts  44.5 us (5%)
  other arithmetic  36.4 us (4%)
  matrix products  21 us (2%)
  between operations  14.4 us (2%)
    ppermute x31, waiting for transfers between devices, shifted(): lax.ppermute(value, axis, [(i, (i + by) % devices) for i in range(devices)])  452 us
    all_gather x1, waiting for transfers between devices, body(): weights = lax.all_gather(w_up, 'dp', axis=1, tiled=True)  212 us
    ppermute x31, starting transfers between devices, shifted(): lax.ppermute(value, axis, [(i, (i + by) % devices) for i in range(devices)])  59.5 us
    ppermute x8, starting transfers between devices, partner_2(): return lax.ppermute(block, axis, route)  36.9 us
    add x31, other arithmetic, turn_one(): shifted(carry, 'dp', 1)  29.4 us
    reshape x6, local copies, waits for them, and re-layouts, body(): product_term.reshape(BS, hidden_width) * keep_f[factor][None, :]  18.8 us
  transfers between devices with their start and end apart: 40, of which 32 were waited for; matrix products, arithmetic and copies ran while one was open for 9% of the time, Pallas kernels for 0%

commit v1 on v0

--- a/solution.py
+++ b/solution.py
@@ -1,9 +1,13 @@
 import jax
 import jax.numpy as jnp
 from jax import lax
+from jax.sharding import Mesh
 from jax.sharding import PartitionSpec as P
 
 BS = 256
+ROWS = "zl"
+COLS = "xx"
+DP = (ROWS, COLS)
 
 
 def partner_2(block, axis, bit):
@@ -14,11 +18,6 @@
         if high != low and high < count:
             route += [(low, high), (high, low)]
     return lax.ppermute(block, axis, route)
-
-
-def shifted(value, axis, by):
-    devices = lax.axis_size(axis)
-    return lax.ppermute(value, axis, [(i, (i + by) % devices) for i in range(devices)])
 
 
 def flip_blocks(values, stride):
@@ -33,8 +32,18 @@
     return 0 if factor == 0 else 2 ** (factor - 1)
 
 
-def pick_rows(stacked, index, replicas):
-    return lax.dynamic_index_in_dim(stacked, index % replicas, 1, keepdims=False)
+def gather_rows(w_up):
+    inner = lax.all_gather(w_up, COLS, axis=1, tiled=True)
+    return lax.all_gather(inner, ROWS, axis=1, tiled=True)
+
+
+def scatter_rows(terms):
+    rows, factor_count, width = terms.shape
+    zl = lax.axis_size(ROWS)
+    xx = lax.axis_size(COLS)
+    part = lax.psum_scatter(terms.reshape(zl, rows // zl, factor_count, width), ROWS, scatter_dimension=0, tiled=True)
+    part = lax.psum_scatter(part.reshape(xx, rows // (zl * xx), factor_count, width), COLS, scatter_dimension=0, tiled=True)
+    return part.reshape(rows // (zl * xx), factor_count, width).transpose(1, 0, 2)
 
 
 def body(tokens, hidden_grad, w_up, pattern):
@@ -43,7 +52,7 @@
     hidden_width = hidden_grad.shape[1]
     local_blocks = local_width // BS
     group_width = hidden_width // local_blocks
-    weights = lax.all_gather(w_up, "dp", axis=1, tiled=True)
+    weights = gather_rows(w_up)
     keep_cols = jnp.broadcast_to(pattern[:, :, None], (factor_count, pattern.shape[1], BS)).reshape(
         factor_count, hidden_width
     )
@@ -84,34 +93,30 @@
             returned = partner_2(contrib.reshape(row_count, local_width), "fly", bit_number)
             input_total = input_total + returned.reshape(row_count, local_blocks, BS)
     input_grad = input_total.reshape(row_count, local_width).astype(jnp.bfloat16)
-    replicas = lax.axis_size("dp")
-    place = lax.axis_index("dp")
-    row_share = BS // replicas
     terms = []
     for factor in range(factor_count):
         product_term = jnp.einsum(
             "ngb,ngc->bgc", gathered[factor], grad_pre, preferred_element_type=jnp.float32
         )
         terms.append(product_term.reshape(BS, hidden_width) * keep_f[factor][None, :])
-    term_stack = jnp.stack(terms).reshape(factor_count, replicas, row_share, hidden_width)
-
-    def turn_one(step, carry):
-        return shifted(carry, "dp", 1) + pick_rows(
-            term_stack, place - step - 2 + 2 * replicas, replicas
-        )
-
-    summed = lax.fori_loop(
-        0, replicas - 1, turn_one, pick_rows(term_stack, place - 1 + replicas, replicas)
-    )
-    weight_grad = summed * (1.0 / replicas)
+    summed = scatter_rows(jnp.stack(terms, axis=1))
+    weight_grad = summed * (1.0 / (lax.axis_size(ROWS) * lax.axis_size(COLS)))
     return (input_grad, weight_grad)
 
 
+def split_mesh(mesh):
+    devices = mesh.devices
+    xs = sorted({d.coords[0] for d in devices[:, 0]})
+    cols = len(xs)
+    return Mesh(devices.reshape(devices.shape[0] // cols, cols, devices.shape[1]), (ROWS, COLS, "fly"))
+
+
 def solution(mesh):
+    grid = split_mesh(mesh)
     return jax.shard_map(
         body,
-        mesh=mesh,
-        in_specs=(P("dp", "fly"), P("dp", "fly"), P(None, "dp", "fly"), P(None, "fly")),
-        out_specs=(P("dp", "fly"), P(None, "dp", "fly")),
+        mesh=grid,
+        in_specs=(P(DP, "fly"), P(DP, "fly"), P(None, DP, "fly"), P(None, "fly")),
+        out_specs=(P(DP, "fly"), P(None, DP, "fly")),
         check_vma=False,
     )

time: 884 us -> 526 us (0.60)
  waiting for transfers between devices: 665 us -> 373 us
  starting transfers between devices: 96.5 us -> 35.6 us
  other arithmetic: 36.4 us -> 15.9 us
  blocking collectives: 0 us -> 14.5 us
    ppermute x31 -> x0, waiting for transfers between devices: 452 us -> none  [shifted(): lax.ppermute(value, axis, [(i, (i + by) % devices) for i in range(devices)])]
    unnamed x1 -> x5, waiting for transfers between devices: 0.68 us -> 296 us
    all_gather x1, waiting for transfers between devices: 212 us -> 57.5 us  [gather_rows(): return lax.all_gather(inner, ROWS, axis=1, tiled=True)]
    ppermute x31 -> x0, starting transfers between devices: 59.5 us -> none  [shifted(): lax.ppermute(value, axis, [(i, (i + by) % devices) for i in range(devices)])]
    add x31 -> x0, other arithmetic: 29.4 us -> none  [turn_one(): shifted(carry, 'dp', 1)]
    ppermute x8, waiting for transfers between devices: 0.02 us -> 20.1 us  [partner_2(): return lax.ppermute(block, axis, route)]
    all_gather x0 -> x1, blocking collectives: none -> 14.5 us  [gather_rows(): inner = lax.all_gather(w_up, COLS, axis=1, tiled=True)]
  transfers between devices with their start and end apart: 40 -> 11, of which waited for: 32 -> 4; matrix products, arithmetic and copies ran while one was open for 9% -> 5% of each run, Pallas kernels for 0% -> 0%
where the time goes in v1:
time: 526 us; the launch traced here: 525 us
  waiting for transfers between devices  373 us (71%)
  local copies, waits for them, and re-layouts  48.9 us (9%)
  starting transfers between devices  35.6 us (7%)
  matrix products  22.5 us (4%)
  other arithmetic  15.9 us (3%)
  blocking collectives  14.5 us (3%)
  between operations  14 us (3%)
    unnamed x5, waiting for transfers between devices  296 us
    all_gather x1, waiting for transfers between devices, gather_rows(): return lax.all_gather(inner, ROWS, axis=1, tiled=True)  57.5 us
    ppermute x8, starting transfers between devices, partner_2(): return lax.ppermute(block, axis, route)  35.3 us
    ppermute x8, waiting for transfers between devices, partner_2(): return lax.ppermute(block, axis, route)  20.1 us
    reshape x6, local copies, waits for them, and re-layouts, body(): product_term.reshape(BS, hidden_width) * keep_f[factor][None, :]  18.7 us
    all_gather x1, blocking collectives, gather_rows(): inner = lax.all_gather(w_up, COLS, axis=1, tiled=True)  14.5 us
    transpose x6, local copies, waits for them, and re-layouts, body(): jnp.einsum('ngb,ngc->bgc', gathered[factor], grad_pre, preferred_element_...  13.5 us
    dot_general x6, matrix products, body(): jnp.einsum('ngb,ngc->bgc', gathered[factor], grad_pre, preferred_element_...  12.2 us
  transfers between devices with their start and end apart: 11, of which 4 were waited for; matrix products, arithmetic and copies ran while one was open for 5% of the time, Pallas kernels for 0%

profile of v1, /device:TPU:24, one launch (start us, length us, event | category | flops | bytes accessed | tf_op | source)
XLA Modules:
  0.0 525.0 jit_solution(2290547591092084717)
XLA Ops:
  7.2 14.5 %all_gather.6 = bf16[6,32,1024]{2,1,0:T(8,128)(2,1)} all-gather(bf16[6,8,1024]{2,1,0:T(8,128)(2,1)} %param.6), channel_id=1, replica_groups=mesh['zl'=8,'xx'=4,'fly'=16] {'xx'}, dimensions={1}, use_global_device_ids=true | all-gather | bytes 491520 | tf_op jit(solution)/shard_map/all_gather | solution.py:36
  21.8 1.7 copy.79
  23.5 15.7 %collective-permute-start.3 = (bf16[128,512]{0,1:T(8,128)(2,1)}, bf16[128,512]{0,1:T(8,128)(2,1)}, u32[]{:S(2)}, u32[]{:S(2)}) collective-permute-start(bf16[128,512]{0,1:T(8,128)(2,1)} %copy.79), channel_id=1, source_target_pairs={{0,8},{8,0},{1,9},{9,1},{2,10},{10,2},{3,11},{11,3},{4,12},{12,4},... | collective-permute-start | bytes 393224 | tf_op jit(solution)/shard_map/ppermute | solution.py:20
  39.2 3.1 collective-permute-start.2
  42.4 1.9 collective-permute-start.1
  44.3 1.9 collective-permute-start
  48.1 1.9 copy.74
  51.7 57.5 %all-gather.2.cloned.1.call-done = bf16[6,256,1024]{2,1,0:T(8,128)(2,1)} async-done(((bf16[6,32,1024]{2,1,0:T(8,128)(2,1)}), bf16[6,256,1024]{2,1,0:T(8,128)(2,1)}) %all-gather.2.cloned.1.call-update) | async-done | bytes 3145744 | tf_op jit(solution)/shard_map/all_gather | solution.py:37
  109.2 2.1 broadcast_multiply_fusion
  114.7 1.2 copy.81
  117.0 1.2 fusion.17
  118.2 1.2 fusion.16
  119.4 1.2 fusion.15
  120.6 1.8 multiply_convert_fusion
  122.5 1.3 convolution_bitcast_fusion.5
  123.7 2.2 convolution_bitcast_fusion.4
  125.9 2.2 convolution_bitcast_fusion.3
  128.0 2.2 convolution_bitcast_fusion.2
  130.3 2.2 convolution_bitcast_fusion.1
  132.4 2.2 convolution_bitcast_fusion
  134.7 2.3 copy.103
  136.9 3.1 reshape.251
  140.0 2.3 copy.104
  142.3 3.1 reshape.252
  145.4 2.3 copy.106
  147.6 3.1 reshape.253
  150.7 2.3 copy.108
  153.0 3.1 reshape.254
  156.1 2.3 copy.110
  158.4 3.1 reshape.255
  161.5 2.3 copy.112
  163.7 3.2 reshape.256
  166.9 2.5 multiply_dynamic-update-slice_fusion.5
  169.4 2.4 multiply_dynamic-update-slice_fusion.4
  171.8 2.4 multiply_dynamic-update-slice_fusion.3
  175.3 1.1 multiply_dynamic-update-slice_fusion.1
  176.5 1.2 multiply_dynamic-update-slice_fusion
  177.9 1.3 dynamic-slice
  179.2 1.3 dynamic-slice.2
  182.9 275.6 %all-reduce.5.cloned.1.call-done = f32[8,32,6,1024]{3,1,0,2:T(8,128)} async-done(((f32[8,32,6,1024]{3,1,0,2:T(8,128)}), f32[8,32,6,1024]{3,1,0,2:T(8,128)}) %all-reduce.5.cloned.1.call-update) | async-done | bytes 6291472
  458.5 2.7 dynamic-slice_bitcast_fusion
  461.7 5.4 %collective-permute-start.7 = (f32[128,512]{0,1:T(8,128)}, f32[128,512]{0,1:T(8,128)S(1)}, u32[]{:S(2)}, u32[]{:S(2)}) collective-permute-start(f32[128,512]{0,1:T(8,128)} %bitcast.151), channel_id=1, source_target_pairs={{0,8},{8,0},{1,9},{9,1},{2,10},{10,2},{3,11},{11,3},{4,12},{12,4},... | collective-permute-start | bytes 786440 | tf_op jit(solution)/shard_map/ppermute | solution.py:20
  467.1 3.3 collective-permute-start.6
  470.5 1.9 collective-permute-start.5
  472.4 1.9 collective-permute-start.4
  475.0 20.0 %collective-permute-done.7 = f32[128,512]{0,1:T(8,128)S(1)} collective-permute-done((f32[128,512]{0,1:T(8,128)}, f32[128,512]{0,1:T(8,128)S(1)}, u32[]{:S(2)}, u32[]{:S(2)}) %collective-permute-start.7) | collective-permute-done | bytes 262176 | tf_op jit(solution)/shard_map/ppermute | solution.py:20
  495.9 20.3 %all-reduce.7.cloned.1.call-done = f32[4,8,6,1024]{3,1,0,2:T(8,128)} async-done(((f32[4,8,6,1024]{3,1,0,2:T(8,128)}), f32[4,8,6,1024]{3,1,0,2:T(8,128)}) %all-reduce.7.cloned.1.call-update) | async-done | bytes 786448
  516.2 2.3 fusion.5
  (64 shorter events, 13.8 us)
Async XLA Ops:
  7.2 102.1 %all-gather.2.cloned.1.call-start = ((), (), s32[]{:S(2)}) async-start(), calls=%async_computation | async-start | bytes 3538944 | tf_op jit(solution)/shard_map/all_gather | solution.py:37
  21.8 436.8 %all-reduce.5.cloned.1.call-start = ((), (), s32[]{:S(2)}) async-start(), calls=%async_computation.1 | async-start | bytes 12582912
  23.5 93.5 %collective-permute-start.3 = (bf16[128,512]{0,1:T(8,128)(2,1)}, bf16[128,512]{0,1:T(8,128)(2,1)}, u32[]{:S(2)}, u32[]{:S(2)}) collective-permute-start(bf16[128,512]{0,1:T(8,128)(2,1)} %copy.79), channel_id=1, source_target_pairs={{0,8},{8,0},{1,9},{9,1},{2,10},{10,2},{3,11},{11,3},{4,12},{12,4},... | collective-permute-start | bytes 393224 | tf_op jit(solution)/shard_map/ppermute | solution.py:20
  39.2 79.0 %collective-permute-start.2 = (bf16[128,512]{0,1:T(8,128)(2,1)}, bf16[128,512]{0,1:T(8,128)(2,1)}, u32[]{:S(2)}, u32[]{:S(2)}) collective-permute-start(bf16[128,512]{0,1:T(8,128)(2,1)} %copy.79), channel_id=1, source_target_pairs={{0,4},{4,0},{1,5},{5,1},{2,6},{6,2},{3,7},{7,3},{8,12},{12,8},{9,1... | collective-permute-start | bytes 393224 | tf_op jit(solution)/shard_map/ppermute | solution.py:20
  42.4 77.0 %collective-permute-start.1 = (bf16[128,512]{0,1:T(8,128)(2,1)}, bf16[128,512]{0,1:T(8,128)(2,1)}, u32[]{:S(2)}, u32[]{:S(2)}) collective-permute-start(bf16[128,512]{0,1:T(8,128)(2,1)} %copy.79), channel_id=1, source_target_pairs={{0,2},{2,0},{1,3},{3,1},{4,6},{6,4},{5,7},{7,5},{8,10},{10,8},{9,1... | collective-permute-start | bytes 393224 | tf_op jit(solution)/shard_map/ppermute | solution.py:20
  44.3 76.3 %collective-permute-start = (bf16[128,512]{0,1:T(8,128)(2,1)}, bf16[128,512]{0,1:T(8,128)(2,1)}, u32[]{:S(2)}, u32[]{:S(2)}) collective-permute-start(bf16[128,512]{0,1:T(8,128)(2,1)} %copy.79), channel_id=1, source_target_pairs={{0,1},{1,0},{2,3},{3,2},{4,5},{5,4},{6,7},{7,6},{8,9},{9,8},{10,11... | collective-permute-start | bytes 393224 | tf_op jit(solution)/shard_map/ppermute | solution.py:20
  50.0 63.2 %copy-start.5 = (bf16[128,1,2,1,256]{4,0,2,3,1:T(8,128)(2,1)}, bf16[128,1,2,1,256]{4,0,2,3,1:T(8,128)(2,1)S(1)}, u32[]{:S(2)}) copy-start(bf16[128,1,2,1,256]{4,0,2,3,1:T(8,128)(2,1)S(1)} %rev.4) | copy-start | bytes 393220
  109.2 3.7 copy-start.4
  161.5 13.9 %copy-start.7 = (f32[1,2,4,128]{3,1,2,0:T(2,128)S(1)}, f32[1,2,4,128]{3,1,2,0:T(2,128)}, u32[]{:S(2)}) copy-start(f32[1,2,4,128]{3,1,2,0:T(2,128)} %copy.144) | copy-start | bytes 12292
  163.7 12.7 %copy-start.6 = (f32[1,2,4,128]{3,1,2,0:T(2,128)S(1)}, f32[1,2,4,128]{3,1,2,0:T(2,128)}, u32[]{:S(2)}) copy-start(f32[1,2,4,128]{3,1,2,0:T(2,128)} %copy.145) | copy-start | bytes 12292
  166.9 7.3 %copy-start = (f32[8,32,1,1024]{3,1,0,2:T(8,128)S(1)}, f32[8,32,1,1024]{3,1,0,2:T(8,128)}, u32[]{:S(2)}) copy-start(f32[8,32,1,1024]{3,1,0,2:T(8,128)} %reshape.254) | copy-start | bytes 3145732
  166.9 8.4 %copy-start.1 = (f32[8,32,1,1024]{3,1,0,2:T(8,128)S(1)}, f32[8,32,1,1024]{3,1,0,2:T(8,128)}, u32[]{:S(2)}) copy-start(f32[8,32,1,1024]{3,1,0,2:T(8,128)} %reshape.255) | copy-start | bytes 3145732
  166.9 9.6 %copy-start.2 = (f32[8,32,1,1024]{3,1,0,2:T(8,128)S(1)}, f32[8,32,1,1024]{3,1,0,2:T(8,128)}, u32[]{:S(2)}) copy-start(f32[8,32,1,1024]{3,1,0,2:T(8,128)} %reshape.256) | copy-start | bytes 3145732
  177.6 283.7 %copy-start.3 = (bf16[1,256,1024]{1,2,0:T(8,128)(2,1)S(1)}, bf16[1,256,1024]{1,2,0:T(8,128)(2,1)}, u32[]{:S(2)}) copy-start(bf16[1,256,1024]{1,2,0:T(8,128)(2,1)} %copy.78) | copy-start | bytes 1572868
  177.7 338.5 %all-reduce.7.cloned.1.call-start = ((), (), s32[]{:S(2)}) async-start(), calls=%async_computation.2 | async-start | bytes 1572864
  461.7 33.4 %collective-permute-start.7 = (f32[128,512]{0,1:T(8,128)}, f32[128,512]{0,1:T(8,128)S(1)}, u32[]{:S(2)}, u32[]{:S(2)}) collective-permute-start(f32[128,512]{0,1:T(8,128)} %bitcast.151), channel_id=1, source_target_pairs={{0,8},{8,0},{1,9},{9,1},{2,10},{10,2},{3,11},{11,3},{4,12},{12,4},... | collective-permute-start | bytes 786440 | tf_op jit(solution)/shard_map/ppermute | solution.py:20
  467.1 28.0 %collective-permute-start.6 = (f32[128,512]{0,1:T(8,128)}, f32[128,512]{0,1:T(8,128)S(1)}, u32[]{:S(2)}, u32[]{:S(2)}) collective-permute-start(f32[128,512]{0,1:T(8,128)} %bitcast.22), channel_id=1, source_target_pairs={{0,4},{4,0},{1,5},{5,1},{2,6},{6,2},{3,7},{7,3},{8,12},{12,8},{9,1... | collective-permute-start | bytes 786440 | tf_op jit(solution)/shard_map/ppermute | solution.py:20
  470.5 24.6 %collective-permute-start.5 = (f32[128,512]{0,1:T(8,128)S(1)}, f32[128,512]{0,1:T(8,128)S(1)}, u32[]{:S(2)}, u32[]{:S(2)}) collective-permute-start(f32[128,512]{0,1:T(8,128)S(1)} %bitcast.150), channel_id=1, source_target_pairs={{0,2},{2,0},{1,3},{3,1},{4,6},{6,4},{5,7},{7,5},{8,10},{10,8},{9,1... | collective-permute-start | bytes 786440 | tf_op jit(solution)/shard_map/ppermute | solution.py:20
  472.4 22.7 %collective-permute-start.4 = (f32[128,512]{0,1:T(8,128)S(1)}, f32[128,512]{0,1:T(8,128)S(1)}, u32[]{:S(2)}, u32[]{:S(2)}) collective-permute-start(f32[128,512]{0,1:T(8,128)S(1)} %bitcast.152), channel_id=1, source_target_pairs={{0,1},{1,0},{2,3},{3,2},{4,5},{5,4},{6,7},{7,6},{8,9},{9,8},{10,11... | collective-permute-start | bytes 786440 | tf_op jit(solution)/shard_map/ppermute | solution.py:20
Sparse Core Ops, SparseCore 0:
  21.9 87.2 all-gather.1
  177.8 280.7 all-reduce.4
  461.4 54.7 all-reduce.6

commit v2 on v1

--- a/solution.py
+++ b/solution.py
@@ -41,9 +41,13 @@
     rows, factor_count, width = terms.shape
     zl = lax.axis_size(ROWS)
     xx = lax.axis_size(COLS)
-    part = lax.psum_scatter(terms.reshape(zl, rows // zl, factor_count, width), ROWS, scatter_dimension=0, tiled=True)
-    part = lax.psum_scatter(part.reshape(xx, rows // (zl * xx), factor_count, width), COLS, scatter_dimension=0, tiled=True)
-    return part.reshape(rows // (zl * xx), factor_count, width).transpose(1, 0, 2)
+    own = rows // (zl * xx)
+    by_col = terms.reshape(zl, xx, own, factor_count, width).transpose(1, 0, 2, 3, 4)
+    got = lax.all_to_all(by_col.astype(jnp.bfloat16), COLS, 0, 0, tiled=True)
+    part = got.astype(jnp.float32).reshape(xx, zl, own, factor_count, width).sum(0)
+    got = lax.all_to_all(part.astype(jnp.bfloat16), ROWS, 0, 0, tiled=True)
+    part = got.astype(jnp.float32).reshape(zl, own, factor_count, width).sum(0)
+    return part.transpose(1, 0, 2)
 
 
 def body(tokens, hidden_grad, w_up, pattern):

time: 526 us -> 285 us (0.54)
  waiting for transfers between devices: 373 us -> 98.1 us
  blocking collectives: 14.5 us -> 55.5 us
  starting transfers between devices: 35.6 us -> 46 us
  other arithmetic: 15.9 us -> 7.2 us
  local copies, waits for them, and re-layouts: 48.9 us -> 42.5 us
    unnamed x5 -> x1, waiting for transfers between devices: 296 us -> 0.02 us
    all_to_all x0 -> x1, blocking collectives: none -> 41 us  [scatter_rows(): got = lax.all_to_all(by_col.astype(jnp.bfloat16), COLS, 0, 0, tiled=True)]
    all_to_all x0 -> x1, waiting for transfers between devices: none -> 28.3 us  [scatter_rows(): got = lax.all_to_all(part.astype(jnp.bfloat16), ROWS, 0, 0, tiled=True)]
    unnamed x5, other arithmetic: 9.57 us -> 0.48 us
    ppermute x8, waiting for transfers between devices: 20.1 us -> 12.3 us  [partner_2(): return lax.ppermute(block, axis, route)]
    all_to_all x0 -> x1, starting transfers between devices: none -> 7.74 us  [scatter_rows(): got = lax.all_to_all(part.astype(jnp.bfloat16), ROWS, 0, 0, tiled=True)]
  transfers between devices with their start and end apart: 11 -> 10, of which waited for: 4 -> 3; matrix products, arithmetic and copies ran while one was open for 5% -> 8% of each run, Pallas kernels for 0% -> 0%
where the time goes in v2:
time: 285 us; the launch traced here: 284 us
  waiting for transfers between devices  98.1 us (34%)
  blocking collectives  55.5 us (19%)
  starting transfers between devices  46 us (16%)
  local copies, waits for them, and re-layouts  42.5 us (15%)
  matrix products  20.1 us (7%)
  between operations  14.6 us (5%)
  other arithmetic  7.2 us (3%)
    all_gather x1, waiting for transfers between devices, gather_rows(): return lax.all_gather(inner, ROWS, axis=1, tiled=True)  57.5 us
    all_to_all x1, blocking collectives, scatter_rows(): got = lax.all_to_all(by_col.astype(jnp.bfloat16), COLS, 0, 0, tiled=True)  41 us
    ppermute x8, starting transfers between devices, partner_2(): return lax.ppermute(block, axis, route)  38.3 us
    all_to_all x1, waiting for transfers between devices, scatter_rows(): got = lax.all_to_all(part.astype(jnp.bfloat16), ROWS, 0, 0, tiled=True)  28.3 us
    reshape x6, local copies, waits for them, and re-layouts, body(): product_term.reshape(BS, hidden_width) * keep_f[factor][None, :]  16.8 us
    all_gather x1, blocking collectives, gather_rows(): inner = lax.all_gather(w_up, COLS, axis=1, tiled=True)  14.5 us
    ppermute x8, waiting for transfers between devices, partner_2(): return lax.ppermute(block, axis, route)  12.3 us
    transpose x6, local copies, waits for them, and re-layouts, body(): jnp.einsum('ngb,ngc->bgc', gathered[factor], grad_pre, preferred_element_...  10.9 us
  transfers between devices with their start and end apart: 10, of which 3 were waited for; matrix products, arithmetic and copies ran while one was open for 8% of the time, Pallas kernels for 0%

profile of v2, /device:TPU:24, one launch (start us, length us, event | category | flops | bytes accessed | tf_op | source)
XLA Modules:
  0.0 283.9 jit_solution(2755230294232068413)
XLA Ops:
  7.2 14.5 %all_gather.6 = bf16[6,32,1024]{2,1,0:T(8,128)(2,1)} all-gather(bf16[6,8,1024]{2,1,0:T(8,128)(2,1)} %param.6), channel_id=1, replica_groups=mesh['zl'=8,'xx'=4,'fly'=16] {'xx'}, dimensions={1}, use_global_device_ids=true | all-gather | bytes 491520 | tf_op jit(solution)/shard_map/all_gather | solution.py:36
  21.8 1.7 copy.79
  23.4 15.7 %collective-permute-start.3 = (bf16[128,512]{0,1:T(8,128)(2,1)}, bf16[128,512]{0,1:T(8,128)(2,1)}, u32[]{:S(2)}, u32[]{:S(2)}) collective-permute-start(bf16[128,512]{0,1:T(8,128)(2,1)} %copy.79), channel_id=1, source_target_pairs={{0,8},{8,0},{1,9},{9,1},{2,10},{10,2},{3,11},{11,3},{4,12},{12,4},... | collective-permute-start | bytes 393224 | tf_op jit(solution)/shard_map/ppermute | solution.py:20
  39.1 3.1 %collective-permute-start.2 = (bf16[128,512]{0,1:T(8,128)(2,1)}, bf16[128,512]{0,1:T(8,128)(2,1)}, u32[]{:S(2)}, u32[]{:S(2)}) collective-permute-start(bf16[128,512]{0,1:T(8,128)(2,1)} %copy.79), channel_id=1, source_target_pairs={{0,4},{4,0},{1,5},{5,1},{2,6},{6,2},{3,7},{7,3},{8,12},{12,8},{9,1... | collective-permute-start | bytes 393224 | tf_op jit(solution)/shard_map/ppermute | solution.py:20
  42.3 1.9 collective-permute-start.1
  44.2 1.9 collective-permute-start
  46.2 0.9 reshape_reshape.3
  48.1 1.9 copy.74
  51.7 57.5 %all-gather.2.cloned.1.call-done = bf16[6,256,1024]{2,1,0:T(8,128)(2,1)} async-done(((bf16[6,32,1024]{2,1,0:T(8,128)(2,1)}), bf16[6,256,1024]{2,1,0:T(8,128)(2,1)}) %all-gather.2.cloned.1.call-update) | async-done | bytes 3145744 | tf_op jit(solution)/shard_map/all_gather | solution.py:37
  109.2 2.1 broadcast_multiply_fusion
  111.3 1.2 fusion.18
  113.2 1.1 convolution_add_fusion.1
  114.7 1.4 copy.81
  116.4 1.4 fusion.22
  117.8 1.2 fusion.21
  119.0 1.2 fusion.20
  120.3 1.3 multiply_convert_fusion.6
  121.7 1.3 convolution_bitcast_fusion.5
  123.2 2.3 convolution_bitcast_fusion.3
  125.5 2.2 convolution_bitcast_fusion.2
  127.7 2.2 convolution_bitcast_fusion.1
  129.9 1.2 convolution_bitcast_fusion
  131.1 1.5 copy.103
  132.5 2.1 reshape.245
  134.7 1.3 copy.104
  136.0 2.1 reshape.246
  138.1 2.3 copy.106
  140.4 3.1 %reshape.247 = f32[8,4,8,1,1024]{4,2,1,0,3:T(8,128)} reshape(f32[256,2,512]{2,1,0:T(2,128)} %copy.106) | data formatting | bytes 2097152 | tf_op jit(solution)/shard_map/reshape | solution.py:105
  143.5 2.3 copy.108
  145.7 3.1 %reshape.248 = f32[8,4,8,1,1024]{4,2,1,0,3:T(8,128)} reshape(f32[256,2,512]{2,1,0:T(2,128)} %copy.108) | data formatting | bytes 2097152 | tf_op jit(solution)/shard_map/reshape | solution.py:105
  148.8 2.3 copy.110
  151.1 3.1 %reshape.249 = f32[8,4,8,1,1024]{4,2,1,0,3:T(8,128)} reshape(f32[256,2,512]{2,1,0:T(2,128)} %copy.110) | data formatting | bytes 2097152 | tf_op jit(solution)/shard_map/reshape | solution.py:105
  154.2 1.3 copy.112
  155.5 3.2 %reshape.250 = f32[8,4,8,1,1024]{4,2,1,0,3:T(8,128)} reshape(f32[256,2,512]{2,1,0:T(2,128)} %copy.112) | data formatting | bytes 2097152 | tf_op jit(solution)/shard_map/reshape | solution.py:105
  161.1 41.0 %all_to_all.10 = bf16[4,8,8,6,1024]{4,2,1,3,0:T(8,128)(2,1)S(1)} all-to-all(bf16[4,8,8,6,1024]{4,2,1,3,0:T(8,128)(2,1)S(1)} %copy.113), channel_id=1, replica_groups=mesh['zl'=8,'xx'=4,'fly'=16] {'xx'}, dimensions={0} | all-to-all | bytes 6291456 | tf_op jit(solution)/shard_map/all_to_all | solution.py:46
  202.1 1.7 reduce_sum.21
  203.8 2.2 copy.115
  206.1 7.7 %all-to-all-start.1 = ((bf16[8,8,6,1024]{3,1,2,0:T(8,128)(2,1)}), bf16[8,8,6,1024]{3,1,2,0:T(8,128)(2,1)}, u32[]{:S(2)}, u32[]{:S(2)}) async-start(bf16[8,8,6,1024]{3,1,2,0:T(8,128)(2,1)} %copy.115), calls=%async_computation.1 | async-start | bytes 1572864 | tf_op jit(solution)/shard_map/all_to_all | solution.py:48
  213.8 1.1 fusion.26
  214.9 8.6 %collective-permute-start.7 = (f32[128,512]{0,1:T(8,128)}, f32[128,512]{0,1:T(8,128)S(1)}, u32[]{:S(2)}, u32[]{:S(2)}) collective-permute-start(f32[128,512]{0,1:T(8,128)} %bitcast.25), channel_id=1, source_target_pairs={{0,8},{8,0},{1,9},{9,1},{2,10},{10,2},{3,11},{11,3},{4,12},{12,4},... | collective-permute-start | bytes 786440 | tf_op jit(solution)/shard_map/ppermute | solution.py:20
  223.5 1.1 fusion.25
  224.5 3.2 %collective-permute-start.6 = (f32[128,512]{0,1:T(8,128)}, f32[128,512]{0,1:T(8,128)S(1)}, u32[]{:S(2)}, u32[]{:S(2)}) collective-permute-start(f32[128,512]{0,1:T(8,128)} %bitcast.22), channel_id=1, source_target_pairs={{0,4},{4,0},{1,5},{5,1},{2,6},{6,2},{3,7},{7,3},{8,12},{12,8},{9,1... | collective-permute-start | bytes 786440 | tf_op jit(solution)/shard_map/ppermute | solution.py:20
  228.0 1.9 collective-permute-start.5
  230.0 1.1 fusion.23
  231.0 1.9 collective-permute-start.4
  233.7 12.3 %collective-permute-done.7 = f32[128,512]{0,1:T(8,128)S(1)} collective-permute-done((f32[128,512]{0,1:T(8,128)}, f32[128,512]{0,1:T(8,128)S(1)}, u32[]{:S(2)}, u32[]{:S(2)}) %collective-permute-start.7) | collective-permute-done | bytes 262176 | tf_op jit(solution)/shard_map/ppermute | solution.py:20
  246.9 28.3 %all-to-all-done.1 = bf16[8,8,6,1024]{3,1,2,0:T(8,128)(2,1)} async-done(((bf16[8,8,6,1024]{3,1,2,0:T(8,128)(2,1)}), bf16[8,8,6,1024]{3,1,2,0:T(8,128)(2,1)}, u32[]{:S(2)}, u32[]{:S(2)}) %all-to-all-start.1) | async-done | bytes 786464 | tf_op jit(solution)/shard_map/all_to_all | solution.py:48
  275.1 1.3 convert_reduce_fusion
  (94 shorter events, 9.3 us)
Async XLA Ops:
  7.2 102.0 %all-gather.2.cloned.1.call-start = ((), (), s32[]{:S(2)}) async-start(), calls=%async_computation.2 | async-start | bytes 3538944 | tf_op jit(solution)/shard_map/all_gather | solution.py:37
  23.4 93.0 %collective-permute-start.3 = (bf16[128,512]{0,1:T(8,128)(2,1)}, bf16[128,512]{0,1:T(8,128)(2,1)}, u32[]{:S(2)}, u32[]{:S(2)}) collective-permute-start(bf16[128,512]{0,1:T(8,128)(2,1)} %copy.79), channel_id=1, source_target_pairs={{0,8},{8,0},{1,9},{9,1},{2,10},{10,2},{3,11},{11,3},{4,12},{12,4},... | collective-permute-start | bytes 393224 | tf_op jit(solution)/shard_map/ppermute | solution.py:20
  39.1 78.7 %collective-permute-start.2 = (bf16[128,512]{0,1:T(8,128)(2,1)}, bf16[128,512]{0,1:T(8,128)(2,1)}, u32[]{:S(2)}, u32[]{:S(2)}) collective-permute-start(bf16[128,512]{0,1:T(8,128)(2,1)} %copy.79), channel_id=1, source_target_pairs={{0,4},{4,0},{1,5},{5,1},{2,6},{6,2},{3,7},{7,3},{8,12},{12,8},{9,1... | collective-permute-start | bytes 393224 | tf_op jit(solution)/shard_map/ppermute | solution.py:20
  42.3 76.7 %collective-permute-start.1 = (bf16[128,512]{0,1:T(8,128)(2,1)}, bf16[128,512]{0,1:T(8,128)(2,1)}, u32[]{:S(2)}, u32[]{:S(2)}) collective-permute-start(bf16[128,512]{0,1:T(8,128)(2,1)} %copy.79), channel_id=1, source_target_pairs={{0,2},{2,0},{1,3},{3,1},{4,6},{6,4},{5,7},{7,5},{8,10},{10,8},{9,1... | collective-permute-start | bytes 393224 | tf_op jit(solution)/shard_map/ppermute | solution.py:20
  44.2 76.1 %collective-permute-start = (bf16[128,512]{0,1:T(8,128)(2,1)}, bf16[128,512]{0,1:T(8,128)(2,1)}, u32[]{:S(2)}, u32[]{:S(2)}) collective-permute-start(bf16[128,512]{0,1:T(8,128)(2,1)} %copy.79), channel_id=1, source_target_pairs={{0,1},{1,0},{2,3},{3,2},{4,5},{5,4},{6,7},{7,6},{8,9},{9,8},{10,11... | collective-permute-start | bytes 393224 | tf_op jit(solution)/shard_map/ppermute | solution.py:20
  50.0 63.2 %copy-start.18 = (bf16[128,1,2,1,256]{4,0,2,3,1:T(8,128)(2,1)}, bf16[128,1,2,1,256]{4,0,2,3,1:T(8,128)(2,1)S(1)}, u32[]{:S(2)}) copy-start(bf16[128,1,2,1,256]{4,0,2,3,1:T(8,128)(2,1)S(1)} %rev.4) | copy-start | bytes 393220
  111.3 1.6 copy-start.17
  112.6 3.5 %copy-start = (bf16[1,256,1024]{1,2,0:T(8,128)(2,1)}, bf16[1,256,1024]{1,2,0:T(8,128)(2,1)S(1)}, u32[]{:S(2)}) copy-start(bf16[1,256,1024]{1,2,0:T(8,128)(2,1)S(1)} %copy.73) | copy-start | bytes 1572868
  112.9 3.5 %copy-start.2 = (bf16[1,256,1024]{1,2,0:T(8,128)(2,1)}, bf16[1,256,1024]{1,2,0:T(8,128)(2,1)S(1)}, u32[]{:S(2)}) copy-start(bf16[1,256,1024]{1,2,0:T(8,128)(2,1)S(1)} %copy.76) | copy-start | bytes 1572868
  114.5 5.8 %copy-start.8 = (bf16[1,256,1024]{1,2,0:T(8,128)(2,1)}, bf16[1,256,1024]{1,2,0:T(8,128)(2,1)S(1)}, u32[]{:S(2)}) copy-start(bf16[1,256,1024]{1,2,0:T(8,128)(2,1)S(1)} %copy.87) | copy-start | bytes 1572868
  114.7 6.9 %copy-start.6 = (bf16[1,256,1024]{1,2,0:T(8,128)(2,1)}, bf16[1,256,1024]{1,2,0:T(8,128)(2,1)S(1)}, u32[]{:S(2)}) copy-start(bf16[1,256,1024]{1,2,0:T(8,128)(2,1)S(1)} %copy.84) | copy-start | bytes 1572868
  116.2 5.5 %copy-start.4 = (bf16[1,256,1024]{1,2,0:T(8,128)(2,1)}, bf16[1,256,1024]{1,2,0:T(8,128)(2,1)S(1)}, u32[]{:S(2)}) copy-start(bf16[1,256,1024]{1,2,0:T(8,128)(2,1)S(1)} %copy.81) | copy-start | bytes 1572868
  116.4 5.3 %copy-start.15 = (bf16[1,256,1024]{1,2,0:T(8,128)(2,1)}, bf16[1,256,1024]{1,2,0:T(8,128)(2,1)S(1)}, u32[]{:S(2)}) copy-start(bf16[1,256,1024]{1,2,0:T(8,128)(2,1)S(1)} %copy.78) | copy-start | bytes 1572868
  116.4 3.9 %copy-start.20 = (f32[128,1024]{0,1:T(8,128)S(1)}, f32[128,1024]{0,1:T(8,128)}, u32[]{:S(2)}) copy-start(f32[128,1024]{0,1:T(8,128)} %copy.74) | copy-start | bytes 1572868
  116.4 3.9 %copy-start.21 = (f32[2,512,128]{2,1,0:T(8,128)S(1)}, f32[2,512,128]{2,1,0:T(8,128)}, u32[]{:S(2)}) copy-start(f32[2,512,128]{2,1,0:T(8,128)} %convolution_add_fusion.1) | copy-start | bytes 1572868
  119.0 3.9 %copy-start.19 = (bf16[128,1,2,1,256]{4,0,2,3,1:T(8,128)(2,1)S(1)}, bf16[128,1,2,1,256]{4,0,2,3,1:T(8,128)(2,1)}, u32[]{:S(2)}) copy-start(bf16[128,1,2,1,256]{4,0,2,3,1:T(8,128)(2,1)} %copy-done.18) | copy-start | bytes 393220
  123.2 7.8 %copy-start.14 = (f32[256,2,512]{0,2,1:T(8,128)S(1)}, f32[256,2,512]{0,2,1:T(8,128)}, u32[]{:S(2)}) copy-start(f32[256,2,512]{0,2,1:T(8,128)} %convolution_bitcast_fusion.5) | copy-start | bytes 3145732
  155.5 3.4 %copy-start.10 = (f32[8,4,8,1,1024]{4,2,1,0,3:T(8,128)S(1)}, f32[8,4,8,1,1024]{4,2,1,0,3:T(8,128)}, u32[]{:S(2)}) copy-start(f32[8,4,8,1,1024]{4,2,1,0,3:T(8,128)} %reshape.247) | copy-start | bytes 3145732
  158.7 1.2 copy-start.11
  158.7 1.5 copy-start.12
  158.7 1.5 copy-start.23
  158.8 1.8 copy-start.13
  158.8 1.8 copy-start.22
  203.8 10.0 %copy-start.9 = (bf16[1,256,1024]{1,2,0:T(8,128)(2,1)S(1)}, bf16[1,256,1024]{1,2,0:T(8,128)(2,1)}, u32[]{:S(2)}) copy-start(bf16[1,256,1024]{1,2,0:T(8,128)(2,1)} %copy-done.8) | copy-start | bytes 1572868
  203.8 19.6 %copy-start.7 = (bf16[1,256,1024]{1,2,0:T(8,128)(2,1)S(1)}, bf16[1,256,1024]{1,2,0:T(8,128)(2,1)}, u32[]{:S(2)}) copy-start(bf16[1,256,1024]{1,2,0:T(8,128)(2,1)} %copy-done.6) | copy-start | bytes 1572868
  203.8 23.9 %copy-start.5 = (bf16[1,256,1024]{1,2,0:T(8,128)(2,1)S(1)}, bf16[1,256,1024]{1,2,0:T(8,128)(2,1)}, u32[]{:S(2)}) copy-start(bf16[1,256,1024]{1,2,0:T(8,128)(2,1)} %copy-done.4) | copy-start | bytes 1572868
  203.8 26.1 %copy-start.16 = (bf16[1,256,1024]{1,2,0:T(8,128)(2,1)S(1)}, bf16[1,256,1024]{1,2,0:T(8,128)(2,1)}, u32[]{:S(2)}) copy-start(bf16[1,256,1024]{1,2,0:T(8,128)(2,1)} %copy-done.15) | copy-start | bytes 1572868
  206.1 26.9 %copy-start.3 = (bf16[1,256,1024]{1,2,0:T(8,128)(2,1)S(1)}, bf16[1,256,1024]{1,2,0:T(8,128)(2,1)}, u32[]{:S(2)}) copy-start(bf16[1,256,1024]{1,2,0:T(8,128)(2,1)} %copy-done.2) | copy-start | bytes 1572868
  206.1 69.1 %all-to-all-start.1 = ((bf16[8,8,6,1024]{3,1,2,0:T(8,128)(2,1)}), bf16[8,8,6,1024]{3,1,2,0:T(8,128)(2,1)}, u32[]{:S(2)}, u32[]{:S(2)}) async-start(bf16[8,8,6,1024]{3,1,2,0:T(8,128)(2,1)} %copy.115), calls=%async_computation.1 | async-start | bytes 1572864 | tf_op jit(solution)/shard_map/all_to_all | solution.py:48
  213.8 19.5 %copy-start.1 = (bf16[1,256,1024]{1,2,0:T(8,128)(2,1)S(1)}, bf16[1,256,1024]{1,2,0:T(8,128)(2,1)}, u32[]{:S(2)}) copy-start(bf16[1,256,1024]{1,2,0:T(8,128)(2,1)} %copy-done) | copy-start | bytes 1572868
  214.9 31.1 %collective-permute-start.7 = (f32[128,512]{0,1:T(8,128)}, f32[128,512]{0,1:T(8,128)S(1)}, u32[]{:S(2)}, u32[]{:S(2)}) collective-permute-start(f32[128,512]{0,1:T(8,128)} %bitcast.25), channel_id=1, source_target_pairs={{0,8},{8,0},{1,9},{9,1},{2,10},{10,2},{3,11},{11,3},{4,12},{12,4},... | collective-permute-start | bytes 786440 | tf_op jit(solution)/shard_map/ppermute | solution.py:20
  224.5 21.5 %collective-permute-start.6 = (f32[128,512]{0,1:T(8,128)}, f32[128,512]{0,1:T(8,128)S(1)}, u32[]{:S(2)}, u32[]{:S(2)}) collective-permute-start(f32[128,512]{0,1:T(8,128)} %bitcast.22), channel_id=1, source_target_pairs={{0,4},{4,0},{1,5},{5,1},{2,6},{6,2},{3,7},{7,3},{8,12},{12,8},{9,1... | collective-permute-start | bytes 786440 | tf_op jit(solution)/shard_map/ppermute | solution.py:20
  228.0 18.0 %collective-permute-start.5 = (f32[128,512]{0,1:T(8,128)S(1)}, f32[128,512]{0,1:T(8,128)S(1)}, u32[]{:S(2)}, u32[]{:S(2)}) collective-permute-start(f32[128,512]{0,1:T(8,128)S(1)} %bitcast.138), channel_id=1, source_target_pairs={{0,2},{2,0},{1,3},{3,1},{4,6},{6,4},{5,7},{7,5},{8,10},{10,8},{9,1... | collective-permute-start | bytes 786440 | tf_op jit(solution)/shard_map/ppermute | solution.py:20
  231.0 15.0 %collective-permute-start.4 = (f32[128,512]{0,1:T(8,128)}, f32[128,512]{0,1:T(8,128)S(1)}, u32[]{:S(2)}, u32[]{:S(2)}) collective-permute-start(f32[128,512]{0,1:T(8,128)} %bitcast.16), channel_id=1, source_target_pairs={{0,1},{1,0},{2,3},{3,2},{4,5},{5,4},{6,7},{7,6},{8,9},{9,8},{10,11... | collective-permute-start | bytes 786440 | tf_op jit(solution)/shard_map/ppermute | solution.py:20
Sparse Core Ops, SparseCore 0:
  21.9 87.2 all-gather.1

commit v3 on v2

--- a/solution.py
+++ b/solution.py
@@ -38,15 +38,11 @@
 
 
 def scatter_rows(terms):
-    rows, factor_count, width = terms.shape
-    zl = lax.axis_size(ROWS)
-    xx = lax.axis_size(COLS)
-    own = rows // (zl * xx)
-    by_col = terms.reshape(zl, xx, own, factor_count, width).transpose(1, 0, 2, 3, 4)
-    got = lax.all_to_all(by_col.astype(jnp.bfloat16), COLS, 0, 0, tiled=True)
-    part = got.astype(jnp.float32).reshape(xx, zl, own, factor_count, width).sum(0)
+    xx, zl, own, factor_count, width = terms.shape
+    got = lax.all_to_all(terms, COLS, 0, 0, tiled=True)
+    part = got.astype(jnp.float32).sum(0)
     got = lax.all_to_all(part.astype(jnp.bfloat16), ROWS, 0, 0, tiled=True)
-    part = got.astype(jnp.float32).reshape(zl, own, factor_count, width).sum(0)
+    part = got.astype(jnp.float32).sum(0)
     return part.transpose(1, 0, 2)
 
 
@@ -56,6 +52,9 @@
     hidden_width = hidden_grad.shape[1]
     local_blocks = local_width // BS
     group_width = hidden_width // local_blocks
+    zl = lax.axis_size(ROWS)
+    xx = lax.axis_size(COLS)
+    own = BS // (zl * xx)
     weights = gather_rows(w_up)
     keep_cols = jnp.broadcast_to(pattern[:, :, None], (factor_count, pattern.shape[1], BS)).reshape(
         factor_count, hidden_width
@@ -63,7 +62,7 @@
     masked = (weights * keep_cols.astype(jnp.bfloat16)[:, None, :]).reshape(
         factor_count, BS, local_blocks, group_width
     )
-    keep_f = keep_cols.astype(jnp.float32)
+    keep_f = keep_cols.astype(jnp.float32).reshape(factor_count, local_blocks, group_width)
     token_blocks = tokens.reshape(row_count, local_blocks, BS)
     gathered = []
     for factor in range(factor_count):
@@ -74,22 +73,36 @@
             bit_number = (stride // local_blocks).bit_length() - 1
             partner = partner_2(tokens, "fly", bit_number)
             gathered.append(partner.reshape(row_count, local_blocks, BS))
-    pre_act = jnp.zeros((row_count, local_blocks, group_width), jnp.float32)
-    for factor in range(factor_count):
-        pre_act = pre_act + jnp.einsum(
-            "ngb,bgc->ngc", gathered[factor], masked[factor], preferred_element_type=jnp.float32
+    reads = jnp.stack(gathered, axis=2)
+    grads = []
+    contribs = []
+    products = []
+    for group in range(local_blocks):
+        lhs = reads[:, group].reshape(row_count, factor_count * BS)
+        rhs = masked[:, :, group, :].reshape(factor_count * BS, group_width)
+        pre_act = jnp.dot(lhs, rhs, preferred_element_type=jnp.float32)
+        squash = jax.nn.sigmoid(pre_act)
+        derivative = squash * (1.0 + pre_act * (1.0 - squash))
+        grad_pre = (hidden_grad[:, group * group_width:(group + 1) * group_width].astype(jnp.float32) * derivative).astype(
+            jnp.bfloat16
         )
-    squash = jax.nn.sigmoid(pre_act)
-    derivative = squash * (1.0 + pre_act * (1.0 - squash))
-    grad_pre = (
-        hidden_grad.reshape(row_count, local_blocks, group_width).astype(jnp.float32) * derivative
-    ).astype(jnp.bfloat16)
+        contribs.append(
+            lax.dot_general(grad_pre, rhs, (((1,), (1,)), ((), ())), preferred_element_type=jnp.float32).reshape(
+                row_count, factor_count, BS
+            )
+        )
+        cols = reads[:, group].reshape(row_count, factor_count, zl, xx, own).transpose(0, 3, 2, 4, 1)
+        products.append(
+            lax.dot_general(
+                cols.reshape(row_count, BS * factor_count), grad_pre, (((0,), (0,)), ((), ())),
+                preferred_element_type=jnp.float32,
+            ).reshape(xx, zl, own, factor_count, group_width)
+        )
+    contrib_all = jnp.stack(contribs, axis=1)
     input_total = jnp.zeros((row_count, local_blocks, BS), jnp.float32)
     for factor in range(factor_count):
         stride = stride_of(factor)
-        contrib = jnp.einsum(
-            "ngc,bgc->ngb", grad_pre, masked[factor], preferred_element_type=jnp.float32
-        )
+        contrib = contrib_all[:, :, factor, :]
         if stride < local_blocks:
             input_total = input_total + flip_blocks(contrib, stride)
         else:
@@ -97,14 +110,9 @@
             returned = partner_2(contrib.reshape(row_count, local_width), "fly", bit_number)
             input_total = input_total + returned.reshape(row_count, local_blocks, BS)
     input_grad = input_total.reshape(row_count, local_width).astype(jnp.bfloat16)
-    terms = []
-    for factor in range(factor_count):
-        product_term = jnp.einsum(
-            "ngb,ngc->bgc", gathered[factor], grad_pre, preferred_element_type=jnp.float32
-        )
-        terms.append(product_term.reshape(BS, hidden_width) * keep_f[factor][None, :])
-    summed = scatter_rows(jnp.stack(terms, axis=1))
-    weight_grad = summed * (1.0 / (lax.axis_size(ROWS) * lax.axis_size(COLS)))
+    terms = jnp.stack(products, axis=4) * keep_f[None, None, None]
+    summed = scatter_rows(terms.reshape(xx, zl, own, factor_count, hidden_width).astype(jnp.bfloat16))
+    weight_grad = summed * (1.0 / (zl * xx))
     return (input_grad, weight_grad)
 
 

time: 285 us -> 262 us (0.919)
  local copies, waits for them, and re-layouts: 42.5 us -> 20.3 us
  matrix products: 20.1 us -> 6.95 us
  waiting for transfers between devices: 98.1 us -> 106 us
  other arithmetic: 7.2 us -> 10.7 us
    reshape x7 -> x2, local copies, waits for them, and re-layouts: 16.8 us -> 0.28 us  [body(): cols.reshape(row_count, BS * factor_count)]
    dot_general x18 -> x6, matrix products: 20.1 us -> 6.95 us  [the longest x2 3.9 us: body(): pre_act = jnp.dot(lhs, rhs, preferred_element_type=jnp.float32)]
    transpose x6 -> x2, local copies, waits for them, and re-layouts: 10.9 us -> 0.55 us  [body(): reads[:, group].reshape(row_count, factor_count, zl, xx, own)]
    ppermute x8, waiting for transfers between devices: 12.3 us -> 17.9 us  [partner_2(): return lax.ppermute(block, axis, route)]
    all_gather x0 -> x1, local copies, waits for them, and re-layouts: none -> 4.66 us  [gather_rows(): return lax.all_gather(inner, ROWS, axis=1, tiled=True)]
    unnamed x61 -> x33, local copies, waits for them, and re-layouts: 5.38 us -> 8.71 us
  transfers between devices with their start and end apart: 10 -> 10, of which waited for: 3 -> 5; matrix products, arithmetic and copies ran while one was open for 8% -> 4% of each run, Pallas kernels for 0% -> 0%
where the time goes in v3:
time: 262 us; the launch traced here: 260 us
  waiting for transfers between devices  106 us (40%)
  blocking collectives  55.9 us (21%)
  starting transfers between devices  45.9 us (18%)
  local copies, waits for them, and re-layouts  20.3 us (8%)
  between operations  14.5 us (6%)
  other arithmetic  10.7 us (4%)
  matrix products  6.95 us (3%)
    all_gather x1, waiting for transfers between devices, gather_rows(): return lax.all_gather(inner, ROWS, axis=1, tiled=True)  57.8 us
    all_to_all x1, blocking collectives, scatter_rows(): got = lax.all_to_all(terms, COLS, 0, 0, tiled=True)  41.3 us
    ppermute x8, starting transfers between devices, partner_2(): return lax.ppermute(block, axis, route)  40.7 us
    all_to_all x1, waiting for transfers between devices, scatter_rows(): got = lax.all_to_all(part.astype(jnp.bfloat16), ROWS, 0, 0, tiled=True)  29.9 us
    ppermute x8, waiting for transfers between devices, partner_2(): return lax.ppermute(block, axis, route)  17.9 us
    all_gather x1, blocking collectives, gather_rows(): inner = lax.all_gather(w_up, COLS, axis=1, tiled=True)  14.5 us
    unnamed x33, local copies, waits for them, and re-layouts  8.71 us
  transfers between devices with their start and end apart: 10, of which 5 were waited for; matrix products, arithmetic and copies ran while one was open for 4% of the time, Pallas kernels for 0%

profile of v3, /device:TPU:24, one launch (start us, length us, event | category | flops | bytes accessed | tf_op | source)
XLA Modules:
  0.0 259.9 jit_solution(12678838551769811864)
XLA Ops:
  7.2 14.5 %all_gather.6 = bf16[6,32,1024]{2,1,0:T(8,128)(2,1)} all-gather(bf16[6,8,1024]{2,1,0:T(8,128)(2,1)} %param.6), channel_id=1, replica_groups=mesh['zl'=8,'xx'=4,'fly'=16] {'xx'}, dimensions={1}, use_global_device_ids=true | all-gather | bytes 491520 | tf_op jit(solution)/shard_map/all_gather | solution.py:36
  21.8 1.9 collective-permute-start
  23.7 2.7 %collective-permute-start.1 = (bf16[128,512]{1,0:T(8,128)(2,1)}, bf16[128,512]{1,0:T(8,128)(2,1)S(1)}, u32[]{:S(2)}, u32[]{:S(2)}) collective-permute-start(bf16[128,512]{1,0:T(8,128)(2,1)} %param.4), channel_id=1, source_target_pairs={{0,2},{2,0},{1,3},{3,1},{4,6},{6,4},{5,7},{7,5},{8,10},{10,8},{9,1... | collective-permute-start | bytes 393224 | tf_op jit(solution)/shard_map/ppermute | solution.py:20
  26.4 7.3 %collective-permute-start.2 = (bf16[128,512]{1,0:T(8,128)(2,1)}, bf16[128,512]{1,0:T(8,128)(2,1)S(1)}, u32[]{:S(2)}, u32[]{:S(2)}) collective-permute-start(bf16[128,512]{1,0:T(8,128)(2,1)} %param.4), channel_id=1, source_target_pairs={{0,4},{4,0},{1,5},{5,1},{2,6},{6,2},{3,7},{7,3},{8,12},{12,8},{9,1... | collective-permute-start | bytes 393224 | tf_op jit(solution)/shard_map/ppermute | solution.py:20
  33.7 11.3 %collective-permute-start.3 = (bf16[128,512]{1,0:T(8,128)(2,1)}, bf16[128,512]{1,0:T(8,128)(2,1)S(1)}, u32[]{:S(2)}, u32[]{:S(2)}) collective-permute-start(bf16[128,512]{1,0:T(8,128)(2,1)} %param.4), channel_id=1, source_target_pairs={{0,8},{8,0},{1,9},{9,1},{2,10},{10,2},{3,11},{11,3},{4,12},{12,4},... | collective-permute-start | bytes 393224 | tf_op jit(solution)/shard_map/ppermute | solution.py:20
  45.0 1.0 copy.30
  46.0 0.8 fusion.30
  47.1 0.6 copy.58
  48.2 7.6 %collective-permute-done.3 = bf16[128,512]{1,0:T(8,128)(2,1)S(1)} collective-permute-done((bf16[128,512]{1,0:T(8,128)(2,1)}, bf16[128,512]{1,0:T(8,128)(2,1)S(1)}, u32[]{:S(2)}, u32[]{:S(2)}) %collective-permute-start.3) | collective-permute-done | bytes 131104 | tf_op jit(solution)/shard_map/ppermute | solution.py:20
  56.1 0.7 copy-done
  56.8 0.3 copy.47
  57.1 0.1 reshape.70
  57.2 0.9 dot_general.45
  58.2 0.3 copy.45
  58.4 0.1 reshape.69
  58.6 0.9 dot_general.41
  59.5 57.8 %all-gather.2.cloned.1.call-done = bf16[6,256,1024]{2,1,0:T(8,128)(2,1)} async-done(((bf16[6,32,1024]{2,1,0:T(8,128)(2,1)}), bf16[6,256,1024]{2,1,0:T(8,128)(2,1)}) %all-gather.2.cloned.1.call-update) | async-done | bytes 3145744 | tf_op jit(solution)/shard_map/all_gather | solution.py:37
  117.3 4.7 %copy.37 = bf16[6,256,1024]{1,2,0:T(8,128)(2,1)} copy(bf16[6,256,1024]{2,1,0:T(8,128)(2,1)} %all-gather.2.cloned.1.call-done) | data formatting | bytes 6291456 | tf_op jit(solution)/shard_map/all_gather | solution.py:37
  122.0 2.4 broadcast_multiply_fusion
  124.4 1.8 fusion.28
  126.2 2.6 copy.55
  128.8 2.6 %copy.54 = bf16[6,256,1,512]{3,1,0,2:T(8,128)(2,1)} copy(bf16[6,256,1,512]{1,3,2,0:T(8,128)(2,1)} %get-tuple-element.6) | data formatting | bytes 3145728
  131.4 2.0 fusion.32
  133.5 1.9 fusion.31
  135.4 0.6 convolution_bitcast_fusion
  136.1 0.6 convolution_bitcast_fusion.1
  136.8 0.8 maximum_bitcast_fusion
  137.6 1.1 copy.56
  138.7 1.0 multiply_convert_fusion
  139.7 41.3 %all_to_all.10 = bf16[4,8,8,6,1024]{4,2,3,1,0:T(8,128)(2,1)} all-to-all(bf16[4,8,8,6,1024]{4,2,3,1,0:T(8,128)(2,1)S(1)} %multiply_convert_fusion), channel_id=1, replica_groups=mesh['zl'=8,'xx'=4,'fly'=16] {'xx'}, dimensions={0} | all-to-all | bytes 6291456 | tf_op jit(solution)/shard_map/all_to_all | solution.py:42
  181.0 3.6 %reduce_sum.21 = bf16[8,8,6,1024]{3,1,2,0:T(8,128)(2,1)} reduce(bf16[4,8,8,6,1024]{4,2,3,1,0:T(8,128)(2,1)} %all_to_all.10, bf16[]{:T(256)} %constant.2.clone.1), dimensions={0}, to_apply=%region_0.0 | reduce | flops 1179648 | bytes 3932162 | tf_op jit(solution)/shard_map/reduce_sum | solution.py:43
  184.6 5.1 %all-to-all-start.1 = ((bf16[8,8,6,1024]{3,1,2,0:T(8,128)(2,1)}), bf16[8,8,6,1024]{3,1,2,0:T(8,128)(2,1)}, u32[]{:S(2)}, u32[]{:S(2)}) async-start(bf16[8,8,6,1024]{3,1,2,0:T(8,128)(2,1)} %reduce_sum.21), calls=%async_computation.1 | async-start | bytes 1572864 | tf_op jit(solution)/shard_map/all_to_all | solution.py:44
  189.8 1.4 fusion.7
  191.2 0.4 fusion.4
  191.9 1.9 collective-permute-start.4
  193.8 0.1 copy.42
  193.9 2.9 %collective-permute-start.5 = (f32[128,512]{0,1:T(8,128)S(1)}, f32[128,512]{0,1:T(8,128)S(1)}, u32[]{:S(2)}, u32[]{:S(2)}) collective-permute-start(f32[128,512]{0,1:T(8,128)S(1)} %bitcast.109), channel_id=1, source_target_pairs={{0,2},{2,0},{1,3},{3,1},{4,6},{6,4},{5,7},{7,5},{8,10},{10,8},{9,1... | collective-permute-start | bytes 786440 | tf_op jit(solution)/shard_map/ppermute | solution.py:20
  196.8 0.1 copy.43
  196.9 4.3 %collective-permute-start.6 = (f32[128,512]{0,1:T(8,128)S(1)}, f32[128,512]{0,1:T(8,128)S(1)}, u32[]{:S(2)}, u32[]{:S(2)}) collective-permute-start(f32[128,512]{0,1:T(8,128)S(1)} %bitcast.110), channel_id=1, source_target_pairs={{0,4},{4,0},{1,5},{5,1},{2,6},{6,2},{3,7},{7,3},{8,12},{12,8},{9,1... | collective-permute-start | bytes 786440 | tf_op jit(solution)/shard_map/ppermute | solution.py:20
  201.3 0.1 copy.44
  201.4 8.5 %collective-permute-start.7 = (f32[128,512]{0,1:T(8,128)S(1)}, f32[128,512]{0,1:T(8,128)S(1)}, u32[]{:S(2)}, u32[]{:S(2)}) collective-permute-start(f32[128,512]{0,1:T(8,128)S(1)} %bitcast.111), channel_id=1, source_target_pairs={{0,8},{8,0},{1,9},{9,1},{2,10},{10,2},{3,11},{11,3},{4,12},{12,4},... | collective-permute-start | bytes 786440 | tf_op jit(solution)/shard_map/ppermute | solution.py:20
  209.9 0.1 copy.40
  210.0 1.5 collective-permute-done.6
  211.5 8.9 %collective-permute-done.7 = f32[128,512]{0,1:T(8,128)S(1)} collective-permute-done((f32[128,512]{0,1:T(8,128)S(1)}, f32[128,512]{0,1:T(8,128)S(1)}, u32[]{:S(2)}, u32[]{:S(2)}) %collective-permute-start.7) | collective-permute-done | bytes 262176 | tf_op jit(solution)/shard_map/ppermute | solution.py:20
  220.4 0.8 copy.51
  221.2 29.9 %all-to-all-done.1 = bf16[8,8,6,1024]{3,1,2,0:T(8,128)(2,1)} async-done(((bf16[8,8,6,1024]{3,1,2,0:T(8,128)(2,1)}), bf16[8,8,6,1024]{3,1,2,0:T(8,128)(2,1)}, u32[]{:S(2)}, u32[]{:S(2)}) %all-to-all-start.1) | async-done | bytes 786464 | tf_op jit(solution)/shard_map/all_to_all | solution.py:44
  251.1 1.3 convert_reduce_fusion
  252.4 0.7 multiply_bitcast_fusion
  (46 shorter events, 1.5 us)
Async XLA Ops:
  7.2 110.2 %all-gather.2.cloned.1.call-start = ((), (), s32[]{:S(2)}) async-start(), calls=%async_computation.2 | async-start | bytes 3538944 | tf_op jit(solution)/shard_map/all_gather | solution.py:37
  21.8 26.0 %collective-permute-start = (bf16[128,512]{1,0:T(8,128)(2,1)}, bf16[128,512]{1,0:T(8,128)(2,1)S(1)}, u32[]{:S(2)}, u32[]{:S(2)}) collective-permute-start(bf16[128,512]{1,0:T(8,128)(2,1)} %param.4), channel_id=1, source_target_pairs={{0,1},{1,0},{2,3},{3,2},{4,5},{5,4},{6,7},{7,6},{8,9},{9,8},{10,11... | collective-permute-start | bytes 393224 | tf_op jit(solution)/shard_map/ppermute | solution.py:20
  23.7 24.2 %collective-permute-start.1 = (bf16[128,512]{1,0:T(8,128)(2,1)}, bf16[128,512]{1,0:T(8,128)(2,1)S(1)}, u32[]{:S(2)}, u32[]{:S(2)}) collective-permute-start(bf16[128,512]{1,0:T(8,128)(2,1)} %param.4), channel_id=1, source_target_pairs={{0,2},{2,0},{1,3},{3,1},{4,6},{6,4},{5,7},{7,5},{8,10},{10,8},{9,1... | collective-permute-start | bytes 393224 | tf_op jit(solution)/shard_map/ppermute | solution.py:20
  26.4 21.7 %collective-permute-start.2 = (bf16[128,512]{1,0:T(8,128)(2,1)}, bf16[128,512]{1,0:T(8,128)(2,1)S(1)}, u32[]{:S(2)}, u32[]{:S(2)}) collective-permute-start(bf16[128,512]{1,0:T(8,128)(2,1)} %param.4), channel_id=1, source_target_pairs={{0,4},{4,0},{1,5},{5,1},{2,6},{6,2},{3,7},{7,3},{8,12},{12,8},{9,1... | collective-permute-start | bytes 393224 | tf_op jit(solution)/shard_map/ppermute | solution.py:20
  33.7 22.1 %collective-permute-start.3 = (bf16[128,512]{1,0:T(8,128)(2,1)}, bf16[128,512]{1,0:T(8,128)(2,1)S(1)}, u32[]{:S(2)}, u32[]{:S(2)}) collective-permute-start(bf16[128,512]{1,0:T(8,128)(2,1)} %param.4), channel_id=1, source_target_pairs={{0,8},{8,0},{1,9},{9,1},{2,10},{10,2},{3,11},{11,3},{4,12},{12,4},... | collective-permute-start | bytes 393224 | tf_op jit(solution)/shard_map/ppermute | solution.py:20
  56.1 0.7 copy-start
  131.4 3.9 %copy-start.1 = (bf16[4,8,8,6,128]{4,3,2,1,0:T(8,128)(2,1)S(1)}, bf16[4,8,8,6,128]{4,3,2,1,0:T(8,128)(2,1)}, u32[]{:S(2)}) copy-start(bf16[4,8,8,6,128]{4,3,2,1,0:T(8,128)(2,1)} %dot_general.45) | copy-start | bytes 1179652
  131.4 4.0 %copy-start.7 = (bf16[128,1024]{1,0:T(8,128)(2,1)S(1)}, bf16[128,1024]{1,0:T(8,128)(2,1)}, u32[]{:S(2)}) copy-start(bf16[128,1024]{1,0:T(8,128)(2,1)} %param.5) | copy-start | bytes 786436
  133.4 2.6 %copy-start.3 = (f32[128,512]{1,0:T(8,128)}, f32[128,512]{1,0:T(8,128)S(1)}, u32[]{:S(2)}) copy-start(f32[128,512]{1,0:T(8,128)S(1)} %fusion.32) | copy-start | bytes 786436
  133.4 2.7 %copy-start.2 = (bf16[4,8,8,6,128]{4,3,2,1,0:T(8,128)(2,1)S(1)}, bf16[4,8,8,6,128]{4,3,2,1,0:T(8,128)(2,1)}, u32[]{:S(2)}) copy-start(bf16[4,8,8,6,128]{4,3,2,1,0:T(8,128)(2,1)} %dot_general.41) | copy-start | bytes 1179652
  135.4 0.7 copy-start.5
  137.6 1.1 copy-start.9
  181.0 8.8 %copy-start.4 = (f32[128,512]{1,0:T(8,128)S(1)}, f32[128,512]{1,0:T(8,128)}, u32[]{:S(2)}) copy-start(f32[128,512]{1,0:T(8,128)} %copy-done.3) | copy-start | bytes 786436
  184.6 66.5 %all-to-all-start.1 = ((bf16[8,8,6,1024]{3,1,2,0:T(8,128)(2,1)}), bf16[8,8,6,1024]{3,1,2,0:T(8,128)(2,1)}, u32[]{:S(2)}, u32[]{:S(2)}) async-start(bf16[8,8,6,1024]{3,1,2,0:T(8,128)(2,1)} %reduce_sum.21), calls=%async_computation.1 | async-start | bytes 1572864 | tf_op jit(solution)/shard_map/all_to_all | solution.py:44
  189.8 1.4 copy-start.6
  189.8 1.4 copy-start.8
  191.9 18.1 %collective-permute-start.4 = (f32[128,512]{0,1:T(8,128)S(1)}, f32[128,512]{0,1:T(8,128)S(1)}, u32[]{:S(2)}, u32[]{:S(2)}) collective-permute-start(f32[128,512]{0,1:T(8,128)S(1)} %bitcast.108), channel_id=1, source_target_pairs={{0,1},{1,0},{2,3},{3,2},{4,5},{5,4},{6,7},{7,6},{8,9},{9,8},{10,11... | collective-permute-start | bytes 786440 | tf_op jit(solution)/shard_map/ppermute | solution.py:20
  193.9 16.1 %collective-permute-start.5 = (f32[128,512]{0,1:T(8,128)S(1)}, f32[128,512]{0,1:T(8,128)S(1)}, u32[]{:S(2)}, u32[]{:S(2)}) collective-permute-start(f32[128,512]{0,1:T(8,128)S(1)} %bitcast.109), channel_id=1, source_target_pairs={{0,2},{2,0},{1,3},{3,1},{4,6},{6,4},{5,7},{7,5},{8,10},{10,8},{9,1... | collective-permute-start | bytes 786440 | tf_op jit(solution)/shard_map/ppermute | solution.py:20
  196.9 14.6 %collective-permute-start.6 = (f32[128,512]{0,1:T(8,128)S(1)}, f32[128,512]{0,1:T(8,128)S(1)}, u32[]{:S(2)}, u32[]{:S(2)}) collective-permute-start(f32[128,512]{0,1:T(8,128)S(1)} %bitcast.110), channel_id=1, source_target_pairs={{0,4},{4,0},{1,5},{5,1},{2,6},{6,2},{3,7},{7,3},{8,12},{12,8},{9,1... | collective-permute-start | bytes 786440 | tf_op jit(solution)/shard_map/ppermute | solution.py:20
  201.4 19.0 %collective-permute-start.7 = (f32[128,512]{0,1:T(8,128)S(1)}, f32[128,512]{0,1:T(8,128)S(1)}, u32[]{:S(2)}, u32[]{:S(2)}) collective-permute-start(f32[128,512]{0,1:T(8,128)S(1)} %bitcast.111), channel_id=1, source_target_pairs={{0,8},{8,0},{1,9},{9,1},{2,10},{10,2},{3,11},{11,3},{4,12},{12,4},... | collective-permute-start | bytes 786440 | tf_op jit(solution)/shard_map/ppermute | solution.py:20
Sparse Core Ops, SparseCore 0:
  21.9 95.3 all-gather.1

commit v4 on v3

--- a/solution.py
+++ b/solution.py
@@ -55,14 +55,9 @@
     zl = lax.axis_size(ROWS)
     xx = lax.axis_size(COLS)
     own = BS // (zl * xx)
-    weights = gather_rows(w_up)
     keep_cols = jnp.broadcast_to(pattern[:, :, None], (factor_count, pattern.shape[1], BS)).reshape(
-        factor_count, hidden_width
+        factor_count, local_blocks, group_width
     )
-    masked = (weights * keep_cols.astype(jnp.bfloat16)[:, None, :]).reshape(
-        factor_count, BS, local_blocks, group_width
-    )
-    keep_f = keep_cols.astype(jnp.float32).reshape(factor_count, local_blocks, group_width)
     token_blocks = tokens.reshape(row_count, local_blocks, BS)
     gathered = []
     for factor in range(factor_count):
@@ -74,12 +69,12 @@
             partner = partner_2(tokens, "fly", bit_number)
             gathered.append(partner.reshape(row_count, local_blocks, BS))
     reads = jnp.stack(gathered, axis=2)
-    grads = []
     contribs = []
-    products = []
+    sums = []
     for group in range(local_blocks):
+        weights = gather_rows(w_up[:, :, group * group_width:(group + 1) * group_width])
+        rhs = (weights * keep_cols[:, group].astype(jnp.bfloat16)[:, None, :]).reshape(factor_count * BS, group_width)
         lhs = reads[:, group].reshape(row_count, factor_count * BS)
-        rhs = masked[:, :, group, :].reshape(factor_count * BS, group_width)
         pre_act = jnp.dot(lhs, rhs, preferred_element_type=jnp.float32)
         squash = jax.nn.sigmoid(pre_act)
         derivative = squash * (1.0 + pre_act * (1.0 - squash))
@@ -92,12 +87,12 @@
             )
         )
         cols = reads[:, group].reshape(row_count, factor_count, zl, xx, own).transpose(0, 3, 2, 4, 1)
-        products.append(
-            lax.dot_general(
-                cols.reshape(row_count, BS * factor_count), grad_pre, (((0,), (0,)), ((), ())),
-                preferred_element_type=jnp.float32,
-            ).reshape(xx, zl, own, factor_count, group_width)
-        )
+        product = lax.dot_general(
+            cols.reshape(row_count, BS * factor_count), grad_pre, (((0,), (0,)), ((), ())),
+            preferred_element_type=jnp.float32,
+        ).reshape(xx, zl, own, factor_count, group_width)
+        product = product * keep_cols[:, group].astype(jnp.float32)[None, None, None]
+        sums.append(scatter_rows(product.astype(jnp.bfloat16)))
     contrib_all = jnp.stack(contribs, axis=1)
     input_total = jnp.zeros((row_count, local_blocks, BS), jnp.float32)
     for factor in range(factor_count):
@@ -110,9 +105,7 @@
             returned = partner_2(contrib.reshape(row_count, local_width), "fly", bit_number)
             input_total = input_total + returned.reshape(row_count, local_blocks, BS)
     input_grad = input_total.reshape(row_count, local_width).astype(jnp.bfloat16)
-    terms = jnp.stack(products, axis=4) * keep_f[None, None, None]
-    summed = scatter_rows(terms.reshape(xx, zl, own, factor_count, hidden_width).astype(jnp.bfloat16))
-    weight_grad = summed * (1.0 / (zl * xx))
+    weight_grad = jnp.concatenate(sums, axis=2) * (1.0 / (zl * xx))
     return (input_grad, weight_grad)
 
 

time: 262 us -> 276 us (1.053)
  the two profiles are of different devices: /device:TPU:24 before, /device:TPU:160 now
where the time goes in v4:
time: 276 us; the launch traced here: 275 us
  waiting for transfers between devices  135 us (49%)
  starting transfers between devices  73.7 us (27%)
  blocking collectives  26.1 us (9%)
  between operations  14.5 us (5%)
  other arithmetic  10.1 us (4%)
  local copies, waits for them, and re-layouts  8.69 us (3%)
  matrix products  6.78 us (2%)
    all_gather x2, waiting for transfers between devices, gather_rows(): return lax.all_gather(inner, ROWS, axis=1, tiled=True)  69.2 us
    ppermute x8, waiting for transfers between devices, partner_2(): return lax.ppermute(block, axis, route)  43.8 us
    ppermute x8, starting transfers between devices, partner_2(): return lax.ppermute(block, axis, route)  38.5 us
    all_to_all x2, starting transfers between devices, scatter_rows(): got = lax.all_to_all(part.astype(jnp.bfloat16), ROWS, 0, 0, tiled=True)  26.5 us
    all_gather x2, blocking collectives, gather_rows(): inner = lax.all_gather(w_up, COLS, axis=1, tiled=True)  26.1 us
    all_to_all x2, waiting for transfers between devices, scatter_rows(): got = lax.all_to_all(terms, COLS, 0, 0, tiled=True)  14.7 us
    all_to_all x2, starting transfers between devices, scatter_rows(): got = lax.all_to_all(terms, COLS, 0, 0, tiled=True)  8.71 us
    all_to_all x2, waiting for transfers between devices, scatter_rows(): got = lax.all_to_all(part.astype(jnp.bfloat16), ROWS, 0, 0, tiled=True)  7.57 us
  transfers between devices with their start and end apart: 14, of which 7 were waited for; matrix products, arithmetic and copies ran while one was open for 8% of the time, Pallas kernels for 0%

profile of v4, /device:TPU:160, one launch (start us, length us, event | category | flops | bytes accessed | tf_op | source)
XLA Modules:
  0.0 275.0 jit_solution(784753864789760765)
XLA Ops:
  7.2 0.8 fusion.17
  8.0 13.2 %all_gather.14 = bf16[6,32,512]{2,1,0:T(8,128)(2,1)} all-gather(bf16[6,8,512]{2,1,0:T(8,128)(2,1)S(1)} %get-tuple-element.16), channel_id=1, replica_groups=mesh['zl'=8,'xx'=4,'fly'=16] {'xx'}, dimensions={1}, use_global_device_ids=true | all-gather | bytes 245760 | tf_op jit(solution)/shard_map/all_gather | solution.py:36
  21.3 12.9 %all_gather.12 = bf16[6,32,512]{2,1,0:T(8,128)(2,1)} all-gather(bf16[6,8,512]{2,1,0:T(8,128)(2,1)S(1)} %get-tuple-element.15), channel_id=1, replica_groups=mesh['zl'=8,'xx'=4,'fly'=16] {'xx'}, dimensions={1}, use_global_device_ids=true | all-gather | bytes 245760 | tf_op jit(solution)/shard_map/all_gather | solution.py:36
  34.2 1.9 collective-permute-start
  36.1 3.5 %collective-permute-start.1 = (bf16[128,512]{1,0:T(8,128)(2,1)}, bf16[128,512]{1,0:T(8,128)(2,1)S(1)}, u32[]{:S(2)}, u32[]{:S(2)}) collective-permute-start(bf16[128,512]{1,0:T(8,128)(2,1)} %param.4), channel_id=1, source_target_pairs={{0,2},{2,0},{1,3},{3,1},{4,6},{6,4},{5,7},{7,5},{8,10},{10,8},{9,1... | collective-permute-start | bytes 393224 | tf_op jit(solution)/shard_map/ppermute | solution.py:20
  39.6 4.8 %collective-permute-start.2 = (bf16[128,512]{1,0:T(8,128)(2,1)}, bf16[128,512]{1,0:T(8,128)(2,1)S(1)}, u32[]{:S(2)}, u32[]{:S(2)}) collective-permute-start(bf16[128,512]{1,0:T(8,128)(2,1)} %param.4), channel_id=1, source_target_pairs={{0,4},{4,0},{1,5},{5,1},{2,6},{6,2},{3,7},{7,3},{8,12},{12,8},{9,1... | collective-permute-start | bytes 393224 | tf_op jit(solution)/shard_map/ppermute | solution.py:20
  44.5 10.0 %collective-permute-start.3 = (bf16[128,512]{1,0:T(8,128)(2,1)}, bf16[128,512]{1,0:T(8,128)(2,1)S(1)}, u32[]{:S(2)}, u32[]{:S(2)}) collective-permute-start(bf16[128,512]{1,0:T(8,128)(2,1)} %param.4), channel_id=1, source_target_pairs={{0,8},{8,0},{1,9},{9,1},{2,10},{10,2},{3,11},{11,3},{4,12},{12,4},... | collective-permute-start | bytes 393224 | tf_op jit(solution)/shard_map/ppermute | solution.py:20
  54.5 1.0 copy.41
  55.5 0.8 copy.47
  56.9 16.5 %collective-permute-done.3 = bf16[128,512]{1,0:T(8,128)(2,1)S(1)} collective-permute-done((bf16[128,512]{1,0:T(8,128)(2,1)}, bf16[128,512]{1,0:T(8,128)(2,1)S(1)}, u32[]{:S(2)}, u32[]{:S(2)}) %collective-permute-start.3) | collective-permute-done | bytes 131104 | tf_op jit(solution)/shard_map/ppermute | solution.py:20
  73.7 0.3 copy.55
  74.0 0.1 reshape.61
  74.2 0.1 dot_general.40
  74.3 15.9 %all-gather.5.cloned.1.call-done = bf16[6,256,512]{2,1,0:T(8,128)(2,1)} async-done(((bf16[6,32,512]{2,1,0:T(8,128)(2,1)}), bf16[6,256,512]{2,1,0:T(8,128)(2,1)}) %all-gather.5.cloned.1.call-update) | async-done | bytes 1572880 | tf_op jit(solution)/shard_map/all_gather | solution.py:37
  90.2 1.5 broadcast_multiply_fusion
  91.7 0.4 fusion.19
  92.1 0.7 copy-done.1
  92.8 1.8 multiply_convert_fusion
  94.6 4.3 %all-to-all-start.2 = ((bf16[4,8,8,6,512]{4,2,3,1,0:T(8,128)(2,1)}), bf16[4,8,8,6,512]{4,2,3,1,0:T(8,128)(2,1)}, u32[]{:S(2)}, u32[]{:S(2)}) async-start(bf16[4,8,8,6,512]{4,2,3,1,0:T(8,128)(2,1)} %multiply_convert_fusion), calls=%async_computation.2 | async-start | bytes 3145728 | tf_op jit(solution)/shard_map/all_to_all | solution.py:42
  99.0 0.6 copy.73
  99.6 0.3 copy.53
  99.9 0.1 reshape.60
  100.1 0.9 dot_general.37
  101.0 53.3 %all-gather.3.cloned.1.call-done = bf16[6,256,512]{2,1,0:T(8,128)(2,1)} async-done(((bf16[6,32,512]{2,1,0:T(8,128)(2,1)}), bf16[6,256,512]{2,1,0:T(8,128)(2,1)}) %all-gather.3.cloned.1.call-update) | async-done | bytes 1572880 | tf_op jit(solution)/shard_map/all_gather | solution.py:37
  154.2 1.5 broadcast_multiply_fusion.1
  155.8 0.4 fusion.18
  156.2 0.7 copy-done.2
  156.9 1.8 multiply_convert_fusion.1
  158.8 4.4 %all-to-all-start = ((bf16[4,8,8,6,512]{4,2,3,1,0:T(8,128)(2,1)}), bf16[4,8,8,6,512]{4,2,3,1,0:T(8,128)(2,1)}, u32[]{:S(2)}, u32[]{:S(2)}) async-start(bf16[4,8,8,6,512]{4,2,3,1,0:T(8,128)(2,1)} %multiply_convert_fusion.1), calls=%async_computation | async-start | bytes 3145728 | tf_op jit(solution)/shard_map/all_to_all | solution.py:42
  163.1 2.5 reduce_sum.44
  165.7 14.7 %all-to-all-done = bf16[4,8,8,6,512]{4,2,3,1,0:T(8,128)(2,1)} async-done(((bf16[4,8,8,6,512]{4,2,3,1,0:T(8,128)(2,1)}), bf16[4,8,8,6,512]{4,2,3,1,0:T(8,128)(2,1)}, u32[]{:S(2)}, u32[]{:S(2)}) %all-to-all-start) | async-done | bytes 1572896 | tf_op jit(solution)/shard_map/all_to_all | solution.py:42
  180.3 14.8 %all-to-all-start.3 = ((bf16[8,8,6,512]{3,1,2,0:T(8,128)(2,1)}), bf16[8,8,6,512]{3,1,2,0:T(8,128)(2,1)S(1)}, u32[]{:S(2)}, u32[]{:S(2)}) async-start(bf16[8,8,6,512]{3,1,2,0:T(8,128)(2,1)} %reduce_sum.44), calls=%async_computation.3 | async-start | bytes 786432 | tf_op jit(solution)/shard_map/all_to_all | solution.py:44
  195.2 2.5 reduce_sum.42
  197.7 7.6 %all-to-all-done.3 = bf16[8,8,6,512]{3,1,2,0:T(8,128)(2,1)S(1)} async-done(((bf16[8,8,6,512]{3,1,2,0:T(8,128)(2,1)}), bf16[8,8,6,512]{3,1,2,0:T(8,128)(2,1)S(1)}, u32[]{:S(2)}, u32[]{:S(2)}) %all-to-all-start.3) | async-done | bytes 393248 | tf_op jit(solution)/shard_map/all_to_all | solution.py:44
  205.2 11.6 %all-to-all-start.1 = ((bf16[8,8,6,512]{3,1,2,0:T(8,128)(2,1)}), bf16[8,8,6,512]{3,1,2,0:T(8,128)(2,1)}, u32[]{:S(2)}, u32[]{:S(2)}) async-start(bf16[8,8,6,512]{3,1,2,0:T(8,128)(2,1)} %reduce_sum.42), calls=%async_computation.1 | async-start | bytes 786432 | tf_op jit(solution)/shard_map/all_to_all | solution.py:44
  216.9 1.7 convolution_bitcast_fusion
  218.6 0.6 convolution_bitcast_fusion.1
  219.4 0.1 copy.49
  219.5 1.9 collective-permute-start.4
  221.6 3.4 %collective-permute-start.5 = (f32[128,512]{0,1:T(8,128)S(1)}, f32[128,512]{0,1:T(8,128)S(1)}, u32[]{:S(2)}, u32[]{:S(2)}) collective-permute-start(f32[128,512]{0,1:T(8,128)S(1)} %bitcast.95), channel_id=1, source_target_pairs={{0,2},{2,0},{1,3},{3,1},{4,6},{6,4},{5,7},{7,5},{8,10},{10,8},{9,1... | collective-permute-start | bytes 786440 | tf_op jit(solution)/shard_map/ppermute | solution.py:20
  225.0 0.1 copy.51
  225.1 4.6 %collective-permute-start.6 = (f32[128,512]{0,1:T(8,128)S(1)}, f32[128,512]{0,1:T(8,128)S(1)}, u32[]{:S(2)}, u32[]{:S(2)}) collective-permute-start(f32[128,512]{0,1:T(8,128)S(1)} %bitcast.96), channel_id=1, source_target_pairs={{0,4},{4,0},{1,5},{5,1},{2,6},{6,2},{3,7},{7,3},{8,12},{12,8},{9,1... | collective-permute-start | bytes 786440 | tf_op jit(solution)/shard_map/ppermute | solution.py:20
  229.9 8.3 %collective-permute-start.7 = (f32[128,512]{0,1:T(8,128)S(1)}, f32[128,512]{0,1:T(8,128)S(1)}, u32[]{:S(2)}, u32[]{:S(2)}) collective-permute-start(f32[128,512]{0,1:T(8,128)S(1)} %bitcast.97), channel_id=1, source_target_pairs={{0,8},{8,0},{1,9},{9,1},{2,10},{10,2},{3,11},{11,3},{4,12},{12,4},... | collective-permute-start | bytes 786440 | tf_op jit(solution)/shard_map/ppermute | solution.py:20
  238.3 1.7 collective-permute-done.6
  240.0 25.6 %collective-permute-done.7 = f32[128,512]{0,1:T(8,128)S(1)} collective-permute-done((f32[128,512]{0,1:T(8,128)S(1)}, f32[128,512]{0,1:T(8,128)S(1)}, u32[]{:S(2)}, u32[]{:S(2)}) %collective-permute-start.7) | collective-permute-done | bytes 262176 | tf_op jit(solution)/shard_map/ppermute | solution.py:20
  265.6 0.8 copy.57
  266.5 1.1 convert_reduce_fusion.1
  267.5 0.7 maximum_multiply_fusion
  (49 shorter events, 1.6 us)
Async XLA Ops:
  7.2 83.0 %all-gather.5.cloned.1.call-start = ((), (), s32[]{:S(2)}) async-start(), calls=%async_computation.5 | async-start | bytes 1769472 | tf_op jit(solution)/shard_map/all_gather | solution.py:37
  21.3 133.0 %all-gather.3.cloned.1.call-start = ((), (), s32[]{:S(2)}) async-start(), calls=%async_computation.4 | async-start | bytes 1769472 | tf_op jit(solution)/shard_map/all_gather | solution.py:37
  34.2 22.3 %collective-permute-start = (bf16[128,512]{1,0:T(8,128)(2,1)}, bf16[128,512]{1,0:T(8,128)(2,1)S(1)}, u32[]{:S(2)}, u32[]{:S(2)}) collective-permute-start(bf16[128,512]{1,0:T(8,128)(2,1)} %param.4), channel_id=1, source_target_pairs={{0,1},{1,0},{2,3},{3,2},{4,5},{5,4},{6,7},{7,6},{8,9},{9,8},{10,11... | collective-permute-start | bytes 393224 | tf_op jit(solution)/shard_map/ppermute | solution.py:20
  36.1 20.5 %collective-permute-start.1 = (bf16[128,512]{1,0:T(8,128)(2,1)}, bf16[128,512]{1,0:T(8,128)(2,1)S(1)}, u32[]{:S(2)}, u32[]{:S(2)}) collective-permute-start(bf16[128,512]{1,0:T(8,128)(2,1)} %param.4), channel_id=1, source_target_pairs={{0,2},{2,0},{1,3},{3,1},{4,6},{6,4},{5,7},{7,5},{8,10},{10,8},{9,1... | collective-permute-start | bytes 393224 | tf_op jit(solution)/shard_map/ppermute | solution.py:20
  39.6 17.1 %collective-permute-start.2 = (bf16[128,512]{1,0:T(8,128)(2,1)}, bf16[128,512]{1,0:T(8,128)(2,1)S(1)}, u32[]{:S(2)}, u32[]{:S(2)}) collective-permute-start(bf16[128,512]{1,0:T(8,128)(2,1)} %param.4), channel_id=1, source_target_pairs={{0,4},{4,0},{1,5},{5,1},{2,6},{6,2},{3,7},{7,3},{8,12},{12,8},{9,1... | collective-permute-start | bytes 393224 | tf_op jit(solution)/shard_map/ppermute | solution.py:20
  44.5 29.0 %collective-permute-start.3 = (bf16[128,512]{1,0:T(8,128)(2,1)}, bf16[128,512]{1,0:T(8,128)(2,1)S(1)}, u32[]{:S(2)}, u32[]{:S(2)}) collective-permute-start(bf16[128,512]{1,0:T(8,128)(2,1)} %param.4), channel_id=1, source_target_pairs={{0,8},{8,0},{1,9},{9,1},{2,10},{10,2},{3,11},{11,3},{4,12},{12,4},... | collective-permute-start | bytes 393224 | tf_op jit(solution)/shard_map/ppermute | solution.py:20
  91.7 1.2 copy-start.5
  92.1 0.7 copy-start.1
  94.6 64.1 %all-to-all-start.2 = ((bf16[4,8,8,6,512]{4,2,3,1,0:T(8,128)(2,1)}), bf16[4,8,8,6,512]{4,2,3,1,0:T(8,128)(2,1)}, u32[]{:S(2)}, u32[]{:S(2)}) async-start(bf16[4,8,8,6,512]{4,2,3,1,0:T(8,128)(2,1)} %multiply_convert_fusion), calls=%async_computation.2 | async-start | bytes 3145728 | tf_op jit(solution)/shard_map/all_to_all | solution.py:42
  155.8 1.1 copy-start
  155.8 1.1 copy-start.4
  155.8 1.1 copy-start.6
  156.2 0.7 copy-start.2
  158.8 21.6 %all-to-all-start = ((bf16[4,8,8,6,512]{4,2,3,1,0:T(8,128)(2,1)}), bf16[4,8,8,6,512]{4,2,3,1,0:T(8,128)(2,1)}, u32[]{:S(2)}, u32[]{:S(2)}) async-start(bf16[4,8,8,6,512]{4,2,3,1,0:T(8,128)(2,1)} %multiply_convert_fusion.1), calls=%async_computation | async-start | bytes 3145728 | tf_op jit(solution)/shard_map/all_to_all | solution.py:42
  180.3 24.9 %all-to-all-start.3 = ((bf16[8,8,6,512]{3,1,2,0:T(8,128)(2,1)}), bf16[8,8,6,512]{3,1,2,0:T(8,128)(2,1)S(1)}, u32[]{:S(2)}, u32[]{:S(2)}) async-start(bf16[8,8,6,512]{3,1,2,0:T(8,128)(2,1)} %reduce_sum.44), calls=%async_computation.3 | async-start | bytes 786432 | tf_op jit(solution)/shard_map/all_to_all | solution.py:44
  205.2 61.2 %all-to-all-start.1 = ((bf16[8,8,6,512]{3,1,2,0:T(8,128)(2,1)}), bf16[8,8,6,512]{3,1,2,0:T(8,128)(2,1)}, u32[]{:S(2)}, u32[]{:S(2)}) async-start(bf16[8,8,6,512]{3,1,2,0:T(8,128)(2,1)} %reduce_sum.42), calls=%async_computation.1 | async-start | bytes 786432 | tf_op jit(solution)/shard_map/all_to_all | solution.py:44
  216.9 1.7 copy-start.3
  216.9 1.7 copy-start.7
  219.5 18.8 %collective-permute-start.4 = (f32[128,512]{0,1:T(8,128)S(1)}, f32[128,512]{0,1:T(8,128)S(1)}, u32[]{:S(2)}, u32[]{:S(2)}) collective-permute-start(f32[128,512]{0,1:T(8,128)S(1)} %bitcast.94), channel_id=1, source_target_pairs={{0,1},{1,0},{2,3},{3,2},{4,5},{5,4},{6,7},{7,6},{8,9},{9,8},{10,11... | collective-permute-start | bytes 786440 | tf_op jit(solution)/shard_map/ppermute | solution.py:20
  221.6 16.8 %collective-permute-start.5 = (f32[128,512]{0,1:T(8,128)S(1)}, f32[128,512]{0,1:T(8,128)S(1)}, u32[]{:S(2)}, u32[]{:S(2)}) collective-permute-start(f32[128,512]{0,1:T(8,128)S(1)} %bitcast.95), channel_id=1, source_target_pairs={{0,2},{2,0},{1,3},{3,1},{4,6},{6,4},{5,7},{7,5},{8,10},{10,8},{9,1... | collective-permute-start | bytes 786440 | tf_op jit(solution)/shard_map/ppermute | solution.py:20
  225.1 14.9 %collective-permute-start.6 = (f32[128,512]{0,1:T(8,128)S(1)}, f32[128,512]{0,1:T(8,128)S(1)}, u32[]{:S(2)}, u32[]{:S(2)}) collective-permute-start(f32[128,512]{0,1:T(8,128)S(1)} %bitcast.96), channel_id=1, source_target_pairs={{0,4},{4,0},{1,5},{5,1},{2,6},{6,2},{3,7},{7,3},{8,12},{12,8},{9,1... | collective-permute-start | bytes 786440 | tf_op jit(solution)/shard_map/ppermute | solution.py:20
  229.9 35.7 %collective-permute-start.7 = (f32[128,512]{0,1:T(8,128)S(1)}, f32[128,512]{0,1:T(8,128)S(1)}, u32[]{:S(2)}, u32[]{:S(2)}) collective-permute-start(f32[128,512]{0,1:T(8,128)S(1)} %bitcast.97), channel_id=1, source_target_pairs={{0,8},{8,0},{1,9},{9,1},{2,10},{10,2},{3,11},{11,3},{4,12},{12,4},... | collective-permute-start | bytes 786440 | tf_op jit(solution)/shard_map/ppermute | solution.py:20
Sparse Core Ops, SparseCore 0:
  21.4 68.7 all-gather.4
  92.2 61.9 all-gather.2

commit v5 on v3

--- a/solution.py
+++ b/solution.py
@@ -33,8 +33,14 @@
 
 
 def gather_rows(w_up):
-    inner = lax.all_gather(w_up, COLS, axis=1, tiled=True)
-    return lax.all_gather(inner, ROWS, axis=1, tiled=True)
+    factor_count, own, width = w_up.shape
+    zl = lax.axis_size(ROWS)
+    xx = lax.axis_size(COLS)
+    copies = jnp.broadcast_to(w_up[None], (zl, factor_count, own, width))
+    by_row = lax.all_to_all(copies, ROWS, 0, 0, tiled=True)
+    copies = jnp.broadcast_to(by_row[None], (xx, zl, factor_count, own, width))
+    both = lax.all_to_all(copies, COLS, 0, 0, tiled=True)
+    return both.transpose(2, 1, 0, 3, 4).reshape(factor_count, zl * xx * own, width)
 
 
 def scatter_rows(terms):

time: 262 us -> 240 us (0.916)
  waiting for transfers between devices: 106 us -> 45.8 us
  blocking collectives: 55.9 us -> 93.3 us
  local copies, waits for them, and re-layouts: 20.3 us -> 40 us
  between operations: 14.5 us -> 1.06 us
  starting transfers between devices: 45.9 us -> 43.1 us
  matrix products: 6.95 us -> 4.33 us
    all_gather x1 -> x0, waiting for transfers between devices: 57.8 us -> none  [gather_rows(): return lax.all_gather(inner, ROWS, axis=1, tiled=True)]
    all_to_all x0 -> x1, blocking collectives: none -> 52.3 us  [gather_rows(): by_row = lax.all_to_all(copies, ROWS, 0, 0, tiled=True)]
    all_gather x1 -> x0, blocking collectives: 14.5 us -> none  [gather_rows(): inner = lax.all_gather(w_up, COLS, axis=1, tiled=True)]
    ppermute x8, starting transfers between devices: 40.7 us -> 34.1 us  [partner_2(): return lax.ppermute(block, axis, route)]
    reshape x0 -> x1, local copies, waits for them, and re-layouts: none -> 6.15 us  [gather_rows(): both.transpose(2, 1, 0, 3, 4).reshape(factor_count, zl * xx * own, width)]
    all_gather x1 -> x0, local copies, waits for them, and re-layouts: 4.66 us -> none  [gather_rows(): return lax.all_gather(inner, ROWS, axis=1, tiled=True)]
    all_to_all x0 -> x1, starting transfers between devices: none -> 4.42 us  [gather_rows(): both = lax.all_to_all(copies, COLS, 0, 0, tiled=True)]
    reshape x2, local copies, waits for them, and re-layouts: 0.28 us -> 3.84 us  [body(): cols.reshape(row_count, BS * factor_count)]
  transfers between devices with their start and end apart: 10 -> 10, of which waited for: 5 -> 4; matrix products, arithmetic and copies ran while one was open for 4% -> 12% of each run, Pallas kernels for 0% -> 0%
where the time goes in v5:
time: 240 us; the launch traced here: 237 us
  blocking collectives  93.3 us (39%)
  waiting for transfers between devices  45.8 us (19%)
  starting transfers between devices  43.1 us (18%)
  local copies, waits for them, and re-layouts  40 us (17%)
  other arithmetic  9.87 us (4%)
  matrix products  4.33 us (2%)
    all_to_all x1, blocking collectives, gather_rows(): by_row = lax.all_to_all(copies, ROWS, 0, 0, tiled=True)  52.3 us
    all_to_all x1, blocking collectives, scatter_rows(): got = lax.all_to_all(terms, COLS, 0, 0, tiled=True)  41 us
    ppermute x8, starting transfers between devices, partner_2(): return lax.ppermute(block, axis, route)  34.1 us
    all_to_all x1, waiting for transfers between devices, scatter_rows(): got = lax.all_to_all(part.astype(jnp.bfloat16), ROWS, 0, 0, tiled=True)  28.2 us
    ppermute x8, waiting for transfers between devices, partner_2(): return lax.ppermute(block, axis, route)  17.5 us
    unnamed x31, local copies, waits for them, and re-layouts  7.98 us
    reshape x1, local copies, waits for them, and re-layouts, gather_rows(): both.transpose(2, 1, 0, 3, 4).reshape(factor_count, zl * xx * own, width)  6.15 us
    reduce_sum x2, other arithmetic, scatter_rows(): part = got.astype(jnp.float32).sum(0)  4.91 us
  transfers between devices with their start and end apart: 10, of which 4 were waited for; matrix products, arithmetic and copies ran while one was open for 12% of the time, Pallas kernels for 0%

profile of v5, /device:TPU:24, one launch (start us, length us, event | category | flops | bytes accessed | tf_op | source)
XLA Modules:
  0.0 237.3 jit_solution(10275078324980596093)
XLA Ops:
  0.6 1.0 broadcast_in_dim.8
  1.6 52.3 %all_to_all.20 = bf16[8,6,8,1024]{3,2,1,0:T(8,128)(2,1)S(1)} all-to-all(bf16[8,6,8,1024]{3,2,1,0:T(8,128)(2,1)S(1)} %broadcast_in_dim.8), channel_id=1, replica_groups=mesh['zl'=8,'xx'=4,'fly'=16] {'zl'}, dimensions={0} | all-to-all | bytes 1572864 | tf_op jit(solution)/shard_map/all_to_all | solution.py:40
  54.0 2.0 broadcast_in_dim.9
  56.0 4.4 %all-to-all-start.1 = ((bf16[4,8,6,8,1024]{4,3,1,2,0:T(8,128)(2,1)}), bf16[4,8,6,8,1024]{4,3,1,2,0:T(8,128)(2,1)S(1)}, u32[]{:S(2)}, u32[]{:S(2)}) async-start(bf16[4,8,6,8,1024]{4,3,1,2,0:T(8,128)(2,1)} %broadcast_in_dim.9), calls=%async_computation.1 | async-start | bytes 6291456 | tf_op jit(solution)/shard_map/all_to_all | solution.py:42
  60.4 1.9 collective-permute-start
  62.4 2.7 %collective-permute-start.1 = (bf16[128,512]{1,0:T(8,128)(2,1)}, bf16[128,512]{1,0:T(8,128)(2,1)S(1)}, u32[]{:S(2)}, u32[]{:S(2)}) collective-permute-start(bf16[128,512]{1,0:T(8,128)(2,1)} %param.4), channel_id=1, source_target_pairs={{0,2},{2,0},{1,3},{3,1},{4,6},{6,4},{5,7},{7,5},{8,10},{10,8},{9,1... | collective-permute-start | bytes 393224 | tf_op jit(solution)/shard_map/ppermute | solution.py:20
  65.0 2.9 %collective-permute-start.2 = (bf16[128,512]{1,0:T(8,128)(2,1)}, bf16[128,512]{1,0:T(8,128)(2,1)}, u32[]{:S(2)}, u32[]{:S(2)}) collective-permute-start(bf16[128,512]{1,0:T(8,128)(2,1)} %param.4), channel_id=1, source_target_pairs={{0,4},{4,0},{1,5},{5,1},{2,6},{6,2},{3,7},{7,3},{8,12},{12,8},{9,1... | collective-permute-start | bytes 393224 | tf_op jit(solution)/shard_map/ppermute | solution.py:20
  67.9 8.2 %collective-permute-start.3 = (bf16[128,512]{1,0:T(8,128)(2,1)}, bf16[128,512]{1,0:T(8,128)(2,1)}, u32[]{:S(2)}, u32[]{:S(2)}) collective-permute-start(bf16[128,512]{1,0:T(8,128)(2,1)} %param.4), channel_id=1, source_target_pairs={{0,8},{8,0},{1,9},{9,1},{2,10},{10,2},{3,11},{11,3},{4,12},{12,4},... | collective-permute-start | bytes 393224 | tf_op jit(solution)/shard_map/ppermute | solution.py:20
  76.1 1.0 copy.29
  77.3 0.7 broadcast_bitcast_fusion
  79.4 0.7 copy.38
  80.1 1.4 copy.55
  81.5 0.7 bitcast_dynamic-update-slice_fusion
  82.4 1.0 copy.33
  83.4 6.8 %collective-permute-done.3 = bf16[128,512]{1,0:T(8,128)(2,1)} collective-permute-done((bf16[128,512]{1,0:T(8,128)(2,1)}, bf16[128,512]{1,0:T(8,128)(2,1)}, u32[]{:S(2)}, u32[]{:S(2)}) %collective-permute-start.3) | collective-permute-done | bytes 131104 | tf_op jit(solution)/shard_map/ppermute | solution.py:20
  90.3 1.7 copy.34
  91.9 0.7 constant_dynamic-update-slice_fusion.3
  92.6 0.7 constant_dynamic-update-slice_fusion.2
  93.2 0.7 constant_dynamic-update-slice_fusion.1
  93.9 1.6 constant_dynamic-update-slice_fusion
  95.5 1.9 fusion.29
  97.4 1.1 copy.45
  98.4 1.9 reshape.75
  100.4 1.9 dot_general.41
  102.3 2.1 copy.47
  104.3 1.9 reshape.76
  106.2 1.9 dot_general.45
  108.2 2.1 copy.36
  110.3 6.1 %reshape.72 = bf16[6,256,2,512]{3,2,1,0:T(2,128)(2,1)} reshape(bf16[6,8,4,8,1024]{4,3,2,1,0:T(8,128)(2,1)} %copy.36) | data formatting | bytes 6291456 | tf_op jit(solution)/shard_map/reshape | solution.py:43
  116.4 2.3 copy_multiply_fusion
  119.0 0.8 copy-done
  121.9 0.8 maximum_bitcast_fusion
  122.8 1.1 copy.54
  123.9 1.0 multiply_convert_fusion
  124.8 41.0 %all_to_all.21 = bf16[4,8,8,6,1024]{4,2,3,1,0:T(8,128)(2,1)} all-to-all(bf16[4,8,8,6,1024]{4,2,3,1,0:T(8,128)(2,1)S(1)} %multiply_convert_fusion), channel_id=1, replica_groups=mesh['zl'=8,'xx'=4,'fly'=16] {'xx'}, dimensions={0} | all-to-all | bytes 6291456 | tf_op jit(solution)/shard_map/all_to_all | solution.py:48
  165.8 3.6 %reduce_sum.21 = bf16[8,8,6,1024]{3,1,2,0:T(8,128)(2,1)} reduce(bf16[4,8,8,6,1024]{4,2,3,1,0:T(8,128)(2,1)} %all_to_all.21, bf16[]{:T(256)} %constant.2.clone.1), dimensions={0}, to_apply=%region_0.0 | reduce | flops 1179648 | bytes 3932162 | tf_op jit(solution)/shard_map/reduce_sum | solution.py:49
  169.5 4.6 %all-to-all-start.3 = ((bf16[8,8,6,1024]{3,1,2,0:T(8,128)(2,1)}), bf16[8,8,6,1024]{3,1,2,0:T(8,128)(2,1)}, u32[]{:S(2)}, u32[]{:S(2)}) async-start(bf16[8,8,6,1024]{3,1,2,0:T(8,128)(2,1)} %reduce_sum.21), calls=%async_computation.3 | async-start | bytes 1572864 | tf_op jit(solution)/shard_map/all_to_all | solution.py:50
  174.1 1.6 fusion.7
  176.6 1.9 collective-permute-start.4
  178.7 2.9 %collective-permute-start.5 = (f32[128,512]{0,1:T(8,128)S(1)}, f32[128,512]{0,1:T(8,128)S(1)}, u32[]{:S(2)}, u32[]{:S(2)}) collective-permute-start(f32[128,512]{0,1:T(8,128)S(1)} %bitcast.104), channel_id=1, source_target_pairs={{0,2},{2,0},{1,3},{3,1},{4,6},{6,4},{5,7},{7,5},{8,10},{10,8},{9,1... | collective-permute-start | bytes 786440 | tf_op jit(solution)/shard_map/ppermute | solution.py:20
  181.7 5.4 %collective-permute-start.6 = (f32[128,512]{0,1:T(8,128)S(1)}, f32[128,512]{0,1:T(8,128)S(1)}, u32[]{:S(2)}, u32[]{:S(2)}) collective-permute-start(f32[128,512]{0,1:T(8,128)S(1)} %bitcast.105), channel_id=1, source_target_pairs={{0,4},{4,0},{1,5},{5,1},{2,6},{6,2},{3,7},{7,3},{8,12},{12,8},{9,1... | collective-permute-start | bytes 786440 | tf_op jit(solution)/shard_map/ppermute | solution.py:20
  187.2 8.2 %collective-permute-start.7 = (f32[128,512]{0,1:T(8,128)S(1)}, f32[128,512]{0,1:T(8,128)S(1)}, u32[]{:S(2)}, u32[]{:S(2)}) collective-permute-start(f32[128,512]{0,1:T(8,128)S(1)} %bitcast.106), channel_id=1, source_target_pairs={{0,8},{8,0},{1,9},{9,1},{2,10},{10,2},{3,11},{11,3},{4,12},{12,4},... | collective-permute-start | bytes 786440 | tf_op jit(solution)/shard_map/ppermute | solution.py:20
  195.6 1.7 collective-permute-done.6
  197.3 9.0 %collective-permute-done.7 = f32[128,512]{0,1:T(8,128)S(1)} collective-permute-done((f32[128,512]{0,1:T(8,128)S(1)}, f32[128,512]{0,1:T(8,128)S(1)}, u32[]{:S(2)}, u32[]{:S(2)}) %collective-permute-start.7) | collective-permute-done | bytes 262176 | tf_op jit(solution)/shard_map/ppermute | solution.py:20
  206.4 0.8 copy.51
  207.1 28.2 %all-to-all-done.3 = bf16[8,8,6,1024]{3,1,2,0:T(8,128)(2,1)} async-done(((bf16[8,8,6,1024]{3,1,2,0:T(8,128)(2,1)}), bf16[8,8,6,1024]{3,1,2,0:T(8,128)(2,1)}, u32[]{:S(2)}, u32[]{:S(2)}) %all-to-all-start.3) | async-done | bytes 786464 | tf_op jit(solution)/shard_map/all_to_all | solution.py:50
  235.4 1.3 convert_reduce_fusion
  236.6 0.7 multiply_bitcast_fusion
  (50 shorter events, 5.7 us)
Async XLA Ops:
  56.0 21.1 %copy-start.10 = (s32[6,4]{0,1:T(4,128)S(1)}, s32[6,4]{0,1:T(4,128)}, u32[]{:S(2)}) copy-start(s32[6,4]{0,1:T(4,128)} %param.7) | copy-start | bytes 292
  56.0 52.2 %all-to-all-start.1 = ((bf16[4,8,6,8,1024]{4,3,1,2,0:T(8,128)(2,1)}), bf16[4,8,6,8,1024]{4,3,1,2,0:T(8,128)(2,1)S(1)}, u32[]{:S(2)}, u32[]{:S(2)}) async-start(bf16[4,8,6,8,1024]{4,3,1,2,0:T(8,128)(2,1)} %broadcast_in_dim.9), calls=%async_computation.1 | async-start | bytes 6291456 | tf_op jit(solution)/shard_map/all_to_all | solution.py:42
  60.4 21.7 %collective-permute-start = (bf16[128,512]{1,0:T(8,128)(2,1)}, bf16[128,512]{1,0:T(8,128)(2,1)S(1)}, u32[]{:S(2)}, u32[]{:S(2)}) collective-permute-start(bf16[128,512]{1,0:T(8,128)(2,1)} %param.4), channel_id=1, source_target_pairs={{0,1},{1,0},{2,3},{3,2},{4,5},{5,4},{6,7},{7,6},{8,9},{9,8},{10,11... | collective-permute-start | bytes 393224 | tf_op jit(solution)/shard_map/ppermute | solution.py:20
  62.4 19.9 %collective-permute-start.1 = (bf16[128,512]{1,0:T(8,128)(2,1)}, bf16[128,512]{1,0:T(8,128)(2,1)S(1)}, u32[]{:S(2)}, u32[]{:S(2)}) collective-permute-start(bf16[128,512]{1,0:T(8,128)(2,1)} %param.4), channel_id=1, source_target_pairs={{0,2},{2,0},{1,3},{3,1},{4,6},{6,4},{5,7},{7,5},{8,10},{10,8},{9,1... | collective-permute-start | bytes 393224 | tf_op jit(solution)/shard_map/ppermute | solution.py:20
  65.0 17.4 %collective-permute-start.2 = (bf16[128,512]{1,0:T(8,128)(2,1)}, bf16[128,512]{1,0:T(8,128)(2,1)}, u32[]{:S(2)}, u32[]{:S(2)}) collective-permute-start(bf16[128,512]{1,0:T(8,128)(2,1)} %param.4), channel_id=1, source_target_pairs={{0,4},{4,0},{1,5},{5,1},{2,6},{6,2},{3,7},{7,3},{8,12},{12,8},{9,1... | collective-permute-start | bytes 393224 | tf_op jit(solution)/shard_map/ppermute | solution.py:20
  67.9 22.4 %collective-permute-start.3 = (bf16[128,512]{1,0:T(8,128)(2,1)}, bf16[128,512]{1,0:T(8,128)(2,1)}, u32[]{:S(2)}, u32[]{:S(2)}) collective-permute-start(bf16[128,512]{1,0:T(8,128)(2,1)} %param.4), channel_id=1, source_target_pairs={{0,8},{8,0},{1,9},{9,1},{2,10},{10,2},{3,11},{11,3},{4,12},{12,4},... | collective-permute-start | bytes 393224 | tf_op jit(solution)/shard_map/ppermute | solution.py:20
  118.7 1.0 copy-start
  118.9 1.6 copy-start.1
  118.9 1.6 copy-start.7
  120.1 1.1 copy-start.3
  120.1 1.2 copy-start.2
  120.6 0.7 copy-start.5
  122.7 1.1 copy-start.9
  165.8 8.2 %copy-start.4 = (f32[128,512]{1,0:T(8,128)S(1)}, f32[128,512]{1,0:T(8,128)}, u32[]{:S(2)}) copy-start(f32[128,512]{1,0:T(8,128)} %copy-done.3) | copy-start | bytes 786436
  169.5 65.9 %all-to-all-start.3 = ((bf16[8,8,6,1024]{3,1,2,0:T(8,128)(2,1)}), bf16[8,8,6,1024]{3,1,2,0:T(8,128)(2,1)}, u32[]{:S(2)}, u32[]{:S(2)}) async-start(bf16[8,8,6,1024]{3,1,2,0:T(8,128)(2,1)} %reduce_sum.21), calls=%async_computation.3 | async-start | bytes 1572864 | tf_op jit(solution)/shard_map/all_to_all | solution.py:50
  174.1 1.6 copy-start.6
  174.1 1.6 copy-start.8
  176.6 19.0 %collective-permute-start.4 = (f32[128,512]{0,1:T(8,128)S(1)}, f32[128,512]{0,1:T(8,128)S(1)}, u32[]{:S(2)}, u32[]{:S(2)}) collective-permute-start(f32[128,512]{0,1:T(8,128)S(1)} %bitcast.103), channel_id=1, source_target_pairs={{0,1},{1,0},{2,3},{3,2},{4,5},{5,4},{6,7},{7,6},{8,9},{9,8},{10,11... | collective-permute-start | bytes 786440 | tf_op jit(solution)/shard_map/ppermute | solution.py:20
  178.7 16.9 %collective-permute-start.5 = (f32[128,512]{0,1:T(8,128)S(1)}, f32[128,512]{0,1:T(8,128)S(1)}, u32[]{:S(2)}, u32[]{:S(2)}) collective-permute-start(f32[128,512]{0,1:T(8,128)S(1)} %bitcast.104), channel_id=1, source_target_pairs={{0,2},{2,0},{1,3},{3,1},{4,6},{6,4},{5,7},{7,5},{8,10},{10,8},{9,1... | collective-permute-start | bytes 786440 | tf_op jit(solution)/shard_map/ppermute | solution.py:20
  181.7 15.6 %collective-permute-start.6 = (f32[128,512]{0,1:T(8,128)S(1)}, f32[128,512]{0,1:T(8,128)S(1)}, u32[]{:S(2)}, u32[]{:S(2)}) collective-permute-start(f32[128,512]{0,1:T(8,128)S(1)} %bitcast.105), channel_id=1, source_target_pairs={{0,4},{4,0},{1,5},{5,1},{2,6},{6,2},{3,7},{7,3},{8,12},{12,8},{9,1... | collective-permute-start | bytes 786440 | tf_op jit(solution)/shard_map/ppermute | solution.py:20
  187.2 19.1 %collective-permute-start.7 = (f32[128,512]{0,1:T(8,128)S(1)}, f32[128,512]{0,1:T(8,128)S(1)}, u32[]{:S(2)}, u32[]{:S(2)}) collective-permute-start(f32[128,512]{0,1:T(8,128)S(1)} %bitcast.106), channel_id=1, source_target_pairs={{0,8},{8,0},{1,9},{9,1},{2,10},{10,2},{3,11},{11,3},{4,12},{12,4},... | collective-permute-start | bytes 786440 | tf_op jit(solution)/shard_map/ppermute | solution.py:20

commit v6 on v5

--- a/solution.py
+++ b/solution.py
@@ -3,6 +3,7 @@
 from jax import lax
 from jax.sharding import Mesh
 from jax.sharding import PartitionSpec as P
+
 
 BS = 256
 ROWS = "zl"
@@ -44,7 +45,6 @@
 
 
 def scatter_rows(terms):
-    xx, zl, own, factor_count, width = terms.shape
     got = lax.all_to_all(terms, COLS, 0, 0, tiled=True)
     part = got.astype(jnp.float32).sum(0)
     got = lax.all_to_all(part.astype(jnp.bfloat16), ROWS, 0, 0, tiled=True)
@@ -52,7 +52,7 @@
     return part.transpose(1, 0, 2)
 
 
-def body(tokens, hidden_grad, w_up, pattern):
+def layer(tokens, hidden_grad, w_up, pattern):
     row_count, local_width = tokens.shape
     factor_count = w_up.shape[0]
     hidden_width = hidden_grad.shape[1]
@@ -80,7 +80,6 @@
             partner = partner_2(tokens, "fly", bit_number)
             gathered.append(partner.reshape(row_count, local_blocks, BS))
     reads = jnp.stack(gathered, axis=2)
-    grads = []
     contribs = []
     products = []
     for group in range(local_blocks):
@@ -132,7 +131,7 @@
 def solution(mesh):
     grid = split_mesh(mesh)
     return jax.shard_map(
-        body,
+        layer,
         mesh=grid,
         in_specs=(P(DP, "fly"), P(DP, "fly"), P(None, DP, "fly"), P(None, "fly")),
         out_specs=(P(DP, "fly"), P(None, DP, "fly")),

time: 240 us -> 240 us (level)
  no operation moved by 1% of the time
where the time goes in v6:
time: 240 us; the launch traced here: 237 us
  blocking collectives  93.3 us (39%)
  waiting for transfers between devices  45.8 us (19%)
  starting transfers between devices  43.1 us (18%)
  local copies, waits for them, and re-layouts  40 us (17%)
  other arithmetic  9.87 us (4%)
  matrix products  4.33 us (2%)
    all_to_all x1, blocking collectives, gather_rows(): by_row = lax.all_to_all(copies, ROWS, 0, 0, tiled=True)  52.3 us
    all_to_all x1, blocking collectives, scatter_rows(): got = lax.all_to_all(terms, COLS, 0, 0, tiled=True)  41 us
    ppermute x8, starting transfers between devices, partner_2(): return lax.ppermute(block, axis, route)  34.1 us
    all_to_all x1, waiting for transfers between devices, scatter_rows(): got = lax.all_to_all(part.astype(jnp.bfloat16), ROWS, 0, 0, tiled=True)  28.2 us
    ppermute x8, waiting for transfers between devices, partner_2(): return lax.ppermute(block, axis, route)  17.5 us
    unnamed x31, local copies, waits for them, and re-layouts  7.98 us
    reshape x1, local copies, waits for them, and re-layouts, gather_rows(): both.transpose(2, 1, 0, 3, 4).reshape(factor_count, zl * xx * own, width)  6.15 us
    reduce_sum x2, other arithmetic, scatter_rows(): part = got.astype(jnp.float32).sum(0)  4.91 us
  transfers between devices with their start and end apart: 10, of which 4 were waited for; matrix products, arithmetic and copies ran while one was open for 12% of the time, Pallas kernels for 0%

profile of v6, /device:TPU:24, one launch (start us, length us, event | category | flops | bytes accessed | tf_op | source)
XLA Modules:
  0.0 237.3 jit_solution(10275078324980596093)
XLA Ops:
  0.6 1.0 broadcast_in_dim.8
  1.6 52.3 %all_to_all.20 = bf16[8,6,8,1024]{3,2,1,0:T(8,128)(2,1)S(1)} all-to-all(bf16[8,6,8,1024]{3,2,1,0:T(8,128)(2,1)S(1)} %broadcast_in_dim.8), channel_id=1, replica_groups=mesh['zl'=8,'xx'=4,'fly'=16] {'zl'}, dimensions={0} | all-to-all | bytes 1572864 | tf_op jit(solution)/shard_map/all_to_all | solution.py:41
  54.0 2.0 broadcast_in_dim.9
  56.0 4.4 %all-to-all-start.1 = ((bf16[4,8,6,8,1024]{4,3,1,2,0:T(8,128)(2,1)}), bf16[4,8,6,8,1024]{4,3,1,2,0:T(8,128)(2,1)S(1)}, u32[]{:S(2)}, u32[]{:S(2)}) async-start(bf16[4,8,6,8,1024]{4,3,1,2,0:T(8,128)(2,1)} %broadcast_in_dim.9), calls=%async_computation.1 | async-start | bytes 6291456 | tf_op jit(solution)/shard_map/all_to_all | solution.py:43
  60.4 1.9 collective-permute-start
  62.4 2.7 %collective-permute-start.1 = (bf16[128,512]{1,0:T(8,128)(2,1)}, bf16[128,512]{1,0:T(8,128)(2,1)S(1)}, u32[]{:S(2)}, u32[]{:S(2)}) collective-permute-start(bf16[128,512]{1,0:T(8,128)(2,1)} %param.4), channel_id=1, source_target_pairs={{0,2},{2,0},{1,3},{3,1},{4,6},{6,4},{5,7},{7,5},{8,10},{10,8},{9,1... | collective-permute-start | bytes 393224 | tf_op jit(solution)/shard_map/ppermute | solution.py:21
  65.0 2.9 %collective-permute-start.2 = (bf16[128,512]{1,0:T(8,128)(2,1)}, bf16[128,512]{1,0:T(8,128)(2,1)}, u32[]{:S(2)}, u32[]{:S(2)}) collective-permute-start(bf16[128,512]{1,0:T(8,128)(2,1)} %param.4), channel_id=1, source_target_pairs={{0,4},{4,0},{1,5},{5,1},{2,6},{6,2},{3,7},{7,3},{8,12},{12,8},{9,1... | collective-permute-start | bytes 393224 | tf_op jit(solution)/shard_map/ppermute | solution.py:21
  67.9 8.2 %collective-permute-start.3 = (bf16[128,512]{1,0:T(8,128)(2,1)}, bf16[128,512]{1,0:T(8,128)(2,1)}, u32[]{:S(2)}, u32[]{:S(2)}) collective-permute-start(bf16[128,512]{1,0:T(8,128)(2,1)} %param.4), channel_id=1, source_target_pairs={{0,8},{8,0},{1,9},{9,1},{2,10},{10,2},{3,11},{11,3},{4,12},{12,4},... | collective-permute-start | bytes 393224 | tf_op jit(solution)/shard_map/ppermute | solution.py:21
  76.1 1.0 copy.29
  77.3 0.7 broadcast_bitcast_fusion
  79.4 0.7 copy.38
  80.1 1.4 copy.55
  81.5 0.7 bitcast_dynamic-update-slice_fusion
  82.4 1.0 copy.33
  83.4 6.8 %collective-permute-done.3 = bf16[128,512]{1,0:T(8,128)(2,1)} collective-permute-done((bf16[128,512]{1,0:T(8,128)(2,1)}, bf16[128,512]{1,0:T(8,128)(2,1)}, u32[]{:S(2)}, u32[]{:S(2)}) %collective-permute-start.3) | collective-permute-done | bytes 131104 | tf_op jit(solution)/shard_map/ppermute | solution.py:21
  90.3 1.7 copy.34
  91.9 0.7 constant_dynamic-update-slice_fusion.3
  92.6 0.7 constant_dynamic-update-slice_fusion.2
  93.2 0.7 constant_dynamic-update-slice_fusion.1
  93.9 1.6 constant_dynamic-update-slice_fusion
  95.5 1.9 fusion.29
  97.4 1.1 copy.45
  98.4 1.9 reshape.75
  100.4 1.9 dot_general.41
  102.3 2.1 copy.47
  104.3 1.9 reshape.76
  106.2 1.9 dot_general.45
  108.2 2.1 copy.36
  110.3 6.1 %reshape.72 = bf16[6,256,2,512]{3,2,1,0:T(2,128)(2,1)} reshape(bf16[6,8,4,8,1024]{4,3,2,1,0:T(8,128)(2,1)} %copy.36) | data formatting | bytes 6291456 | tf_op jit(solution)/shard_map/reshape | solution.py:44
  116.4 2.3 copy_multiply_fusion
  119.0 0.8 copy-done
  121.9 0.8 maximum_bitcast_fusion
  122.8 1.1 copy.54
  123.9 1.0 multiply_convert_fusion
  124.8 41.0 %all_to_all.21 = bf16[4,8,8,6,1024]{4,2,3,1,0:T(8,128)(2,1)} all-to-all(bf16[4,8,8,6,1024]{4,2,3,1,0:T(8,128)(2,1)S(1)} %multiply_convert_fusion), channel_id=1, replica_groups=mesh['zl'=8,'xx'=4,'fly'=16] {'xx'}, dimensions={0} | all-to-all | bytes 6291456 | tf_op jit(solution)/shard_map/all_to_all | solution.py:48
  165.8 3.6 %reduce_sum.21 = bf16[8,8,6,1024]{3,1,2,0:T(8,128)(2,1)} reduce(bf16[4,8,8,6,1024]{4,2,3,1,0:T(8,128)(2,1)} %all_to_all.21, bf16[]{:T(256)} %constant.2.clone.1), dimensions={0}, to_apply=%region_0.0 | reduce | flops 1179648 | bytes 3932162 | tf_op jit(solution)/shard_map/reduce_sum | solution.py:49
  169.5 4.6 %all-to-all-start.3 = ((bf16[8,8,6,1024]{3,1,2,0:T(8,128)(2,1)}), bf16[8,8,6,1024]{3,1,2,0:T(8,128)(2,1)}, u32[]{:S(2)}, u32[]{:S(2)}) async-start(bf16[8,8,6,1024]{3,1,2,0:T(8,128)(2,1)} %reduce_sum.21), calls=%async_computation.3 | async-start | bytes 1572864 | tf_op jit(solution)/shard_map/all_to_all | solution.py:50
  174.1 1.6 fusion.7
  176.6 1.9 collective-permute-start.4
  178.7 2.9 %collective-permute-start.5 = (f32[128,512]{0,1:T(8,128)S(1)}, f32[128,512]{0,1:T(8,128)S(1)}, u32[]{:S(2)}, u32[]{:S(2)}) collective-permute-start(f32[128,512]{0,1:T(8,128)S(1)} %bitcast.104), channel_id=1, source_target_pairs={{0,2},{2,0},{1,3},{3,1},{4,6},{6,4},{5,7},{7,5},{8,10},{10,8},{9,1... | collective-permute-start | bytes 786440 | tf_op jit(solution)/shard_map/ppermute | solution.py:21
  181.7 5.4 %collective-permute-start.6 = (f32[128,512]{0,1:T(8,128)S(1)}, f32[128,512]{0,1:T(8,128)S(1)}, u32[]{:S(2)}, u32[]{:S(2)}) collective-permute-start(f32[128,512]{0,1:T(8,128)S(1)} %bitcast.105), channel_id=1, source_target_pairs={{0,4},{4,0},{1,5},{5,1},{2,6},{6,2},{3,7},{7,3},{8,12},{12,8},{9,1... | collective-permute-start | bytes 786440 | tf_op jit(solution)/shard_map/ppermute | solution.py:21
  187.2 8.2 %collective-permute-start.7 = (f32[128,512]{0,1:T(8,128)S(1)}, f32[128,512]{0,1:T(8,128)S(1)}, u32[]{:S(2)}, u32[]{:S(2)}) collective-permute-start(f32[128,512]{0,1:T(8,128)S(1)} %bitcast.106), channel_id=1, source_target_pairs={{0,8},{8,0},{1,9},{9,1},{2,10},{10,2},{3,11},{11,3},{4,12},{12,4},... | collective-permute-start | bytes 786440 | tf_op jit(solution)/shard_map/ppermute | solution.py:21
  195.6 1.7 collective-permute-done.6
  197.3 9.0 %collective-permute-done.7 = f32[128,512]{0,1:T(8,128)S(1)} collective-permute-done((f32[128,512]{0,1:T(8,128)S(1)}, f32[128,512]{0,1:T(8,128)S(1)}, u32[]{:S(2)}, u32[]{:S(2)}) %collective-permute-start.7) | collective-permute-done | bytes 262176 | tf_op jit(solution)/shard_map/ppermute | solution.py:21
  206.4 0.8 copy.51
  207.1 28.2 %all-to-all-done.3 = bf16[8,8,6,1024]{3,1,2,0:T(8,128)(2,1)} async-done(((bf16[8,8,6,1024]{3,1,2,0:T(8,128)(2,1)}), bf16[8,8,6,1024]{3,1,2,0:T(8,128)(2,1)}, u32[]{:S(2)}, u32[]{:S(2)}) %all-to-all-start.3) | async-done | bytes 786464 | tf_op jit(solution)/shard_map/all_to_all | solution.py:50
  235.4 1.3 convert_reduce_fusion
  236.6 0.7 multiply_bitcast_fusion
  (50 shorter events, 5.7 us)
Async XLA Ops:
  56.0 21.1 %copy-start.10 = (s32[6,4]{0,1:T(4,128)S(1)}, s32[6,4]{0,1:T(4,128)}, u32[]{:S(2)}) copy-start(s32[6,4]{0,1:T(4,128)} %param.7) | copy-start | bytes 292
  56.0 52.2 %all-to-all-start.1 = ((bf16[4,8,6,8,1024]{4,3,1,2,0:T(8,128)(2,1)}), bf16[4,8,6,8,1024]{4,3,1,2,0:T(8,128)(2,1)S(1)}, u32[]{:S(2)}, u32[]{:S(2)}) async-start(bf16[4,8,6,8,1024]{4,3,1,2,0:T(8,128)(2,1)} %broadcast_in_dim.9), calls=%async_computation.1 | async-start | bytes 6291456 | tf_op jit(solution)/shard_map/all_to_all | solution.py:43
  60.4 21.7 %collective-permute-start = (bf16[128,512]{1,0:T(8,128)(2,1)}, bf16[128,512]{1,0:T(8,128)(2,1)S(1)}, u32[]{:S(2)}, u32[]{:S(2)}) collective-permute-start(bf16[128,512]{1,0:T(8,128)(2,1)} %param.4), channel_id=1, source_target_pairs={{0,1},{1,0},{2,3},{3,2},{4,5},{5,4},{6,7},{7,6},{8,9},{9,8},{10,11... | collective-permute-start | bytes 393224 | tf_op jit(solution)/shard_map/ppermute | solution.py:21
  62.4 19.9 %collective-permute-start.1 = (bf16[128,512]{1,0:T(8,128)(2,1)}, bf16[128,512]{1,0:T(8,128)(2,1)S(1)}, u32[]{:S(2)}, u32[]{:S(2)}) collective-permute-start(bf16[128,512]{1,0:T(8,128)(2,1)} %param.4), channel_id=1, source_target_pairs={{0,2},{2,0},{1,3},{3,1},{4,6},{6,4},{5,7},{7,5},{8,10},{10,8},{9,1... | collective-permute-start | bytes 393224 | tf_op jit(solution)/shard_map/ppermute | solution.py:21
  65.0 17.4 %collective-permute-start.2 = (bf16[128,512]{1,0:T(8,128)(2,1)}, bf16[128,512]{1,0:T(8,128)(2,1)}, u32[]{:S(2)}, u32[]{:S(2)}) collective-permute-start(bf16[128,512]{1,0:T(8,128)(2,1)} %param.4), channel_id=1, source_target_pairs={{0,4},{4,0},{1,5},{5,1},{2,6},{6,2},{3,7},{7,3},{8,12},{12,8},{9,1... | collective-permute-start | bytes 393224 | tf_op jit(solution)/shard_map/ppermute | solution.py:21
  67.9 22.4 %collective-permute-start.3 = (bf16[128,512]{1,0:T(8,128)(2,1)}, bf16[128,512]{1,0:T(8,128)(2,1)}, u32[]{:S(2)}, u32[]{:S(2)}) collective-permute-start(bf16[128,512]{1,0:T(8,128)(2,1)} %param.4), channel_id=1, source_target_pairs={{0,8},{8,0},{1,9},{9,1},{2,10},{10,2},{3,11},{11,3},{4,12},{12,4},... | collective-permute-start | bytes 393224 | tf_op jit(solution)/shard_map/ppermute | solution.py:21
  118.7 1.0 copy-start
  118.9 1.6 copy-start.1
  118.9 1.6 copy-start.7
  120.1 1.1 copy-start.3
  120.1 1.2 copy-start.2
  120.6 0.7 copy-start.5
  122.7 1.1 copy-start.9
  165.8 8.2 %copy-start.4 = (f32[128,512]{1,0:T(8,128)S(1)}, f32[128,512]{1,0:T(8,128)}, u32[]{:S(2)}) copy-start(f32[128,512]{1,0:T(8,128)} %copy-done.3) | copy-start | bytes 786436
  169.5 65.9 %all-to-all-start.3 = ((bf16[8,8,6,1024]{3,1,2,0:T(8,128)(2,1)}), bf16[8,8,6,1024]{3,1,2,0:T(8,128)(2,1)}, u32[]{:S(2)}, u32[]{:S(2)}) async-start(bf16[8,8,6,1024]{3,1,2,0:T(8,128)(2,1)} %reduce_sum.21), calls=%async_computation.3 | async-start | bytes 1572864 | tf_op jit(solution)/shard_map/all_to_all | solution.py:50
  174.1 1.6 copy-start.6
  174.1 1.6 copy-start.8
  176.6 19.0 %collective-permute-start.4 = (f32[128,512]{0,1:T(8,128)S(1)}, f32[128,512]{0,1:T(8,128)S(1)}, u32[]{:S(2)}, u32[]{:S(2)}) collective-permute-start(f32[128,512]{0,1:T(8,128)S(1)} %bitcast.103), channel_id=1, source_target_pairs={{0,1},{1,0},{2,3},{3,2},{4,5},{5,4},{6,7},{7,6},{8,9},{9,8},{10,11... | collective-permute-start | bytes 786440 | tf_op jit(solution)/shard_map/ppermute | solution.py:21
  178.7 16.9 %collective-permute-start.5 = (f32[128,512]{0,1:T(8,128)S(1)}, f32[128,512]{0,1:T(8,128)S(1)}, u32[]{:S(2)}, u32[]{:S(2)}) collective-permute-start(f32[128,512]{0,1:T(8,128)S(1)} %bitcast.104), channel_id=1, source_target_pairs={{0,2},{2,0},{1,3},{3,1},{4,6},{6,4},{5,7},{7,5},{8,10},{10,8},{9,1... | collective-permute-start | bytes 786440 | tf_op jit(solution)/shard_map/ppermute | solution.py:21
  181.7 15.6 %collective-permute-start.6 = (f32[128,512]{0,1:T(8,128)S(1)}, f32[128,512]{0,1:T(8,128)S(1)}, u32[]{:S(2)}, u32[]{:S(2)}) collective-permute-start(f32[128,512]{0,1:T(8,128)S(1)} %bitcast.105), channel_id=1, source_target_pairs={{0,4},{4,0},{1,5},{5,1},{2,6},{6,2},{3,7},{7,3},{8,12},{12,8},{9,1... | collective-permute-start | bytes 786440 | tf_op jit(solution)/shard_map/ppermute | solution.py:21
  187.2 19.1 %collective-permute-start.7 = (f32[128,512]{0,1:T(8,128)S(1)}, f32[128,512]{0,1:T(8,128)S(1)}, u32[]{:S(2)}, u32[]{:S(2)}) collective-permute-start(f32[128,512]{0,1:T(8,128)S(1)} %bitcast.106), channel_id=1, source_target_pairs={{0,8},{8,0},{1,9},{9,1},{2,10},{10,2},{3,11},{11,3},{4,12},{12,4},... | collective-permute-start | bytes 786440 | tf_op jit(solution)/shard_map/ppermute | solution.py:21

commit v7 on v4

--- a/solution.py
+++ b/solution.py
@@ -3,6 +3,7 @@
 from jax import lax
 from jax.sharding import Mesh
 from jax.sharding import PartitionSpec as P
+
 
 BS = 256
 ROWS = "zl"
@@ -32,13 +33,32 @@
     return 0 if factor == 0 else 2 ** (factor - 1)
 
 
+def gather_line(block, axis):
+    count = lax.axis_size(axis)
+    bits = count.bit_length() - 1
+    assert 1 << bits == count
+    place = lax.axis_index(axis)
+    held = block[None]
+    for step in range(bits):
+        dist = count >> (step + 1)
+        got = lax.ppermute(held, axis, [(i, i ^ dist) for i in range(count)])
+        upper = (place & dist) != 0
+        held = jnp.where(upper, jnp.stack([got, held]), jnp.stack([held, got]))
+    order = tuple(reversed(range(bits))) + tuple(range(bits, bits + block.ndim))
+    return held.reshape((2,) * bits + block.shape).transpose(order).reshape((count,) + block.shape)
+
+
 def gather_rows(w_up):
-    inner = lax.all_gather(w_up, COLS, axis=1, tiled=True)
-    return lax.all_gather(inner, ROWS, axis=1, tiled=True)
+    factor_count, own, width = w_up.shape
+    zl = lax.axis_size(ROWS)
+    xx = lax.axis_size(COLS)
+    by_row = gather_line(w_up, ROWS)
+    copies = jnp.broadcast_to(by_row[None], (xx, zl, factor_count, own, width))
+    both = lax.all_to_all(copies, COLS, 0, 0, tiled=True)
+    return both.transpose(2, 1, 0, 3, 4).reshape(factor_count, zl * xx * own, width)
 
 
 def scatter_rows(terms):
-    xx, zl, own, factor_count, width = terms.shape
     got = lax.all_to_all(terms, COLS, 0, 0, tiled=True)
     part = got.astype(jnp.float32).sum(0)
     got = lax.all_to_all(part.astype(jnp.bfloat16), ROWS, 0, 0, tiled=True)
@@ -46,7 +66,7 @@
     return part.transpose(1, 0, 2)
 
 
-def body(tokens, hidden_grad, w_up, pattern):
+def layer(tokens, hidden_grad, w_up, pattern):
     row_count, local_width = tokens.shape
     factor_count = w_up.shape[0]
     hidden_width = hidden_grad.shape[1]
@@ -119,7 +139,7 @@
 def solution(mesh):
     grid = split_mesh(mesh)
     return jax.shard_map(
-        body,
+        layer,
         mesh=grid,
         in_specs=(P(DP, "fly"), P(DP, "fly"), P(None, DP, "fly"), P(None, "fly")),
         out_specs=(P(DP, "fly"), P(None, DP, "fly")),

time: 276 us -> 232 us (0.84)
  the two profiles are of different devices: /device:TPU:160 before, /device:TPU:217 now
where the time goes in v7:
time: 232 us; the launch traced here: 230 us
  waiting for transfers between devices  94.6 us (41%)
  starting transfers between devices  93.8 us (40%)
  local copies, waits for them, and re-layouts  25.3 us (11%)
  other arithmetic  8.54 us (4%)
  matrix products  6.71 us (3%)
    ppermute x8, starting transfers between devices, partner_2(): return lax.ppermute(block, axis, route)  33.5 us
    ppermute x8, waiting for transfers between devices, partner_2(): return lax.ppermute(block, axis, route)  29.5 us
    ppermute x6, waiting for transfers between devices, gather_line(): got = lax.ppermute(held, axis, [(i, i ^ dist) for i in range(count)])  28 us
    all_to_all x2, starting transfers between devices, scatter_rows(): got = lax.all_to_all(part.astype(jnp.bfloat16), ROWS, 0, 0, tiled=True)  27.4 us
    all_to_all x2, waiting for transfers between devices, scatter_rows(): got = lax.all_to_all(terms, COLS, 0, 0, tiled=True)  18.3 us
    ppermute x6, starting transfers between devices, gather_line(): got = lax.ppermute(held, axis, [(i, i ^ dist) for i in range(count)])  16.1 us
    all_to_all x2, waiting for transfers between devices, scatter_rows(): got = lax.all_to_all(part.astype(jnp.bfloat16), ROWS, 0, 0, tiled=True)  13.1 us
    all_to_all x2, starting transfers between devices, scatter_rows(): got = lax.all_to_all(terms, COLS, 0, 0, tiled=True)  8.68 us
  transfers between devices with their start and end apart: 20, of which 11 were waited for; matrix products, arithmetic and copies ran while one was open for 15% of the time, Pallas kernels for 0%

profile of v7, /device:TPU:217, one launch (start us, length us, event | category | flops | bytes accessed | tf_op | source)
XLA Modules:
  0.0 230.1 jit_solution(5362667031659345052)
XLA Ops:
  1.5 1.9 collective-permute-start.7
  3.4 8.7 %collective-permute-done.7 = bf16[1,6,8,512]{3,2,1,0:T(8,128)(2,1)S(1)} collective-permute-done((bf16[1,6,8,512]{3,2,1,0:T(8,128)(2,1)S(1)}, bf16[1,6,8,512]{3,2,1,0:T(8,128)(2,1)S(1)}, u32[]{:S(2)}, u32[]{:S(2)}) %collective-permute-start.7) | collective-permute-done | bytes 49184 | tf_op jit(solution)/shard_map/ppermute | solution.py:44
  12.2 1.9 collective-permute-start.8
  14.1 4.6 %collective-permute-done.8 = bf16[2,1,6,8,512]{4,3,2,0,1:T(8,128)(2,1)S(1)} collective-permute-done((bf16[2,1,6,8,512]{4,3,2,0,1:T(8,128)(2,1)S(1)}, bf16[2,1,6,8,512]{4,3,2,0,1:T(8,128)(2,1)S(1)}, u32[]{:S(2)}, u32[]{:S(2)}) %collective-permute-start.8) | collective-permute-done | bytes 98336 | tf_op jit(solution)/shard_map/ppermute | solution.py:44
  18.8 6.1 %collective-permute-start.9 = (bf16[2,2,1,6,8,512]{5,4,3,1,0,2:T(8,128)(2,1)S(1)}, bf16[2,2,1,6,8,512]{5,4,3,1,0,2:T(8,128)(2,1)S(1)}, u32[]{:S(2)}, u32[]{:S(2)}) collective-permute-start(bf16[2,2,1,6,8,512]{5,4,3,1,0,2:T(8,128)(2,1)S(1)} %maximum_select_fusion.3), channel_id=1, source_target_pairs={{0,64},{64,0},{128,192},{192,128},{256,320},{320,256},{384,448},{4... | collective-permute-start | bytes 589832 | tf_op jit(solution)/shard_map/ppermute | solution.py:44
  24.9 2.7 %collective-permute-start = (bf16[128,512]{1,0:T(8,128)(2,1)}, bf16[128,512]{1,0:T(8,128)(2,1)S(1)}, u32[]{:S(2)}, u32[]{:S(2)}) collective-permute-start(bf16[128,512]{1,0:T(8,128)(2,1)} %param.4), channel_id=1, source_target_pairs={{0,1},{1,0},{2,3},{3,2},{4,5},{5,4},{6,7},{7,6},{8,9},{9,8},{10,11... | collective-permute-start | bytes 393224 | tf_op jit(solution)/shard_map/ppermute | solution.py:21
  27.6 2.4 %collective-permute-start.1 = (bf16[128,512]{1,0:T(8,128)(2,1)}, bf16[128,512]{1,0:T(8,128)(2,1)}, u32[]{:S(2)}, u32[]{:S(2)}) collective-permute-start(bf16[128,512]{1,0:T(8,128)(2,1)} %param.4), channel_id=1, source_target_pairs={{0,2},{2,0},{1,3},{3,1},{4,6},{6,4},{5,7},{7,5},{8,10},{10,8},{9,1... | collective-permute-start | bytes 393224 | tf_op jit(solution)/shard_map/ppermute | solution.py:21
  30.0 2.6 %collective-permute-start.2 = (bf16[128,512]{1,0:T(8,128)(2,1)}, bf16[128,512]{1,0:T(8,128)(2,1)S(1)}, u32[]{:S(2)}, u32[]{:S(2)}) collective-permute-start(bf16[128,512]{1,0:T(8,128)(2,1)} %param.4), channel_id=1, source_target_pairs={{0,4},{4,0},{1,5},{5,1},{2,6},{6,2},{3,7},{7,3},{8,12},{12,8},{9,1... | collective-permute-start | bytes 393224 | tf_op jit(solution)/shard_map/ppermute | solution.py:21
  32.6 8.7 %collective-permute-start.3 = (bf16[128,512]{1,0:T(8,128)(2,1)}, bf16[128,512]{1,0:T(8,128)(2,1)S(1)}, u32[]{:S(2)}, u32[]{:S(2)}) collective-permute-start(bf16[128,512]{1,0:T(8,128)(2,1)} %param.4), channel_id=1, source_target_pairs={{0,8},{8,0},{1,9},{9,1},{2,10},{10,2},{3,11},{11,3},{4,12},{12,4},... | collective-permute-start | bytes 393224 | tf_op jit(solution)/shard_map/ppermute | solution.py:21
  42.2 2.3 collective-permute-start.4
  44.6 1.4 broadcast_in_dim.36
  45.9 4.1 %all-to-all-start.1 = ((bf16[4,8,6,8,512]{4,3,1,2,0:T(8,128)(2,1)}), bf16[4,8,6,8,512]{4,3,1,2,0:T(8,128)(2,1)S(1)}, u32[]{:S(2)}, u32[]{:S(2)}) async-start(bf16[4,8,6,8,512]{4,3,1,2,0:T(8,128)(2,1)} %broadcast_in_dim.36), calls=%async_computation.1 | async-start | bytes 3145728 | tf_op jit(solution)/shard_map/all_to_all | solution.py:57
  51.5 7.1 %collective-permute-done.4 = bf16[1,6,8,512]{3,2,1,0:T(8,128)(2,1)S(1)} collective-permute-done((bf16[1,6,8,512]{3,2,1,0:T(8,128)(2,1)S(1)}, bf16[1,6,8,512]{3,2,1,0:T(8,128)(2,1)S(1)}, u32[]{:S(2)}, u32[]{:S(2)}) %collective-permute-start.4) | collective-permute-done | bytes 49184 | tf_op jit(solution)/shard_map/ppermute | solution.py:44
  58.6 1.9 collective-permute-start.5
  60.7 1.0 copy.101
  62.1 3.1 %collective-permute-done.5 = bf16[2,1,6,8,512]{4,3,2,0,1:T(8,128)(2,1)S(1)} collective-permute-done((bf16[2,1,6,8,512]{4,3,2,0,1:T(8,128)(2,1)S(1)}, bf16[2,1,6,8,512]{4,3,2,0,1:T(8,128)(2,1)S(1)}, u32[]{:S(2)}, u32[]{:S(2)}) %collective-permute-start.5) | collective-permute-done | bytes 98336 | tf_op jit(solution)/shard_map/ppermute | solution.py:44
  65.2 1.9 collective-permute-start.6
  67.2 4.4 %collective-permute-done.6 = bf16[2,2,1,6,8,512]{5,4,3,1,2,0:T(8,128)(2,1)S(1)} collective-permute-done((bf16[2,2,1,6,8,512]{5,4,3,1,2,0:T(8,128)(2,1)S(1)}, bf16[2,2,1,6,8,512]{5,4,3,1,2,0:T(8,128)(2,1)S(1)}, u32[]{:S(2)}, u32[]{:S(2)}) %collective-permute-start.6) | collective-permute-done | bytes 196640 | tf_op jit(solution)/shard_map/ppermute | solution.py:44
  71.8 1.4 broadcast_in_dim.32
  73.1 4.0 %all-to-all-start = ((bf16[4,8,6,8,512]{4,3,1,2,0:T(8,128)(2,1)}), bf16[4,8,6,8,512]{4,3,1,2,0:T(8,128)(2,1)S(1)}, u32[]{:S(2)}, u32[]{:S(2)}) async-start(bf16[4,8,6,8,512]{4,3,1,2,0:T(8,128)(2,1)} %broadcast_in_dim.32), calls=%async_computation | async-start | bytes 3145728 | tf_op jit(solution)/shard_map/all_to_all | solution.py:57
  77.8 1.2 fusion.23
  79.7 1.1 copy.125
  80.8 1.9 reshape.929
  82.7 1.9 dot_general.40
  86.7 1.8 multiply_convert_fusion
  88.6 5.7 %all-to-all-done = bf16[4,8,6,8,512]{4,3,1,2,0:T(8,128)(2,1)S(1)} async-done(((bf16[4,8,6,8,512]{4,3,1,2,0:T(8,128)(2,1)}), bf16[4,8,6,8,512]{4,3,1,2,0:T(8,128)(2,1)S(1)}, u32[]{:S(2)}, u32[]{:S(2)}) %all-to-all-start) | async-done | bytes 1572896 | tf_op jit(solution)/shard_map/all_to_all | solution.py:57
  94.2 4.3 %all-to-all-start.4 = ((bf16[4,8,8,6,512]{4,2,3,1,0:T(8,128)(2,1)}), bf16[4,8,8,6,512]{4,2,3,1,0:T(8,128)(2,1)}, u32[]{:S(2)}, u32[]{:S(2)}) async-start(bf16[4,8,8,6,512]{4,2,3,1,0:T(8,128)(2,1)} %multiply_convert_fusion), calls=%async_computation.4 | async-start | bytes 3145728 | tf_op jit(solution)/shard_map/all_to_all | solution.py:62
  99.3 1.3 copy.147
  100.6 1.1 copy.123
  101.7 1.9 reshape.928
  103.6 1.9 dot_general.37
  106.8 1.8 multiply_convert_fusion.1
  108.6 6.0 %all-to-all-done.4 = bf16[4,8,8,6,512]{4,2,3,1,0:T(8,128)(2,1)} async-done(((bf16[4,8,8,6,512]{4,2,3,1,0:T(8,128)(2,1)}), bf16[4,8,8,6,512]{4,2,3,1,0:T(8,128)(2,1)}, u32[]{:S(2)}, u32[]{:S(2)}) %all-to-all-start.4) | async-done | bytes 1572896 | tf_op jit(solution)/shard_map/all_to_all | solution.py:62
  114.6 4.3 %all-to-all-start.2 = ((bf16[4,8,8,6,512]{4,2,3,1,0:T(8,128)(2,1)}), bf16[4,8,8,6,512]{4,2,3,1,0:T(8,128)(2,1)}, u32[]{:S(2)}, u32[]{:S(2)}) async-start(bf16[4,8,8,6,512]{4,2,3,1,0:T(8,128)(2,1)} %multiply_convert_fusion.1), calls=%async_computation.2 | async-start | bytes 3145728 | tf_op jit(solution)/shard_map/all_to_all | solution.py:62
  118.9 2.5 %reduce_sum.44 = bf16[8,8,6,512]{3,1,2,0:T(8,128)(2,1)} reduce(bf16[4,8,8,6,512]{4,2,3,1,0:T(8,128)(2,1)} %all-to-all-done.4, bf16[]{:T(256)} %constant.20.clone.1), dimensions={0}, to_apply=%region_2.3 | reduce | flops 589824 | bytes 1966082 | tf_op jit(solution)/shard_map/reduce_sum | solution.py:63
  121.5 12.3 %all-to-all-done.2 = bf16[4,8,8,6,512]{4,2,3,1,0:T(8,128)(2,1)} async-done(((bf16[4,8,8,6,512]{4,2,3,1,0:T(8,128)(2,1)}), bf16[4,8,8,6,512]{4,2,3,1,0:T(8,128)(2,1)}, u32[]{:S(2)}, u32[]{:S(2)}) %all-to-all-start.2) | async-done | bytes 1572896 | tf_op jit(solution)/shard_map/all_to_all | solution.py:62
  133.8 17.2 %all-to-all-start.5 = ((bf16[8,8,6,512]{3,1,2,0:T(8,128)(2,1)}), bf16[8,8,6,512]{3,1,2,0:T(8,128)(2,1)S(1)}, u32[]{:S(2)}, u32[]{:S(2)}) async-start(bf16[8,8,6,512]{3,1,2,0:T(8,128)(2,1)} %reduce_sum.44), calls=%async_computation.5 | async-start | bytes 786432 | tf_op jit(solution)/shard_map/all_to_all | solution.py:64
  151.9 2.5 %reduce_sum.42 = bf16[8,8,6,512]{3,1,2,0:T(8,128)(2,1)} reduce(bf16[4,8,8,6,512]{4,2,3,1,0:T(8,128)(2,1)} %all-to-all-done.2, bf16[]{:T(256)} %constant.20.clone.1), dimensions={0}, to_apply=%region_0.1 | reduce | flops 589824 | bytes 1966082 | tf_op jit(solution)/shard_map/reduce_sum | solution.py:63
  154.4 13.1 %all-to-all-done.5 = bf16[8,8,6,512]{3,1,2,0:T(8,128)(2,1)S(1)} async-done(((bf16[8,8,6,512]{3,1,2,0:T(8,128)(2,1)}), bf16[8,8,6,512]{3,1,2,0:T(8,128)(2,1)S(1)}, u32[]{:S(2)}, u32[]{:S(2)}) %all-to-all-start.5) | async-done | bytes 393248 | tf_op jit(solution)/shard_map/all_to_all | solution.py:64
  167.5 10.2 %all-to-all-start.3 = ((bf16[8,8,6,512]{3,1,2,0:T(8,128)(2,1)}), bf16[8,8,6,512]{3,1,2,0:T(8,128)(2,1)}, u32[]{:S(2)}, u32[]{:S(2)}) async-start(bf16[8,8,6,512]{3,1,2,0:T(8,128)(2,1)} %reduce_sum.42), calls=%async_computation.3 | async-start | bytes 786432 | tf_op jit(solution)/shard_map/all_to_all | solution.py:64
  177.6 1.7 convolution_bitcast_fusion
  180.3 3.9 %collective-permute-start.10 = (f32[128,512]{0,1:T(8,128)S(1)}, f32[128,512]{0,1:T(8,128)S(1)}, u32[]{:S(2)}, u32[]{:S(2)}) collective-permute-start(f32[128,512]{0,1:T(8,128)S(1)} %bitcast.169), channel_id=1, source_target_pairs={{0,1},{1,0},{2,3},{3,2},{4,5},{5,4},{6,7},{7,6},{8,9},{9,8},{10,11... | collective-permute-start | bytes 786440 | tf_op jit(solution)/shard_map/ppermute | solution.py:21
  184.3 2.6 %collective-permute-start.11 = (f32[128,512]{0,1:T(8,128)S(1)}, f32[128,512]{0,1:T(8,128)S(1)}, u32[]{:S(2)}, u32[]{:S(2)}) collective-permute-start(f32[128,512]{0,1:T(8,128)S(1)} %bitcast.170), channel_id=1, source_target_pairs={{0,2},{2,0},{1,3},{3,1},{4,6},{6,4},{5,7},{7,5},{8,10},{10,8},{9,1... | collective-permute-start | bytes 786440 | tf_op jit(solution)/shard_map/ppermute | solution.py:21
  187.1 5.1 %collective-permute-start.12 = (f32[128,512]{0,1:T(8,128)S(1)}, f32[128,512]{0,1:T(8,128)S(1)}, u32[]{:S(2)}, u32[]{:S(2)}) collective-permute-start(f32[128,512]{0,1:T(8,128)S(1)} %bitcast.171), channel_id=1, source_target_pairs={{0,4},{4,0},{1,5},{5,1},{2,6},{6,2},{3,7},{7,3},{8,12},{12,8},{9,1... | collective-permute-start | bytes 786440 | tf_op jit(solution)/shard_map/ppermute | solution.py:21
  192.3 5.5 %collective-permute-start.13 = (f32[128,512]{0,1:T(8,128)S(1)}, f32[128,512]{0,1:T(8,128)S(1)}, u32[]{:S(2)}, u32[]{:S(2)}) collective-permute-start(f32[128,512]{0,1:T(8,128)S(1)} %bitcast.172), channel_id=1, source_target_pairs={{0,8},{8,0},{1,9},{9,1},{2,10},{10,2},{3,11},{11,3},{4,12},{12,4},... | collective-permute-start | bytes 786440 | tf_op jit(solution)/shard_map/ppermute | solution.py:21
  198.0 4.1 %collective-permute-done.12 = f32[128,512]{0,1:T(8,128)S(1)} collective-permute-done((f32[128,512]{0,1:T(8,128)S(1)}, f32[128,512]{0,1:T(8,128)S(1)}, u32[]{:S(2)}, u32[]{:S(2)}) %collective-permute-start.12) | collective-permute-done | bytes 262176 | tf_op jit(solution)/shard_map/ppermute | solution.py:21
  202.2 25.3 %collective-permute-done.13 = f32[128,512]{0,1:T(8,128)S(1)} collective-permute-done((f32[128,512]{0,1:T(8,128)S(1)}, f32[128,512]{0,1:T(8,128)S(1)}, u32[]{:S(2)}, u32[]{:S(2)}) %collective-permute-start.13) | collective-permute-done | bytes 262176 | tf_op jit(solution)/shard_map/ppermute | solution.py:21
  228.4 1.1 convert_reduce_fusion.1
  (89 shorter events, 13.1 us)
Async XLA Ops:
  1.5 10.7 %collective-permute-start.7 = (bf16[1,6,8,512]{3,2,1,0:T(8,128)(2,1)S(1)}, bf16[1,6,8,512]{3,2,1,0:T(8,128)(2,1)S(1)}, u32[]{:S(2)}, u32[]{:S(2)}) collective-permute-start(bf16[1,6,8,512]{3,2,1,0:T(8,128)(2,1)S(1)} %get-tuple-element.21), channel_id=1, source_target_pairs={{0,256},{64,320},{128,384},{192,448},{256,0},{320,64},{384,128},{4... | collective-permute-start | bytes 147464 | tf_op jit(solution)/shard_map/ppermute | solution.py:44
  12.2 6.6 %collective-permute-start.8 = (bf16[2,1,6,8,512]{4,3,2,0,1:T(8,128)(2,1)S(1)}, bf16[2,1,6,8,512]{4,3,2,0,1:T(8,128)(2,1)S(1)}, u32[]{:S(2)}, u32[]{:S(2)}) collective-permute-start(bf16[2,1,6,8,512]{4,3,2,0,1:T(8,128)(2,1)S(1)} %fusion.18), channel_id=1, source_target_pairs={{0,128},{64,192},{128,0},{192,64},{256,384},{320,448},{384,256},{4... | collective-permute-start | bytes 294920 | tf_op jit(solution)/shard_map/ppermute | solution.py:44
  18.8 23.4 %collective-permute-start.9 = (bf16[2,2,1,6,8,512]{5,4,3,1,0,2:T(8,128)(2,1)S(1)}, bf16[2,2,1,6,8,512]{5,4,3,1,0,2:T(8,128)(2,1)S(1)}, u32[]{:S(2)}, u32[]{:S(2)}) collective-permute-start(bf16[2,2,1,6,8,512]{5,4,3,1,0,2:T(8,128)(2,1)S(1)} %maximum_select_fusion.3), channel_id=1, source_target_pairs={{0,64},{64,0},{128,192},{192,128},{256,320},{320,256},{384,448},{4... | collective-permute-start | bytes 589832 | tf_op jit(solution)/shard_map/ppermute | solution.py:44
  24.9 35.7 %collective-permute-start = (bf16[128,512]{1,0:T(8,128)(2,1)}, bf16[128,512]{1,0:T(8,128)(2,1)S(1)}, u32[]{:S(2)}, u32[]{:S(2)}) collective-permute-start(bf16[128,512]{1,0:T(8,128)(2,1)} %param.4), channel_id=1, source_target_pairs={{0,1},{1,0},{2,3},{3,2},{4,5},{5,4},{6,7},{7,6},{8,9},{9,8},{10,11... | collective-permute-start | bytes 393224 | tf_op jit(solution)/shard_map/ppermute | solution.py:21
  27.6 33.1 %collective-permute-start.1 = (bf16[128,512]{1,0:T(8,128)(2,1)}, bf16[128,512]{1,0:T(8,128)(2,1)}, u32[]{:S(2)}, u32[]{:S(2)}) collective-permute-start(bf16[128,512]{1,0:T(8,128)(2,1)} %param.4), channel_id=1, source_target_pairs={{0,2},{2,0},{1,3},{3,1},{4,6},{6,4},{5,7},{7,5},{8,10},{10,8},{9,1... | collective-permute-start | bytes 393224 | tf_op jit(solution)/shard_map/ppermute | solution.py:21
  30.0 31.8 %collective-permute-start.2 = (bf16[128,512]{1,0:T(8,128)(2,1)}, bf16[128,512]{1,0:T(8,128)(2,1)S(1)}, u32[]{:S(2)}, u32[]{:S(2)}) collective-permute-start(bf16[128,512]{1,0:T(8,128)(2,1)} %param.4), channel_id=1, source_target_pairs={{0,4},{4,0},{1,5},{5,1},{2,6},{6,2},{3,7},{7,3},{8,12},{12,8},{9,1... | collective-permute-start | bytes 393224 | tf_op jit(solution)/shard_map/ppermute | solution.py:21
  32.6 29.3 %collective-permute-start.3 = (bf16[128,512]{1,0:T(8,128)(2,1)}, bf16[128,512]{1,0:T(8,128)(2,1)S(1)}, u32[]{:S(2)}, u32[]{:S(2)}) collective-permute-start(bf16[128,512]{1,0:T(8,128)(2,1)} %param.4), channel_id=1, source_target_pairs={{0,8},{8,0},{1,9},{9,1},{2,10},{10,2},{3,11},{11,3},{4,12},{12,4},... | collective-permute-start | bytes 393224 | tf_op jit(solution)/shard_map/ppermute | solution.py:21
  42.2 16.5 %collective-permute-start.4 = (bf16[1,6,8,512]{3,2,1,0:T(8,128)(2,1)S(1)}, bf16[1,6,8,512]{3,2,1,0:T(8,128)(2,1)S(1)}, u32[]{:S(2)}, u32[]{:S(2)}) collective-permute-start(bf16[1,6,8,512]{3,2,1,0:T(8,128)(2,1)S(1)} %get-tuple-element.22), channel_id=1, source_target_pairs={{0,256},{64,320},{128,384},{192,448},{256,0},{320,64},{384,128},{4... | collective-permute-start | bytes 147464 | tf_op jit(solution)/shard_map/ppermute | solution.py:44
  45.9 4.8 %copy-start.8 = (bf16[128,512]{1,0:T(8,128)(2,1)S(1)}, bf16[128,512]{1,0:T(8,128)(2,1)}, u32[]{:S(2)}) copy-start(bf16[128,512]{1,0:T(8,128)(2,1)} %param.4) | copy-start | bytes 393220
  45.9 25.8 %all-to-all-start.1 = ((bf16[4,8,6,8,512]{4,3,1,2,0:T(8,128)(2,1)}), bf16[4,8,6,8,512]{4,3,1,2,0:T(8,128)(2,1)S(1)}, u32[]{:S(2)}, u32[]{:S(2)}) async-start(bf16[4,8,6,8,512]{4,3,1,2,0:T(8,128)(2,1)} %broadcast_in_dim.36), calls=%async_computation.1 | async-start | bytes 3145728 | tf_op jit(solution)/shard_map/all_to_all | solution.py:57
  58.6 6.6 %collective-permute-start.5 = (bf16[2,1,6,8,512]{4,3,2,0,1:T(8,128)(2,1)S(1)}, bf16[2,1,6,8,512]{4,3,2,0,1:T(8,128)(2,1)S(1)}, u32[]{:S(2)}, u32[]{:S(2)}) collective-permute-start(bf16[2,1,6,8,512]{4,3,2,0,1:T(8,128)(2,1)S(1)} %maximum_select_fusion.5), channel_id=1, source_target_pairs={{0,128},{64,192},{128,0},{192,64},{256,384},{320,448},{384,256},{4... | collective-permute-start | bytes 294920 | tf_op jit(solution)/shard_map/ppermute | solution.py:44
  65.2 6.4 %collective-permute-start.6 = (bf16[2,2,1,6,8,512]{5,4,3,1,2,0:T(8,128)(2,1)S(1)}, bf16[2,2,1,6,8,512]{5,4,3,1,2,0:T(8,128)(2,1)S(1)}, u32[]{:S(2)}, u32[]{:S(2)}) collective-permute-start(bf16[2,2,1,6,8,512]{5,4,3,1,2,0:T(8,128)(2,1)S(1)} %bitcast_select_fusion), channel_id=1, source_target_pairs={{0,64},{64,0},{128,192},{192,128},{256,320},{320,256},{384,448},{4... | collective-permute-start | bytes 589832 | tf_op jit(solution)/shard_map/ppermute | solution.py:44
  67.2 4.5 %copy-start.2 = (bf16[128,2,6,256]{0,3,2,1:T(8,128)(2,1)}, bf16[128,2,6,256]{0,3,2,1:T(8,128)(2,1)S(1)}, u32[]{:S(2)}) copy-start(bf16[128,2,6,256]{0,3,2,1:T(8,128)(2,1)S(1)} %constant_dynamic-update-slice_fusion.1) | copy-start | bytes 2359300
  73.1 21.1 %all-to-all-start = ((bf16[4,8,6,8,512]{4,3,1,2,0:T(8,128)(2,1)}), bf16[4,8,6,8,512]{4,3,1,2,0:T(8,128)(2,1)S(1)}, u32[]{:S(2)}, u32[]{:S(2)}) async-start(bf16[4,8,6,8,512]{4,3,1,2,0:T(8,128)(2,1)} %broadcast_in_dim.32), calls=%async_computation | async-start | bytes 3145728 | tf_op jit(solution)/shard_map/all_to_all | solution.py:57
  79.0 0.8 copy-start
  84.6 1.0 copy-start.1
  84.7 2.0 copy-start.3
  84.7 2.0 copy-start.9
  84.8 2.0 copy-start.11
  86.0 0.7 copy-start.5
  94.2 20.4 %all-to-all-start.4 = ((bf16[4,8,8,6,512]{4,2,3,1,0:T(8,128)(2,1)}), bf16[4,8,8,6,512]{4,2,3,1,0:T(8,128)(2,1)}, u32[]{:S(2)}, u32[]{:S(2)}) async-start(bf16[4,8,8,6,512]{4,2,3,1,0:T(8,128)(2,1)} %multiply_convert_fusion), calls=%async_computation.4 | async-start | bytes 3145728 | tf_op jit(solution)/shard_map/all_to_all | solution.py:62
  105.6 1.2 copy-start.4
  105.6 1.1 copy-start.10
  105.6 1.1 copy-start.12
  106.1 0.7 copy-start.6
  114.6 19.2 %all-to-all-start.2 = ((bf16[4,8,8,6,512]{4,2,3,1,0:T(8,128)(2,1)}), bf16[4,8,8,6,512]{4,2,3,1,0:T(8,128)(2,1)}, u32[]{:S(2)}, u32[]{:S(2)}) async-start(bf16[4,8,8,6,512]{4,2,3,1,0:T(8,128)(2,1)} %multiply_convert_fusion.1), calls=%async_computation.2 | async-start | bytes 3145728 | tf_op jit(solution)/shard_map/all_to_all | solution.py:62
  133.8 33.6 %all-to-all-start.5 = ((bf16[8,8,6,512]{3,1,2,0:T(8,128)(2,1)}), bf16[8,8,6,512]{3,1,2,0:T(8,128)(2,1)S(1)}, u32[]{:S(2)}, u32[]{:S(2)}) async-start(bf16[8,8,6,512]{3,1,2,0:T(8,128)(2,1)} %reduce_sum.44), calls=%async_computation.5 | async-start | bytes 786432 | tf_op jit(solution)/shard_map/all_to_all | solution.py:64
  167.5 60.9 %all-to-all-start.3 = ((bf16[8,8,6,512]{3,1,2,0:T(8,128)(2,1)}), bf16[8,8,6,512]{3,1,2,0:T(8,128)(2,1)}, u32[]{:S(2)}, u32[]{:S(2)}) async-start(bf16[8,8,6,512]{3,1,2,0:T(8,128)(2,1)} %reduce_sum.42), calls=%async_computation.3 | async-start | bytes 786432 | tf_op jit(solution)/shard_map/all_to_all | solution.py:64
  177.6 1.7 copy-start.7
  177.6 1.7 copy-start.13
  180.3 17.7 %collective-permute-start.10 = (f32[128,512]{0,1:T(8,128)S(1)}, f32[128,512]{0,1:T(8,128)S(1)}, u32[]{:S(2)}, u32[]{:S(2)}) collective-permute-start(f32[128,512]{0,1:T(8,128)S(1)} %bitcast.169), channel_id=1, source_target_pairs={{0,1},{1,0},{2,3},{3,2},{4,5},{5,4},{6,7},{7,6},{8,9},{9,8},{10,11... | collective-permute-start | bytes 786440 | tf_op jit(solution)/shard_map/ppermute | solution.py:21
  184.3 13.7 %collective-permute-start.11 = (f32[128,512]{0,1:T(8,128)S(1)}, f32[128,512]{0,1:T(8,128)S(1)}, u32[]{:S(2)}, u32[]{:S(2)}) collective-permute-start(f32[128,512]{0,1:T(8,128)S(1)} %bitcast.170), channel_id=1, source_target_pairs={{0,2},{2,0},{1,3},{3,1},{4,6},{6,4},{5,7},{7,5},{8,10},{10,8},{9,1... | collective-permute-start | bytes 786440 | tf_op jit(solution)/shard_map/ppermute | solution.py:21
  187.1 15.1 %collective-permute-start.12 = (f32[128,512]{0,1:T(8,128)S(1)}, f32[128,512]{0,1:T(8,128)S(1)}, u32[]{:S(2)}, u32[]{:S(2)}) collective-permute-start(f32[128,512]{0,1:T(8,128)S(1)} %bitcast.171), channel_id=1, source_target_pairs={{0,4},{4,0},{1,5},{5,1},{2,6},{6,2},{3,7},{7,3},{8,12},{12,8},{9,1... | collective-permute-start | bytes 786440 | tf_op jit(solution)/shard_map/ppermute | solution.py:21
  192.3 35.1 %collective-permute-start.13 = (f32[128,512]{0,1:T(8,128)S(1)}, f32[128,512]{0,1:T(8,128)S(1)}, u32[]{:S(2)}, u32[]{:S(2)}) collective-permute-start(f32[128,512]{0,1:T(8,128)S(1)} %bitcast.172), channel_id=1, source_target_pairs={{0,8},{8,0},{1,9},{9,1},{2,10},{10,2},{3,11},{11,3},{4,12},{12,4},... | collective-permute-start | bytes 786440 | tf_op jit(solution)/shard_map/ppermute | solution.py:21

commit v8 on v7

--- a/solution.py
+++ b/solution.py
@@ -66,6 +66,32 @@
     return part.transpose(1, 0, 2)
 
 
+def chunk_math(reads, weights, hidden_grad, keep_cols, group):
+    row_count = reads.shape[0]
+    factor_count, _, group_width = weights.shape
+    zl = lax.axis_size(ROWS)
+    xx = lax.axis_size(COLS)
+    own = BS // (zl * xx)
+    rhs = (weights * keep_cols[:, group].astype(jnp.bfloat16)[:, None, :]).reshape(factor_count * BS, group_width)
+    lhs = reads.reshape(row_count, factor_count * BS)
+    pre_act = jnp.dot(lhs, rhs, preferred_element_type=jnp.float32)
+    squash = jax.nn.sigmoid(pre_act)
+    derivative = squash * (1.0 + pre_act * (1.0 - squash))
+    grad_pre = (hidden_grad[:, group * group_width:(group + 1) * group_width].astype(jnp.float32) * derivative).astype(
+        jnp.bfloat16
+    )
+    contrib = lax.dot_general(grad_pre, rhs, (((1,), (1,)), ((), ())), preferred_element_type=jnp.float32).reshape(
+        row_count, factor_count, BS
+    )
+    cols = reads.reshape(row_count, factor_count, zl, xx, own).transpose(0, 3, 2, 4, 1)
+    product = lax.dot_general(
+        cols.reshape(row_count, BS * factor_count), grad_pre, (((0,), (0,)), ((), ())),
+        preferred_element_type=jnp.float32,
+    ).reshape(xx, zl, own, factor_count, group_width)
+    product = product * keep_cols[:, group].astype(jnp.float32)[None, None, None]
+    return grad_pre, contrib, product.astype(jnp.bfloat16)
+
+
 def layer(tokens, hidden_grad, w_up, pattern):
     row_count, local_width = tokens.shape
     factor_count = w_up.shape[0]
@@ -74,7 +100,6 @@
     group_width = hidden_width // local_blocks
     zl = lax.axis_size(ROWS)
     xx = lax.axis_size(COLS)
-    own = BS // (zl * xx)
     keep_cols = jnp.broadcast_to(pattern[:, :, None], (factor_count, pattern.shape[1], BS)).reshape(
         factor_count, local_blocks, group_width
     )
@@ -93,26 +118,9 @@
     sums = []
     for group in range(local_blocks):
         weights = gather_rows(w_up[:, :, group * group_width:(group + 1) * group_width])
-        rhs = (weights * keep_cols[:, group].astype(jnp.bfloat16)[:, None, :]).reshape(factor_count * BS, group_width)
-        lhs = reads[:, group].reshape(row_count, factor_count * BS)
-        pre_act = jnp.dot(lhs, rhs, preferred_element_type=jnp.float32)
-        squash = jax.nn.sigmoid(pre_act)
-        derivative = squash * (1.0 + pre_act * (1.0 - squash))
-        grad_pre = (hidden_grad[:, group * group_width:(group + 1) * group_width].astype(jnp.float32) * derivative).astype(
-            jnp.bfloat16
-        )
-        contribs.append(
-            lax.dot_general(grad_pre, rhs, (((1,), (1,)), ((), ())), preferred_element_type=jnp.float32).reshape(
-                row_count, factor_count, BS
-            )
-        )
-        cols = reads[:, group].reshape(row_count, factor_count, zl, xx, own).transpose(0, 3, 2, 4, 1)
-        product = lax.dot_general(
-            cols.reshape(row_count, BS * factor_count), grad_pre, (((0,), (0,)), ((), ())),
-            preferred_element_type=jnp.float32,
-        ).reshape(xx, zl, own, factor_count, group_width)
-        product = product * keep_cols[:, group].astype(jnp.float32)[None, None, None]
-        sums.append(scatter_rows(product.astype(jnp.bfloat16)))
+        _, contrib, product = chunk_math(reads[:, group], weights, hidden_grad, keep_cols, group)
+        contribs.append(contrib)
+        sums.append(product)
     contrib_all = jnp.stack(contribs, axis=1)
     input_total = jnp.zeros((row_count, local_blocks, BS), jnp.float32)
     for factor in range(factor_count):
@@ -125,7 +133,7 @@
             returned = partner_2(contrib.reshape(row_count, local_width), "fly", bit_number)
             input_total = input_total + returned.reshape(row_count, local_blocks, BS)
     input_grad = input_total.reshape(row_count, local_width).astype(jnp.bfloat16)
-    weight_grad = jnp.concatenate(sums, axis=2) * (1.0 / (zl * xx))
+    weight_grad = scatter_rows(jnp.concatenate(sums, axis=4)) * (1.0 / (zl * xx))
     return (input_grad, weight_grad)
 
 

time: 232 us -> 223 us (0.961)
  the two profiles are of different devices: /device:TPU:217 before, /device:TPU:24 now
where the time goes in v8:
time: 223 us; the launch traced here: 220 us
  starting transfers between devices  73.9 us (33%)
  waiting for transfers between devices  68.5 us (31%)
  blocking collectives  39.4 us (18%)
  local copies, waits for them, and re-layouts  25.3 us (11%)
  other arithmetic  7.17 us (3%)
  matrix products  4.08 us (2%)
    all_to_all x1, blocking collectives, scatter_rows(): got = lax.all_to_all(terms, COLS, 0, 0, tiled=True)  39.4 us
    ppermute x8, starting transfers between devices, partner_2(): return lax.ppermute(block, axis, route)  36.7 us
    all_to_all x1, waiting for transfers between devices, scatter_rows(): got = lax.all_to_all(part.astype(jnp.bfloat16), ROWS, 0, 0, tiled=True)  31.1 us
    ppermute x6, waiting for transfers between devices, gather_line(): got = lax.ppermute(held, axis, [(i, i ^ dist) for i in range(count)])  25.9 us
    ppermute x6, starting transfers between devices, gather_line(): got = lax.ppermute(held, axis, [(i, i ^ dist) for i in range(count)])  24.3 us
    all_to_all x2, starting transfers between devices, gather_rows(): both = lax.all_to_all(copies, COLS, 0, 0, tiled=True)  8.72 us
    ppermute x8, waiting for transfers between devices, partner_2(): return lax.ppermute(block, axis, route)  8.24 us
    unnamed x35, local copies, waits for them, and re-layouts  6.69 us
  transfers between devices with their start and end apart: 17, of which 8 were waited for; matrix products, arithmetic and copies ran while one was open for 11% of the time, Pallas kernels for 0%

profile of v8, /device:TPU:24, one launch (start us, length us, event | category | flops | bytes accessed | tf_op | source)
XLA Modules:
  0.0 219.6 jit_solution(8636829641405061823)
XLA Ops:
  0.6 0.8 slice_bitcast_fusion.2
  1.5 9.1 %collective-permute-start.4 = (bf16[1,6,8,512]{3,2,1,0:T(8,128)(2,1)S(1)}, bf16[1,6,8,512]{3,2,1,0:T(8,128)(2,1)S(1)}, u32[]{:S(2)}, u32[]{:S(2)}) collective-permute-start(bf16[1,6,8,512]{3,2,1,0:T(8,128)(2,1)S(1)} %get-tuple-element.22), channel_id=1, source_target_pairs={{0,256},{64,320},{128,384},{192,448},{256,0},{320,64},{384,128},{4... | collective-permute-start | bytes 147464 | tf_op jit(solution)/shard_map/ppermute | solution.py:44
  10.6 2.1 collective-permute-done.4
  12.7 5.3 %collective-permute-start.5 = (bf16[2,1,6,8,512]{4,3,2,0,1:T(8,128)(2,1)S(1)}, bf16[2,1,6,8,512]{4,3,2,0,1:T(8,128)(2,1)S(1)}, u32[]{:S(2)}, u32[]{:S(2)}) collective-permute-start(bf16[2,1,6,8,512]{4,3,2,0,1:T(8,128)(2,1)S(1)} %maximum_select_fusion.5), channel_id=1, source_target_pairs={{0,128},{64,192},{128,0},{192,64},{256,384},{320,448},{384,256},{4... | collective-permute-start | bytes 294920 | tf_op jit(solution)/shard_map/ppermute | solution.py:44
  18.0 5.0 %collective-permute-done.5 = bf16[2,1,6,8,512]{4,3,2,0,1:T(8,128)(2,1)S(1)} collective-permute-done((bf16[2,1,6,8,512]{4,3,2,0,1:T(8,128)(2,1)S(1)}, bf16[2,1,6,8,512]{4,3,2,0,1:T(8,128)(2,1)S(1)}, u32[]{:S(2)}, u32[]{:S(2)}) %collective-permute-start.5) | collective-permute-done | bytes 98336 | tf_op jit(solution)/shard_map/ppermute | solution.py:44
  23.0 2.6 %collective-permute-start.6 = (bf16[2,2,1,6,8,512]{5,4,3,1,2,0:T(8,128)(2,1)S(1)}, bf16[2,2,1,6,8,512]{5,4,3,1,2,0:T(8,128)(2,1)S(1)}, u32[]{:S(2)}, u32[]{:S(2)}) collective-permute-start(bf16[2,2,1,6,8,512]{5,4,3,1,2,0:T(8,128)(2,1)S(1)} %bitcast_select_fusion), channel_id=1, source_target_pairs={{0,64},{64,0},{128,192},{192,128},{256,320},{320,256},{384,448},{4... | collective-permute-start | bytes 589832 | tf_op jit(solution)/shard_map/ppermute | solution.py:44
  25.7 1.9 collective-permute-start
  27.6 2.7 %collective-permute-start.1 = (bf16[128,512]{1,0:T(8,128)(2,1)}, bf16[128,512]{1,0:T(8,128)(2,1)S(1)}, u32[]{:S(2)}, u32[]{:S(2)}) collective-permute-start(bf16[128,512]{1,0:T(8,128)(2,1)} %param.4), channel_id=1, source_target_pairs={{0,2},{2,0},{1,3},{3,1},{4,6},{6,4},{5,7},{7,5},{8,10},{10,8},{9,1... | collective-permute-start | bytes 393224 | tf_op jit(solution)/shard_map/ppermute | solution.py:21
  30.3 3.8 %collective-permute-start.2 = (bf16[128,512]{1,0:T(8,128)(2,1)}, bf16[128,512]{1,0:T(8,128)(2,1)S(1)}, u32[]{:S(2)}, u32[]{:S(2)}) collective-permute-start(bf16[128,512]{1,0:T(8,128)(2,1)} %param.4), channel_id=1, source_target_pairs={{0,4},{4,0},{1,5},{5,1},{2,6},{6,2},{3,7},{7,3},{8,12},{12,8},{9,1... | collective-permute-start | bytes 393224 | tf_op jit(solution)/shard_map/ppermute | solution.py:21
  34.0 13.0 %collective-permute-start.3 = (bf16[128,512]{1,0:T(8,128)(2,1)}, bf16[128,512]{1,0:T(8,128)(2,1)S(1)}, u32[]{:S(2)}, u32[]{:S(2)}) collective-permute-start(bf16[128,512]{1,0:T(8,128)(2,1)} %param.4), channel_id=1, source_target_pairs={{0,8},{8,0},{1,9},{9,1},{2,10},{10,2},{3,11},{11,3},{4,12},{12,4},... | collective-permute-start | bytes 393224 | tf_op jit(solution)/shard_map/ppermute | solution.py:21
  47.0 0.8 copy.112
  47.9 3.4 %collective-permute-start.7 = (bf16[1,6,8,512]{3,2,1,0:T(8,128)(2,1)S(1)}, bf16[1,6,8,512]{3,2,1,0:T(8,128)(2,1)S(1)}, u32[]{:S(2)}, u32[]{:S(2)}) collective-permute-start(bf16[1,6,8,512]{3,2,1,0:T(8,128)(2,1)S(1)} %get-tuple-element.21), channel_id=1, source_target_pairs={{0,256},{64,320},{128,384},{192,448},{256,0},{320,64},{384,128},{4... | collective-permute-start | bytes 147464 | tf_op jit(solution)/shard_map/ppermute | solution.py:44
  51.4 1.4 broadcast_in_dim.32
  52.8 4.4 %all-to-all-start = ((bf16[4,8,6,8,512]{4,3,1,2,0:T(8,128)(2,1)}), bf16[4,8,6,8,512]{4,3,1,2,0:T(8,128)(2,1)S(1)}, u32[]{:S(2)}, u32[]{:S(2)}) async-start(bf16[4,8,6,8,512]{4,3,1,2,0:T(8,128)(2,1)} %broadcast_in_dim.32), calls=%async_computation | async-start | bytes 3145728 | tf_op jit(solution)/shard_map/all_to_all | solution.py:57
  58.1 6.0 %collective-permute-done.7 = bf16[1,6,8,512]{3,2,1,0:T(8,128)(2,1)S(1)} collective-permute-done((bf16[1,6,8,512]{3,2,1,0:T(8,128)(2,1)S(1)}, bf16[1,6,8,512]{3,2,1,0:T(8,128)(2,1)S(1)}, u32[]{:S(2)}, u32[]{:S(2)}) %collective-permute-start.7) | collective-permute-done | bytes 49184 | tf_op jit(solution)/shard_map/ppermute | solution.py:44
  64.1 1.9 collective-permute-start.8
  66.6 6.1 %collective-permute-done.8 = bf16[2,1,6,8,512]{4,3,2,0,1:T(8,128)(2,1)S(1)} collective-permute-done((bf16[2,1,6,8,512]{4,3,2,0,1:T(8,128)(2,1)S(1)}, bf16[2,1,6,8,512]{4,3,2,0,1:T(8,128)(2,1)S(1)}, u32[]{:S(2)}, u32[]{:S(2)}) %collective-permute-start.8) | collective-permute-done | bytes 98336 | tf_op jit(solution)/shard_map/ppermute | solution.py:44
  72.7 1.9 collective-permute-start.9
  74.7 6.7 %collective-permute-done.9 = bf16[2,2,1,6,8,512]{5,4,3,1,0,2:T(8,128)(2,1)S(1)} collective-permute-done((bf16[2,2,1,6,8,512]{5,4,3,1,0,2:T(8,128)(2,1)S(1)}, bf16[2,2,1,6,8,512]{5,4,3,1,0,2:T(8,128)(2,1)S(1)}, u32[]{:S(2)}, u32[]{:S(2)}) %collective-permute-start.9) | collective-permute-done | bytes 196640 | tf_op jit(solution)/shard_map/ppermute | solution.py:44
  81.6 1.4 broadcast_in_dim.36
  82.9 4.3 %all-to-all-start.1 = ((bf16[4,8,6,8,512]{4,3,1,2,0:T(8,128)(2,1)}), bf16[4,8,6,8,512]{4,3,1,2,0:T(8,128)(2,1)S(1)}, u32[]{:S(2)}, u32[]{:S(2)}) async-start(bf16[4,8,6,8,512]{4,3,1,2,0:T(8,128)(2,1)} %broadcast_in_dim.36), calls=%async_computation.1 | async-start | bytes 3145728 | tf_op jit(solution)/shard_map/all_to_all | solution.py:57
  87.9 0.7 constant_dynamic-update-slice_fusion.1
  88.5 0.7 constant_dynamic-update-slice_fusion
  89.2 1.9 fusion.23
  91.1 1.1 copy.125
  92.2 1.9 reshape.929
  94.1 1.9 dot_general.40
  96.0 2.1 copy.123
  98.1 1.9 reshape.928
  100.0 1.9 dot_general.37
  102.0 0.9 copy-done
  102.9 1.1 fusion.24
  104.0 3.2 %all-to-all-done.1 = bf16[4,8,6,8,512]{4,3,1,2,0:T(8,128)(2,1)S(1)} async-done(((bf16[4,8,6,8,512]{4,3,1,2,0:T(8,128)(2,1)}), bf16[4,8,6,8,512]{4,3,1,2,0:T(8,128)(2,1)S(1)}, u32[]{:S(2)}, u32[]{:S(2)}) %all-to-all-start.1) | async-done | bytes 1572896 | tf_op jit(solution)/shard_map/all_to_all | solution.py:57
  109.2 0.7 multiply_convert_fusion.1
  110.3 39.4 %all_to_all.20 = bf16[4,8,8,6,1024]{4,2,3,1,0:T(8,128)(2,1)} all-to-all(bf16[4,8,8,6,1024]{4,2,3,1,0:T(8,128)(2,1)S(1)} %pad_maximum_fusion), channel_id=1, replica_groups=mesh['zl'=8,'xx'=4,'fly'=16] {'xx'}, dimensions={0} | all-to-all | bytes 6291456 | tf_op jit(solution)/shard_map/all_to_all | solution.py:62
  149.7 3.6 %reduce_sum.21 = bf16[8,8,6,1024]{3,1,2,0:T(8,128)(2,1)} reduce(bf16[4,8,8,6,1024]{4,2,3,1,0:T(8,128)(2,1)} %all_to_all.20, bf16[]{:T(256)} %constant.19.clone.1), dimensions={0}, to_apply=%region_0.1 | reduce | flops 1179648 | bytes 3932162 | tf_op jit(solution)/shard_map/reduce_sum | solution.py:63
  153.3 4.2 %all-to-all-start.3 = ((bf16[8,8,6,1024]{3,1,2,0:T(8,128)(2,1)}), bf16[8,8,6,1024]{3,1,2,0:T(8,128)(2,1)}, u32[]{:S(2)}, u32[]{:S(2)}) async-start(bf16[8,8,6,1024]{3,1,2,0:T(8,128)(2,1)} %reduce_sum.21), calls=%async_computation.3 | async-start | bytes 1572864 | tf_op jit(solution)/shard_map/all_to_all | solution.py:64
  158.2 0.7 copy-done.11
  159.8 0.7 copy-done.6
  161.5 5.8 %collective-permute-start.13 = (f32[128,512]{0,1:T(8,128)S(1)}, f32[128,512]{0,1:T(8,128)S(1)}, u32[]{:S(2)}, u32[]{:S(2)}) collective-permute-start(f32[128,512]{0,1:T(8,128)S(1)} %bitcast.165), channel_id=1, source_target_pairs={{0,8},{8,0},{1,9},{9,1},{2,10},{10,2},{3,11},{11,3},{4,12},{12,4},... | collective-permute-start | bytes 786440 | tf_op jit(solution)/shard_map/ppermute | solution.py:21
  167.4 4.5 %collective-permute-start.12 = (f32[128,512]{0,1:T(8,128)S(1)}, f32[128,512]{0,1:T(8,128)S(1)}, u32[]{:S(2)}, u32[]{:S(2)}) collective-permute-start(f32[128,512]{0,1:T(8,128)S(1)} %bitcast.166), channel_id=1, source_target_pairs={{0,4},{4,0},{1,5},{5,1},{2,6},{6,2},{3,7},{7,3},{8,12},{12,8},{9,1... | collective-permute-start | bytes 786440 | tf_op jit(solution)/shard_map/ppermute | solution.py:21
  172.1 3.2 %collective-permute-start.11 = (f32[128,512]{0,1:T(8,128)S(1)}, f32[128,512]{0,1:T(8,128)S(1)}, u32[]{:S(2)}, u32[]{:S(2)}) collective-permute-start(f32[128,512]{0,1:T(8,128)S(1)} %bitcast.167), channel_id=1, source_target_pairs={{0,2},{2,0},{1,3},{3,1},{4,6},{6,4},{5,7},{7,5},{8,10},{10,8},{9,1... | collective-permute-start | bytes 786440 | tf_op jit(solution)/shard_map/ppermute | solution.py:21
  175.4 1.9 collective-permute-start.10
  177.5 8.2 %collective-permute-done.13 = f32[128,512]{0,1:T(8,128)S(1)} collective-permute-done((f32[128,512]{0,1:T(8,128)S(1)}, f32[128,512]{0,1:T(8,128)S(1)}, u32[]{:S(2)}, u32[]{:S(2)}) %collective-permute-start.13) | collective-permute-done | bytes 262176 | tf_op jit(solution)/shard_map/ppermute | solution.py:21
  185.8 0.8 copy.127
  186.5 31.1 %all-to-all-done.3 = bf16[8,8,6,1024]{3,1,2,0:T(8,128)(2,1)} async-done(((bf16[8,8,6,1024]{3,1,2,0:T(8,128)(2,1)}), bf16[8,8,6,1024]{3,1,2,0:T(8,128)(2,1)}, u32[]{:S(2)}, u32[]{:S(2)}) %all-to-all-start.3) | async-done | bytes 786464 | tf_op jit(solution)/shard_map/all_to_all | solution.py:64
  217.6 1.3 convert_reduce_fusion
  218.9 0.7 multiply_bitcast_fusion
  (78 shorter events, 7.8 us)
Async XLA Ops:
  1.5 11.2 %collective-permute-start.4 = (bf16[1,6,8,512]{3,2,1,0:T(8,128)(2,1)S(1)}, bf16[1,6,8,512]{3,2,1,0:T(8,128)(2,1)S(1)}, u32[]{:S(2)}, u32[]{:S(2)}) collective-permute-start(bf16[1,6,8,512]{3,2,1,0:T(8,128)(2,1)S(1)} %get-tuple-element.22), channel_id=1, source_target_pairs={{0,256},{64,320},{128,384},{192,448},{256,0},{320,64},{384,128},{4... | collective-permute-start | bytes 147464 | tf_op jit(solution)/shard_map/ppermute | solution.py:44
  12.7 10.4 %collective-permute-start.5 = (bf16[2,1,6,8,512]{4,3,2,0,1:T(8,128)(2,1)S(1)}, bf16[2,1,6,8,512]{4,3,2,0,1:T(8,128)(2,1)S(1)}, u32[]{:S(2)}, u32[]{:S(2)}) collective-permute-start(bf16[2,1,6,8,512]{4,3,2,0,1:T(8,128)(2,1)S(1)} %maximum_select_fusion.5), channel_id=1, source_target_pairs={{0,128},{64,192},{128,0},{192,64},{256,384},{320,448},{384,256},{4... | collective-permute-start | bytes 294920 | tf_op jit(solution)/shard_map/ppermute | solution.py:44
  23.0 24.9 %collective-permute-start.6 = (bf16[2,2,1,6,8,512]{5,4,3,1,2,0:T(8,128)(2,1)S(1)}, bf16[2,2,1,6,8,512]{5,4,3,1,2,0:T(8,128)(2,1)S(1)}, u32[]{:S(2)}, u32[]{:S(2)}) collective-permute-start(bf16[2,2,1,6,8,512]{5,4,3,1,2,0:T(8,128)(2,1)S(1)} %bitcast_select_fusion), channel_id=1, source_target_pairs={{0,64},{64,0},{128,192},{192,128},{256,320},{320,256},{384,448},{4... | collective-permute-start | bytes 589832 | tf_op jit(solution)/shard_map/ppermute | solution.py:44
  25.7 40.4 %collective-permute-start = (bf16[128,512]{1,0:T(8,128)(2,1)}, bf16[128,512]{1,0:T(8,128)(2,1)S(1)}, u32[]{:S(2)}, u32[]{:S(2)}) collective-permute-start(bf16[128,512]{1,0:T(8,128)(2,1)} %param.4), channel_id=1, source_target_pairs={{0,1},{1,0},{2,3},{3,2},{4,5},{5,4},{6,7},{7,6},{8,9},{9,8},{10,11... | collective-permute-start | bytes 393224 | tf_op jit(solution)/shard_map/ppermute | solution.py:21
  27.6 38.6 %collective-permute-start.1 = (bf16[128,512]{1,0:T(8,128)(2,1)}, bf16[128,512]{1,0:T(8,128)(2,1)S(1)}, u32[]{:S(2)}, u32[]{:S(2)}) collective-permute-start(bf16[128,512]{1,0:T(8,128)(2,1)} %param.4), channel_id=1, source_target_pairs={{0,2},{2,0},{1,3},{3,1},{4,6},{6,4},{5,7},{7,5},{8,10},{10,8},{9,1... | collective-permute-start | bytes 393224 | tf_op jit(solution)/shard_map/ppermute | solution.py:21
  30.3 36.1 %collective-permute-start.2 = (bf16[128,512]{1,0:T(8,128)(2,1)}, bf16[128,512]{1,0:T(8,128)(2,1)S(1)}, u32[]{:S(2)}, u32[]{:S(2)}) collective-permute-start(bf16[128,512]{1,0:T(8,128)(2,1)} %param.4), channel_id=1, source_target_pairs={{0,4},{4,0},{1,5},{5,1},{2,6},{6,2},{3,7},{7,3},{8,12},{12,8},{9,1... | collective-permute-start | bytes 393224 | tf_op jit(solution)/shard_map/ppermute | solution.py:21
  34.0 32.4 %collective-permute-start.3 = (bf16[128,512]{1,0:T(8,128)(2,1)}, bf16[128,512]{1,0:T(8,128)(2,1)S(1)}, u32[]{:S(2)}, u32[]{:S(2)}) collective-permute-start(bf16[128,512]{1,0:T(8,128)(2,1)} %param.4), channel_id=1, source_target_pairs={{0,8},{8,0},{1,9},{9,1},{2,10},{10,2},{3,11},{11,3},{4,12},{12,4},... | collective-permute-start | bytes 393224 | tf_op jit(solution)/shard_map/ppermute | solution.py:21
  47.9 16.1 %collective-permute-start.7 = (bf16[1,6,8,512]{3,2,1,0:T(8,128)(2,1)S(1)}, bf16[1,6,8,512]{3,2,1,0:T(8,128)(2,1)S(1)}, u32[]{:S(2)}, u32[]{:S(2)}) collective-permute-start(bf16[1,6,8,512]{3,2,1,0:T(8,128)(2,1)S(1)} %get-tuple-element.21), channel_id=1, source_target_pairs={{0,256},{64,320},{128,384},{192,448},{256,0},{320,64},{384,128},{4... | collective-permute-start | bytes 147464 | tf_op jit(solution)/shard_map/ppermute | solution.py:44
  52.8 4.5 %copy-start.7 = (bf16[128,512]{1,0:T(8,128)(2,1)S(1)}, bf16[128,512]{1,0:T(8,128)(2,1)}, u32[]{:S(2)}) copy-start(bf16[128,512]{1,0:T(8,128)(2,1)} %param.4) | copy-start | bytes 393220
  52.8 28.8 %all-to-all-start = ((bf16[4,8,6,8,512]{4,3,1,2,0:T(8,128)(2,1)}), bf16[4,8,6,8,512]{4,3,1,2,0:T(8,128)(2,1)S(1)}, u32[]{:S(2)}, u32[]{:S(2)}) async-start(bf16[4,8,6,8,512]{4,3,1,2,0:T(8,128)(2,1)} %broadcast_in_dim.32), calls=%async_computation | async-start | bytes 3145728 | tf_op jit(solution)/shard_map/all_to_all | solution.py:57
  64.1 8.6 %collective-permute-start.8 = (bf16[2,1,6,8,512]{4,3,2,0,1:T(8,128)(2,1)S(1)}, bf16[2,1,6,8,512]{4,3,2,0,1:T(8,128)(2,1)S(1)}, u32[]{:S(2)}, u32[]{:S(2)}) collective-permute-start(bf16[2,1,6,8,512]{4,3,2,0,1:T(8,128)(2,1)S(1)} %fusion.18), channel_id=1, source_target_pairs={{0,128},{64,192},{128,0},{192,64},{256,384},{320,448},{384,256},{4... | collective-permute-start | bytes 294920 | tf_op jit(solution)/shard_map/ppermute | solution.py:44
  72.7 8.7 %collective-permute-start.9 = (bf16[2,2,1,6,8,512]{5,4,3,1,0,2:T(8,128)(2,1)S(1)}, bf16[2,2,1,6,8,512]{5,4,3,1,0,2:T(8,128)(2,1)S(1)}, u32[]{:S(2)}, u32[]{:S(2)}) collective-permute-start(bf16[2,2,1,6,8,512]{5,4,3,1,0,2:T(8,128)(2,1)S(1)} %maximum_select_fusion.3), channel_id=1, source_target_pairs={{0,64},{64,0},{128,192},{192,128},{256,320},{320,256},{384,448},{4... | collective-permute-start | bytes 589832 | tf_op jit(solution)/shard_map/ppermute | solution.py:44
  74.7 6.9 %copy-start.1 = (bf16[128,2,6,256]{0,3,2,1:T(8,128)(2,1)}, bf16[128,2,6,256]{0,3,2,1:T(8,128)(2,1)S(1)}, u32[]{:S(2)}) copy-start(bf16[128,2,6,256]{0,3,2,1:T(8,128)(2,1)S(1)} %constant_dynamic-update-slice_fusion.3) | copy-start | bytes 2359300
  82.9 24.3 %all-to-all-start.1 = ((bf16[4,8,6,8,512]{4,3,1,2,0:T(8,128)(2,1)}), bf16[4,8,6,8,512]{4,3,1,2,0:T(8,128)(2,1)S(1)}, u32[]{:S(2)}, u32[]{:S(2)}) async-start(bf16[4,8,6,8,512]{4,3,1,2,0:T(8,128)(2,1)} %broadcast_in_dim.36), calls=%async_computation.1 | async-start | bytes 3145728 | tf_op jit(solution)/shard_map/all_to_all | solution.py:57
  101.9 1.0 copy-start
  107.4 1.0 copy-start.2
  107.4 1.0 copy-start.9
  107.4 1.1 copy-start.10
  107.8 1.3 copy-start.5
  107.8 1.3 copy-start.3
  107.8 1.3 copy-start.4
  107.8 1.3 copy-start.8
  153.3 64.3 %all-to-all-start.3 = ((bf16[8,8,6,1024]{3,1,2,0:T(8,128)(2,1)}), bf16[8,8,6,1024]{3,1,2,0:T(8,128)(2,1)}, u32[]{:S(2)}, u32[]{:S(2)}) async-start(bf16[8,8,6,1024]{3,1,2,0:T(8,128)(2,1)} %reduce_sum.21), calls=%async_computation.3 | async-start | bytes 1572864 | tf_op jit(solution)/shard_map/all_to_all | solution.py:64
  158.0 1.0 copy-start.11
  159.6 1.0 copy-start.6
  161.5 24.2 %collective-permute-start.13 = (f32[128,512]{0,1:T(8,128)S(1)}, f32[128,512]{0,1:T(8,128)S(1)}, u32[]{:S(2)}, u32[]{:S(2)}) collective-permute-start(f32[128,512]{0,1:T(8,128)S(1)} %bitcast.165), channel_id=1, source_target_pairs={{0,8},{8,0},{1,9},{9,1},{2,10},{10,2},{3,11},{11,3},{4,12},{12,4},... | collective-permute-start | bytes 786440 | tf_op jit(solution)/shard_map/ppermute | solution.py:21
  167.4 18.3 %collective-permute-start.12 = (f32[128,512]{0,1:T(8,128)S(1)}, f32[128,512]{0,1:T(8,128)S(1)}, u32[]{:S(2)}, u32[]{:S(2)}) collective-permute-start(f32[128,512]{0,1:T(8,128)S(1)} %bitcast.166), channel_id=1, source_target_pairs={{0,4},{4,0},{1,5},{5,1},{2,6},{6,2},{3,7},{7,3},{8,12},{12,8},{9,1... | collective-permute-start | bytes 786440 | tf_op jit(solution)/shard_map/ppermute | solution.py:21
  172.1 13.6 %collective-permute-start.11 = (f32[128,512]{0,1:T(8,128)S(1)}, f32[128,512]{0,1:T(8,128)S(1)}, u32[]{:S(2)}, u32[]{:S(2)}) collective-permute-start(f32[128,512]{0,1:T(8,128)S(1)} %bitcast.167), channel_id=1, source_target_pairs={{0,2},{2,0},{1,3},{3,1},{4,6},{6,4},{5,7},{7,5},{8,10},{10,8},{9,1... | collective-permute-start | bytes 786440 | tf_op jit(solution)/shard_map/ppermute | solution.py:21
  175.4 10.3 %collective-permute-start.10 = (f32[128,512]{0,1:T(8,128)S(1)}, f32[128,512]{0,1:T(8,128)S(1)}, u32[]{:S(2)}, u32[]{:S(2)}) collective-permute-start(f32[128,512]{0,1:T(8,128)S(1)} %bitcast.168), channel_id=1, source_target_pairs={{0,1},{1,0},{2,3},{3,2},{4,5},{5,4},{6,7},{7,6},{8,9},{9,8},{10,11... | collective-permute-start | bytes 786440 | tf_op jit(solution)/shard_map/ppermute | solution.py:21

commit v9 on v8

--- a/solution.py
+++ b/solution.py
@@ -6,9 +6,11 @@
 
 
 BS = 256
-ROWS = "zl"
+HALF = "zh"
+QUARTER = "zq"
+ROWS = (HALF, QUARTER)
 COLS = "xx"
-DP = (ROWS, COLS)
+DP = (HALF, QUARTER, COLS)
 
 
 def partner_2(block, axis, bit):
@@ -58,10 +60,38 @@
     return both.transpose(2, 1, 0, 3, 4).reshape(factor_count, zl * xx * own, width)
 
 
+def ring_scatter(terms, axis):
+    count = lax.axis_size(axis)
+    assert count == 4
+    place = lax.axis_index(axis)
+    half = terms.shape[-1] // 2
+
+    def chunk(shift):
+        return lax.dynamic_index_in_dim(terms, (place + shift) % count, 0, keepdims=False)
+
+    right = [(i, (i + 1) % count) for i in range(count)]
+    left = [(i, (i - 1) % count) for i in range(count)]
+    opposite = chunk(2).astype(jnp.bfloat16)
+    from_left = lax.ppermute(opposite[..., :half], axis, right).astype(jnp.float32)
+    from_right = lax.ppermute(opposite[..., half:], axis, left).astype(jnp.float32)
+    to_right = chunk(1)
+    to_right = jnp.concatenate([to_right[..., :half] + from_left, to_right[..., half:]], axis=-1)
+    to_left = chunk(3)
+    to_left = jnp.concatenate([to_left[..., :half], to_left[..., half:] + from_right], axis=-1)
+    got_left = lax.ppermute(to_right.astype(jnp.bfloat16), axis, right)
+    got_right = lax.ppermute(to_left.astype(jnp.bfloat16), axis, left)
+    own = chunk(0).astype(jnp.bfloat16).astype(jnp.float32)
+    return own + got_left.astype(jnp.float32) + got_right.astype(jnp.float32)
+
+
 def scatter_rows(terms):
-    got = lax.all_to_all(terms, COLS, 0, 0, tiled=True)
+    _, zl, own, factor_count, width = terms.shape
+    halves = lax.axis_size(HALF)
+    part = ring_scatter(terms, COLS)
+    part = part.reshape(halves, zl // halves, own, factor_count, width)
+    got = lax.all_to_all(part.transpose(1, 0, 2, 3, 4).astype(jnp.bfloat16), QUARTER, 0, 0, tiled=True)
     part = got.astype(jnp.float32).sum(0)
-    got = lax.all_to_all(part.astype(jnp.bfloat16), ROWS, 0, 0, tiled=True)
+    got = lax.all_to_all(part.astype(jnp.bfloat16), HALF, 0, 0, tiled=True)
     part = got.astype(jnp.float32).sum(0)
     return part.transpose(1, 0, 2)
 
@@ -89,7 +119,7 @@
         preferred_element_type=jnp.float32,
     ).reshape(xx, zl, own, factor_count, group_width)
     product = product * keep_cols[:, group].astype(jnp.float32)[None, None, None]
-    return grad_pre, contrib, product.astype(jnp.bfloat16)
+    return grad_pre, contrib, product
 
 
 def layer(tokens, hidden_grad, w_up, pattern):
@@ -141,7 +171,8 @@
     devices = mesh.devices
     xs = sorted({d.coords[0] for d in devices[:, 0]})
     cols = len(xs)
-    return Mesh(devices.reshape(devices.shape[0] // cols, cols, devices.shape[1]), (ROWS, COLS, "fly"))
+    lines = devices.shape[0] // cols
+    return Mesh(devices.reshape(2, lines // 2, cols, devices.shape[1]), (HALF, QUARTER, COLS, "fly"))
 
 
 def solution(mesh):

time: 223 us -> 215 us (0.964)
  blocking collectives: 39.4 us -> 0 us
  starting transfers between devices: 73.9 us -> 96 us
  local copies, waits for them, and re-layouts: 25.3 us -> 31.8 us
  other arithmetic: 7.17 us -> 9.74 us
    all_to_all x1 -> x0, blocking collectives: 39.4 us -> none  [scatter_rows(): got = lax.all_to_all(terms, COLS, 0, 0, tiled=True)]
    ppermute x0 -> x4, waiting for transfers between devices: none -> 21.4 us  [the longest x1 11.5 us: ring_scatter(): got_right = lax.ppermute(to_left.astype(jnp.bfloat16), axis, left)]
    all_to_all x1 -> x2, starting transfers between devices: 4.21 us -> 17.4 us  [the longest x1 13.9 us: scatter_rows(): got = lax.all_to_all(part.astype(jnp.bfloat16), HALF, 0, 0, tiled=True)]
    ppermute x0 -> x4, starting transfers between devices: none -> 12 us  [the longest x1 4.28 us: ring_scatter(): got_right = lax.ppermute(to_left.astype(jnp.bfloat16), axis, left)]
    all_to_all x1 -> x2, waiting for transfers between devices: 31.1 us -> 21.7 us  [the longest x1 13.8 us: scatter_rows(): lax.all_to_all(part.transpose(1, 0, 2, 3, 4).astype(jnp.bfloat16), QUARTE...]
    ppermute x8, waiting for transfers between devices: 8.24 us -> 0.02 us  [partner_2(): return lax.ppermute(block, axis, route)]
    unnamed x35 -> x45, local copies, waits for them, and re-layouts: 6.69 us -> 10.9 us
    reduce_sum x2, other arithmetic: 4.91 us -> 0.86 us  [scatter_rows(): part = got.astype(jnp.float32).sum(0)]
  transfers between devices with their start and end apart: 17 -> 22, of which waited for: 8 -> 11; matrix products, arithmetic and copies ran while one was open for 11% -> 14% of each run, Pallas kernels for 0% -> 0%
where the time goes in v9:
time: 215 us; the launch traced here: 213 us
  starting transfers between devices  96 us (45%)
  waiting for transfers between devices  69.7 us (32%)
  local copies, waits for them, and re-layouts  31.8 us (15%)
  other arithmetic  9.74 us (5%)
  matrix products  4.06 us (2%)
    ppermute x8, starting transfers between devices, partner_2(): return lax.ppermute(block, axis, route)  33.6 us
    ppermute x6, starting transfers between devices, gather_line(): got = lax.ppermute(held, axis, [(i, i ^ dist) for i in range(count)])  24.3 us
    ppermute x6, waiting for transfers between devices, gather_line(): got = lax.ppermute(held, axis, [(i, i ^ dist) for i in range(count)])  23.4 us
    all_to_all x1, starting transfers between devices, scatter_rows(): got = lax.all_to_all(part.astype(jnp.bfloat16), HALF, 0, 0, tiled=True)  13.9 us
    all_to_all x1, waiting for transfers between devices, scatter_rows(): lax.all_to_all(part.transpose(1, 0, 2, 3, 4).astype(jnp.bfloat16), QUARTE...  13.8 us
    ppermute x1, waiting for transfers between devices, ring_scatter(): got_right = lax.ppermute(to_left.astype(jnp.bfloat16), axis, left)  11.5 us
    unnamed x45, local copies, waits for them, and re-layouts  10.9 us
    all_to_all x2, starting transfers between devices, gather_rows(): both = lax.all_to_all(copies, COLS, 0, 0, tiled=True)  8.72 us
  transfers between devices with their start and end apart: 22, of which 11 were waited for; matrix products, arithmetic and copies ran while one was open for 14% of the time, Pallas kernels for 0%

profile of v9, /device:TPU:24, one launch (start us, length us, event | category | flops | bytes accessed | tf_op | source)
XLA Modules:
  0.0 212.7 jit_solution(7431581612948636315)
XLA Ops:
  1.5 9.1 %collective-permute-start.4 = (bf16[1,6,8,512]{3,2,1,0:T(8,128)(2,1)S(1)}, bf16[1,6,8,512]{3,2,1,0:T(8,128)(2,1)S(1)}, u32[]{:S(2)}, u32[]{:S(2)}) collective-permute-start(bf16[1,6,8,512]{3,2,1,0:T(8,128)(2,1)S(1)} %get-tuple-element.26), channel_id=1, source_target_pairs={{0,256},{64,320},{128,384},{192,448},{256,0},{320,64},{384,128},{4... | collective-permute-start | bytes 147464 | tf_op jit(solution)/shard_map/ppermute | solution.py:46
  10.6 2.1 collective-permute-done.4
  12.7 5.3 %collective-permute-start.5 = (bf16[2,1,6,8,512]{4,3,2,0,1:T(8,128)(2,1)S(1)}, bf16[2,1,6,8,512]{4,3,2,0,1:T(8,128)(2,1)S(1)}, u32[]{:S(2)}, u32[]{:S(2)}) collective-permute-start(bf16[2,1,6,8,512]{4,3,2,0,1:T(8,128)(2,1)S(1)} %maximum_select_fusion.5), channel_id=1, source_target_pairs={{0,128},{64,192},{128,0},{192,64},{256,384},{320,448},{384,256},{4... | collective-permute-start | bytes 294920 | tf_op jit(solution)/shard_map/ppermute | solution.py:46
  18.0 5.0 %collective-permute-done.5 = bf16[2,1,6,8,512]{4,3,2,0,1:T(8,128)(2,1)S(1)} collective-permute-done((bf16[2,1,6,8,512]{4,3,2,0,1:T(8,128)(2,1)S(1)}, bf16[2,1,6,8,512]{4,3,2,0,1:T(8,128)(2,1)S(1)}, u32[]{:S(2)}, u32[]{:S(2)}) %collective-permute-start.5) | collective-permute-done | bytes 98336 | tf_op jit(solution)/shard_map/ppermute | solution.py:46
  23.0 2.6 %collective-permute-start.6 = (bf16[2,2,1,6,8,512]{5,4,3,1,2,0:T(8,128)(2,1)S(1)}, bf16[2,2,1,6,8,512]{5,4,3,1,2,0:T(8,128)(2,1)S(1)}, u32[]{:S(2)}, u32[]{:S(2)}) collective-permute-start(bf16[2,2,1,6,8,512]{5,4,3,1,2,0:T(8,128)(2,1)S(1)} %bitcast_select_fusion), channel_id=1, source_target_pairs={{0,64},{64,0},{128,192},{192,128},{256,320},{320,256},{384,448},{4... | collective-permute-start | bytes 589832 | tf_op jit(solution)/shard_map/ppermute | solution.py:46
  25.7 1.9 collective-permute-start
  27.6 2.7 %collective-permute-start.1 = (bf16[128,512]{1,0:T(8,128)(2,1)}, bf16[128,512]{1,0:T(8,128)(2,1)S(1)}, u32[]{:S(2)}, u32[]{:S(2)}) collective-permute-start(bf16[128,512]{1,0:T(8,128)(2,1)} %param.4), channel_id=1, source_target_pairs={{0,2},{2,0},{1,3},{3,1},{4,6},{6,4},{5,7},{7,5},{8,10},{10,8},{9,1... | collective-permute-start | bytes 393224 | tf_op jit(solution)/shard_map/ppermute | solution.py:23
  30.3 13.9 %collective-permute-start.3 = (bf16[128,512]{1,0:T(8,128)(2,1)}, bf16[128,512]{1,0:T(8,128)(2,1)S(1)}, u32[]{:S(2)}, u32[]{:S(2)}) collective-permute-start(bf16[128,512]{1,0:T(8,128)(2,1)} %param.4), channel_id=1, source_target_pairs={{0,8},{8,0},{1,9},{9,1},{2,10},{10,2},{3,11},{11,3},{4,12},{12,4},... | collective-permute-start | bytes 393224 | tf_op jit(solution)/shard_map/ppermute | solution.py:23
  44.2 2.9 %collective-permute-start.2 = (bf16[128,512]{1,0:T(8,128)(2,1)}, bf16[128,512]{1,0:T(8,128)(2,1)S(1)}, u32[]{:S(2)}, u32[]{:S(2)}) collective-permute-start(bf16[128,512]{1,0:T(8,128)(2,1)} %param.4), channel_id=1, source_target_pairs={{0,4},{4,0},{1,5},{5,1},{2,6},{6,2},{3,7},{7,3},{8,12},{12,8},{9,1... | collective-permute-start | bytes 393224 | tf_op jit(solution)/shard_map/ppermute | solution.py:23
  47.9 3.4 %collective-permute-start.7 = (bf16[1,6,8,512]{3,2,1,0:T(8,128)(2,1)S(1)}, bf16[1,6,8,512]{3,2,1,0:T(8,128)(2,1)S(1)}, u32[]{:S(2)}, u32[]{:S(2)}) collective-permute-start(bf16[1,6,8,512]{3,2,1,0:T(8,128)(2,1)S(1)} %get-tuple-element.25), channel_id=1, source_target_pairs={{0,256},{64,320},{128,384},{192,448},{256,0},{320,64},{384,128},{4... | collective-permute-start | bytes 147464 | tf_op jit(solution)/shard_map/ppermute | solution.py:46
  51.4 1.4 broadcast_in_dim.32
  52.8 4.4 %all-to-all-start = ((bf16[4,8,6,8,512]{4,3,1,2,0:T(8,128)(2,1)}), bf16[4,8,6,8,512]{4,3,1,2,0:T(8,128)(2,1)S(1)}, u32[]{:S(2)}, u32[]{:S(2)}) async-start(bf16[4,8,6,8,512]{4,3,1,2,0:T(8,128)(2,1)} %broadcast_in_dim.32), calls=%async_computation | async-start | bytes 3145728 | tf_op jit(solution)/shard_map/all_to_all | solution.py:59
  58.1 3.4 %collective-permute-done.7 = bf16[1,6,8,512]{3,2,1,0:T(8,128)(2,1)S(1)} collective-permute-done((bf16[1,6,8,512]{3,2,1,0:T(8,128)(2,1)S(1)}, bf16[1,6,8,512]{3,2,1,0:T(8,128)(2,1)S(1)}, u32[]{:S(2)}, u32[]{:S(2)}) %collective-permute-start.7) | collective-permute-done | bytes 49184 | tf_op jit(solution)/shard_map/ppermute | solution.py:46
  61.5 1.9 collective-permute-start.8
  64.0 6.2 %collective-permute-done.8 = bf16[2,1,6,8,512]{4,3,2,0,1:T(8,128)(2,1)S(1)} collective-permute-done((bf16[2,1,6,8,512]{4,3,2,0,1:T(8,128)(2,1)S(1)}, bf16[2,1,6,8,512]{4,3,2,0,1:T(8,128)(2,1)S(1)}, u32[]{:S(2)}, u32[]{:S(2)}) %collective-permute-start.8) | collective-permute-done | bytes 98336 | tf_op jit(solution)/shard_map/ppermute | solution.py:46
  70.2 1.9 collective-permute-start.9
  72.2 6.7 %collective-permute-done.9 = bf16[2,2,1,6,8,512]{5,4,3,1,0,2:T(8,128)(2,1)S(1)} collective-permute-done((bf16[2,2,1,6,8,512]{5,4,3,1,0,2:T(8,128)(2,1)S(1)}, bf16[2,2,1,6,8,512]{5,4,3,1,0,2:T(8,128)(2,1)S(1)}, u32[]{:S(2)}, u32[]{:S(2)}) %collective-permute-start.9) | collective-permute-done | bytes 196640 | tf_op jit(solution)/shard_map/ppermute | solution.py:46
  79.1 1.5 broadcast_in_dim.36
  80.6 4.3 %all-to-all-start.1 = ((bf16[4,8,6,8,512]{4,3,1,2,0:T(8,128)(2,1)}), bf16[4,8,6,8,512]{4,3,1,2,0:T(8,128)(2,1)S(1)}, u32[]{:S(2)}, u32[]{:S(2)}) async-start(bf16[4,8,6,8,512]{4,3,1,2,0:T(8,128)(2,1)} %broadcast_in_dim.36), calls=%async_computation.1 | async-start | bytes 3145728 | tf_op jit(solution)/shard_map/all_to_all | solution.py:59
  86.9 1.9 fusion.37
  89.9 2.0 reshape.935
  91.8 1.9 dot_general.40
  93.8 2.1 copy.125
  95.8 1.9 reshape.934
  97.8 1.9 dot_general.37
  100.7 1.1 fusion.38
  101.8 3.2 %all-to-all-done.1 = bf16[4,8,6,8,512]{4,3,1,2,0:T(8,128)(2,1)S(1)} async-done(((bf16[4,8,6,8,512]{4,3,1,2,0:T(8,128)(2,1)}), bf16[4,8,6,8,512]{4,3,1,2,0:T(8,128)(2,1)S(1)}, u32[]{:S(2)}, u32[]{:S(2)}) %all-to-all-start.1) | async-done | bytes 1572896 | tf_op jit(solution)/shard_map/all_to_all | solution.py:59
  105.1 1.1 copy-done.3
  109.2 1.5 copy-done
  111.7 3.1 %collective-permute-start.16 = (bf16[8,8,6,512]{3,1,2,0:T(8,128)(2,1)}, bf16[8,8,6,512]{3,1,2,0:T(8,128)(2,1)}, u32[]{:S(2)}, u32[]{:S(2)}) collective-permute-start(bf16[8,8,6,512]{3,1,2,0:T(8,128)(2,1)} %get-tuple-element.18), channel_id=1, source_target_pairs={{0,48},{16,0},{32,16},{48,32},{1,49},{17,1},{33,17},{49,33},{2,50}... | collective-permute-start | bytes 1179656 | tf_op jit(solution)/shard_map/ppermute | solution.py:76
  114.8 2.8 %collective-permute-start.14 = (bf16[8,8,6,512]{3,1,2,0:T(8,128)(2,1)}, bf16[8,8,6,512]{3,1,2,0:T(8,128)(2,1)S(1)}, u32[]{:S(2)}, u32[]{:S(2)}) collective-permute-start(bf16[8,8,6,512]{3,1,2,0:T(8,128)(2,1)} %get-tuple-element.17), channel_id=1, source_target_pairs={{0,16},{16,32},{32,48},{48,0},{1,17},{17,33},{33,49},{49,1},{2,18}... | collective-permute-start | bytes 1179656 | tf_op jit(solution)/shard_map/ppermute | solution.py:75
  117.5 1.7 fusion.5
  119.3 3.6 %collective-permute-done.16 = bf16[8,8,6,512]{3,1,2,0:T(8,128)(2,1)} collective-permute-done((bf16[8,8,6,512]{3,1,2,0:T(8,128)(2,1)}, bf16[8,8,6,512]{3,1,2,0:T(8,128)(2,1)}, u32[]{:S(2)}, u32[]{:S(2)}) %collective-permute-start.16) | collective-permute-done | bytes 393248 | tf_op jit(solution)/shard_map/ppermute | solution.py:76
  122.9 1.1 fusion.10
  125.1 4.3 %collective-permute-start.17 = (bf16[8,8,6,1024]{3,1,2,0:T(8,128)(2,1)}, bf16[8,8,6,1024]{3,1,2,0:T(8,128)(2,1)}, u32[]{:S(2)}, u32[]{:S(2)}) collective-permute-start(bf16[8,8,6,1024]{3,1,2,0:T(8,128)(2,1)} %pad_maximum_fusion.1), channel_id=1, source_target_pairs={{0,48},{16,0},{32,16},{48,32},{1,49},{17,1},{33,17},{49,33},{2,50}... | collective-permute-start | bytes 2359304 | tf_op jit(solution)/shard_map/ppermute | solution.py:82
  130.5 1.9 collective-permute-start.15
  132.5 11.5 %collective-permute-done.17 = bf16[8,8,6,1024]{3,1,2,0:T(8,128)(2,1)} collective-permute-done((bf16[8,8,6,1024]{3,1,2,0:T(8,128)(2,1)}, bf16[8,8,6,1024]{3,1,2,0:T(8,128)(2,1)}, u32[]{:S(2)}, u32[]{:S(2)}) %collective-permute-start.17) | collective-permute-done | bytes 786464 | tf_op jit(solution)/shard_map/ppermute | solution.py:82
  143.9 6.4 %collective-permute-done.15 = bf16[8,8,6,1024]{3,1,2,0:T(8,128)(2,1)} collective-permute-done((bf16[8,8,6,1024]{3,1,2,0:T(8,128)(2,1)}, bf16[8,8,6,1024]{3,1,2,0:T(8,128)(2,1)}, u32[]{:S(2)}, u32[]{:S(2)}) %collective-permute-start.15) | collective-permute-done | bytes 786464 | tf_op jit(solution)/shard_map/ppermute | solution.py:81
  150.3 2.0 fusion.9
  153.2 3.5 %all-to-all-start.2 = ((bf16[4,2,8,6,1024]{4,2,3,1,0:T(8,128)(2,1)}), bf16[4,2,8,6,1024]{4,2,3,1,0:T(8,128)(2,1)S(1)}, u32[]{:S(2)}, u32[]{:S(2)}) async-start(bf16[4,2,8,6,1024]{4,2,3,1,0:T(8,128)(2,1)} %bitcast.153), calls=%async_computation.2 | async-start | bytes 1572864 | tf_op jit(solution)/shard_map/all_to_all | solution.py:92
  157.0 1.2 copy-done.4
  162.2 1.9 collective-permute-start.12
  164.1 5.3 %collective-permute-start.13 = (f32[128,512]{0,1:T(8,128)S(1)}, f32[128,512]{0,1:T(8,128)S(1)}, u32[]{:S(2)}, u32[]{:S(2)}) collective-permute-start(f32[128,512]{0,1:T(8,128)S(1)} %bitcast.181), channel_id=1, source_target_pairs={{0,8},{8,0},{1,9},{9,1},{2,10},{10,2},{3,11},{11,3},{4,12},{12,4},... | collective-permute-start | bytes 786440 | tf_op jit(solution)/shard_map/ppermute | solution.py:23
  169.4 3.2 %collective-permute-start.11 = (f32[128,512]{0,1:T(8,128)S(1)}, f32[128,512]{0,1:T(8,128)S(1)}, u32[]{:S(2)}, u32[]{:S(2)}) collective-permute-start(f32[128,512]{0,1:T(8,128)S(1)} %bitcast.180), channel_id=1, source_target_pairs={{0,2},{2,0},{1,3},{3,1},{4,6},{6,4},{5,7},{7,5},{8,10},{10,8},{9,1... | collective-permute-start | bytes 786440 | tf_op jit(solution)/shard_map/ppermute | solution.py:23
  172.6 1.9 collective-permute-start.10
  174.5 13.8 %all-to-all-done.2 = bf16[4,2,8,6,1024]{4,2,3,1,0:T(8,128)(2,1)S(1)} async-done(((bf16[4,2,8,6,1024]{4,2,3,1,0:T(8,128)(2,1)}), bf16[4,2,8,6,1024]{4,2,3,1,0:T(8,128)(2,1)S(1)}, u32[]{:S(2)}, u32[]{:S(2)}) %all-to-all-start.2) | async-done | bytes 786464 | tf_op jit(solution)/shard_map/all_to_all | solution.py:92
  189.2 13.9 %all-to-all-start.3 = ((bf16[2,8,6,1024]{3,1,2,0:T(8,128)(2,1)}), bf16[2,8,6,1024]{3,1,2,0:T(8,128)(2,1)S(1)}, u32[]{:S(2)}, u32[]{:S(2)}) async-start(bf16[2,8,6,1024]{3,1,2,0:T(8,128)(2,1)} %reduce_sum.21), calls=%async_computation.3 | async-start | bytes 393216 | tf_op jit(solution)/shard_map/all_to_all | solution.py:94
  204.1 7.9 %all-to-all-done.3 = bf16[2,8,6,1024]{3,1,2,0:T(8,128)(2,1)S(1)} async-done(((bf16[2,8,6,1024]{3,1,2,0:T(8,128)(2,1)}), bf16[2,8,6,1024]{3,1,2,0:T(8,128)(2,1)S(1)}, u32[]{:S(2)}, u32[]{:S(2)}) %all-to-all-start.3) | async-done | bytes 196640 | tf_op jit(solution)/shard_map/all_to_all | solution.py:94
  (107 shorter events, 21.4 us)
Async XLA Ops:
  1.5 11.2 %collective-permute-start.4 = (bf16[1,6,8,512]{3,2,1,0:T(8,128)(2,1)S(1)}, bf16[1,6,8,512]{3,2,1,0:T(8,128)(2,1)S(1)}, u32[]{:S(2)}, u32[]{:S(2)}) collective-permute-start(bf16[1,6,8,512]{3,2,1,0:T(8,128)(2,1)S(1)} %get-tuple-element.26), channel_id=1, source_target_pairs={{0,256},{64,320},{128,384},{192,448},{256,0},{320,64},{384,128},{4... | collective-permute-start | bytes 147464 | tf_op jit(solution)/shard_map/ppermute | solution.py:46
  12.7 10.4 %collective-permute-start.5 = (bf16[2,1,6,8,512]{4,3,2,0,1:T(8,128)(2,1)S(1)}, bf16[2,1,6,8,512]{4,3,2,0,1:T(8,128)(2,1)S(1)}, u32[]{:S(2)}, u32[]{:S(2)}) collective-permute-start(bf16[2,1,6,8,512]{4,3,2,0,1:T(8,128)(2,1)S(1)} %maximum_select_fusion.5), channel_id=1, source_target_pairs={{0,128},{64,192},{128,0},{192,64},{256,384},{320,448},{384,256},{4... | collective-permute-start | bytes 294920 | tf_op jit(solution)/shard_map/ppermute | solution.py:46
  23.0 24.9 %collective-permute-start.6 = (bf16[2,2,1,6,8,512]{5,4,3,1,2,0:T(8,128)(2,1)S(1)}, bf16[2,2,1,6,8,512]{5,4,3,1,2,0:T(8,128)(2,1)S(1)}, u32[]{:S(2)}, u32[]{:S(2)}) collective-permute-start(bf16[2,2,1,6,8,512]{5,4,3,1,2,0:T(8,128)(2,1)S(1)} %bitcast_select_fusion), channel_id=1, source_target_pairs={{0,64},{64,0},{128,192},{192,128},{256,320},{320,256},{384,448},{4... | collective-permute-start | bytes 589832 | tf_op jit(solution)/shard_map/ppermute | solution.py:46
  25.7 37.8 %collective-permute-start = (bf16[128,512]{1,0:T(8,128)(2,1)}, bf16[128,512]{1,0:T(8,128)(2,1)S(1)}, u32[]{:S(2)}, u32[]{:S(2)}) collective-permute-start(bf16[128,512]{1,0:T(8,128)(2,1)} %param.4), channel_id=1, source_target_pairs={{0,1},{1,0},{2,3},{3,2},{4,5},{5,4},{6,7},{7,6},{8,9},{9,8},{10,11... | collective-permute-start | bytes 393224 | tf_op jit(solution)/shard_map/ppermute | solution.py:23
  27.6 36.0 %collective-permute-start.1 = (bf16[128,512]{1,0:T(8,128)(2,1)}, bf16[128,512]{1,0:T(8,128)(2,1)S(1)}, u32[]{:S(2)}, u32[]{:S(2)}) collective-permute-start(bf16[128,512]{1,0:T(8,128)(2,1)} %param.4), channel_id=1, source_target_pairs={{0,2},{2,0},{1,3},{3,1},{4,6},{6,4},{5,7},{7,5},{8,10},{10,8},{9,1... | collective-permute-start | bytes 393224 | tf_op jit(solution)/shard_map/ppermute | solution.py:23
  30.3 33.5 %collective-permute-start.3 = (bf16[128,512]{1,0:T(8,128)(2,1)}, bf16[128,512]{1,0:T(8,128)(2,1)S(1)}, u32[]{:S(2)}, u32[]{:S(2)}) collective-permute-start(bf16[128,512]{1,0:T(8,128)(2,1)} %param.4), channel_id=1, source_target_pairs={{0,8},{8,0},{1,9},{9,1},{2,10},{10,2},{3,11},{11,3},{4,12},{12,4},... | collective-permute-start | bytes 393224 | tf_op jit(solution)/shard_map/ppermute | solution.py:23
  44.2 19.7 %collective-permute-start.2 = (bf16[128,512]{1,0:T(8,128)(2,1)}, bf16[128,512]{1,0:T(8,128)(2,1)S(1)}, u32[]{:S(2)}, u32[]{:S(2)}) collective-permute-start(bf16[128,512]{1,0:T(8,128)(2,1)} %param.4), channel_id=1, source_target_pairs={{0,4},{4,0},{1,5},{5,1},{2,6},{6,2},{3,7},{7,3},{8,12},{12,8},{9,1... | collective-permute-start | bytes 393224 | tf_op jit(solution)/shard_map/ppermute | solution.py:23
  47.9 13.6 %collective-permute-start.7 = (bf16[1,6,8,512]{3,2,1,0:T(8,128)(2,1)S(1)}, bf16[1,6,8,512]{3,2,1,0:T(8,128)(2,1)S(1)}, u32[]{:S(2)}, u32[]{:S(2)}) collective-permute-start(bf16[1,6,8,512]{3,2,1,0:T(8,128)(2,1)S(1)} %get-tuple-element.25), channel_id=1, source_target_pairs={{0,256},{64,320},{128,384},{192,448},{256,0},{320,64},{384,128},{4... | collective-permute-start | bytes 147464 | tf_op jit(solution)/shard_map/ppermute | solution.py:46
  52.8 4.5 %copy-start.14 = (bf16[128,512]{1,0:T(8,128)(2,1)S(1)}, bf16[128,512]{1,0:T(8,128)(2,1)}, u32[]{:S(2)}) copy-start(bf16[128,512]{1,0:T(8,128)(2,1)} %param.4) | copy-start | bytes 393220
  52.8 26.3 %all-to-all-start = ((bf16[4,8,6,8,512]{4,3,1,2,0:T(8,128)(2,1)}), bf16[4,8,6,8,512]{4,3,1,2,0:T(8,128)(2,1)S(1)}, u32[]{:S(2)}, u32[]{:S(2)}) async-start(bf16[4,8,6,8,512]{4,3,1,2,0:T(8,128)(2,1)} %broadcast_in_dim.32), calls=%async_computation | async-start | bytes 3145728 | tf_op jit(solution)/shard_map/all_to_all | solution.py:59
  61.5 8.7 %collective-permute-start.8 = (bf16[2,1,6,8,512]{4,3,2,0,1:T(8,128)(2,1)S(1)}, bf16[2,1,6,8,512]{4,3,2,0,1:T(8,128)(2,1)S(1)}, u32[]{:S(2)}, u32[]{:S(2)}) collective-permute-start(bf16[2,1,6,8,512]{4,3,2,0,1:T(8,128)(2,1)S(1)} %fusion.31), channel_id=1, source_target_pairs={{0,128},{64,192},{128,0},{192,64},{256,384},{320,448},{384,256},{4... | collective-permute-start | bytes 294920 | tf_op jit(solution)/shard_map/ppermute | solution.py:46
  70.2 8.7 %collective-permute-start.9 = (bf16[2,2,1,6,8,512]{5,4,3,1,0,2:T(8,128)(2,1)S(1)}, bf16[2,2,1,6,8,512]{5,4,3,1,0,2:T(8,128)(2,1)S(1)}, u32[]{:S(2)}, u32[]{:S(2)}) collective-permute-start(bf16[2,2,1,6,8,512]{5,4,3,1,0,2:T(8,128)(2,1)S(1)} %maximum_select_fusion.3), channel_id=1, source_target_pairs={{0,64},{64,0},{128,192},{192,128},{256,320},{320,256},{384,448},{4... | collective-permute-start | bytes 589832 | tf_op jit(solution)/shard_map/ppermute | solution.py:46
  72.2 6.9 %copy-start.8 = (bf16[128,2,6,256]{0,3,2,1:T(8,128)(2,1)}, bf16[128,2,6,256]{0,3,2,1:T(8,128)(2,1)S(1)}, u32[]{:S(2)}) copy-start(bf16[128,2,6,256]{0,3,2,1:T(8,128)(2,1)S(1)} %constant_dynamic-update-slice_fusion.3) | copy-start | bytes 2359300
  79.1 20.6 %copy-start.1 = (bf16[4,8,6,8,512]{4,3,1,2,0:T(8,128)(2,1)}, bf16[4,8,6,8,512]{4,3,1,2,0:T(8,128)(2,1)S(1)}, u32[]{:S(2)}) copy-start(bf16[4,8,6,8,512]{4,3,1,2,0:T(8,128)(2,1)S(1)} %all-to-all-done) | copy-start | bytes 4718596
  80.6 24.3 %all-to-all-start.1 = ((bf16[4,8,6,8,512]{4,3,1,2,0:T(8,128)(2,1)}), bf16[4,8,6,8,512]{4,3,1,2,0:T(8,128)(2,1)S(1)}, u32[]{:S(2)}, u32[]{:S(2)}) async-start(bf16[4,8,6,8,512]{4,3,1,2,0:T(8,128)(2,1)} %broadcast_in_dim.36), calls=%async_computation.1 | async-start | bytes 3145728 | tf_op jit(solution)/shard_map/all_to_all | solution.py:59
  99.7 1.0 copy-start.5
  105.0 1.2 copy-start.3
  106.2 1.0 copy-start.6
  106.2 1.1 copy-start.12
  106.2 1.1 copy-start.16
  106.6 1.4 copy-start.10
  107.3 1.0 copy-start.7
  107.3 1.1 copy-start.9
  107.3 1.1 copy-start.15
  109.0 1.6 copy-start
  111.7 11.3 %collective-permute-start.16 = (bf16[8,8,6,512]{3,1,2,0:T(8,128)(2,1)}, bf16[8,8,6,512]{3,1,2,0:T(8,128)(2,1)}, u32[]{:S(2)}, u32[]{:S(2)}) collective-permute-start(bf16[8,8,6,512]{3,1,2,0:T(8,128)(2,1)} %get-tuple-element.18), channel_id=1, source_target_pairs={{0,48},{16,0},{32,16},{48,32},{1,49},{17,1},{33,17},{49,33},{2,50}... | collective-permute-start | bytes 1179656 | tf_op jit(solution)/shard_map/ppermute | solution.py:76
  114.8 14.6 %collective-permute-start.14 = (bf16[8,8,6,512]{3,1,2,0:T(8,128)(2,1)}, bf16[8,8,6,512]{3,1,2,0:T(8,128)(2,1)S(1)}, u32[]{:S(2)}, u32[]{:S(2)}) collective-permute-start(bf16[8,8,6,512]{3,1,2,0:T(8,128)(2,1)} %get-tuple-element.17), channel_id=1, source_target_pairs={{0,16},{16,32},{32,48},{48,0},{1,17},{17,33},{33,49},{49,1},{2,18}... | collective-permute-start | bytes 1179656 | tf_op jit(solution)/shard_map/ppermute | solution.py:75
  125.1 18.8 %collective-permute-start.17 = (bf16[8,8,6,1024]{3,1,2,0:T(8,128)(2,1)}, bf16[8,8,6,1024]{3,1,2,0:T(8,128)(2,1)}, u32[]{:S(2)}, u32[]{:S(2)}) collective-permute-start(bf16[8,8,6,1024]{3,1,2,0:T(8,128)(2,1)} %pad_maximum_fusion.1), channel_id=1, source_target_pairs={{0,48},{16,0},{32,16},{48,32},{1,49},{17,1},{33,17},{49,33},{2,50}... | collective-permute-start | bytes 2359304 | tf_op jit(solution)/shard_map/ppermute | solution.py:82
  130.5 19.8 %collective-permute-start.15 = (bf16[8,8,6,1024]{3,1,2,0:T(8,128)(2,1)}, bf16[8,8,6,1024]{3,1,2,0:T(8,128)(2,1)}, u32[]{:S(2)}, u32[]{:S(2)}) collective-permute-start(bf16[8,8,6,1024]{3,1,2,0:T(8,128)(2,1)} %pad_maximum_fusion), channel_id=1, source_target_pairs={{0,16},{16,32},{32,48},{48,0},{1,17},{17,33},{33,49},{49,1},{2,18}... | collective-permute-start | bytes 2359304 | tf_op jit(solution)/shard_map/ppermute | solution.py:81
  152.3 4.5 %copy-start.2 = (bf16[4,8,6,8,512]{4,3,1,2,0:T(8,128)(2,1)S(1)}, bf16[4,8,6,8,512]{4,3,1,2,0:T(8,128)(2,1)}, u32[]{:S(2)}) copy-start(bf16[4,8,6,8,512]{4,3,1,2,0:T(8,128)(2,1)} %copy-done.1) | copy-start | bytes 4718596
  153.2 35.1 %all-to-all-start.2 = ((bf16[4,2,8,6,1024]{4,2,3,1,0:T(8,128)(2,1)}), bf16[4,2,8,6,1024]{4,2,3,1,0:T(8,128)(2,1)S(1)}, u32[]{:S(2)}, u32[]{:S(2)}) async-start(bf16[4,2,8,6,1024]{4,2,3,1,0:T(8,128)(2,1)} %bitcast.153), calls=%async_computation.2 | async-start | bytes 1572864 | tf_op jit(solution)/shard_map/all_to_all | solution.py:92
  156.7 1.4 copy-start.4
  158.3 1.0 copy-start.13
  159.9 1.0 copy-start.11
  162.2 41.0 %collective-permute-start.12 = (f32[128,512]{0,1:T(8,128)S(1)}, f32[128,512]{0,1:T(8,128)S(1)}, u32[]{:S(2)}, u32[]{:S(2)}) collective-permute-start(f32[128,512]{0,1:T(8,128)S(1)} %bitcast.182), channel_id=1, source_target_pairs={{0,4},{4,0},{1,5},{5,1},{2,6},{6,2},{3,7},{7,3},{8,12},{12,8},{9,1... | collective-permute-start | bytes 786440 | tf_op jit(solution)/shard_map/ppermute | solution.py:23
  164.1 39.1 %collective-permute-start.13 = (f32[128,512]{0,1:T(8,128)S(1)}, f32[128,512]{0,1:T(8,128)S(1)}, u32[]{:S(2)}, u32[]{:S(2)}) collective-permute-start(f32[128,512]{0,1:T(8,128)S(1)} %bitcast.181), channel_id=1, source_target_pairs={{0,8},{8,0},{1,9},{9,1},{2,10},{10,2},{3,11},{11,3},{4,12},{12,4},... | collective-permute-start | bytes 786440 | tf_op jit(solution)/shard_map/ppermute | solution.py:23
  169.4 33.8 %collective-permute-start.11 = (f32[128,512]{0,1:T(8,128)S(1)}, f32[128,512]{0,1:T(8,128)S(1)}, u32[]{:S(2)}, u32[]{:S(2)}) collective-permute-start(f32[128,512]{0,1:T(8,128)S(1)} %bitcast.180), channel_id=1, source_target_pairs={{0,2},{2,0},{1,3},{3,1},{4,6},{6,4},{5,7},{7,5},{8,10},{10,8},{9,1... | collective-permute-start | bytes 786440 | tf_op jit(solution)/shard_map/ppermute | solution.py:23
  172.6 30.7 %collective-permute-start.10 = (f32[128,512]{0,1:T(8,128)S(1)}, f32[128,512]{0,1:T(8,128)S(1)}, u32[]{:S(2)}, u32[]{:S(2)}) collective-permute-start(f32[128,512]{0,1:T(8,128)S(1)} %bitcast.179), channel_id=1, source_target_pairs={{0,1},{1,0},{2,3},{3,2},{4,5},{5,4},{6,7},{7,6},{8,9},{9,8},{10,11... | collective-permute-start | bytes 786440 | tf_op jit(solution)/shard_map/ppermute | solution.py:23
  189.2 22.8 %all-to-all-start.3 = ((bf16[2,8,6,1024]{3,1,2,0:T(8,128)(2,1)}), bf16[2,8,6,1024]{3,1,2,0:T(8,128)(2,1)S(1)}, u32[]{:S(2)}, u32[]{:S(2)}) async-start(bf16[2,8,6,1024]{3,1,2,0:T(8,128)(2,1)} %reduce_sum.21), calls=%async_computation.3 | async-start | bytes 393216 | tf_op jit(solution)/shard_map/all_to_all | solution.py:94

commit v10 on v8

--- a/solution.py
+++ b/solution.py
@@ -6,9 +6,11 @@
 
 
 BS = 256
-ROWS = "zl"
+HALF = "zh"
+QUARTER = "zq"
+ROWS = (HALF, QUARTER)
 COLS = "xx"
-DP = (ROWS, COLS)
+DP = (HALF, QUARTER, COLS)
 
 
 def partner_2(block, axis, bit):
@@ -59,9 +61,13 @@
 
 
 def scatter_rows(terms):
+    _, zl, own, factor_count, width = terms.shape
+    halves = lax.axis_size(HALF)
     got = lax.all_to_all(terms, COLS, 0, 0, tiled=True)
+    part = got.astype(jnp.float32).sum(0).reshape(halves, zl // halves, own, factor_count, width)
+    got = lax.all_to_all(part.transpose(1, 0, 2, 3, 4).astype(jnp.bfloat16), QUARTER, 0, 0, tiled=True)
     part = got.astype(jnp.float32).sum(0)
-    got = lax.all_to_all(part.astype(jnp.bfloat16), ROWS, 0, 0, tiled=True)
+    got = lax.all_to_all(part.astype(jnp.bfloat16), HALF, 0, 0, tiled=True)
     part = got.astype(jnp.float32).sum(0)
     return part.transpose(1, 0, 2)
 
@@ -130,8 +136,8 @@
             input_total = input_total + flip_blocks(contrib, stride)
         else:
             bit_number = (stride // local_blocks).bit_length() - 1
-            returned = partner_2(contrib.reshape(row_count, local_width), "fly", bit_number)
-            input_total = input_total + returned.reshape(row_count, local_blocks, BS)
+            returned = partner_2(contrib.reshape(row_count, local_width).astype(jnp.bfloat16), "fly", bit_number)
+            input_total = input_total + returned.astype(jnp.float32).reshape(row_count, local_blocks, BS)
     input_grad = input_total.reshape(row_count, local_width).astype(jnp.bfloat16)
     weight_grad = scatter_rows(jnp.concatenate(sums, axis=4)) * (1.0 / (zl * xx))
     return (input_grad, weight_grad)
@@ -141,7 +147,8 @@
     devices = mesh.devices
     xs = sorted({d.coords[0] for d in devices[:, 0]})
     cols = len(xs)
-    return Mesh(devices.reshape(devices.shape[0] // cols, cols, devices.shape[1]), (ROWS, COLS, "fly"))
+    lines = devices.shape[0] // cols
+    return Mesh(devices.reshape(2, lines // 2, cols, devices.shape[1]), (HALF, QUARTER, COLS, "fly"))
 
 
 def solution(mesh):

time: 223 us -> 211 us (0.946)
  the two profiles are of different devices: /device:TPU:24 before, /device:TPU:1 now
where the time goes in v10:
time: 211 us; the launch traced here: 210 us
  starting transfers between devices  84.1 us (40%)
  waiting for transfers between devices  46.4 us (22%)
  blocking collectives  38.5 us (18%)
  local copies, waits for them, and re-layouts  27.5 us (13%)
  other arithmetic  7.94 us (4%)
  matrix products  4.09 us (2%)
    ppermute x8, starting transfers between devices, partner_2(): return lax.ppermute(block, axis, route)  41.2 us
    all_to_all x1, blocking collectives, scatter_rows(): got = lax.all_to_all(terms, COLS, 0, 0, tiled=True)  38.5 us
    ppermute x6, starting transfers between devices, gather_line(): got = lax.ppermute(held, axis, [(i, i ^ dist) for i in range(count)])  27.1 us
    ppermute x6, waiting for transfers between devices, gather_line(): got = lax.ppermute(held, axis, [(i, i ^ dist) for i in range(count)])  22.3 us
    all_to_all x1, waiting for transfers between devices, scatter_rows(): got = lax.all_to_all(part.astype(jnp.bfloat16), HALF, 0, 0, tiled=True)  11.8 us
    all_to_all x1, waiting for transfers between devices, scatter_rows(): lax.all_to_all(part.transpose(1, 0, 2, 3, 4).astype(jnp.bfloat16), QUARTE...  10 us
    all_to_all x2, starting transfers between devices, gather_rows(): both = lax.all_to_all(copies, COLS, 0, 0, tiled=True)  8.16 us
    unnamed x35, local copies, waits for them, and re-layouts  6.7 us
  transfers between devices with their start and end apart: 18, of which 8 were waited for; matrix products, arithmetic and copies ran while one was open for 12% of the time, Pallas kernels for 0%

profile of v10, /device:TPU:1, one launch (start us, length us, event | category | flops | bytes accessed | tf_op | source)
XLA Modules:
  0.0 209.9 jit_solution(3729852795561535303)
XLA Ops:
  0.6 0.8 slice_bitcast_fusion
  1.5 9.6 %collective-permute-start.4 = (bf16[1,6,8,512]{3,2,1,0:T(8,128)(2,1)S(1)}, bf16[1,6,8,512]{3,2,1,0:T(8,128)(2,1)S(1)}, u32[]{:S(2)}, u32[]{:S(2)}) collective-permute-start(bf16[1,6,8,512]{3,2,1,0:T(8,128)(2,1)S(1)} %get-tuple-element.21), channel_id=1, source_target_pairs={{0,256},{64,320},{128,384},{192,448},{256,0},{320,64},{384,128},{4... | collective-permute-start | bytes 147464 | tf_op jit(solution)/shard_map/ppermute | solution.py:46
  11.1 1.5 collective-permute-done.4
  12.6 6.1 %collective-permute-start.5 = (bf16[2,1,6,8,512]{4,3,2,0,1:T(8,128)(2,1)S(1)}, bf16[2,1,6,8,512]{4,3,2,0,1:T(8,128)(2,1)S(1)}, u32[]{:S(2)}, u32[]{:S(2)}) collective-permute-start(bf16[2,1,6,8,512]{4,3,2,0,1:T(8,128)(2,1)S(1)} %maximum_select_fusion.5), channel_id=1, source_target_pairs={{0,128},{64,192},{128,0},{192,64},{256,384},{320,448},{384,256},{4... | collective-permute-start | bytes 294920 | tf_op jit(solution)/shard_map/ppermute | solution.py:46
  18.7 2.0 collective-permute-done.5
  20.7 4.5 %collective-permute-start.6 = (bf16[2,2,1,6,8,512]{5,4,3,1,2,0:T(8,128)(2,1)S(1)}, bf16[2,2,1,6,8,512]{5,4,3,1,2,0:T(8,128)(2,1)S(1)}, u32[]{:S(2)}, u32[]{:S(2)}) collective-permute-start(bf16[2,2,1,6,8,512]{5,4,3,1,2,0:T(8,128)(2,1)S(1)} %bitcast_select_fusion), channel_id=1, source_target_pairs={{0,64},{64,0},{128,192},{192,128},{256,320},{320,256},{384,448},{4... | collective-permute-start | bytes 589832 | tf_op jit(solution)/shard_map/ppermute | solution.py:46
  25.2 4.8 %collective-permute-start = (bf16[128,512]{1,0:T(8,128)(2,1)}, bf16[128,512]{1,0:T(8,128)(2,1)S(1)}, u32[]{:S(2)}, u32[]{:S(2)}) collective-permute-start(bf16[128,512]{1,0:T(8,128)(2,1)} %param.4), channel_id=1, source_target_pairs={{0,1},{1,0},{2,3},{3,2},{4,5},{5,4},{6,7},{7,6},{8,9},{9,8},{10,11... | collective-permute-start | bytes 393224 | tf_op jit(solution)/shard_map/ppermute | solution.py:23
  30.0 2.3 %collective-permute-start.1 = (bf16[128,512]{1,0:T(8,128)(2,1)}, bf16[128,512]{1,0:T(8,128)(2,1)S(1)}, u32[]{:S(2)}, u32[]{:S(2)}) collective-permute-start(bf16[128,512]{1,0:T(8,128)(2,1)} %param.4), channel_id=1, source_target_pairs={{0,2},{2,0},{1,3},{3,1},{4,6},{6,4},{5,7},{7,5},{8,10},{10,8},{9,1... | collective-permute-start | bytes 393224 | tf_op jit(solution)/shard_map/ppermute | solution.py:23
  32.3 4.5 %collective-permute-start.2 = (bf16[128,512]{1,0:T(8,128)(2,1)}, bf16[128,512]{1,0:T(8,128)(2,1)S(1)}, u32[]{:S(2)}, u32[]{:S(2)}) collective-permute-start(bf16[128,512]{1,0:T(8,128)(2,1)} %param.4), channel_id=1, source_target_pairs={{0,4},{4,0},{1,5},{5,1},{2,6},{6,2},{3,7},{7,3},{8,12},{12,8},{9,1... | collective-permute-start | bytes 393224 | tf_op jit(solution)/shard_map/ppermute | solution.py:23
  36.8 13.6 %collective-permute-start.3 = (bf16[128,512]{1,0:T(8,128)(2,1)}, bf16[128,512]{1,0:T(8,128)(2,1)S(1)}, u32[]{:S(2)}, u32[]{:S(2)}) collective-permute-start(bf16[128,512]{1,0:T(8,128)(2,1)} %param.4), channel_id=1, source_target_pairs={{0,8},{8,0},{1,9},{9,1},{2,10},{10,2},{3,11},{11,3},{4,12},{12,4},... | collective-permute-start | bytes 393224 | tf_op jit(solution)/shard_map/ppermute | solution.py:23
  50.5 0.8 copy.113
  51.4 3.1 %collective-permute-start.7 = (bf16[1,6,8,512]{3,2,1,0:T(8,128)(2,1)S(1)}, bf16[1,6,8,512]{3,2,1,0:T(8,128)(2,1)S(1)}, u32[]{:S(2)}, u32[]{:S(2)}) collective-permute-start(bf16[1,6,8,512]{3,2,1,0:T(8,128)(2,1)S(1)} %get-tuple-element.20), channel_id=1, source_target_pairs={{0,256},{64,320},{128,384},{192,448},{256,0},{320,64},{384,128},{4... | collective-permute-start | bytes 147464 | tf_op jit(solution)/shard_map/ppermute | solution.py:46
  54.6 1.4 broadcast_in_dim.32
  56.0 4.1 %all-to-all-start = ((bf16[4,8,6,8,512]{4,3,1,2,0:T(8,128)(2,1)}), bf16[4,8,6,8,512]{4,3,1,2,0:T(8,128)(2,1)S(1)}, u32[]{:S(2)}, u32[]{:S(2)}) async-start(bf16[4,8,6,8,512]{4,3,1,2,0:T(8,128)(2,1)} %broadcast_in_dim.32), calls=%async_computation | async-start | bytes 3145728 | tf_op jit(solution)/shard_map/all_to_all | solution.py:59
  61.0 6.9 %collective-permute-done.7 = bf16[1,6,8,512]{3,2,1,0:T(8,128)(2,1)S(1)} collective-permute-done((bf16[1,6,8,512]{3,2,1,0:T(8,128)(2,1)S(1)}, bf16[1,6,8,512]{3,2,1,0:T(8,128)(2,1)S(1)}, u32[]{:S(2)}, u32[]{:S(2)}) %collective-permute-start.7) | collective-permute-done | bytes 49184 | tf_op jit(solution)/shard_map/ppermute | solution.py:46
  67.9 1.9 collective-permute-start.8
  70.4 6.1 %collective-permute-done.8 = bf16[2,1,6,8,512]{4,3,2,0,1:T(8,128)(2,1)S(1)} collective-permute-done((bf16[2,1,6,8,512]{4,3,2,0,1:T(8,128)(2,1)S(1)}, bf16[2,1,6,8,512]{4,3,2,0,1:T(8,128)(2,1)S(1)}, u32[]{:S(2)}, u32[]{:S(2)}) %collective-permute-start.8) | collective-permute-done | bytes 98336 | tf_op jit(solution)/shard_map/ppermute | solution.py:46
  76.5 1.9 collective-permute-start.9
  78.5 5.9 %collective-permute-done.9 = bf16[2,2,1,6,8,512]{5,4,3,1,0,2:T(8,128)(2,1)S(1)} collective-permute-done((bf16[2,2,1,6,8,512]{5,4,3,1,0,2:T(8,128)(2,1)S(1)}, bf16[2,2,1,6,8,512]{5,4,3,1,0,2:T(8,128)(2,1)S(1)}, u32[]{:S(2)}, u32[]{:S(2)}) %collective-permute-start.9) | collective-permute-done | bytes 196640 | tf_op jit(solution)/shard_map/ppermute | solution.py:46
  84.5 1.4 broadcast_in_dim.36
  85.9 4.0 %all-to-all-start.1 = ((bf16[4,8,6,8,512]{4,3,1,2,0:T(8,128)(2,1)}), bf16[4,8,6,8,512]{4,3,1,2,0:T(8,128)(2,1)S(1)}, u32[]{:S(2)}, u32[]{:S(2)}) async-start(bf16[4,8,6,8,512]{4,3,1,2,0:T(8,128)(2,1)} %broadcast_in_dim.36), calls=%async_computation.1 | async-start | bytes 3145728 | tf_op jit(solution)/shard_map/all_to_all | solution.py:59
  91.2 0.7 constant_dynamic-update-slice_fusion
  91.9 1.9 fusion.22
  93.8 1.1 copy.126
  94.9 1.9 reshape.935
  96.8 1.9 dot_general.40
  98.7 2.1 copy.124
  100.8 1.9 reshape.934
  102.7 1.9 dot_general.37
  104.8 0.9 copy-done
  105.7 1.1 fusion.23
  106.8 2.3 %all-to-all-done.1 = bf16[4,8,6,8,512]{4,3,1,2,0:T(8,128)(2,1)S(1)} async-done(((bf16[4,8,6,8,512]{4,3,1,2,0:T(8,128)(2,1)}), bf16[4,8,6,8,512]{4,3,1,2,0:T(8,128)(2,1)S(1)}, u32[]{:S(2)}, u32[]{:S(2)}) %all-to-all-start.1) | async-done | bytes 1572896 | tf_op jit(solution)/shard_map/all_to_all | solution.py:59
  112.1 38.5 %all_to_all.25 = bf16[4,8,8,6,1024]{4,2,3,1,0:T(8,128)(2,1)} all-to-all(bf16[4,8,8,6,1024]{4,2,3,1,0:T(8,128)(2,1)S(1)} %pad_maximum_fusion), channel_id=1, replica_groups=mesh['zh'=2,'zq'=4,'xx'=4,'fly'=16] {'xx'}, dimensions={0} | all-to-all | bytes 6291456 | tf_op jit(solution)/shard_map/all_to_all | solution.py:66
  150.6 3.6 %reduce_sum.33 = bf16[8,8,6,1024]{3,1,2,0:T(8,128)(2,1)} reduce(bf16[4,8,8,6,1024]{4,2,3,1,0:T(8,128)(2,1)} %all_to_all.25, bf16[]{:T(256)} %constant.26.clone.1), dimensions={0}, to_apply=%region_0.1 | reduce | flops 1179648 | bytes 3932162 | tf_op jit(solution)/shard_map/reduce_sum | solution.py:67
  154.3 2.1 copy.148
  156.4 4.2 %all-to-all-start.3 = ((bf16[4,2,8,6,1024]{4,2,3,1,0:T(8,128)(2,1)}), bf16[4,2,8,6,1024]{4,2,3,1,0:T(8,128)(2,1)}, u32[]{:S(2)}, u32[]{:S(2)}) async-start(bf16[4,2,8,6,1024]{4,2,3,1,0:T(8,128)(2,1)} %bitcast.154), calls=%async_computation.3 | async-start | bytes 1572864 | tf_op jit(solution)/shard_map/all_to_all | solution.py:68
  161.3 0.7 copy-done.11
  162.9 0.7 copy-done.6
  164.5 5.5 %collective-permute-start.13 = (bf16[128,512]{0,1:T(8,128)(2,1)S(1)}, bf16[128,512]{0,1:T(8,128)(2,1)S(1)}, u32[]{:S(2)}, u32[]{:S(2)}) collective-permute-start(bf16[128,512]{0,1:T(8,128)(2,1)S(1)} %bitcast.176), channel_id=1, source_target_pairs={{0,8},{8,0},{1,9},{9,1},{2,10},{10,2},{3,11},{11,3},{4,12},{12,4},... | collective-permute-start | bytes 393224 | tf_op jit(solution)/shard_map/ppermute | solution.py:23
  170.1 2.3 %collective-permute-start.12 = (bf16[128,512]{0,1:T(8,128)(2,1)S(1)}, bf16[128,512]{0,1:T(8,128)(2,1)S(1)}, u32[]{:S(2)}, u32[]{:S(2)}) collective-permute-start(bf16[128,512]{0,1:T(8,128)(2,1)S(1)} %bitcast.177), channel_id=1, source_target_pairs={{0,4},{4,0},{1,5},{5,1},{2,6},{6,2},{3,7},{7,3},{8,12},{12,8},{9,1... | collective-permute-start | bytes 393224 | tf_op jit(solution)/shard_map/ppermute | solution.py:23
  172.5 2.1 collective-permute-start.11
  174.7 6.1 %collective-permute-start.10 = (bf16[128,512]{0,1:T(8,128)(2,1)S(1)}, bf16[128,512]{0,1:T(8,128)(2,1)S(1)}, u32[]{:S(2)}, u32[]{:S(2)}) collective-permute-start(bf16[128,512]{0,1:T(8,128)(2,1)S(1)} %bitcast.179), channel_id=1, source_target_pairs={{0,1},{1,0},{2,3},{3,2},{4,5},{5,4},{6,7},{7,6},{8,9},{9,8},{10,11... | collective-permute-start | bytes 393224 | tf_op jit(solution)/shard_map/ppermute | solution.py:23
  180.8 10.0 %all-to-all-done.3 = bf16[4,2,8,6,1024]{4,2,3,1,0:T(8,128)(2,1)} async-done(((bf16[4,2,8,6,1024]{4,2,3,1,0:T(8,128)(2,1)}), bf16[4,2,8,6,1024]{4,2,3,1,0:T(8,128)(2,1)}, u32[]{:S(2)}, u32[]{:S(2)}) %all-to-all-start.3) | async-done | bytes 786464 | tf_op jit(solution)/shard_map/all_to_all | solution.py:68
  190.8 2.0 reduce_sum.34
  192.8 3.4 %all-to-all-start.4 = ((bf16[2,8,6,1024]{3,1,2,0:T(8,128)(2,1)}), bf16[2,8,6,1024]{3,1,2,0:T(8,128)(2,1)S(1)}, u32[]{:S(2)}, u32[]{:S(2)}) async-start(bf16[2,8,6,1024]{3,1,2,0:T(8,128)(2,1)} %reduce_sum.34), calls=%async_computation.4 | async-start | bytes 393216 | tf_op jit(solution)/shard_map/all_to_all | solution.py:70
  196.6 0.8 copy.129
  197.4 11.8 %all-to-all-done.4 = bf16[2,8,6,1024]{3,1,2,0:T(8,128)(2,1)S(1)} async-done(((bf16[2,8,6,1024]{3,1,2,0:T(8,128)(2,1)}), bf16[2,8,6,1024]{3,1,2,0:T(8,128)(2,1)S(1)}, u32[]{:S(2)}, u32[]{:S(2)}) %all-to-all-start.4) | async-done | bytes 196640 | tf_op jit(solution)/shard_map/all_to_all | solution.py:70
  209.2 0.7 multiply_bitcast_fusion
  (84 shorter events, 9.2 us)
Async XLA Ops:
  1.5 11.1 %collective-permute-start.4 = (bf16[1,6,8,512]{3,2,1,0:T(8,128)(2,1)S(1)}, bf16[1,6,8,512]{3,2,1,0:T(8,128)(2,1)S(1)}, u32[]{:S(2)}, u32[]{:S(2)}) collective-permute-start(bf16[1,6,8,512]{3,2,1,0:T(8,128)(2,1)S(1)} %get-tuple-element.21), channel_id=1, source_target_pairs={{0,256},{64,320},{128,384},{192,448},{256,0},{320,64},{384,128},{4... | collective-permute-start | bytes 147464 | tf_op jit(solution)/shard_map/ppermute | solution.py:46
  12.6 8.1 %collective-permute-start.5 = (bf16[2,1,6,8,512]{4,3,2,0,1:T(8,128)(2,1)S(1)}, bf16[2,1,6,8,512]{4,3,2,0,1:T(8,128)(2,1)S(1)}, u32[]{:S(2)}, u32[]{:S(2)}) collective-permute-start(bf16[2,1,6,8,512]{4,3,2,0,1:T(8,128)(2,1)S(1)} %maximum_select_fusion.5), channel_id=1, source_target_pairs={{0,128},{64,192},{128,0},{192,64},{256,384},{320,448},{384,256},{4... | collective-permute-start | bytes 294920 | tf_op jit(solution)/shard_map/ppermute | solution.py:46
  20.7 30.7 %collective-permute-start.6 = (bf16[2,2,1,6,8,512]{5,4,3,1,2,0:T(8,128)(2,1)S(1)}, bf16[2,2,1,6,8,512]{5,4,3,1,2,0:T(8,128)(2,1)S(1)}, u32[]{:S(2)}, u32[]{:S(2)}) collective-permute-start(bf16[2,2,1,6,8,512]{5,4,3,1,2,0:T(8,128)(2,1)S(1)} %bitcast_select_fusion), channel_id=1, source_target_pairs={{0,64},{64,0},{128,192},{192,128},{256,320},{320,256},{384,448},{4... | collective-permute-start | bytes 589832 | tf_op jit(solution)/shard_map/ppermute | solution.py:46
  25.2 44.7 %collective-permute-start = (bf16[128,512]{1,0:T(8,128)(2,1)}, bf16[128,512]{1,0:T(8,128)(2,1)S(1)}, u32[]{:S(2)}, u32[]{:S(2)}) collective-permute-start(bf16[128,512]{1,0:T(8,128)(2,1)} %param.4), channel_id=1, source_target_pairs={{0,1},{1,0},{2,3},{3,2},{4,5},{5,4},{6,7},{7,6},{8,9},{9,8},{10,11... | collective-permute-start | bytes 393224 | tf_op jit(solution)/shard_map/ppermute | solution.py:23
  30.0 40.0 %collective-permute-start.1 = (bf16[128,512]{1,0:T(8,128)(2,1)}, bf16[128,512]{1,0:T(8,128)(2,1)S(1)}, u32[]{:S(2)}, u32[]{:S(2)}) collective-permute-start(bf16[128,512]{1,0:T(8,128)(2,1)} %param.4), channel_id=1, source_target_pairs={{0,2},{2,0},{1,3},{3,1},{4,6},{6,4},{5,7},{7,5},{8,10},{10,8},{9,1... | collective-permute-start | bytes 393224 | tf_op jit(solution)/shard_map/ppermute | solution.py:23
  32.3 37.8 %collective-permute-start.2 = (bf16[128,512]{1,0:T(8,128)(2,1)}, bf16[128,512]{1,0:T(8,128)(2,1)S(1)}, u32[]{:S(2)}, u32[]{:S(2)}) collective-permute-start(bf16[128,512]{1,0:T(8,128)(2,1)} %param.4), channel_id=1, source_target_pairs={{0,4},{4,0},{1,5},{5,1},{2,6},{6,2},{3,7},{7,3},{8,12},{12,8},{9,1... | collective-permute-start | bytes 393224 | tf_op jit(solution)/shard_map/ppermute | solution.py:23
  36.8 33.4 %collective-permute-start.3 = (bf16[128,512]{1,0:T(8,128)(2,1)}, bf16[128,512]{1,0:T(8,128)(2,1)S(1)}, u32[]{:S(2)}, u32[]{:S(2)}) collective-permute-start(bf16[128,512]{1,0:T(8,128)(2,1)} %param.4), channel_id=1, source_target_pairs={{0,8},{8,0},{1,9},{9,1},{2,10},{10,2},{3,11},{11,3},{4,12},{12,4},... | collective-permute-start | bytes 393224 | tf_op jit(solution)/shard_map/ppermute | solution.py:23
  51.4 16.5 %collective-permute-start.7 = (bf16[1,6,8,512]{3,2,1,0:T(8,128)(2,1)S(1)}, bf16[1,6,8,512]{3,2,1,0:T(8,128)(2,1)S(1)}, u32[]{:S(2)}, u32[]{:S(2)}) collective-permute-start(bf16[1,6,8,512]{3,2,1,0:T(8,128)(2,1)S(1)} %get-tuple-element.20), channel_id=1, source_target_pairs={{0,256},{64,320},{128,384},{192,448},{256,0},{320,64},{384,128},{4... | collective-permute-start | bytes 147464 | tf_op jit(solution)/shard_map/ppermute | solution.py:46
  56.0 4.2 %copy-start.7 = (bf16[128,512]{1,0:T(8,128)(2,1)S(1)}, bf16[128,512]{1,0:T(8,128)(2,1)}, u32[]{:S(2)}) copy-start(bf16[128,512]{1,0:T(8,128)(2,1)} %param.4) | copy-start | bytes 393220
  56.0 28.5 %all-to-all-start = ((bf16[4,8,6,8,512]{4,3,1,2,0:T(8,128)(2,1)}), bf16[4,8,6,8,512]{4,3,1,2,0:T(8,128)(2,1)S(1)}, u32[]{:S(2)}, u32[]{:S(2)}) async-start(bf16[4,8,6,8,512]{4,3,1,2,0:T(8,128)(2,1)} %broadcast_in_dim.32), calls=%async_computation | async-start | bytes 3145728 | tf_op jit(solution)/shard_map/all_to_all | solution.py:59
  67.9 8.6 %collective-permute-start.8 = (bf16[2,1,6,8,512]{4,3,2,0,1:T(8,128)(2,1)S(1)}, bf16[2,1,6,8,512]{4,3,2,0,1:T(8,128)(2,1)S(1)}, u32[]{:S(2)}, u32[]{:S(2)}) collective-permute-start(bf16[2,1,6,8,512]{4,3,2,0,1:T(8,128)(2,1)S(1)} %fusion.16), channel_id=1, source_target_pairs={{0,128},{64,192},{128,0},{192,64},{256,384},{320,448},{384,256},{4... | collective-permute-start | bytes 294920 | tf_op jit(solution)/shard_map/ppermute | solution.py:46
  76.5 7.9 %collective-permute-start.9 = (bf16[2,2,1,6,8,512]{5,4,3,1,0,2:T(8,128)(2,1)S(1)}, bf16[2,2,1,6,8,512]{5,4,3,1,0,2:T(8,128)(2,1)S(1)}, u32[]{:S(2)}, u32[]{:S(2)}) collective-permute-start(bf16[2,2,1,6,8,512]{5,4,3,1,0,2:T(8,128)(2,1)S(1)} %maximum_select_fusion.3), channel_id=1, source_target_pairs={{0,64},{64,0},{128,192},{192,128},{256,320},{320,256},{384,448},{4... | collective-permute-start | bytes 589832 | tf_op jit(solution)/shard_map/ppermute | solution.py:46
  78.5 6.0 %copy-start.1 = (bf16[128,2,6,256]{0,3,2,1:T(8,128)(2,1)}, bf16[128,2,6,256]{0,3,2,1:T(8,128)(2,1)S(1)}, u32[]{:S(2)}) copy-start(bf16[128,2,6,256]{0,3,2,1:T(8,128)(2,1)S(1)} %constant_dynamic-update-slice_fusion.3) | copy-start | bytes 2359300
  85.9 23.2 %all-to-all-start.1 = ((bf16[4,8,6,8,512]{4,3,1,2,0:T(8,128)(2,1)}), bf16[4,8,6,8,512]{4,3,1,2,0:T(8,128)(2,1)S(1)}, u32[]{:S(2)}, u32[]{:S(2)}) async-start(bf16[4,8,6,8,512]{4,3,1,2,0:T(8,128)(2,1)} %broadcast_in_dim.36), calls=%async_computation.1 | async-start | bytes 3145728 | tf_op jit(solution)/shard_map/all_to_all | solution.py:59
  104.7 1.0 copy-start
  109.2 1.0 copy-start.2
  109.2 1.0 copy-start.9
  109.2 1.1 copy-start.10
  109.6 1.3 copy-start.5
  109.6 1.3 copy-start.3
  109.6 1.3 copy-start.4
  109.7 1.3 copy-start.8
  156.4 34.5 %all-to-all-start.3 = ((bf16[4,2,8,6,1024]{4,2,3,1,0:T(8,128)(2,1)}), bf16[4,2,8,6,1024]{4,2,3,1,0:T(8,128)(2,1)}, u32[]{:S(2)}, u32[]{:S(2)}) async-start(bf16[4,2,8,6,1024]{4,2,3,1,0:T(8,128)(2,1)} %bitcast.154), calls=%async_computation.3 | async-start | bytes 1572864 | tf_op jit(solution)/shard_map/all_to_all | solution.py:68
  161.0 1.0 copy-start.11
  162.6 1.0 copy-start.6
  164.5 32.0 %collective-permute-start.13 = (bf16[128,512]{0,1:T(8,128)(2,1)S(1)}, bf16[128,512]{0,1:T(8,128)(2,1)S(1)}, u32[]{:S(2)}, u32[]{:S(2)}) collective-permute-start(bf16[128,512]{0,1:T(8,128)(2,1)S(1)} %bitcast.176), channel_id=1, source_target_pairs={{0,8},{8,0},{1,9},{9,1},{2,10},{10,2},{3,11},{11,3},{4,12},{12,4},... | collective-permute-start | bytes 393224 | tf_op jit(solution)/shard_map/ppermute | solution.py:23
  170.1 26.4 %collective-permute-start.12 = (bf16[128,512]{0,1:T(8,128)(2,1)S(1)}, bf16[128,512]{0,1:T(8,128)(2,1)S(1)}, u32[]{:S(2)}, u32[]{:S(2)}) collective-permute-start(bf16[128,512]{0,1:T(8,128)(2,1)S(1)} %bitcast.177), channel_id=1, source_target_pairs={{0,4},{4,0},{1,5},{5,1},{2,6},{6,2},{3,7},{7,3},{8,12},{12,8},{9,1... | collective-permute-start | bytes 393224 | tf_op jit(solution)/shard_map/ppermute | solution.py:23
  172.5 24.0 %collective-permute-start.11 = (bf16[128,512]{0,1:T(8,128)(2,1)S(1)}, bf16[128,512]{0,1:T(8,128)(2,1)S(1)}, u32[]{:S(2)}, u32[]{:S(2)}) collective-permute-start(bf16[128,512]{0,1:T(8,128)(2,1)S(1)} %bitcast.178), channel_id=1, source_target_pairs={{0,2},{2,0},{1,3},{3,1},{4,6},{6,4},{5,7},{7,5},{8,10},{10,8},{9,1... | collective-permute-start | bytes 393224 | tf_op jit(solution)/shard_map/ppermute | solution.py:23
  174.7 21.8 %collective-permute-start.10 = (bf16[128,512]{0,1:T(8,128)(2,1)S(1)}, bf16[128,512]{0,1:T(8,128)(2,1)S(1)}, u32[]{:S(2)}, u32[]{:S(2)}) collective-permute-start(bf16[128,512]{0,1:T(8,128)(2,1)S(1)} %bitcast.179), channel_id=1, source_target_pairs={{0,1},{1,0},{2,3},{3,2},{4,5},{5,4},{6,7},{7,6},{8,9},{9,8},{10,11... | collective-permute-start | bytes 393224 | tf_op jit(solution)/shard_map/ppermute | solution.py:23
  192.8 16.3 %all-to-all-start.4 = ((bf16[2,8,6,1024]{3,1,2,0:T(8,128)(2,1)}), bf16[2,8,6,1024]{3,1,2,0:T(8,128)(2,1)S(1)}, u32[]{:S(2)}, u32[]{:S(2)}) async-start(bf16[2,8,6,1024]{3,1,2,0:T(8,128)(2,1)} %reduce_sum.34), calls=%async_computation.4 | async-start | bytes 393216 | tf_op jit(solution)/shard_map/all_to_all | solution.py:70

commit v11 on v10

--- a/solution.py
+++ b/solution.py
@@ -67,8 +67,10 @@
     part = got.astype(jnp.float32).sum(0).reshape(halves, zl // halves, own, factor_count, width)
     got = lax.all_to_all(part.transpose(1, 0, 2, 3, 4).astype(jnp.bfloat16), QUARTER, 0, 0, tiled=True)
     part = got.astype(jnp.float32).sum(0)
-    got = lax.all_to_all(part.astype(jnp.bfloat16), HALF, 0, 0, tiled=True)
-    part = got.astype(jnp.float32).sum(0)
+    sent = part.astype(jnp.bfloat16)
+    place = lax.axis_index(HALF)
+    got = lax.ppermute(lax.dynamic_index_in_dim(sent, 1 - place, 0, keepdims=False), HALF, [(0, 1), (1, 0)])
+    part = lax.dynamic_index_in_dim(sent, place, 0, keepdims=False).astype(jnp.float32) + got.astype(jnp.float32)
     return part.transpose(1, 0, 2)
 
 

time: 211 us -> 209 us (level)
    all_to_all x1 -> x0, waiting for transfers between devices: 11.8 us -> none  [scatter_rows(): got = lax.all_to_all(part.astype(jnp.bfloat16), HALF, 0, 0, tiled=True)]
    ppermute x0 -> x1, waiting for transfers between devices: none -> 11.7 us  [scatter_rows(): lax.ppermute(lax.dynamic_index_in_dim(sent, 1 - place, 0, keepdims=False)...]
    all_to_all x1 -> x0, starting transfers between devices: 3.43 us -> none  [scatter_rows(): got = lax.all_to_all(part.astype(jnp.bfloat16), HALF, 0, 0, tiled=True)]
where the time goes in v11:
time: 209 us; the launch traced here: 207 us
  starting transfers between devices  82.6 us (40%)
  waiting for transfers between devices  46.2 us (22%)
  blocking collectives  38.5 us (18%)
  local copies, waits for them, and re-layouts  27.5 us (13%)
  other arithmetic  7.19 us (3%)
  matrix products  4.06 us (2%)
    ppermute x8, starting transfers between devices, partner_2(): return lax.ppermute(block, axis, route)  41.2 us
    all_to_all x1, blocking collectives, scatter_rows(): got = lax.all_to_all(terms, COLS, 0, 0, tiled=True)  38.5 us
    ppermute x6, starting transfers between devices, gather_line(): got = lax.ppermute(held, axis, [(i, i ^ dist) for i in range(count)])  27.1 us
    ppermute x6, waiting for transfers between devices, gather_line(): got = lax.ppermute(held, axis, [(i, i ^ dist) for i in range(count)])  22.3 us
    ppermute x1, waiting for transfers between devices, scatter_rows(): lax.ppermute(lax.dynamic_index_in_dim(sent, 1 - place, 0, keepdims=False)...  11.7 us
    all_to_all x1, waiting for transfers between devices, scatter_rows(): lax.all_to_all(part.transpose(1, 0, 2, 3, 4).astype(jnp.bfloat16), QUARTE...  9.81 us
    all_to_all x2, starting transfers between devices, gather_rows(): both = lax.all_to_all(copies, COLS, 0, 0, tiled=True)  8.16 us
    unnamed x35, local copies, waits for them, and re-layouts  6.71 us
  transfers between devices with their start and end apart: 18, of which 8 were waited for; matrix products, arithmetic and copies ran while one was open for 12% of the time, Pallas kernels for 0%

profile of v11, /device:TPU:1, one launch (start us, length us, event | category | flops | bytes accessed | tf_op | source)
XLA Modules:
  0.0 207.4 jit_solution(11439233080632037731)
XLA Ops:
  0.6 0.8 slice_bitcast_fusion
  1.5 9.6 %collective-permute-start.4 = (bf16[1,6,8,512]{3,2,1,0:T(8,128)(2,1)S(1)}, bf16[1,6,8,512]{3,2,1,0:T(8,128)(2,1)S(1)}, u32[]{:S(2)}, u32[]{:S(2)}) collective-permute-start(bf16[1,6,8,512]{3,2,1,0:T(8,128)(2,1)S(1)} %get-tuple-element.21), channel_id=1, source_target_pairs={{0,256},{64,320},{128,384},{192,448},{256,0},{320,64},{384,128},{4... | collective-permute-start | bytes 147464 | tf_op jit(solution)/shard_map/ppermute | solution.py:46
  11.1 1.5 collective-permute-done.4
  12.6 6.1 %collective-permute-start.5 = (bf16[2,1,6,8,512]{4,3,2,0,1:T(8,128)(2,1)S(1)}, bf16[2,1,6,8,512]{4,3,2,0,1:T(8,128)(2,1)S(1)}, u32[]{:S(2)}, u32[]{:S(2)}) collective-permute-start(bf16[2,1,6,8,512]{4,3,2,0,1:T(8,128)(2,1)S(1)} %maximum_select_fusion.5), channel_id=1, source_target_pairs={{0,128},{64,192},{128,0},{192,64},{256,384},{320,448},{384,256},{4... | collective-permute-start | bytes 294920 | tf_op jit(solution)/shard_map/ppermute | solution.py:46
  18.7 2.0 collective-permute-done.5
  20.7 4.5 %collective-permute-start.6 = (bf16[2,2,1,6,8,512]{5,4,3,1,2,0:T(8,128)(2,1)S(1)}, bf16[2,2,1,6,8,512]{5,4,3,1,2,0:T(8,128)(2,1)S(1)}, u32[]{:S(2)}, u32[]{:S(2)}) collective-permute-start(bf16[2,2,1,6,8,512]{5,4,3,1,2,0:T(8,128)(2,1)S(1)} %bitcast_select_fusion), channel_id=1, source_target_pairs={{0,64},{64,0},{128,192},{192,128},{256,320},{320,256},{384,448},{4... | collective-permute-start | bytes 589832 | tf_op jit(solution)/shard_map/ppermute | solution.py:46
  25.2 4.8 %collective-permute-start = (bf16[128,512]{1,0:T(8,128)(2,1)}, bf16[128,512]{1,0:T(8,128)(2,1)S(1)}, u32[]{:S(2)}, u32[]{:S(2)}) collective-permute-start(bf16[128,512]{1,0:T(8,128)(2,1)} %param.4), channel_id=1, source_target_pairs={{0,1},{1,0},{2,3},{3,2},{4,5},{5,4},{6,7},{7,6},{8,9},{9,8},{10,11... | collective-permute-start | bytes 393224 | tf_op jit(solution)/shard_map/ppermute | solution.py:23
  30.0 2.3 %collective-permute-start.1 = (bf16[128,512]{1,0:T(8,128)(2,1)}, bf16[128,512]{1,0:T(8,128)(2,1)S(1)}, u32[]{:S(2)}, u32[]{:S(2)}) collective-permute-start(bf16[128,512]{1,0:T(8,128)(2,1)} %param.4), channel_id=1, source_target_pairs={{0,2},{2,0},{1,3},{3,1},{4,6},{6,4},{5,7},{7,5},{8,10},{10,8},{9,1... | collective-permute-start | bytes 393224 | tf_op jit(solution)/shard_map/ppermute | solution.py:23
  32.3 4.5 %collective-permute-start.2 = (bf16[128,512]{1,0:T(8,128)(2,1)}, bf16[128,512]{1,0:T(8,128)(2,1)S(1)}, u32[]{:S(2)}, u32[]{:S(2)}) collective-permute-start(bf16[128,512]{1,0:T(8,128)(2,1)} %param.4), channel_id=1, source_target_pairs={{0,4},{4,0},{1,5},{5,1},{2,6},{6,2},{3,7},{7,3},{8,12},{12,8},{9,1... | collective-permute-start | bytes 393224 | tf_op jit(solution)/shard_map/ppermute | solution.py:23
  36.8 13.6 %collective-permute-start.3 = (bf16[128,512]{1,0:T(8,128)(2,1)}, bf16[128,512]{1,0:T(8,128)(2,1)S(1)}, u32[]{:S(2)}, u32[]{:S(2)}) collective-permute-start(bf16[128,512]{1,0:T(8,128)(2,1)} %param.4), channel_id=1, source_target_pairs={{0,8},{8,0},{1,9},{9,1},{2,10},{10,2},{3,11},{11,3},{4,12},{12,4},... | collective-permute-start | bytes 393224 | tf_op jit(solution)/shard_map/ppermute | solution.py:23
  50.5 0.8 copy.113
  51.4 3.1 %collective-permute-start.7 = (bf16[1,6,8,512]{3,2,1,0:T(8,128)(2,1)S(1)}, bf16[1,6,8,512]{3,2,1,0:T(8,128)(2,1)S(1)}, u32[]{:S(2)}, u32[]{:S(2)}) collective-permute-start(bf16[1,6,8,512]{3,2,1,0:T(8,128)(2,1)S(1)} %get-tuple-element.20), channel_id=1, source_target_pairs={{0,256},{64,320},{128,384},{192,448},{256,0},{320,64},{384,128},{4... | collective-permute-start | bytes 147464 | tf_op jit(solution)/shard_map/ppermute | solution.py:46
  54.6 1.4 broadcast_in_dim.32
  56.0 4.1 %all-to-all-start = ((bf16[4,8,6,8,512]{4,3,1,2,0:T(8,128)(2,1)}), bf16[4,8,6,8,512]{4,3,1,2,0:T(8,128)(2,1)S(1)}, u32[]{:S(2)}, u32[]{:S(2)}) async-start(bf16[4,8,6,8,512]{4,3,1,2,0:T(8,128)(2,1)} %broadcast_in_dim.32), calls=%async_computation | async-start | bytes 3145728 | tf_op jit(solution)/shard_map/all_to_all | solution.py:59
  60.9 6.9 %collective-permute-done.7 = bf16[1,6,8,512]{3,2,1,0:T(8,128)(2,1)S(1)} collective-permute-done((bf16[1,6,8,512]{3,2,1,0:T(8,128)(2,1)S(1)}, bf16[1,6,8,512]{3,2,1,0:T(8,128)(2,1)S(1)}, u32[]{:S(2)}, u32[]{:S(2)}) %collective-permute-start.7) | collective-permute-done | bytes 49184 | tf_op jit(solution)/shard_map/ppermute | solution.py:46
  67.9 1.9 collective-permute-start.8
  70.4 6.1 %collective-permute-done.8 = bf16[2,1,6,8,512]{4,3,2,0,1:T(8,128)(2,1)S(1)} collective-permute-done((bf16[2,1,6,8,512]{4,3,2,0,1:T(8,128)(2,1)S(1)}, bf16[2,1,6,8,512]{4,3,2,0,1:T(8,128)(2,1)S(1)}, u32[]{:S(2)}, u32[]{:S(2)}) %collective-permute-start.8) | collective-permute-done | bytes 98336 | tf_op jit(solution)/shard_map/ppermute | solution.py:46
  76.5 1.9 collective-permute-start.9
  78.5 5.9 %collective-permute-done.9 = bf16[2,2,1,6,8,512]{5,4,3,1,0,2:T(8,128)(2,1)S(1)} collective-permute-done((bf16[2,2,1,6,8,512]{5,4,3,1,0,2:T(8,128)(2,1)S(1)}, bf16[2,2,1,6,8,512]{5,4,3,1,0,2:T(8,128)(2,1)S(1)}, u32[]{:S(2)}, u32[]{:S(2)}) %collective-permute-start.9) | collective-permute-done | bytes 196640 | tf_op jit(solution)/shard_map/ppermute | solution.py:46
  84.5 1.4 broadcast_in_dim.36
  85.9 4.0 %all-to-all-start.1 = ((bf16[4,8,6,8,512]{4,3,1,2,0:T(8,128)(2,1)}), bf16[4,8,6,8,512]{4,3,1,2,0:T(8,128)(2,1)S(1)}, u32[]{:S(2)}, u32[]{:S(2)}) async-start(bf16[4,8,6,8,512]{4,3,1,2,0:T(8,128)(2,1)} %broadcast_in_dim.36), calls=%async_computation.1 | async-start | bytes 3145728 | tf_op jit(solution)/shard_map/all_to_all | solution.py:59
  90.5 0.7 constant_dynamic-update-slice_fusion.1
  91.9 1.9 fusion.24
  93.8 1.1 copy.126
  94.8 1.9 reshape.937
  96.8 1.9 dot_general.40
  98.7 2.1 copy.124
  100.8 1.9 reshape.936
  102.7 1.9 dot_general.37
  104.7 0.9 copy-done
  105.6 1.1 fusion.25
  106.7 2.4 %all-to-all-done.1 = bf16[4,8,6,8,512]{4,3,1,2,0:T(8,128)(2,1)S(1)} async-done(((bf16[4,8,6,8,512]{4,3,1,2,0:T(8,128)(2,1)}), bf16[4,8,6,8,512]{4,3,1,2,0:T(8,128)(2,1)S(1)}, u32[]{:S(2)}, u32[]{:S(2)}) %all-to-all-start.1) | async-done | bytes 1572896 | tf_op jit(solution)/shard_map/all_to_all | solution.py:59
  112.1 38.5 %all_to_all.20 = bf16[4,8,8,6,1024]{4,2,3,1,0:T(8,128)(2,1)} all-to-all(bf16[4,8,8,6,1024]{4,2,3,1,0:T(8,128)(2,1)S(1)} %pad_maximum_fusion), channel_id=1, replica_groups=mesh['zh'=2,'zq'=4,'xx'=4,'fly'=16] {'xx'}, dimensions={0} | all-to-all | bytes 6291456 | tf_op jit(solution)/shard_map/all_to_all | solution.py:66
  150.6 3.6 %reduce_sum.24 = bf16[8,8,6,1024]{3,1,2,0:T(8,128)(2,1)} reduce(bf16[4,8,8,6,1024]{4,2,3,1,0:T(8,128)(2,1)} %all_to_all.20, bf16[]{:T(256)} %constant.33.clone.1), dimensions={0}, to_apply=%region_0.1 | reduce | flops 1179648 | bytes 3932162 | tf_op jit(solution)/shard_map/reduce_sum | solution.py:67
  154.3 2.1 %copy.148 = bf16[2,4,8,6,1024]{4,2,3,0,1:T(8,128)(2,1)} copy(bf16[2,4,8,6,1024]{4,2,3,1,0:T(8,128)(2,1)} %bitcast.160) | data formatting | bytes 1572864 | tf_op jit(solution)/shard_map/convert_element_type | solution.py:68
  156.4 4.2 %all-to-all-start.3 = ((bf16[4,2,8,6,1024]{4,2,3,1,0:T(8,128)(2,1)}), bf16[4,2,8,6,1024]{4,2,3,1,0:T(8,128)(2,1)}, u32[]{:S(2)}, u32[]{:S(2)}) async-start(bf16[4,2,8,6,1024]{4,2,3,1,0:T(8,128)(2,1)} %bitcast.159), calls=%async_computation.3 | async-start | bytes 1572864 | tf_op jit(solution)/shard_map/all_to_all | solution.py:68
  161.2 0.7 copy-done.11
  162.8 0.7 copy-done.6
  164.5 5.5 %collective-permute-start.13 = (bf16[128,512]{0,1:T(8,128)(2,1)S(1)}, bf16[128,512]{0,1:T(8,128)(2,1)S(1)}, u32[]{:S(2)}, u32[]{:S(2)}) collective-permute-start(bf16[128,512]{0,1:T(8,128)(2,1)S(1)} %bitcast.181), channel_id=1, source_target_pairs={{0,8},{8,0},{1,9},{9,1},{2,10},{10,2},{3,11},{11,3},{4,12},{12,4},... | collective-permute-start | bytes 393224 | tf_op jit(solution)/shard_map/ppermute | solution.py:23
  170.1 2.2 %collective-permute-start.12 = (bf16[128,512]{0,1:T(8,128)(2,1)S(1)}, bf16[128,512]{0,1:T(8,128)(2,1)S(1)}, u32[]{:S(2)}, u32[]{:S(2)}) collective-permute-start(bf16[128,512]{0,1:T(8,128)(2,1)S(1)} %bitcast.182), channel_id=1, source_target_pairs={{0,4},{4,0},{1,5},{5,1},{2,6},{6,2},{3,7},{7,3},{8,12},{12,8},{9,1... | collective-permute-start | bytes 393224 | tf_op jit(solution)/shard_map/ppermute | solution.py:23
  172.5 2.1 %collective-permute-start.11 = (bf16[128,512]{0,1:T(8,128)(2,1)S(1)}, bf16[128,512]{0,1:T(8,128)(2,1)S(1)}, u32[]{:S(2)}, u32[]{:S(2)}) collective-permute-start(bf16[128,512]{0,1:T(8,128)(2,1)S(1)} %bitcast.183), channel_id=1, source_target_pairs={{0,2},{2,0},{1,3},{3,1},{4,6},{6,4},{5,7},{7,5},{8,10},{10,8},{9,1... | collective-permute-start | bytes 393224 | tf_op jit(solution)/shard_map/ppermute | solution.py:23
  174.7 6.1 %collective-permute-start.10 = (bf16[128,512]{0,1:T(8,128)(2,1)S(1)}, bf16[128,512]{0,1:T(8,128)(2,1)S(1)}, u32[]{:S(2)}, u32[]{:S(2)}) collective-permute-start(bf16[128,512]{0,1:T(8,128)(2,1)S(1)} %bitcast.184), channel_id=1, source_target_pairs={{0,1},{1,0},{2,3},{3,2},{4,5},{5,4},{6,7},{7,6},{8,9},{9,8},{10,11... | collective-permute-start | bytes 393224 | tf_op jit(solution)/shard_map/ppermute | solution.py:23
  181.0 9.8 %all-to-all-done.3 = bf16[4,2,8,6,1024]{4,2,3,1,0:T(8,128)(2,1)} async-done(((bf16[4,2,8,6,1024]{4,2,3,1,0:T(8,128)(2,1)}), bf16[4,2,8,6,1024]{4,2,3,1,0:T(8,128)(2,1)}, u32[]{:S(2)}, u32[]{:S(2)}) %all-to-all-start.3) | async-done | bytes 786464 | tf_op jit(solution)/shard_map/all_to_all | solution.py:68
  190.8 1.3 reduce_sum.25
  192.1 1.9 collective-permute-start.14
  194.2 0.8 copy.129
  195.0 11.7 %collective-permute-done.14 = bf16[8,6,1024]{2,0,1:T(8,128)(2,1)S(1)} collective-permute-done((bf16[8,6,1024]{2,0,1:T(8,128)(2,1)S(1)}, bf16[8,6,1024]{2,0,1:T(8,128)(2,1)S(1)}, u32[]{:S(2)}, u32[]{:S(2)}) %collective-permute-start.14) | collective-permute-done | bytes 98336 | tf_op jit(solution)/shard_map/ppermute | solution.py:72
  206.7 0.7 fusion.12
  (84 shorter events, 9.1 us)
Async XLA Ops:
  1.5 11.1 %collective-permute-start.4 = (bf16[1,6,8,512]{3,2,1,0:T(8,128)(2,1)S(1)}, bf16[1,6,8,512]{3,2,1,0:T(8,128)(2,1)S(1)}, u32[]{:S(2)}, u32[]{:S(2)}) collective-permute-start(bf16[1,6,8,512]{3,2,1,0:T(8,128)(2,1)S(1)} %get-tuple-element.21), channel_id=1, source_target_pairs={{0,256},{64,320},{128,384},{192,448},{256,0},{320,64},{384,128},{4... | collective-permute-start | bytes 147464 | tf_op jit(solution)/shard_map/ppermute | solution.py:46
  12.6 8.1 %collective-permute-start.5 = (bf16[2,1,6,8,512]{4,3,2,0,1:T(8,128)(2,1)S(1)}, bf16[2,1,6,8,512]{4,3,2,0,1:T(8,128)(2,1)S(1)}, u32[]{:S(2)}, u32[]{:S(2)}) collective-permute-start(bf16[2,1,6,8,512]{4,3,2,0,1:T(8,128)(2,1)S(1)} %maximum_select_fusion.5), channel_id=1, source_target_pairs={{0,128},{64,192},{128,0},{192,64},{256,384},{320,448},{384,256},{4... | collective-permute-start | bytes 294920 | tf_op jit(solution)/shard_map/ppermute | solution.py:46
  20.7 30.7 %collective-permute-start.6 = (bf16[2,2,1,6,8,512]{5,4,3,1,2,0:T(8,128)(2,1)S(1)}, bf16[2,2,1,6,8,512]{5,4,3,1,2,0:T(8,128)(2,1)S(1)}, u32[]{:S(2)}, u32[]{:S(2)}) collective-permute-start(bf16[2,2,1,6,8,512]{5,4,3,1,2,0:T(8,128)(2,1)S(1)} %bitcast_select_fusion), channel_id=1, source_target_pairs={{0,64},{64,0},{128,192},{192,128},{256,320},{320,256},{384,448},{4... | collective-permute-start | bytes 589832 | tf_op jit(solution)/shard_map/ppermute | solution.py:46
  25.2 44.7 %collective-permute-start = (bf16[128,512]{1,0:T(8,128)(2,1)}, bf16[128,512]{1,0:T(8,128)(2,1)S(1)}, u32[]{:S(2)}, u32[]{:S(2)}) collective-permute-start(bf16[128,512]{1,0:T(8,128)(2,1)} %param.4), channel_id=1, source_target_pairs={{0,1},{1,0},{2,3},{3,2},{4,5},{5,4},{6,7},{7,6},{8,9},{9,8},{10,11... | collective-permute-start | bytes 393224 | tf_op jit(solution)/shard_map/ppermute | solution.py:23
  30.0 40.0 %collective-permute-start.1 = (bf16[128,512]{1,0:T(8,128)(2,1)}, bf16[128,512]{1,0:T(8,128)(2,1)S(1)}, u32[]{:S(2)}, u32[]{:S(2)}) collective-permute-start(bf16[128,512]{1,0:T(8,128)(2,1)} %param.4), channel_id=1, source_target_pairs={{0,2},{2,0},{1,3},{3,1},{4,6},{6,4},{5,7},{7,5},{8,10},{10,8},{9,1... | collective-permute-start | bytes 393224 | tf_op jit(solution)/shard_map/ppermute | solution.py:23
  32.3 37.8 %collective-permute-start.2 = (bf16[128,512]{1,0:T(8,128)(2,1)}, bf16[128,512]{1,0:T(8,128)(2,1)S(1)}, u32[]{:S(2)}, u32[]{:S(2)}) collective-permute-start(bf16[128,512]{1,0:T(8,128)(2,1)} %param.4), channel_id=1, source_target_pairs={{0,4},{4,0},{1,5},{5,1},{2,6},{6,2},{3,7},{7,3},{8,12},{12,8},{9,1... | collective-permute-start | bytes 393224 | tf_op jit(solution)/shard_map/ppermute | solution.py:23
  36.8 33.4 %collective-permute-start.3 = (bf16[128,512]{1,0:T(8,128)(2,1)}, bf16[128,512]{1,0:T(8,128)(2,1)S(1)}, u32[]{:S(2)}, u32[]{:S(2)}) collective-permute-start(bf16[128,512]{1,0:T(8,128)(2,1)} %param.4), channel_id=1, source_target_pairs={{0,8},{8,0},{1,9},{9,1},{2,10},{10,2},{3,11},{11,3},{4,12},{12,4},... | collective-permute-start | bytes 393224 | tf_op jit(solution)/shard_map/ppermute | solution.py:23
  51.4 16.5 %collective-permute-start.7 = (bf16[1,6,8,512]{3,2,1,0:T(8,128)(2,1)S(1)}, bf16[1,6,8,512]{3,2,1,0:T(8,128)(2,1)S(1)}, u32[]{:S(2)}, u32[]{:S(2)}) collective-permute-start(bf16[1,6,8,512]{3,2,1,0:T(8,128)(2,1)S(1)} %get-tuple-element.20), channel_id=1, source_target_pairs={{0,256},{64,320},{128,384},{192,448},{256,0},{320,64},{384,128},{4... | collective-permute-start | bytes 147464 | tf_op jit(solution)/shard_map/ppermute | solution.py:46
  56.0 4.2 %copy-start.7 = (bf16[128,512]{1,0:T(8,128)(2,1)S(1)}, bf16[128,512]{1,0:T(8,128)(2,1)}, u32[]{:S(2)}) copy-start(bf16[128,512]{1,0:T(8,128)(2,1)} %param.4) | copy-start | bytes 393220
  56.0 28.5 %all-to-all-start = ((bf16[4,8,6,8,512]{4,3,1,2,0:T(8,128)(2,1)}), bf16[4,8,6,8,512]{4,3,1,2,0:T(8,128)(2,1)S(1)}, u32[]{:S(2)}, u32[]{:S(2)}) async-start(bf16[4,8,6,8,512]{4,3,1,2,0:T(8,128)(2,1)} %broadcast_in_dim.32), calls=%async_computation | async-start | bytes 3145728 | tf_op jit(solution)/shard_map/all_to_all | solution.py:59
  67.9 8.6 %collective-permute-start.8 = (bf16[2,1,6,8,512]{4,3,2,0,1:T(8,128)(2,1)S(1)}, bf16[2,1,6,8,512]{4,3,2,0,1:T(8,128)(2,1)S(1)}, u32[]{:S(2)}, u32[]{:S(2)}) collective-permute-start(bf16[2,1,6,8,512]{4,3,2,0,1:T(8,128)(2,1)S(1)} %fusion.18), channel_id=1, source_target_pairs={{0,128},{64,192},{128,0},{192,64},{256,384},{320,448},{384,256},{4... | collective-permute-start | bytes 294920 | tf_op jit(solution)/shard_map/ppermute | solution.py:46
  76.5 7.9 %collective-permute-start.9 = (bf16[2,2,1,6,8,512]{5,4,3,1,0,2:T(8,128)(2,1)S(1)}, bf16[2,2,1,6,8,512]{5,4,3,1,0,2:T(8,128)(2,1)S(1)}, u32[]{:S(2)}, u32[]{:S(2)}) collective-permute-start(bf16[2,2,1,6,8,512]{5,4,3,1,0,2:T(8,128)(2,1)S(1)} %maximum_select_fusion.3), channel_id=1, source_target_pairs={{0,64},{64,0},{128,192},{192,128},{256,320},{320,256},{384,448},{4... | collective-permute-start | bytes 589832 | tf_op jit(solution)/shard_map/ppermute | solution.py:46
  78.5 6.0 %copy-start.1 = (bf16[128,2,6,256]{0,3,2,1:T(8,128)(2,1)}, bf16[128,2,6,256]{0,3,2,1:T(8,128)(2,1)S(1)}, u32[]{:S(2)}) copy-start(bf16[128,2,6,256]{0,3,2,1:T(8,128)(2,1)S(1)} %constant_dynamic-update-slice_fusion.3) | copy-start | bytes 2359300
  85.9 23.2 %all-to-all-start.1 = ((bf16[4,8,6,8,512]{4,3,1,2,0:T(8,128)(2,1)}), bf16[4,8,6,8,512]{4,3,1,2,0:T(8,128)(2,1)S(1)}, u32[]{:S(2)}, u32[]{:S(2)}) async-start(bf16[4,8,6,8,512]{4,3,1,2,0:T(8,128)(2,1)} %broadcast_in_dim.36), calls=%async_computation.1 | async-start | bytes 3145728 | tf_op jit(solution)/shard_map/all_to_all | solution.py:59
  104.6 1.0 copy-start
  109.2 1.0 copy-start.2
  109.2 1.0 copy-start.9
  109.2 1.1 copy-start.10
  109.6 1.3 copy-start.5
  109.6 1.3 copy-start.3
  109.6 1.3 copy-start.4
  109.6 1.3 copy-start.8
  156.4 34.5 %all-to-all-start.3 = ((bf16[4,2,8,6,1024]{4,2,3,1,0:T(8,128)(2,1)}), bf16[4,2,8,6,1024]{4,2,3,1,0:T(8,128)(2,1)}, u32[]{:S(2)}, u32[]{:S(2)}) async-start(bf16[4,2,8,6,1024]{4,2,3,1,0:T(8,128)(2,1)} %bitcast.159), calls=%async_computation.3 | async-start | bytes 1572864 | tf_op jit(solution)/shard_map/all_to_all | solution.py:68
  161.0 1.0 copy-start.11
  162.6 1.0 copy-start.6
  164.5 29.6 %collective-permute-start.13 = (bf16[128,512]{0,1:T(8,128)(2,1)S(1)}, bf16[128,512]{0,1:T(8,128)(2,1)S(1)}, u32[]{:S(2)}, u32[]{:S(2)}) collective-permute-start(bf16[128,512]{0,1:T(8,128)(2,1)S(1)} %bitcast.181), channel_id=1, source_target_pairs={{0,8},{8,0},{1,9},{9,1},{2,10},{10,2},{3,11},{11,3},{4,12},{12,4},... | collective-permute-start | bytes 393224 | tf_op jit(solution)/shard_map/ppermute | solution.py:23
  170.1 23.9 %collective-permute-start.12 = (bf16[128,512]{0,1:T(8,128)(2,1)S(1)}, bf16[128,512]{0,1:T(8,128)(2,1)S(1)}, u32[]{:S(2)}, u32[]{:S(2)}) collective-permute-start(bf16[128,512]{0,1:T(8,128)(2,1)S(1)} %bitcast.182), channel_id=1, source_target_pairs={{0,4},{4,0},{1,5},{5,1},{2,6},{6,2},{3,7},{7,3},{8,12},{12,8},{9,1... | collective-permute-start | bytes 393224 | tf_op jit(solution)/shard_map/ppermute | solution.py:23
  172.5 21.6 %collective-permute-start.11 = (bf16[128,512]{0,1:T(8,128)(2,1)S(1)}, bf16[128,512]{0,1:T(8,128)(2,1)S(1)}, u32[]{:S(2)}, u32[]{:S(2)}) collective-permute-start(bf16[128,512]{0,1:T(8,128)(2,1)S(1)} %bitcast.183), channel_id=1, source_target_pairs={{0,2},{2,0},{1,3},{3,1},{4,6},{6,4},{5,7},{7,5},{8,10},{10,8},{9,1... | collective-permute-start | bytes 393224 | tf_op jit(solution)/shard_map/ppermute | solution.py:23
  174.7 19.4 %collective-permute-start.10 = (bf16[128,512]{0,1:T(8,128)(2,1)S(1)}, bf16[128,512]{0,1:T(8,128)(2,1)S(1)}, u32[]{:S(2)}, u32[]{:S(2)}) collective-permute-start(bf16[128,512]{0,1:T(8,128)(2,1)S(1)} %bitcast.184), channel_id=1, source_target_pairs={{0,1},{1,0},{2,3},{3,2},{4,5},{5,4},{6,7},{7,6},{8,9},{9,8},{10,11... | collective-permute-start | bytes 393224 | tf_op jit(solution)/shard_map/ppermute | solution.py:23
  192.1 14.6 %collective-permute-start.14 = (bf16[8,6,1024]{2,0,1:T(8,128)(2,1)S(1)}, bf16[8,6,1024]{2,0,1:T(8,128)(2,1)S(1)}, u32[]{:S(2)}, u32[]{:S(2)}) collective-permute-start(bf16[8,6,1024]{2,0,1:T(8,128)(2,1)S(1)} %dynamic-slice_bitcast_fusion), channel_id=1, source_target_pairs={{0,256},{256,0},{1,257},{257,1},{2,258},{258,2},{3,259},{259,3},{4... | collective-permute-start | bytes 294920 | tf_op jit(solution)/shard_map/ppermute | solution.py:72

commit v12 on v11

--- a/solution.py
+++ b/solution.py
@@ -65,8 +65,15 @@
     halves = lax.axis_size(HALF)
     got = lax.all_to_all(terms, COLS, 0, 0, tiled=True)
     part = got.astype(jnp.float32).sum(0).reshape(halves, zl // halves, own, factor_count, width)
-    got = lax.all_to_all(part.transpose(1, 0, 2, 3, 4).astype(jnp.bfloat16), QUARTER, 0, 0, tiled=True)
-    part = got.astype(jnp.float32).sum(0)
+    data = part.transpose(1, 0, 2, 3, 4).astype(jnp.bfloat16)
+    count = lax.axis_size(QUARTER)
+    at = lax.axis_index(QUARTER)
+    part = lax.dynamic_index_in_dim(data, at, 0, keepdims=False).astype(jnp.float32)
+    for step in range(1, count):
+        got = lax.ppermute(
+            lax.dynamic_index_in_dim(data, at ^ step, 0, keepdims=False), QUARTER, [(i, i ^ step) for i in range(count)]
+        )
+        part = part + got.astype(jnp.float32)
     sent = part.astype(jnp.bfloat16)
     place = lax.axis_index(HALF)
     got = lax.ppermute(lax.dynamic_index_in_dim(sent, 1 - place, 0, keepdims=False), HALF, [(0, 1), (1, 0)])

time: 209 us -> 208 us (level)
  blocking collectives: 38.5 us -> 0 us
  waiting for transfers between devices: 46.2 us -> 78.6 us
  starting transfers between devices: 82.6 us -> 89.8 us
    all_to_all x1 -> x0, blocking collectives: 38.5 us -> none  [scatter_rows(): got = lax.all_to_all(terms, COLS, 0, 0, tiled=True)]
    all_to_all x1, waiting for transfers between devices: 9.81 us -> 31.3 us  [scatter_rows(): got = lax.all_to_all(terms, COLS, 0, 0, tiled=True)]
    ppermute x0 -> x3, waiting for transfers between devices: none -> 11.1 us  [scatter_rows(): lax.ppermute(lax.dynamic_index_in_dim(data, at ^ step, 0, keepdims=False)...]
    ppermute x0 -> x3, starting transfers between devices: none -> 9.26 us  [scatter_rows(): lax.ppermute(lax.dynamic_index_in_dim(data, at ^ step, 0, keepdims=False)...]
    ppermute x8, starting transfers between devices: 41.2 us -> 38.7 us  [partner_2(): return lax.ppermute(block, axis, route)]
  transfers between devices with their start and end apart: 18 -> 21, of which waited for: 8 -> 9; matrix products, arithmetic and copies ran while one was open for 12% -> 11% of each run, Pallas kernels for 0% -> 0%
where the time goes in v12:
time: 208 us; the launch traced here: 207 us
  starting transfers between devices  89.8 us (43%)
  waiting for transfers between devices  78.6 us (38%)
  local copies, waits for them, and re-layouts  26.2 us (13%)
  other arithmetic  6.64 us (3%)
  matrix products  4.07 us (2%)
    ppermute x8, starting transfers between devices, partner_2(): return lax.ppermute(block, axis, route)  38.7 us
    all_to_all x1, waiting for transfers between devices, scatter_rows(): got = lax.all_to_all(terms, COLS, 0, 0, tiled=True)  31.3 us
    ppermute x6, starting transfers between devices, gather_line(): got = lax.ppermute(held, axis, [(i, i ^ dist) for i in range(count)])  27.1 us
    ppermute x6, waiting for transfers between devices, gather_line(): got = lax.ppermute(held, axis, [(i, i ^ dist) for i in range(count)])  22.3 us
    ppermute x1, waiting for transfers between devices, scatter_rows(): lax.ppermute(lax.dynamic_index_in_dim(sent, 1 - place, 0, keepdims=False)...  11.5 us
    ppermute x3, waiting for transfers between devices, scatter_rows(): lax.ppermute(lax.dynamic_index_in_dim(data, at ^ step, 0, keepdims=False)...  11.1 us
    ppermute x3, starting transfers between devices, scatter_rows(): lax.ppermute(lax.dynamic_index_in_dim(data, at ^ step, 0, keepdims=False)...  9.26 us
    all_to_all x2, starting transfers between devices, gather_rows(): both = lax.all_to_all(copies, COLS, 0, 0, tiled=True)  8.16 us
  transfers between devices with their start and end apart: 21, of which 9 were waited for; matrix products, arithmetic and copies ran while one was open for 11% of the time, Pallas kernels for 0%

profile of v12, /device:TPU:1, one launch (start us, length us, event | category | flops | bytes accessed | tf_op | source)
XLA Modules:
  0.0 206.7 jit_solution(7465951641037509052)
XLA Ops:
  0.6 0.8 slice_bitcast_fusion
  1.5 9.6 %collective-permute-start.4 = (bf16[1,6,8,512]{3,2,1,0:T(8,128)(2,1)S(1)}, bf16[1,6,8,512]{3,2,1,0:T(8,128)(2,1)S(1)}, u32[]{:S(2)}, u32[]{:S(2)}) collective-permute-start(bf16[1,6,8,512]{3,2,1,0:T(8,128)(2,1)S(1)} %get-tuple-element.24), channel_id=1, source_target_pairs={{0,256},{64,320},{128,384},{192,448},{256,0},{320,64},{384,128},{4... | collective-permute-start | bytes 147464 | tf_op jit(solution)/shard_map/ppermute | solution.py:46
  11.1 1.4 collective-permute-done.4
  12.6 6.1 %collective-permute-start.5 = (bf16[2,1,6,8,512]{4,3,2,0,1:T(8,128)(2,1)S(1)}, bf16[2,1,6,8,512]{4,3,2,0,1:T(8,128)(2,1)S(1)}, u32[]{:S(2)}, u32[]{:S(2)}) collective-permute-start(bf16[2,1,6,8,512]{4,3,2,0,1:T(8,128)(2,1)S(1)} %maximum_select_fusion.5), channel_id=1, source_target_pairs={{0,128},{64,192},{128,0},{192,64},{256,384},{320,448},{384,256},{4... | collective-permute-start | bytes 294920 | tf_op jit(solution)/shard_map/ppermute | solution.py:46
  18.7 2.0 collective-permute-done.5
  20.7 4.5 %collective-permute-start.6 = (bf16[2,2,1,6,8,512]{5,4,3,1,2,0:T(8,128)(2,1)S(1)}, bf16[2,2,1,6,8,512]{5,4,3,1,2,0:T(8,128)(2,1)S(1)}, u32[]{:S(2)}, u32[]{:S(2)}) collective-permute-start(bf16[2,2,1,6,8,512]{5,4,3,1,2,0:T(8,128)(2,1)S(1)} %bitcast_select_fusion), channel_id=1, source_target_pairs={{0,64},{64,0},{128,192},{192,128},{256,320},{320,256},{384,448},{4... | collective-permute-start | bytes 589832 | tf_op jit(solution)/shard_map/ppermute | solution.py:46
  25.2 4.8 %collective-permute-start = (bf16[128,512]{1,0:T(8,128)(2,1)}, bf16[128,512]{1,0:T(8,128)(2,1)S(1)}, u32[]{:S(2)}, u32[]{:S(2)}) collective-permute-start(bf16[128,512]{1,0:T(8,128)(2,1)} %param.4), channel_id=1, source_target_pairs={{0,1},{1,0},{2,3},{3,2},{4,5},{5,4},{6,7},{7,6},{8,9},{9,8},{10,11... | collective-permute-start | bytes 393224 | tf_op jit(solution)/shard_map/ppermute | solution.py:23
  30.0 2.3 %collective-permute-start.1 = (bf16[128,512]{1,0:T(8,128)(2,1)}, bf16[128,512]{1,0:T(8,128)(2,1)S(1)}, u32[]{:S(2)}, u32[]{:S(2)}) collective-permute-start(bf16[128,512]{1,0:T(8,128)(2,1)} %param.4), channel_id=1, source_target_pairs={{0,2},{2,0},{1,3},{3,1},{4,6},{6,4},{5,7},{7,5},{8,10},{10,8},{9,1... | collective-permute-start | bytes 393224 | tf_op jit(solution)/shard_map/ppermute | solution.py:23
  32.3 4.5 %collective-permute-start.2 = (bf16[128,512]{1,0:T(8,128)(2,1)}, bf16[128,512]{1,0:T(8,128)(2,1)S(1)}, u32[]{:S(2)}, u32[]{:S(2)}) collective-permute-start(bf16[128,512]{1,0:T(8,128)(2,1)} %param.4), channel_id=1, source_target_pairs={{0,4},{4,0},{1,5},{5,1},{2,6},{6,2},{3,7},{7,3},{8,12},{12,8},{9,1... | collective-permute-start | bytes 393224 | tf_op jit(solution)/shard_map/ppermute | solution.py:23
  36.8 13.6 %collective-permute-start.3 = (bf16[128,512]{1,0:T(8,128)(2,1)}, bf16[128,512]{1,0:T(8,128)(2,1)S(1)}, u32[]{:S(2)}, u32[]{:S(2)}) collective-permute-start(bf16[128,512]{1,0:T(8,128)(2,1)} %param.4), channel_id=1, source_target_pairs={{0,8},{8,0},{1,9},{9,1},{2,10},{10,2},{3,11},{11,3},{4,12},{12,4},... | collective-permute-start | bytes 393224 | tf_op jit(solution)/shard_map/ppermute | solution.py:23
  50.5 0.8 copy.112
  51.4 3.1 %collective-permute-start.7 = (bf16[1,6,8,512]{3,2,1,0:T(8,128)(2,1)S(1)}, bf16[1,6,8,512]{3,2,1,0:T(8,128)(2,1)S(1)}, u32[]{:S(2)}, u32[]{:S(2)}) collective-permute-start(bf16[1,6,8,512]{3,2,1,0:T(8,128)(2,1)S(1)} %get-tuple-element.23), channel_id=1, source_target_pairs={{0,256},{64,320},{128,384},{192,448},{256,0},{320,64},{384,128},{4... | collective-permute-start | bytes 147464 | tf_op jit(solution)/shard_map/ppermute | solution.py:46
  54.6 1.4 broadcast_in_dim.32
  56.0 4.1 %all-to-all-start = ((bf16[4,8,6,8,512]{4,3,1,2,0:T(8,128)(2,1)}), bf16[4,8,6,8,512]{4,3,1,2,0:T(8,128)(2,1)S(1)}, u32[]{:S(2)}, u32[]{:S(2)}) async-start(bf16[4,8,6,8,512]{4,3,1,2,0:T(8,128)(2,1)} %broadcast_in_dim.32), calls=%async_computation | async-start | bytes 3145728 | tf_op jit(solution)/shard_map/all_to_all | solution.py:59
  61.0 6.9 %collective-permute-done.7 = bf16[1,6,8,512]{3,2,1,0:T(8,128)(2,1)S(1)} collective-permute-done((bf16[1,6,8,512]{3,2,1,0:T(8,128)(2,1)S(1)}, bf16[1,6,8,512]{3,2,1,0:T(8,128)(2,1)S(1)}, u32[]{:S(2)}, u32[]{:S(2)}) %collective-permute-start.7) | collective-permute-done | bytes 49184 | tf_op jit(solution)/shard_map/ppermute | solution.py:46
  67.9 1.9 collective-permute-start.8
  70.4 6.1 %collective-permute-done.8 = bf16[2,1,6,8,512]{4,3,2,0,1:T(8,128)(2,1)S(1)} collective-permute-done((bf16[2,1,6,8,512]{4,3,2,0,1:T(8,128)(2,1)S(1)}, bf16[2,1,6,8,512]{4,3,2,0,1:T(8,128)(2,1)S(1)}, u32[]{:S(2)}, u32[]{:S(2)}) %collective-permute-start.8) | collective-permute-done | bytes 98336 | tf_op jit(solution)/shard_map/ppermute | solution.py:46
  76.5 1.9 collective-permute-start.9
  78.5 5.9 %collective-permute-done.9 = bf16[2,2,1,6,8,512]{5,4,3,1,0,2:T(8,128)(2,1)S(1)} collective-permute-done((bf16[2,2,1,6,8,512]{5,4,3,1,0,2:T(8,128)(2,1)S(1)}, bf16[2,2,1,6,8,512]{5,4,3,1,0,2:T(8,128)(2,1)S(1)}, u32[]{:S(2)}, u32[]{:S(2)}) %collective-permute-start.9) | collective-permute-done | bytes 196640 | tf_op jit(solution)/shard_map/ppermute | solution.py:46
  84.5 1.4 broadcast_in_dim.36
  85.9 4.0 %all-to-all-start.1 = ((bf16[4,8,6,8,512]{4,3,1,2,0:T(8,128)(2,1)}), bf16[4,8,6,8,512]{4,3,1,2,0:T(8,128)(2,1)S(1)}, u32[]{:S(2)}, u32[]{:S(2)}) async-start(bf16[4,8,6,8,512]{4,3,1,2,0:T(8,128)(2,1)} %broadcast_in_dim.36), calls=%async_computation.1 | async-start | bytes 3145728 | tf_op jit(solution)/shard_map/all_to_all | solution.py:59
  91.9 1.9 fusion.27
  93.8 1.1 copy.125
  94.8 1.9 reshape.948
  96.8 1.9 dot_general.40
  98.7 2.1 %copy.123 = bf16[128,4,8,8,6]{0,4,3,2,1:T(8,128)(2,1)} copy(bf16[128,4,8,8,6]{0,3,1,2,4:T(8,128)(2,1)} %bitcast.163) | data formatting | bytes 786432 | tf_op jit(solution)/shard_map/transpose | solution.py:101
  100.8 1.9 reshape.947
  102.7 1.9 dot_general.37
  104.7 0.9 copy-done
  105.6 1.1 fusion.28
  106.7 2.3 %all-to-all-done.1 = bf16[4,8,6,8,512]{4,3,1,2,0:T(8,128)(2,1)S(1)} async-done(((bf16[4,8,6,8,512]{4,3,1,2,0:T(8,128)(2,1)}), bf16[4,8,6,8,512]{4,3,1,2,0:T(8,128)(2,1)S(1)}, u32[]{:S(2)}, u32[]{:S(2)}) %all-to-all-start.1) | async-done | bytes 1572896 | tf_op jit(solution)/shard_map/all_to_all | solution.py:59
  111.7 2.1 %pad_maximum_fusion = bf16[4,8,8,6,1024]{4,2,3,1,0:T(8,128)(2,1)} fusion(bf16[4,8,8,6,512]{4,2,3,1,0:T(8,128)(2,1)S(1)} %multiply_convert_fusion, bf16[4,8,8,6,512]{4,2,3,1,0:T(8,128)(2,1)S(1)} %multiply_convert_fusion.1), kind=kLoop, calls=%fused_computation | loop fusion | flops 6291456 | bytes 6291456 | tf_op jit(solution)/shard_map/concatenate | solution.py:151
  113.8 4.7 %all-to-all-start.2 = ((bf16[4,8,8,6,1024]{4,2,3,1,0:T(8,128)(2,1)}), bf16[4,8,8,6,1024]{4,2,3,1,0:T(8,128)(2,1)}, u32[]{:S(2)}, u32[]{:S(2)}) async-start(bf16[4,8,8,6,1024]{4,2,3,1,0:T(8,128)(2,1)} %pad_maximum_fusion), calls=%async_computation.2 | async-start | bytes 6291456 | tf_op jit(solution)/shard_map/all_to_all | solution.py:66
  119.1 0.7 copy-done.11
  122.4 31.3 %all-to-all-done.2 = bf16[4,8,8,6,1024]{4,2,3,1,0:T(8,128)(2,1)} async-done(((bf16[4,8,8,6,1024]{4,2,3,1,0:T(8,128)(2,1)}), bf16[4,8,8,6,1024]{4,2,3,1,0:T(8,128)(2,1)}, u32[]{:S(2)}, u32[]{:S(2)}) %all-to-all-start.2) | async-done | bytes 3145760 | tf_op jit(solution)/shard_map/all_to_all | solution.py:66
  153.7 2.6 %reduce_sum.12 = bf16[8,8,6,1024]{3,1,2,0:T(8,128)(2,1)S(1)} reduce(bf16[4,8,8,6,1024]{4,2,3,1,0:T(8,128)(2,1)} %all-to-all-done.2, bf16[]{:T(256)} %constant.43.clone.1), dimensions={0}, to_apply=%region_0.1 | reduce | flops 1179648 | bytes 3932162 | tf_op jit(solution)/shard_map/reduce_sum | solution.py:67
  156.3 0.7 dynamic-slice_bitcast_fusion.2
  157.0 1.9 collective-permute-start.16
  158.9 3.9 %collective-permute-start.15 = (bf16[2,8,6,1024]{3,1,2,0:T(8,128)(2,1)S(1)}, bf16[2,8,6,1024]{3,1,2,0:T(8,128)(2,1)S(1)}, u32[]{:S(2)}, u32[]{:S(2)}) collective-permute-start(bf16[2,8,6,1024]{3,1,2,0:T(8,128)(2,1)S(1)} %get-tuple-element.12), channel_id=1, source_target_pairs={{0,128},{64,192},{128,0},{192,64},{1,129},{65,193},{129,1},{193,65... | collective-permute-start | bytes 589832 | tf_op jit(solution)/shard_map/ppermute | solution.py:73
  162.8 3.4 %collective-permute-start.14 = (bf16[2,8,6,1024]{3,1,2,0:T(8,128)(2,1)S(1)}, bf16[2,8,6,1024]{3,1,2,0:T(8,128)(2,1)S(1)}, u32[]{:S(2)}, u32[]{:S(2)}) collective-permute-start(bf16[2,8,6,1024]{3,1,2,0:T(8,128)(2,1)S(1)} %get-tuple-element.10), channel_id=1, source_target_pairs={{0,64},{64,0},{128,192},{192,128},{1,65},{65,1},{129,193},{193,129... | collective-permute-start | bytes 589832 | tf_op jit(solution)/shard_map/ppermute | solution.py:73
  166.4 5.5 %collective-permute-start.13 = (bf16[128,512]{0,1:T(8,128)(2,1)S(1)}, bf16[128,512]{0,1:T(8,128)(2,1)S(1)}, u32[]{:S(2)}, u32[]{:S(2)}) collective-permute-start(bf16[128,512]{0,1:T(8,128)(2,1)S(1)} %bitcast.187), channel_id=1, source_target_pairs={{0,8},{8,0},{1,9},{9,1},{2,10},{10,2},{3,11},{11,3},{4,12},{12,4},... | collective-permute-start | bytes 393224 | tf_op jit(solution)/shard_map/ppermute | solution.py:23
  172.1 2.3 %collective-permute-start.12 = (bf16[128,512]{0,1:T(8,128)(2,1)S(1)}, bf16[128,512]{0,1:T(8,128)(2,1)S(1)}, u32[]{:S(2)}, u32[]{:S(2)}) collective-permute-start(bf16[128,512]{0,1:T(8,128)(2,1)S(1)} %bitcast.188), channel_id=1, source_target_pairs={{0,4},{4,0},{1,5},{5,1},{2,6},{6,2},{3,7},{7,3},{8,12},{12,8},{9,1... | collective-permute-start | bytes 393224 | tf_op jit(solution)/shard_map/ppermute | solution.py:23
  174.6 2.1 %collective-permute-start.11 = (bf16[128,512]{0,1:T(8,128)(2,1)S(1)}, bf16[128,512]{0,1:T(8,128)(2,1)S(1)}, u32[]{:S(2)}, u32[]{:S(2)}) collective-permute-start(bf16[128,512]{0,1:T(8,128)(2,1)S(1)} %bitcast.190), channel_id=1, source_target_pairs={{0,2},{2,0},{1,3},{3,1},{4,6},{6,4},{5,7},{7,5},{8,10},{10,8},{9,1... | collective-permute-start | bytes 393224 | tf_op jit(solution)/shard_map/ppermute | solution.py:23
  176.7 11.1 %collective-permute-done.15 = bf16[2,8,6,1024]{3,1,2,0:T(8,128)(2,1)S(1)} collective-permute-done((bf16[2,8,6,1024]{3,1,2,0:T(8,128)(2,1)S(1)}, bf16[2,8,6,1024]{3,1,2,0:T(8,128)(2,1)S(1)}, u32[]{:S(2)}, u32[]{:S(2)}) %collective-permute-start.15) | collective-permute-done | bytes 196640 | tf_op jit(solution)/shard_map/ppermute | solution.py:73
  187.8 3.6 %collective-permute-start.10 = (bf16[128,512]{0,1:T(8,128)(2,1)S(1)}, bf16[128,512]{0,1:T(8,128)(2,1)S(1)}, u32[]{:S(2)}, u32[]{:S(2)}) collective-permute-start(bf16[128,512]{0,1:T(8,128)(2,1)S(1)} %bitcast.189), channel_id=1, source_target_pairs={{0,1},{1,0},{2,3},{3,2},{4,5},{5,4},{6,7},{7,6},{8,9},{9,8},{10,11... | collective-permute-start | bytes 393224 | tf_op jit(solution)/shard_map/ppermute | solution.py:23
  191.6 1.9 collective-permute-start.17
  193.7 0.8 copy.127
  194.5 11.5 %collective-permute-done.17 = bf16[8,6,1024]{2,0,1:T(8,128)(2,1)S(1)} collective-permute-done((bf16[8,6,1024]{2,0,1:T(8,128)(2,1)S(1)}, bf16[8,6,1024]{2,0,1:T(8,128)(2,1)S(1)}, u32[]{:S(2)}, u32[]{:S(2)}) %collective-permute-start.17) | collective-permute-done | bytes 98336 | tf_op jit(solution)/shard_map/ppermute | solution.py:79
  (89 shorter events, 10.9 us)
Async XLA Ops:
  1.5 11.1 %collective-permute-start.4 = (bf16[1,6,8,512]{3,2,1,0:T(8,128)(2,1)S(1)}, bf16[1,6,8,512]{3,2,1,0:T(8,128)(2,1)S(1)}, u32[]{:S(2)}, u32[]{:S(2)}) collective-permute-start(bf16[1,6,8,512]{3,2,1,0:T(8,128)(2,1)S(1)} %get-tuple-element.24), channel_id=1, source_target_pairs={{0,256},{64,320},{128,384},{192,448},{256,0},{320,64},{384,128},{4... | collective-permute-start | bytes 147464 | tf_op jit(solution)/shard_map/ppermute | solution.py:46
  12.6 8.1 %collective-permute-start.5 = (bf16[2,1,6,8,512]{4,3,2,0,1:T(8,128)(2,1)S(1)}, bf16[2,1,6,8,512]{4,3,2,0,1:T(8,128)(2,1)S(1)}, u32[]{:S(2)}, u32[]{:S(2)}) collective-permute-start(bf16[2,1,6,8,512]{4,3,2,0,1:T(8,128)(2,1)S(1)} %maximum_select_fusion.5), channel_id=1, source_target_pairs={{0,128},{64,192},{128,0},{192,64},{256,384},{320,448},{384,256},{4... | collective-permute-start | bytes 294920 | tf_op jit(solution)/shard_map/ppermute | solution.py:46
  20.7 30.7 %collective-permute-start.6 = (bf16[2,2,1,6,8,512]{5,4,3,1,2,0:T(8,128)(2,1)S(1)}, bf16[2,2,1,6,8,512]{5,4,3,1,2,0:T(8,128)(2,1)S(1)}, u32[]{:S(2)}, u32[]{:S(2)}) collective-permute-start(bf16[2,2,1,6,8,512]{5,4,3,1,2,0:T(8,128)(2,1)S(1)} %bitcast_select_fusion), channel_id=1, source_target_pairs={{0,64},{64,0},{128,192},{192,128},{256,320},{320,256},{384,448},{4... | collective-permute-start | bytes 589832 | tf_op jit(solution)/shard_map/ppermute | solution.py:46
  25.2 44.7 %collective-permute-start = (bf16[128,512]{1,0:T(8,128)(2,1)}, bf16[128,512]{1,0:T(8,128)(2,1)S(1)}, u32[]{:S(2)}, u32[]{:S(2)}) collective-permute-start(bf16[128,512]{1,0:T(8,128)(2,1)} %param.4), channel_id=1, source_target_pairs={{0,1},{1,0},{2,3},{3,2},{4,5},{5,4},{6,7},{7,6},{8,9},{9,8},{10,11... | collective-permute-start | bytes 393224 | tf_op jit(solution)/shard_map/ppermute | solution.py:23
  30.0 40.0 %collective-permute-start.1 = (bf16[128,512]{1,0:T(8,128)(2,1)}, bf16[128,512]{1,0:T(8,128)(2,1)S(1)}, u32[]{:S(2)}, u32[]{:S(2)}) collective-permute-start(bf16[128,512]{1,0:T(8,128)(2,1)} %param.4), channel_id=1, source_target_pairs={{0,2},{2,0},{1,3},{3,1},{4,6},{6,4},{5,7},{7,5},{8,10},{10,8},{9,1... | collective-permute-start | bytes 393224 | tf_op jit(solution)/shard_map/ppermute | solution.py:23
  32.3 37.8 %collective-permute-start.2 = (bf16[128,512]{1,0:T(8,128)(2,1)}, bf16[128,512]{1,0:T(8,128)(2,1)S(1)}, u32[]{:S(2)}, u32[]{:S(2)}) collective-permute-start(bf16[128,512]{1,0:T(8,128)(2,1)} %param.4), channel_id=1, source_target_pairs={{0,4},{4,0},{1,5},{5,1},{2,6},{6,2},{3,7},{7,3},{8,12},{12,8},{9,1... | collective-permute-start | bytes 393224 | tf_op jit(solution)/shard_map/ppermute | solution.py:23
  36.8 33.4 %collective-permute-start.3 = (bf16[128,512]{1,0:T(8,128)(2,1)}, bf16[128,512]{1,0:T(8,128)(2,1)S(1)}, u32[]{:S(2)}, u32[]{:S(2)}) collective-permute-start(bf16[128,512]{1,0:T(8,128)(2,1)} %param.4), channel_id=1, source_target_pairs={{0,8},{8,0},{1,9},{9,1},{2,10},{10,2},{3,11},{11,3},{4,12},{12,4},... | collective-permute-start | bytes 393224 | tf_op jit(solution)/shard_map/ppermute | solution.py:23
  51.4 16.5 %collective-permute-start.7 = (bf16[1,6,8,512]{3,2,1,0:T(8,128)(2,1)S(1)}, bf16[1,6,8,512]{3,2,1,0:T(8,128)(2,1)S(1)}, u32[]{:S(2)}, u32[]{:S(2)}) collective-permute-start(bf16[1,6,8,512]{3,2,1,0:T(8,128)(2,1)S(1)} %get-tuple-element.23), channel_id=1, source_target_pairs={{0,256},{64,320},{128,384},{192,448},{256,0},{320,64},{384,128},{4... | collective-permute-start | bytes 147464 | tf_op jit(solution)/shard_map/ppermute | solution.py:46
  56.0 4.2 %copy-start.7 = (bf16[128,512]{1,0:T(8,128)(2,1)S(1)}, bf16[128,512]{1,0:T(8,128)(2,1)}, u32[]{:S(2)}) copy-start(bf16[128,512]{1,0:T(8,128)(2,1)} %param.4) | copy-start | bytes 393220
  56.0 28.5 %all-to-all-start = ((bf16[4,8,6,8,512]{4,3,1,2,0:T(8,128)(2,1)}), bf16[4,8,6,8,512]{4,3,1,2,0:T(8,128)(2,1)S(1)}, u32[]{:S(2)}, u32[]{:S(2)}) async-start(bf16[4,8,6,8,512]{4,3,1,2,0:T(8,128)(2,1)} %broadcast_in_dim.32), calls=%async_computation | async-start | bytes 3145728 | tf_op jit(solution)/shard_map/all_to_all | solution.py:59
  67.9 8.6 %collective-permute-start.8 = (bf16[2,1,6,8,512]{4,3,2,0,1:T(8,128)(2,1)S(1)}, bf16[2,1,6,8,512]{4,3,2,0,1:T(8,128)(2,1)S(1)}, u32[]{:S(2)}, u32[]{:S(2)}) collective-permute-start(bf16[2,1,6,8,512]{4,3,2,0,1:T(8,128)(2,1)S(1)} %fusion.21), channel_id=1, source_target_pairs={{0,128},{64,192},{128,0},{192,64},{256,384},{320,448},{384,256},{4... | collective-permute-start | bytes 294920 | tf_op jit(solution)/shard_map/ppermute | solution.py:46
  76.5 7.9 %collective-permute-start.9 = (bf16[2,2,1,6,8,512]{5,4,3,1,0,2:T(8,128)(2,1)S(1)}, bf16[2,2,1,6,8,512]{5,4,3,1,0,2:T(8,128)(2,1)S(1)}, u32[]{:S(2)}, u32[]{:S(2)}) collective-permute-start(bf16[2,2,1,6,8,512]{5,4,3,1,0,2:T(8,128)(2,1)S(1)} %maximum_select_fusion.3), channel_id=1, source_target_pairs={{0,64},{64,0},{128,192},{192,128},{256,320},{320,256},{384,448},{4... | collective-permute-start | bytes 589832 | tf_op jit(solution)/shard_map/ppermute | solution.py:46
  78.5 6.0 %copy-start.1 = (bf16[128,2,6,256]{0,3,2,1:T(8,128)(2,1)}, bf16[128,2,6,256]{0,3,2,1:T(8,128)(2,1)S(1)}, u32[]{:S(2)}) copy-start(bf16[128,2,6,256]{0,3,2,1:T(8,128)(2,1)S(1)} %constant_dynamic-update-slice_fusion.3) | copy-start | bytes 2359300
  85.9 23.2 %all-to-all-start.1 = ((bf16[4,8,6,8,512]{4,3,1,2,0:T(8,128)(2,1)}), bf16[4,8,6,8,512]{4,3,1,2,0:T(8,128)(2,1)S(1)}, u32[]{:S(2)}, u32[]{:S(2)}) async-start(bf16[4,8,6,8,512]{4,3,1,2,0:T(8,128)(2,1)} %broadcast_in_dim.36), calls=%async_computation.1 | async-start | bytes 3145728 | tf_op jit(solution)/shard_map/all_to_all | solution.py:59
  104.6 1.0 copy-start
  109.2 1.0 copy-start.2
  109.2 1.0 copy-start.9
  109.2 1.1 copy-start.10
  109.6 1.3 copy-start.5
  109.6 1.3 copy-start.3
  109.6 1.3 copy-start.4
  109.6 1.3 copy-start.8
  113.8 39.9 %all-to-all-start.2 = ((bf16[4,8,8,6,1024]{4,2,3,1,0:T(8,128)(2,1)}), bf16[4,8,8,6,1024]{4,2,3,1,0:T(8,128)(2,1)}, u32[]{:S(2)}, u32[]{:S(2)}) async-start(bf16[4,8,8,6,1024]{4,2,3,1,0:T(8,128)(2,1)} %pad_maximum_fusion), calls=%async_computation.2 | async-start | bytes 6291456 | tf_op jit(solution)/shard_map/all_to_all | solution.py:66
  118.9 1.0 copy-start.11
  120.5 1.0 copy-start.6
  157.0 17.6 %collective-permute-start.16 = (bf16[2,8,6,1024]{3,1,2,0:T(8,128)(2,1)}, bf16[2,8,6,1024]{3,1,2,0:T(8,128)(2,1)S(1)}, u32[]{:S(2)}, u32[]{:S(2)}) collective-permute-start(bf16[2,8,6,1024]{3,1,2,0:T(8,128)(2,1)} %get-tuple-element.11), channel_id=1, source_target_pairs={{0,192},{64,128},{128,64},{192,0},{1,193},{65,129},{129,65},{193,1... | collective-permute-start | bytes 589832 | tf_op jit(solution)/shard_map/ppermute | solution.py:73
  158.9 28.9 %collective-permute-start.15 = (bf16[2,8,6,1024]{3,1,2,0:T(8,128)(2,1)S(1)}, bf16[2,8,6,1024]{3,1,2,0:T(8,128)(2,1)S(1)}, u32[]{:S(2)}, u32[]{:S(2)}) collective-permute-start(bf16[2,8,6,1024]{3,1,2,0:T(8,128)(2,1)S(1)} %get-tuple-element.12), channel_id=1, source_target_pairs={{0,128},{64,192},{128,0},{192,64},{1,129},{65,193},{129,1},{193,65... | collective-permute-start | bytes 589832 | tf_op jit(solution)/shard_map/ppermute | solution.py:73
  162.8 28.6 %collective-permute-start.14 = (bf16[2,8,6,1024]{3,1,2,0:T(8,128)(2,1)S(1)}, bf16[2,8,6,1024]{3,1,2,0:T(8,128)(2,1)S(1)}, u32[]{:S(2)}, u32[]{:S(2)}) collective-permute-start(bf16[2,8,6,1024]{3,1,2,0:T(8,128)(2,1)S(1)} %get-tuple-element.10), channel_id=1, source_target_pairs={{0,64},{64,0},{128,192},{192,128},{1,65},{65,1},{129,193},{193,129... | collective-permute-start | bytes 589832 | tf_op jit(solution)/shard_map/ppermute | solution.py:73
  166.4 27.1 %collective-permute-start.13 = (bf16[128,512]{0,1:T(8,128)(2,1)S(1)}, bf16[128,512]{0,1:T(8,128)(2,1)S(1)}, u32[]{:S(2)}, u32[]{:S(2)}) collective-permute-start(bf16[128,512]{0,1:T(8,128)(2,1)S(1)} %bitcast.187), channel_id=1, source_target_pairs={{0,8},{8,0},{1,9},{9,1},{2,10},{10,2},{3,11},{11,3},{4,12},{12,4},... | collective-permute-start | bytes 393224 | tf_op jit(solution)/shard_map/ppermute | solution.py:23
  172.1 21.5 %collective-permute-start.12 = (bf16[128,512]{0,1:T(8,128)(2,1)S(1)}, bf16[128,512]{0,1:T(8,128)(2,1)S(1)}, u32[]{:S(2)}, u32[]{:S(2)}) collective-permute-start(bf16[128,512]{0,1:T(8,128)(2,1)S(1)} %bitcast.188), channel_id=1, source_target_pairs={{0,4},{4,0},{1,5},{5,1},{2,6},{6,2},{3,7},{7,3},{8,12},{12,8},{9,1... | collective-permute-start | bytes 393224 | tf_op jit(solution)/shard_map/ppermute | solution.py:23
  174.6 19.0 %collective-permute-start.11 = (bf16[128,512]{0,1:T(8,128)(2,1)S(1)}, bf16[128,512]{0,1:T(8,128)(2,1)S(1)}, u32[]{:S(2)}, u32[]{:S(2)}) collective-permute-start(bf16[128,512]{0,1:T(8,128)(2,1)S(1)} %bitcast.190), channel_id=1, source_target_pairs={{0,2},{2,0},{1,3},{3,1},{4,6},{6,4},{5,7},{7,5},{8,10},{10,8},{9,1... | collective-permute-start | bytes 393224 | tf_op jit(solution)/shard_map/ppermute | solution.py:23
  187.8 5.8 %collective-permute-start.10 = (bf16[128,512]{0,1:T(8,128)(2,1)S(1)}, bf16[128,512]{0,1:T(8,128)(2,1)S(1)}, u32[]{:S(2)}, u32[]{:S(2)}) collective-permute-start(bf16[128,512]{0,1:T(8,128)(2,1)S(1)} %bitcast.189), channel_id=1, source_target_pairs={{0,1},{1,0},{2,3},{3,2},{4,5},{5,4},{6,7},{7,6},{8,9},{9,8},{10,11... | collective-permute-start | bytes 393224 | tf_op jit(solution)/shard_map/ppermute | solution.py:23
  191.6 14.3 %collective-permute-start.17 = (bf16[8,6,1024]{2,0,1:T(8,128)(2,1)S(1)}, bf16[8,6,1024]{2,0,1:T(8,128)(2,1)S(1)}, u32[]{:S(2)}, u32[]{:S(2)}) collective-permute-start(bf16[8,6,1024]{2,0,1:T(8,128)(2,1)S(1)} %dynamic-slice_bitcast_fusion.3), channel_id=1, source_target_pairs={{0,256},{256,0},{1,257},{257,1},{2,258},{258,2},{3,259},{259,3},{4... | collective-permute-start | bytes 294920 | tf_op jit(solution)/shard_map/ppermute | solution.py:79

commit v13 on v12

--- a/solution.py
+++ b/solution.py
@@ -63,8 +63,15 @@
 def scatter_rows(terms):
     _, zl, own, factor_count, width = terms.shape
     halves = lax.axis_size(HALF)
-    got = lax.all_to_all(terms, COLS, 0, 0, tiled=True)
-    part = got.astype(jnp.float32).sum(0).reshape(halves, zl // halves, own, factor_count, width)
+    ring = lax.axis_size(COLS)
+    me = lax.axis_index(COLS)
+    part = lax.dynamic_index_in_dim(terms, me, 0, keepdims=False).astype(jnp.float32)
+    for step in range(1, ring):
+        got = lax.ppermute(
+            lax.dynamic_index_in_dim(terms, me ^ step, 0, keepdims=False), COLS, [(i, i ^ step) for i in range(ring)]
+        )
+        part = part + got.astype(jnp.float32)
+    part = part.reshape(halves, zl // halves, own, factor_count, width)
     data = part.transpose(1, 0, 2, 3, 4).astype(jnp.bfloat16)
     count = lax.axis_size(QUARTER)
     at = lax.axis_index(QUARTER)

time: 208 us -> 204 us (0.981)
  waiting for transfers between devices: 78.6 us -> 70.8 us
  starting transfers between devices: 89.8 us -> 95.4 us
  local copies, waits for them, and re-layouts: 26.2 us -> 24 us
    all_to_all x1 -> x0, waiting for transfers between devices: 31.3 us -> none  [scatter_rows(): got = lax.all_to_all(terms, COLS, 0, 0, tiled=True)]
    ppermute x0 -> x3, waiting for transfers between devices: none -> 25.8 us  [scatter_rows(): lax.ppermute(lax.dynamic_index_in_dim(terms, me ^ step, 0, keepdims=False...]
    ppermute x6, waiting for transfers between devices: 22.3 us -> 32.3 us  [gather_line(): got = lax.ppermute(held, axis, [(i, i ^ dist) for i in range(count)])]
    ppermute x0 -> x3, starting transfers between devices: none -> 8.97 us  [scatter_rows(): lax.ppermute(lax.dynamic_index_in_dim(terms, me ^ step, 0, keepdims=False...]
    ppermute x3, waiting for transfers between devices: 11.1 us -> 4.12 us  [scatter_rows(): lax.ppermute(lax.dynamic_index_in_dim(data, at ^ step, 0, keepdims=False)...]
    ppermute x1, waiting for transfers between devices: 11.5 us -> 5.57 us  [scatter_rows(): lax.ppermute(lax.dynamic_index_in_dim(sent, 1 - place, 0, keepdims=False)...]
    ppermute x6, starting transfers between devices: 27.1 us -> 21.8 us  [gather_line(): got = lax.ppermute(held, axis, [(i, i ^ dist) for i in range(count)])]
    ppermute x1, starting transfers between devices: 1.92 us -> 6.57 us  [scatter_rows(): lax.ppermute(lax.dynamic_index_in_dim(sent, 1 - place, 0, keepdims=False)...]
  transfers between devices with their start and end apart: 21 -> 23, of which waited for: 9 -> 11; matrix products, arithmetic and copies ran while one was open for 11% -> 11% of each run, Pallas kernels for 0% -> 0%
where the time goes in v13:
time: 204 us; the launch traced here: 203 us
  starting transfers between devices  95.4 us (47%)
  waiting for transfers between devices  70.8 us (35%)
  local copies, waits for them, and re-layouts  24 us (12%)
  other arithmetic  7.58 us (4%)
  matrix products  3.36 us (2%)
    ppermute x8, starting transfers between devices, partner_2(): return lax.ppermute(block, axis, route)  41.1 us
    ppermute x6, waiting for transfers between devices, gather_line(): got = lax.ppermute(held, axis, [(i, i ^ dist) for i in range(count)])  32.3 us
    ppermute x3, waiting for transfers between devices, scatter_rows(): lax.ppermute(lax.dynamic_index_in_dim(terms, me ^ step, 0, keepdims=False...  25.8 us
    ppermute x6, starting transfers between devices, gather_line(): got = lax.ppermute(held, axis, [(i, i ^ dist) for i in range(count)])  21.8 us
    ppermute x3, starting transfers between devices, scatter_rows(): lax.ppermute(lax.dynamic_index_in_dim(data, at ^ step, 0, keepdims=False)...  9.27 us
    ppermute x3, starting transfers between devices, scatter_rows(): lax.ppermute(lax.dynamic_index_in_dim(terms, me ^ step, 0, keepdims=False...  8.97 us
    all_to_all x2, starting transfers between devices, gather_rows(): both = lax.all_to_all(copies, COLS, 0, 0, tiled=True)  7.71 us
    ppermute x1, starting transfers between devices, scatter_rows(): lax.ppermute(lax.dynamic_index_in_dim(sent, 1 - place, 0, keepdims=False)...  6.57 us
  transfers between devices with their start and end apart: 23, of which 11 were waited for; matrix products, arithmetic and copies ran while one was open for 11% of the time, Pallas kernels for 0%

profile of v13, /device:TPU:1, one launch (start us, length us, event | category | flops | bytes accessed | tf_op | source)
XLA Modules:
  0.0 202.6 jit_solution(9509584518751300146)
XLA Ops:
  1.5 9.6 %collective-permute-start.4 = (bf16[1,6,8,512]{3,2,1,0:T(8,128)(2,1)S(1)}, bf16[1,6,8,512]{3,2,1,0:T(8,128)(2,1)S(1)}, u32[]{:S(2)}, u32[]{:S(2)}) collective-permute-start(bf16[1,6,8,512]{3,2,1,0:T(8,128)(2,1)S(1)} %get-tuple-element.27), channel_id=1, source_target_pairs={{0,256},{64,320},{128,384},{192,448},{256,0},{320,64},{384,128},{4... | collective-permute-start | bytes 147464 | tf_op jit(solution)/shard_map/ppermute | solution.py:46
  11.1 2.9 %collective-permute-start = (bf16[128,512]{1,0:T(8,128)(2,1)}, bf16[128,512]{1,0:T(8,128)(2,1)S(1)}, u32[]{:S(2)}, u32[]{:S(2)}) collective-permute-start(bf16[128,512]{1,0:T(8,128)(2,1)} %param.4), channel_id=1, source_target_pairs={{0,1},{1,0},{2,3},{3,2},{4,5},{5,4},{6,7},{7,6},{8,9},{9,8},{10,11... | collective-permute-start | bytes 393224 | tf_op jit(solution)/shard_map/ppermute | solution.py:23
  14.0 3.2 %collective-permute-start.1 = (bf16[128,512]{1,0:T(8,128)(2,1)}, bf16[128,512]{1,0:T(8,128)(2,1)}, u32[]{:S(2)}, u32[]{:S(2)}) collective-permute-start(bf16[128,512]{1,0:T(8,128)(2,1)} %param.4), channel_id=1, source_target_pairs={{0,2},{2,0},{1,3},{3,1},{4,6},{6,4},{5,7},{7,5},{8,10},{10,8},{9,1... | collective-permute-start | bytes 393224 | tf_op jit(solution)/shard_map/ppermute | solution.py:23
  17.2 4.5 %collective-permute-start.2 = (bf16[128,512]{1,0:T(8,128)(2,1)}, bf16[128,512]{1,0:T(8,128)(2,1)S(1)}, u32[]{:S(2)}, u32[]{:S(2)}) collective-permute-start(bf16[128,512]{1,0:T(8,128)(2,1)} %param.4), channel_id=1, source_target_pairs={{0,4},{4,0},{1,5},{5,1},{2,6},{6,2},{3,7},{7,3},{8,12},{12,8},{9,1... | collective-permute-start | bytes 393224 | tf_op jit(solution)/shard_map/ppermute | solution.py:23
  21.7 10.6 %collective-permute-start.3 = (bf16[128,512]{1,0:T(8,128)(2,1)}, bf16[128,512]{1,0:T(8,128)(2,1)S(1)}, u32[]{:S(2)}, u32[]{:S(2)}) collective-permute-start(bf16[128,512]{1,0:T(8,128)(2,1)} %param.4), channel_id=1, source_target_pairs={{0,8},{8,0},{1,9},{9,1},{2,10},{10,2},{3,11},{11,3},{4,12},{12,4},... | collective-permute-start | bytes 393224 | tf_op jit(solution)/shard_map/ppermute | solution.py:23
  33.3 3.1 %collective-permute-start.5 = (bf16[2,1,6,8,512]{4,3,2,0,1:T(8,128)(2,1)S(1)}, bf16[2,1,6,8,512]{4,3,2,0,1:T(8,128)(2,1)S(1)}, u32[]{:S(2)}, u32[]{:S(2)}) collective-permute-start(bf16[2,1,6,8,512]{4,3,2,0,1:T(8,128)(2,1)S(1)} %maximum_select_fusion.5), channel_id=1, source_target_pairs={{0,128},{64,192},{128,0},{192,64},{256,384},{320,448},{384,256},{4... | collective-permute-start | bytes 294920 | tf_op jit(solution)/shard_map/ppermute | solution.py:46
  36.5 14.5 %collective-permute-done.5 = bf16[2,1,6,8,512]{4,3,2,0,1:T(8,128)(2,1)S(1)} collective-permute-done((bf16[2,1,6,8,512]{4,3,2,0,1:T(8,128)(2,1)S(1)}, bf16[2,1,6,8,512]{4,3,2,0,1:T(8,128)(2,1)S(1)}, u32[]{:S(2)}, u32[]{:S(2)}) %collective-permute-start.5) | collective-permute-done | bytes 98336 | tf_op jit(solution)/shard_map/ppermute | solution.py:46
  50.9 1.9 collective-permute-start.6
  52.9 5.9 %collective-permute-done.6 = bf16[2,2,1,6,8,512]{5,4,3,1,2,0:T(8,128)(2,1)S(1)} collective-permute-done((bf16[2,2,1,6,8,512]{5,4,3,1,2,0:T(8,128)(2,1)S(1)}, bf16[2,2,1,6,8,512]{5,4,3,1,2,0:T(8,128)(2,1)S(1)}, u32[]{:S(2)}, u32[]{:S(2)}) %collective-permute-start.6) | collective-permute-done | bytes 196640 | tf_op jit(solution)/shard_map/ppermute | solution.py:46
  58.8 3.3 %collective-permute-start.7 = (bf16[1,6,8,512]{3,2,1,0:T(8,128)(2,1)S(1)}, bf16[1,6,8,512]{3,2,1,0:T(8,128)(2,1)S(1)}, u32[]{:S(2)}, u32[]{:S(2)}) collective-permute-start(bf16[1,6,8,512]{3,2,1,0:T(8,128)(2,1)S(1)} %get-tuple-element.26), channel_id=1, source_target_pairs={{0,256},{64,320},{128,384},{192,448},{256,0},{320,64},{384,128},{4... | collective-permute-start | bytes 147464 | tf_op jit(solution)/shard_map/ppermute | solution.py:46
  62.2 1.4 broadcast_in_dim.32
  63.6 4.1 %all-to-all-start = ((bf16[4,8,6,8,512]{4,3,1,2,0:T(8,128)(2,1)}), bf16[4,8,6,8,512]{4,3,1,2,0:T(8,128)(2,1)S(1)}, u32[]{:S(2)}, u32[]{:S(2)}) async-start(bf16[4,8,6,8,512]{4,3,1,2,0:T(8,128)(2,1)} %broadcast_in_dim.32), calls=%async_computation | async-start | bytes 3145728 | tf_op jit(solution)/shard_map/all_to_all | solution.py:59
  68.6 1.8 collective-permute-done.7
  70.4 1.9 collective-permute-start.8
  72.5 1.0 copy.105
  73.9 4.7 %collective-permute-done.8 = bf16[2,1,6,8,512]{4,3,2,0,1:T(8,128)(2,1)S(1)} collective-permute-done((bf16[2,1,6,8,512]{4,3,2,0,1:T(8,128)(2,1)S(1)}, bf16[2,1,6,8,512]{4,3,2,0,1:T(8,128)(2,1)S(1)}, u32[]{:S(2)}, u32[]{:S(2)}) %collective-permute-start.8) | collective-permute-done | bytes 98336 | tf_op jit(solution)/shard_map/ppermute | solution.py:46
  78.6 1.9 collective-permute-start.9
  80.6 5.5 %collective-permute-done.9 = bf16[2,2,1,6,8,512]{5,4,3,1,0,2:T(8,128)(2,1)S(1)} collective-permute-done((bf16[2,2,1,6,8,512]{5,4,3,1,0,2:T(8,128)(2,1)S(1)}, bf16[2,2,1,6,8,512]{5,4,3,1,0,2:T(8,128)(2,1)S(1)}, u32[]{:S(2)}, u32[]{:S(2)}) %collective-permute-start.9) | collective-permute-done | bytes 196640 | tf_op jit(solution)/shard_map/ppermute | solution.py:46
  86.6 1.4 broadcast_in_dim.36
  88.0 3.6 %all-to-all-start.1 = ((bf16[4,8,6,8,512]{4,3,1,2,0:T(8,128)(2,1)}), bf16[4,8,6,8,512]{4,3,1,2,0:T(8,128)(2,1)S(1)}, u32[]{:S(2)}, u32[]{:S(2)}) async-start(bf16[4,8,6,8,512]{4,3,1,2,0:T(8,128)(2,1)} %broadcast_in_dim.36), calls=%async_computation.1 | async-start | bytes 3145728 | tf_op jit(solution)/shard_map/all_to_all | solution.py:59
  92.2 1.2 fusion.38
  94.1 1.1 copy.127
  95.2 1.9 reshape.949
  97.1 1.9 dot_general.37
  99.0 1.1 copy.129
  100.1 1.9 reshape.950
  102.1 1.9 dot_general.40
  104.3 0.9 copy-done.3
  105.6 1.4 bitcast_multiply_fusion.1
  107.0 2.6 %all-to-all-done.1 = bf16[4,8,6,8,512]{4,3,1,2,0:T(8,128)(2,1)S(1)} async-done(((bf16[4,8,6,8,512]{4,3,1,2,0:T(8,128)(2,1)}), bf16[4,8,6,8,512]{4,3,1,2,0:T(8,128)(2,1)S(1)}, u32[]{:S(2)}, u32[]{:S(2)}) %all-to-all-start.1) | async-done | bytes 1572896 | tf_op jit(solution)/shard_map/all_to_all | solution.py:59
  112.6 1.6 fusion.9
  114.5 2.8 %collective-permute-start.16 = (bf16[8,8,6,1024]{3,1,2,0:T(8,128)(2,1)}, bf16[8,8,6,1024]{3,1,2,0:T(8,128)(2,1)}, u32[]{:S(2)}, u32[]{:S(2)}) collective-permute-start(bf16[8,8,6,1024]{3,1,2,0:T(8,128)(2,1)} %get-tuple-element.12), channel_id=1, source_target_pairs={{0,48},{16,32},{32,16},{48,0},{1,49},{17,33},{33,17},{49,1},{2,50}... | collective-permute-start | bytes 2359304 | tf_op jit(solution)/shard_map/ppermute | solution.py:70
  117.3 3.1 %collective-permute-start.15 = (bf16[8,8,6,1024]{3,1,2,0:T(8,128)(2,1)}, bf16[8,8,6,1024]{3,1,2,0:T(8,128)(2,1)}, u32[]{:S(2)}, u32[]{:S(2)}) collective-permute-start(bf16[8,8,6,1024]{3,1,2,0:T(8,128)(2,1)} %get-tuple-element.11), channel_id=1, source_target_pairs={{0,32},{16,48},{32,0},{48,16},{1,33},{17,49},{33,1},{49,17},{2,34}... | collective-permute-start | bytes 2359304 | tf_op jit(solution)/shard_map/ppermute | solution.py:70
  120.4 3.1 %collective-permute-start.14 = (bf16[8,8,6,1024]{3,1,2,0:T(8,128)(2,1)}, bf16[8,8,6,1024]{3,1,2,0:T(8,128)(2,1)}, u32[]{:S(2)}, u32[]{:S(2)}) collective-permute-start(bf16[8,8,6,1024]{3,1,2,0:T(8,128)(2,1)} %get-tuple-element.10), channel_id=1, source_target_pairs={{0,16},{16,0},{32,48},{48,32},{1,17},{17,1},{33,49},{49,33},{2,18}... | collective-permute-start | bytes 2359304 | tf_op jit(solution)/shard_map/ppermute | solution.py:70
  125.6 1.1 copy.122
  126.8 24.4 %collective-permute-done.16 = bf16[8,8,6,1024]{3,1,2,0:T(8,128)(2,1)} collective-permute-done((bf16[8,8,6,1024]{3,1,2,0:T(8,128)(2,1)}, bf16[8,8,6,1024]{3,1,2,0:T(8,128)(2,1)}, u32[]{:S(2)}, u32[]{:S(2)}) %collective-permute-start.16) | collective-permute-done | bytes 786464 | tf_op jit(solution)/shard_map/ppermute | solution.py:70
  151.2 1.4 collective-permute-done.14
  152.6 2.2 %fusion.3 = bf16[8,8,6,1024]{3,1,2,0:T(8,128)(2,1)S(1)} fusion(bf16[8,8,6,1024]{3,1,2,0:T(8,128)(2,1)} %collective-permute-done.16, bf16[8,8,6,1024]{3,1,2,0:T(8,128)(2,1)} %collective-permute-done.15, bf16[8,8,6,1024]{3,1,2,0:T(8,128)(2,1)} %collective-permute-done.14, s32[]{:T(128)S(6)} %select_n.206, ...), kind=kLoop, calls=%fused_computation.19 | loop fusion | flops 4718592 | bytes 6291460 | tf_op jit(solution)/shard_map/convert_element_type | solution.py:75
  154.8 4.4 %collective-permute-start.19 = (bf16[2,8,6,1024]{3,1,2,0:T(8,128)(2,1)S(1)}, bf16[2,8,6,1024]{3,1,2,0:T(8,128)(2,1)S(1)}, u32[]{:S(2)}, u32[]{:S(2)}) collective-permute-start(bf16[2,8,6,1024]{3,1,2,0:T(8,128)(2,1)S(1)} %get-tuple-element.14), channel_id=1, source_target_pairs={{0,192},{64,128},{128,64},{192,0},{1,193},{65,129},{129,65},{193,1... | collective-permute-start | bytes 589832 | tf_op jit(solution)/shard_map/ppermute | solution.py:80
  159.2 1.9 collective-permute-start.18
  161.1 3.0 %collective-permute-start.17 = (bf16[2,8,6,1024]{3,1,2,0:T(8,128)(2,1)S(1)}, bf16[2,8,6,1024]{3,1,2,0:T(8,128)(2,1)S(1)}, u32[]{:S(2)}, u32[]{:S(2)}) collective-permute-start(bf16[2,8,6,1024]{3,1,2,0:T(8,128)(2,1)S(1)} %get-tuple-element.13), channel_id=1, source_target_pairs={{0,64},{64,0},{128,192},{192,128},{1,65},{65,1},{129,193},{193,129... | collective-permute-start | bytes 589832 | tf_op jit(solution)/shard_map/ppermute | solution.py:80
  164.3 4.0 %collective-permute-start.13 = (bf16[128,512]{0,1:T(8,128)(2,1)S(1)}, bf16[128,512]{0,1:T(8,128)(2,1)S(1)}, u32[]{:S(2)}, u32[]{:S(2)}) collective-permute-start(bf16[128,512]{0,1:T(8,128)(2,1)S(1)} %bitcast.200), channel_id=1, source_target_pairs={{0,8},{8,0},{1,9},{9,1},{2,10},{10,2},{3,11},{11,3},{4,12},{12,4},... | collective-permute-start | bytes 393224 | tf_op jit(solution)/shard_map/ppermute | solution.py:23
  168.4 2.3 %collective-permute-start.12 = (bf16[128,512]{0,1:T(8,128)(2,1)S(1)}, bf16[128,512]{0,1:T(8,128)(2,1)S(1)}, u32[]{:S(2)}, u32[]{:S(2)}) collective-permute-start(bf16[128,512]{0,1:T(8,128)(2,1)S(1)} %bitcast.201), channel_id=1, source_target_pairs={{0,4},{4,0},{1,5},{5,1},{2,6},{6,2},{3,7},{7,3},{8,12},{12,8},{9,1... | collective-permute-start | bytes 393224 | tf_op jit(solution)/shard_map/ppermute | solution.py:23
  170.9 2.4 %collective-permute-start.11 = (bf16[128,512]{0,1:T(8,128)(2,1)S(1)}, bf16[128,512]{0,1:T(8,128)(2,1)S(1)}, u32[]{:S(2)}, u32[]{:S(2)}) collective-permute-start(bf16[128,512]{0,1:T(8,128)(2,1)S(1)} %bitcast.203), channel_id=1, source_target_pairs={{0,2},{2,0},{1,3},{3,1},{4,6},{6,4},{5,7},{7,5},{8,10},{10,8},{9,1... | collective-permute-start | bytes 393224 | tf_op jit(solution)/shard_map/ppermute | solution.py:23
  173.4 4.1 %collective-permute-done.18 = bf16[2,8,6,1024]{3,1,2,0:T(8,128)(2,1)S(1)} collective-permute-done((bf16[2,8,6,1024]{3,1,2,0:T(8,128)(2,1)S(1)}, bf16[2,8,6,1024]{3,1,2,0:T(8,128)(2,1)S(1)}, u32[]{:S(2)}, u32[]{:S(2)}) %collective-permute-start.18) | collective-permute-done | bytes 196640 | tf_op jit(solution)/shard_map/ppermute | solution.py:80
  177.5 11.2 %collective-permute-start.10 = (bf16[128,512]{0,1:T(8,128)(2,1)S(1)}, bf16[128,512]{0,1:T(8,128)(2,1)S(1)}, u32[]{:S(2)}, u32[]{:S(2)}) collective-permute-start(bf16[128,512]{0,1:T(8,128)(2,1)S(1)} %bitcast.202), channel_id=1, source_target_pairs={{0,1},{1,0},{2,3},{3,2},{4,5},{5,4},{6,7},{7,6},{8,9},{9,8},{10,11... | collective-permute-start | bytes 393224 | tf_op jit(solution)/shard_map/ppermute | solution.py:23
  188.9 6.6 %collective-permute-start.20 = (bf16[8,6,1024]{2,0,1:T(8,128)(2,1)S(1)}, bf16[8,6,1024]{2,0,1:T(8,128)(2,1)S(1)}, u32[]{:S(2)}, u32[]{:S(2)}) collective-permute-start(bf16[8,6,1024]{2,0,1:T(8,128)(2,1)S(1)} %dynamic-slice_bitcast_fusion.3), channel_id=1, source_target_pairs={{0,256},{256,0},{1,257},{257,1},{2,258},{258,2},{3,259},{259,3},{4... | collective-permute-start | bytes 294920 | tf_op jit(solution)/shard_map/ppermute | solution.py:86
  196.3 5.6 %collective-permute-done.20 = bf16[8,6,1024]{2,0,1:T(8,128)(2,1)S(1)} collective-permute-done((bf16[8,6,1024]{2,0,1:T(8,128)(2,1)S(1)}, bf16[8,6,1024]{2,0,1:T(8,128)(2,1)S(1)}, u32[]{:S(2)}, u32[]{:S(2)}) %collective-permute-start.20) | collective-permute-done | bytes 98336 | tf_op jit(solution)/shard_map/ppermute | solution.py:86
  (97 shorter events, 13.6 us)
Async XLA Ops:
  1.5 31.8 %collective-permute-start.4 = (bf16[1,6,8,512]{3,2,1,0:T(8,128)(2,1)S(1)}, bf16[1,6,8,512]{3,2,1,0:T(8,128)(2,1)S(1)}, u32[]{:S(2)}, u32[]{:S(2)}) collective-permute-start(bf16[1,6,8,512]{3,2,1,0:T(8,128)(2,1)S(1)} %get-tuple-element.27), channel_id=1, source_target_pairs={{0,256},{64,320},{128,384},{192,448},{256,0},{320,64},{384,128},{4... | collective-permute-start | bytes 147464 | tf_op jit(solution)/shard_map/ppermute | solution.py:46
  11.1 61.2 %collective-permute-start = (bf16[128,512]{1,0:T(8,128)(2,1)}, bf16[128,512]{1,0:T(8,128)(2,1)S(1)}, u32[]{:S(2)}, u32[]{:S(2)}) collective-permute-start(bf16[128,512]{1,0:T(8,128)(2,1)} %param.4), channel_id=1, source_target_pairs={{0,1},{1,0},{2,3},{3,2},{4,5},{5,4},{6,7},{7,6},{8,9},{9,8},{10,11... | collective-permute-start | bytes 393224 | tf_op jit(solution)/shard_map/ppermute | solution.py:23
  14.0 58.5 %collective-permute-start.1 = (bf16[128,512]{1,0:T(8,128)(2,1)}, bf16[128,512]{1,0:T(8,128)(2,1)}, u32[]{:S(2)}, u32[]{:S(2)}) collective-permute-start(bf16[128,512]{1,0:T(8,128)(2,1)} %param.4), channel_id=1, source_target_pairs={{0,2},{2,0},{1,3},{3,1},{4,6},{6,4},{5,7},{7,5},{8,10},{10,8},{9,1... | collective-permute-start | bytes 393224 | tf_op jit(solution)/shard_map/ppermute | solution.py:23
  17.2 56.3 %collective-permute-start.2 = (bf16[128,512]{1,0:T(8,128)(2,1)}, bf16[128,512]{1,0:T(8,128)(2,1)S(1)}, u32[]{:S(2)}, u32[]{:S(2)}) collective-permute-start(bf16[128,512]{1,0:T(8,128)(2,1)} %param.4), channel_id=1, source_target_pairs={{0,4},{4,0},{1,5},{5,1},{2,6},{6,2},{3,7},{7,3},{8,12},{12,8},{9,1... | collective-permute-start | bytes 393224 | tf_op jit(solution)/shard_map/ppermute | solution.py:23
  21.7 51.9 %collective-permute-start.3 = (bf16[128,512]{1,0:T(8,128)(2,1)}, bf16[128,512]{1,0:T(8,128)(2,1)S(1)}, u32[]{:S(2)}, u32[]{:S(2)}) collective-permute-start(bf16[128,512]{1,0:T(8,128)(2,1)} %param.4), channel_id=1, source_target_pairs={{0,8},{8,0},{1,9},{9,1},{2,10},{10,2},{3,11},{11,3},{4,12},{12,4},... | collective-permute-start | bytes 393224 | tf_op jit(solution)/shard_map/ppermute | solution.py:23
  33.3 17.6 %collective-permute-start.5 = (bf16[2,1,6,8,512]{4,3,2,0,1:T(8,128)(2,1)S(1)}, bf16[2,1,6,8,512]{4,3,2,0,1:T(8,128)(2,1)S(1)}, u32[]{:S(2)}, u32[]{:S(2)}) collective-permute-start(bf16[2,1,6,8,512]{4,3,2,0,1:T(8,128)(2,1)S(1)} %maximum_select_fusion.5), channel_id=1, source_target_pairs={{0,128},{64,192},{128,0},{192,64},{256,384},{320,448},{384,256},{4... | collective-permute-start | bytes 294920 | tf_op jit(solution)/shard_map/ppermute | solution.py:46
  50.9 7.9 %collective-permute-start.6 = (bf16[2,2,1,6,8,512]{5,4,3,1,2,0:T(8,128)(2,1)S(1)}, bf16[2,2,1,6,8,512]{5,4,3,1,2,0:T(8,128)(2,1)S(1)}, u32[]{:S(2)}, u32[]{:S(2)}) collective-permute-start(bf16[2,2,1,6,8,512]{5,4,3,1,2,0:T(8,128)(2,1)S(1)} %bitcast_select_fusion), channel_id=1, source_target_pairs={{0,64},{64,0},{128,192},{192,128},{256,320},{320,256},{384,448},{4... | collective-permute-start | bytes 589832 | tf_op jit(solution)/shard_map/ppermute | solution.py:46
  58.8 11.6 %collective-permute-start.7 = (bf16[1,6,8,512]{3,2,1,0:T(8,128)(2,1)S(1)}, bf16[1,6,8,512]{3,2,1,0:T(8,128)(2,1)S(1)}, u32[]{:S(2)}, u32[]{:S(2)}) collective-permute-start(bf16[1,6,8,512]{3,2,1,0:T(8,128)(2,1)S(1)} %get-tuple-element.26), channel_id=1, source_target_pairs={{0,256},{64,320},{128,384},{192,448},{256,0},{320,64},{384,128},{4... | collective-permute-start | bytes 147464 | tf_op jit(solution)/shard_map/ppermute | solution.py:46
  63.6 4.8 %copy-start.10 = (bf16[128,512]{1,0:T(8,128)(2,1)S(1)}, bf16[128,512]{1,0:T(8,128)(2,1)}, u32[]{:S(2)}) copy-start(bf16[128,512]{1,0:T(8,128)(2,1)} %param.4) | copy-start | bytes 393220
  63.6 23.0 %all-to-all-start = ((bf16[4,8,6,8,512]{4,3,1,2,0:T(8,128)(2,1)}), bf16[4,8,6,8,512]{4,3,1,2,0:T(8,128)(2,1)S(1)}, u32[]{:S(2)}, u32[]{:S(2)}) async-start(bf16[4,8,6,8,512]{4,3,1,2,0:T(8,128)(2,1)} %broadcast_in_dim.32), calls=%async_computation | async-start | bytes 3145728 | tf_op jit(solution)/shard_map/all_to_all | solution.py:59
  70.4 8.2 %collective-permute-start.8 = (bf16[2,1,6,8,512]{4,3,2,0,1:T(8,128)(2,1)S(1)}, bf16[2,1,6,8,512]{4,3,2,0,1:T(8,128)(2,1)S(1)}, u32[]{:S(2)}, u32[]{:S(2)}) collective-permute-start(bf16[2,1,6,8,512]{4,3,2,0,1:T(8,128)(2,1)S(1)} %fusion.32), channel_id=1, source_target_pairs={{0,128},{64,192},{128,0},{192,64},{256,384},{320,448},{384,256},{4... | collective-permute-start | bytes 294920 | tf_op jit(solution)/shard_map/ppermute | solution.py:46
  78.6 7.5 %collective-permute-start.9 = (bf16[2,2,1,6,8,512]{5,4,3,1,0,2:T(8,128)(2,1)S(1)}, bf16[2,2,1,6,8,512]{5,4,3,1,0,2:T(8,128)(2,1)S(1)}, u32[]{:S(2)}, u32[]{:S(2)}) collective-permute-start(bf16[2,2,1,6,8,512]{5,4,3,1,0,2:T(8,128)(2,1)S(1)} %maximum_select_fusion.3), channel_id=1, source_target_pairs={{0,64},{64,0},{128,192},{192,128},{256,320},{320,256},{384,448},{4... | collective-permute-start | bytes 589832 | tf_op jit(solution)/shard_map/ppermute | solution.py:46
  80.5 5.6 %copy-start.5 = (bf16[128,2,6,256]{0,3,2,1:T(8,128)(2,1)}, bf16[128,2,6,256]{0,3,2,1:T(8,128)(2,1)S(1)}, u32[]{:S(2)}) copy-start(bf16[128,2,6,256]{0,3,2,1:T(8,128)(2,1)S(1)} %constant_dynamic-update-slice_fusion.1) | copy-start | bytes 2359300
  88.0 21.6 %all-to-all-start.1 = ((bf16[4,8,6,8,512]{4,3,1,2,0:T(8,128)(2,1)}), bf16[4,8,6,8,512]{4,3,1,2,0:T(8,128)(2,1)S(1)}, u32[]{:S(2)}, u32[]{:S(2)}) async-start(bf16[4,8,6,8,512]{4,3,1,2,0:T(8,128)(2,1)} %broadcast_in_dim.36), calls=%async_computation.1 | async-start | bytes 3145728 | tf_op jit(solution)/shard_map/all_to_all | solution.py:59
  93.4 0.8 copy-start.2
  104.2 1.0 copy-start.3
  105.6 5.0 %copy-start.8 = (f32[128,512]{1,0:T(8,128)}, f32[128,512]{1,0:T(8,128)S(1)}, u32[]{:S(2)}) copy-start(f32[128,512]{1,0:T(8,128)S(1)} %fusion.39) | copy-start | bytes 786436
  110.1 1.0 copy-start.6
  110.1 1.0 copy-start.12
  110.1 1.1 copy-start.13
  110.5 1.3 copy-start.7
  110.5 1.3 copy-start.11
  112.6 2.0 copy-start
  112.6 11.0 %copy-start.4 = (bf16[6,256,512]{2,1,0:T(8,128)(2,1)S(1)}, bf16[6,256,512]{2,1,0:T(8,128)(2,1)}, u32[]{:S(2)}) copy-start(bf16[6,256,512]{2,1,0:T(8,128)(2,1)} %bitcast_multiply_fusion.1) | copy-start | bytes 4718596
  112.6 11.0 %copy-start.9 = (f32[128,512]{1,0:T(8,128)S(1)}, f32[128,512]{1,0:T(8,128)}, u32[]{:S(2)}) copy-start(f32[128,512]{1,0:T(8,128)} %copy-done.8) | copy-start | bytes 786436
  114.5 36.6 %collective-permute-start.16 = (bf16[8,8,6,1024]{3,1,2,0:T(8,128)(2,1)}, bf16[8,8,6,1024]{3,1,2,0:T(8,128)(2,1)}, u32[]{:S(2)}, u32[]{:S(2)}) collective-permute-start(bf16[8,8,6,1024]{3,1,2,0:T(8,128)(2,1)} %get-tuple-element.12), channel_id=1, source_target_pairs={{0,48},{16,32},{32,16},{48,0},{1,49},{17,33},{33,17},{49,1},{2,50}... | collective-permute-start | bytes 2359304 | tf_op jit(solution)/shard_map/ppermute | solution.py:70
  117.3 33.8 %collective-permute-start.15 = (bf16[8,8,6,1024]{3,1,2,0:T(8,128)(2,1)}, bf16[8,8,6,1024]{3,1,2,0:T(8,128)(2,1)}, u32[]{:S(2)}, u32[]{:S(2)}) collective-permute-start(bf16[8,8,6,1024]{3,1,2,0:T(8,128)(2,1)} %get-tuple-element.11), channel_id=1, source_target_pairs={{0,32},{16,48},{32,0},{48,16},{1,33},{17,49},{33,1},{49,17},{2,34}... | collective-permute-start | bytes 2359304 | tf_op jit(solution)/shard_map/ppermute | solution.py:70
  120.4 32.1 %collective-permute-start.14 = (bf16[8,8,6,1024]{3,1,2,0:T(8,128)(2,1)}, bf16[8,8,6,1024]{3,1,2,0:T(8,128)(2,1)}, u32[]{:S(2)}, u32[]{:S(2)}) collective-permute-start(bf16[8,8,6,1024]{3,1,2,0:T(8,128)(2,1)} %get-tuple-element.10), channel_id=1, source_target_pairs={{0,16},{16,0},{32,48},{48,32},{1,17},{17,1},{33,49},{49,33},{2,18}... | collective-permute-start | bytes 2359304 | tf_op jit(solution)/shard_map/ppermute | solution.py:70
  126.7 25.9 %copy-start.1 = (bf16[4,8,8,6,512]{4,2,3,1,0:T(8,128)(2,1)S(1)}, bf16[4,8,8,6,512]{4,2,3,1,0:T(8,128)(2,1)}, u32[]{:S(2)}) copy-start(bf16[4,8,8,6,512]{4,2,3,1,0:T(8,128)(2,1)} %copy-done) | copy-start | bytes 4718596
  154.8 16.1 %collective-permute-start.19 = (bf16[2,8,6,1024]{3,1,2,0:T(8,128)(2,1)S(1)}, bf16[2,8,6,1024]{3,1,2,0:T(8,128)(2,1)S(1)}, u32[]{:S(2)}, u32[]{:S(2)}) collective-permute-start(bf16[2,8,6,1024]{3,1,2,0:T(8,128)(2,1)S(1)} %get-tuple-element.14), channel_id=1, source_target_pairs={{0,192},{64,128},{128,64},{192,0},{1,193},{65,129},{129,65},{193,1... | collective-permute-start | bytes 589832 | tf_op jit(solution)/shard_map/ppermute | solution.py:80
  159.2 18.3 %collective-permute-start.18 = (bf16[2,8,6,1024]{3,1,2,0:T(8,128)(2,1)S(1)}, bf16[2,8,6,1024]{3,1,2,0:T(8,128)(2,1)S(1)}, u32[]{:S(2)}, u32[]{:S(2)}) collective-permute-start(bf16[2,8,6,1024]{3,1,2,0:T(8,128)(2,1)S(1)} %get-tuple-element.15), channel_id=1, source_target_pairs={{0,128},{64,192},{128,0},{192,64},{1,129},{65,193},{129,1},{193,65... | collective-permute-start | bytes 589832 | tf_op jit(solution)/shard_map/ppermute | solution.py:80
  161.1 27.6 %collective-permute-start.17 = (bf16[2,8,6,1024]{3,1,2,0:T(8,128)(2,1)S(1)}, bf16[2,8,6,1024]{3,1,2,0:T(8,128)(2,1)S(1)}, u32[]{:S(2)}, u32[]{:S(2)}) collective-permute-start(bf16[2,8,6,1024]{3,1,2,0:T(8,128)(2,1)S(1)} %get-tuple-element.13), channel_id=1, source_target_pairs={{0,64},{64,0},{128,192},{192,128},{1,65},{65,1},{129,193},{193,129... | collective-permute-start | bytes 589832 | tf_op jit(solution)/shard_map/ppermute | solution.py:80
  164.3 31.2 %collective-permute-start.13 = (bf16[128,512]{0,1:T(8,128)(2,1)S(1)}, bf16[128,512]{0,1:T(8,128)(2,1)S(1)}, u32[]{:S(2)}, u32[]{:S(2)}) collective-permute-start(bf16[128,512]{0,1:T(8,128)(2,1)S(1)} %bitcast.200), channel_id=1, source_target_pairs={{0,8},{8,0},{1,9},{9,1},{2,10},{10,2},{3,11},{11,3},{4,12},{12,4},... | collective-permute-start | bytes 393224 | tf_op jit(solution)/shard_map/ppermute | solution.py:23
  168.4 27.0 %collective-permute-start.12 = (bf16[128,512]{0,1:T(8,128)(2,1)S(1)}, bf16[128,512]{0,1:T(8,128)(2,1)S(1)}, u32[]{:S(2)}, u32[]{:S(2)}) collective-permute-start(bf16[128,512]{0,1:T(8,128)(2,1)S(1)} %bitcast.201), channel_id=1, source_target_pairs={{0,4},{4,0},{1,5},{5,1},{2,6},{6,2},{3,7},{7,3},{8,12},{12,8},{9,1... | collective-permute-start | bytes 393224 | tf_op jit(solution)/shard_map/ppermute | solution.py:23
  170.9 24.5 %collective-permute-start.11 = (bf16[128,512]{0,1:T(8,128)(2,1)S(1)}, bf16[128,512]{0,1:T(8,128)(2,1)S(1)}, u32[]{:S(2)}, u32[]{:S(2)}) collective-permute-start(bf16[128,512]{0,1:T(8,128)(2,1)S(1)} %bitcast.203), channel_id=1, source_target_pairs={{0,2},{2,0},{1,3},{3,1},{4,6},{6,4},{5,7},{7,5},{8,10},{10,8},{9,1... | collective-permute-start | bytes 393224 | tf_op jit(solution)/shard_map/ppermute | solution.py:23
  177.5 18.0 %collective-permute-start.10 = (bf16[128,512]{0,1:T(8,128)(2,1)S(1)}, bf16[128,512]{0,1:T(8,128)(2,1)S(1)}, u32[]{:S(2)}, u32[]{:S(2)}) collective-permute-start(bf16[128,512]{0,1:T(8,128)(2,1)S(1)} %bitcast.202), channel_id=1, source_target_pairs={{0,1},{1,0},{2,3},{3,2},{4,5},{5,4},{6,7},{7,6},{8,9},{9,8},{10,11... | collective-permute-start | bytes 393224 | tf_op jit(solution)/shard_map/ppermute | solution.py:23
  188.9 13.1 %collective-permute-start.20 = (bf16[8,6,1024]{2,0,1:T(8,128)(2,1)S(1)}, bf16[8,6,1024]{2,0,1:T(8,128)(2,1)S(1)}, u32[]{:S(2)}, u32[]{:S(2)}) collective-permute-start(bf16[8,6,1024]{2,0,1:T(8,128)(2,1)S(1)} %dynamic-slice_bitcast_fusion.3), channel_id=1, source_target_pairs={{0,256},{256,0},{1,257},{257,1},{2,258},{258,2},{3,259},{259,3},{4... | collective-permute-start | bytes 294920 | tf_op jit(solution)/shard_map/ppermute | solution.py:86
